TPU v7x, 32 devices: a whole 2x2x4 slice. The times are simulated.
32 devices in a mesh: grp: 2 (over x), slab: 16 (over z, y, core).
Axes of the slice: x: 2, y: 2, z: 4, core: 2. Of those that a mesh axis runs over, the one named last changes fastest.
Arguments:
- volume: bfloat16 [32, 64, 16, 256], P(None, ('grp', 'slab')), parts along dimension 1, may hold values from -6 to 6
- weight_one: bfloat16 [27, 32, 32], replicated, may hold values from -0.21875 to 0.21875
- weight_two: bfloat16 [27, 32, 32], replicated, may hold values from -0.21875 to 0.21875
- cotangent: bfloat16 [32, 32, 8, 128], P(None, ('grp', 'slab')), parts along dimension 1, may hold values from -6 to 6
Outputs:
- output: bfloat16 [32, 32, 8, 128], P(None, ('grp', 'slab')), parts along dimension 1
- grad_volume: bfloat16 [32, 64, 16, 256], P(None, ('grp', 'slab')), parts along dimension 1
- grad_one: float32 [54, 32, 32], P('grp'), parts along dimension 0
- grad_two: float32 [54, 32, 32], P('grp'), parts along dimension 0
There are 2 independent parts, one for each index of `grp`. A program takes and returns all parts, laid end to end along the dimension named above; an argument that names none is the same for every part. Nothing has to cross between parts.
All inputs are finite; a program needn't handle non-finite values.
Results may differ from a plain program's by a relative error of at most 0.0051.
Values may be sent and summed in bfloat16 or wider, within the bound.
No kernel may reach another device: no remote copies, remote signals or barrier semaphores. Data moves between devices by JAX's collectives and lax.ppermute only.
A program may use at most 64 MiB of HBM per device.

v0:
```python
import jax
import jax.numpy as jnp
from jax import lax
from jax.sharding import PartitionSpec as P


def extended_2(shard, sides, width):
    for axis, dim in sides:
        devices, length = (lax.axis_size(axis), shard.shape[dim])
        up = [(i, (i + 1) % devices) for i in range(devices - 1)]
        down = [(j, i) for i, j in up]
        last = lax.slice_in_dim(shard, length - width, length, axis=dim)
        initial = lax.slice_in_dim(shard, 0, width, axis=dim)
        before = lax.ppermute(last, axis, up)
        after = lax.ppermute(initial, axis, down)
        shard = jnp.concatenate([before, shard, after], axis=dim)
    return shard


def passed_along(block, axis, distance):
    devices = range(lax.axis_size(axis))
    route = [(i - distance, i) for i in devices if i - distance in devices]
    return lax.ppermute(block, axis, route)


def pad_sides(field):
    return jnp.pad(field, ((0, 0), (0, 0), (1, 1), (1, 1)))


def column_stack(field, stride, count, start):
    pieces = []
    for along_cols in range(3):
        first = start(along_cols)
        pieces.append(field[..., first : first + stride * (count - 1) + 1 : stride])
    return jnp.concatenate(pieces, 0)


def forward_kernel(weights):
    size = weights.shape[1]
    return (
        weights.reshape(3, 3, 3, size, size).transpose(0, 1, 3, 2, 4).reshape(3, 3, size, 3 * size)
    )


def backward_kernel(weights):
    size = weights.shape[1]
    return weights.reshape(3, 3, 3 * size, size)


def fold_term(term):
    size = term.shape[0]
    return term.reshape(size, 3, size).transpose(1, 0, 2)


def gather_terms(listed):
    stacked = jnp.stack(listed)
    return stacked.reshape(27, stacked.shape[2], stacked.shape[3])


def on_device(volume, weight_one, weight_two, cotangent):
    channels, planes, height, columns = volume.shape
    half_planes = planes // 2
    half_rows = height // 2
    half_cols = columns // 2
    front_one = forward_kernel(weight_one)
    front_two = forward_kernel(weight_two)
    rear_one = backward_kernel(weight_one)
    padded = pad_sides(extended_2(volume, (("slab", 1),), 1))
    volume_cols = column_stack(padded, 1, columns, lambda along_cols: along_cols)
    preact = jnp.zeros((channels, planes, height, columns), jnp.float32)
    for along_depth in range(3):
        for along_rows in range(3):
            window = volume_cols[
                :, along_depth : along_depth + planes, along_rows : along_rows + height, :
            ]
            preact = preact + jnp.einsum(
                "ok,kdhw->odhw",
                front_one[along_depth, along_rows],
                window,
                preferred_element_type=jnp.float32,
            )
    hidden = jax.nn.silu(preact).astype(jnp.bfloat16)
    upper_plane = passed_along(cotangent, "slab", -1)
    lower_plane = passed_along(hidden[:, planes - 1 :], "slab", 1)
    stacked = pad_sides(jnp.concatenate([lower_plane, hidden], 1))
    hidden_cols = column_stack(stacked, 2, half_cols, lambda along_cols: along_cols)
    output = jnp.zeros((channels, half_planes, half_rows, half_cols), jnp.float32)
    terms_two = []
    for along_depth in range(3):
        for along_rows in range(3):
            window = hidden_cols[
                :,
                along_depth : along_depth + planes - 1 : 2,
                along_rows : along_rows + height - 1 : 2,
                :,
            ]
            output = output + jnp.einsum(
                "ok,kdhw->odhw",
                front_two[along_depth, along_rows],
                window,
                preferred_element_type=jnp.float32,
            )
            terms_two.append(
                fold_term(
                    jnp.einsum(
                        "odhw,kdhw->ok", cotangent, window, preferred_element_type=jnp.float32
                    )
                )
            )
    extended = jnp.concatenate([cotangent, upper_plane], 1)
    extended = jnp.pad(extended, ((0, 0), (0, 0), (0, 1), (0, 1)))
    parity_taps = [[(1, 0)], [(2, 0), (0, 1)]]
    classes = []
    for depth_parity in range(2):
        for row_parity in range(2):
            for col_parity in range(2):
                pieces = []
                kernels = []
                for tap_depth, skip_depth in parity_taps[depth_parity]:
                    for tap_row, skip_row in parity_taps[row_parity]:
                        for tap_col, skip_col in parity_taps[col_parity]:
                            pieces.append(
                                extended[
                                    :,
                                    skip_depth : skip_depth + half_planes,
                                    skip_row : skip_row + half_rows,
                                    skip_col : skip_col + half_cols,
                                ]
                            )
                            kernels.append(weight_two[9 * tap_depth + 3 * tap_row + tap_col])
                joined = jnp.concatenate(pieces, 0)
                joined_kernel = jnp.concatenate(kernels, 0)
                classes.append(
                    jnp.einsum(
                        "kq,kdhw->qdhw", joined_kernel, joined, preferred_element_type=jnp.float32
                    )
                )
    parity_grid = jnp.stack(classes).reshape(2, 2, 2, channels, half_planes, half_rows, half_cols)
    grad_hidden = parity_grid.transpose(3, 4, 0, 5, 1, 6, 2).reshape(
        channels, planes, height, columns
    )
    sigma = jax.nn.sigmoid(preact)
    grad_pre = (grad_hidden * (sigma * (1.0 + preact * (1.0 - sigma)))).astype(jnp.bfloat16)
    rimmed = pad_sides(extended_2(grad_pre, (("slab", 1),), 1))
    rimmed_cols = column_stack(rimmed, 1, columns, lambda along_cols: 2 - along_cols)
    grad_volume = jnp.zeros((channels, planes, height, columns), jnp.float32)
    terms_one = []
    for along_depth in range(3):
        for along_rows in range(3):
            window = volume_cols[
                :, along_depth : along_depth + planes, along_rows : along_rows + height, :
            ]
            terms_one.append(
                fold_term(
                    jnp.einsum(
                        "odhw,kdhw->ok", grad_pre, window, preferred_element_type=jnp.float32
                    )
                )
            )
            back_window = rimmed_cols[
                :,
                2 - along_depth : 2 - along_depth + planes,
                2 - along_rows : 2 - along_rows + height,
                :,
            ]
            grad_volume = grad_volume + jnp.einsum(
                "kq,kdhw->qdhw",
                rear_one[along_depth, along_rows],
                back_window,
                preferred_element_type=jnp.float32,
            )
    grad_one, grad_two = lax.psum((gather_terms(terms_one), gather_terms(terms_two)), "slab")
    return (output.astype(jnp.bfloat16), grad_volume.astype(jnp.bfloat16), grad_one, grad_two)


def solution(mesh):
    in_specs = (
        P(None, ("grp", "slab"), None, None),
        P(),
        P(),
        P(None, ("grp", "slab"), None, None),
    )
    out_specs = (
        P(None, ("grp", "slab"), None, None),
        P(None, ("grp", "slab"), None, None),
        P("grp", None, None),
        P("grp", None, None),
    )
    return jax.shard_map(
        on_device, mesh=mesh, in_specs=in_specs, out_specs=out_specs, check_vma=False
    )
```

profile of v0, /device:TPU:0, one launch (start us, length us, event | category | flops | bytes accessed | tf_op | source)
XLA Modules:
  0.0 246.7 jit_solution(13429199726997256875)
XLA Ops:
  7.2 0.9 constant_dynamic-update-slice_fusion.7
  8.2 1.3 collective-permute-start.3
  9.5 1.3 copy.148
  10.8 0.7 fusion.263
  11.6 3.7 %collective-permute-start = (bf16[32,1,16,256]{3,0,2,1:T(8,128)(2,1)}, bf16[32,1,16,256]{3,0,2,1:T(8,128)(2,1)}, u32[]{:S(2)}, u32[]{:S(2)}) collective-permute-start(bf16[32,1,16,256]{3,0,2,1:T(8,128)(2,1)} %get-tuple-element.37), channel_id=1, source_target_pairs={{0,1},{1,2},{2,3},{3,4},{4,5},{5,6},{6,7},{7,8},{8,9},{9,10},{10,1... | collective-permute-start | bytes 786440 | tf_op jit(solution)/shard_map/ppermute | solution.py:14
  15.3 1.3 collective-permute-start.1
  19.7 0.8 reshape.196
  21.8 0.2 fusion.126
  22.2 0.2 fusion.124
  22.5 0.2 fusion.123
  22.7 4.4 %copy.190 = f32[2,2,2,32,1,8,128]{3,2,6,1,5,0,4:T(2,128)} copy(f32[2,2,2,32,1,8,128]{6,3,5,2,1,0,4:T(8,128)S(1)} %bitcast.531) | data formatting | bytes 2097152 | tf_op jit(solution)/shard_map/reshape | solution.py:138
  27.1 2.8 %copy.191 = f32[32,2,16,256]{3,0,2,1:T(8,128)S(1)} copy(f32[32,2,16,256]{0,3,2,1:T(8,128)} %bitcast.519) | data formatting | bytes 2097152 | tf_op jit(solution)/shard_map/reshape | solution.py:139
  29.9 2.1 select_maximum_fusion.2
  32.0 0.9 fusion.260
  32.9 0.3 pad_maximum_fusion
  33.2 0.3 fusion.29
  33.5 0.3 fusion.33
  33.9 0.3 fusion.37
  34.2 0.3 fusion.41
  34.6 0.3 fusion.45
  34.9 0.3 fusion.49
  35.3 0.3 fusion.53
  35.6 0.3 fusion.57
  36.0 0.9 multiply_convert_fusion
  36.9 0.6 fusion.157
  37.5 0.7 fusion.154
  38.2 0.7 fusion.151
  38.8 0.7 fusion.148
  39.5 0.7 fusion.145
  40.1 0.7 fusion.142
  40.8 0.7 fusion.160
  41.5 0.7 fusion.163
  42.1 0.7 fusion.166
  42.8 4.5 %collective-permute-start.2 = (bf16[32,1,16,256]{3,0,2,1:T(8,128)(2,1)S(1)}, bf16[32,1,16,256]{3,0,2,1:T(8,128)(2,1)S(1)}, u32[]{:S(2)}, u32[]{:S(2)}) collective-permute-start(bf16[32,1,16,256]{3,0,2,1:T(8,128)(2,1)S(1)} %slice.469), channel_id=1, source_target_pairs={{0,1},{1,2},{2,3},{3,4},{4,5},{5,6},{6,7},{7,8},{8,9},{9,10},{10,1... | collective-permute-start | bytes 786440 | tf_op jit(solution)/shard_map/ppermute | solution.py:23
  48.4 0.8 copy.202
  49.2 4.3 %collective-permute-start.4 = (bf16[32,1,16,256]{3,0,2,1:T(8,128)(2,1)S(1)}, bf16[32,1,16,256]{3,0,2,1:T(8,128)(2,1)}, u32[]{:S(2)}, u32[]{:S(2)}) collective-permute-start(bf16[32,1,16,256]{3,0,2,1:T(8,128)(2,1)S(1)} %get-tuple-element.35), channel_id=1, source_target_pairs={{0,1},{1,2},{2,3},{3,4},{4,5},{5,6},{6,7},{7,8},{8,9},{9,10},{10,1... | collective-permute-start | bytes 786440 | tf_op jit(solution)/shard_map/ppermute | solution.py:14
  53.6 1.5 collective-permute-start.5
  55.1 0.7 fusion.115
  55.8 18.8 %slice.368 = bf16[32,3,18,128]{3,0,2,1:T(8,128)(2,1)} slice(bf16[32,3,18,258]{3,0,2,1:T(8,128)(2,1)S(1)} %fusion.115), slice={[0:32:1], [0:3:1], [0:18:1], [0:255:2]} | slice | bytes 884736 | tf_op jit(solution)/shard_map/slice | solution.py:34
  74.6 18.8 %slice.369 = bf16[32,3,18,128]{3,0,2,1:T(8,128)(2,1)} slice(bf16[32,3,18,258]{3,0,2,1:T(8,128)(2,1)S(1)} %fusion.115), slice={[0:32:1], [0:3:1], [0:18:1], [1:256:2]} | slice | bytes 884736 | tf_op jit(solution)/shard_map/slice | solution.py:34
  93.4 19.2 %slice.370 = bf16[32,3,18,128]{3,0,2,1:T(8,128)(2,1)} slice(bf16[32,3,18,258]{3,0,2,1:T(8,128)(2,1)S(1)} %fusion.115), slice={[0:32:1], [0:3:1], [0:18:1], [2:257:2]} | slice | bytes 884736 | tf_op jit(solution)/shard_map/slice | solution.py:34
  112.7 2.1 select_maximum_fusion
  114.8 0.9 fusion.259
  115.7 0.5 pad_maximum_fusion.1
  116.2 0.4 copy-done.9
  116.6 1.4 fusion.11
  118.0 1.4 fusion.13
  119.4 1.4 fusion.15
  120.7 1.4 fusion.17
  122.1 1.4 fusion.19
  123.5 1.4 fusion.21
  124.9 1.4 fusion.7
  126.2 1.4 fusion.9
  127.7 0.2 fusion.261
  128.0 0.8 copy-done
  130.6 0.8 copy-done.10
  131.3 2.0 copy.212
  133.3 4.2 %fusion.120 = bf16[32,2,16,256]{3,0,2,1:T(8,128)(2,1)S(1)} fusion(f32[2,16,256,32]{2,3,1,0:T(8,128)} %fusion.7, f32[2,16,256,32]{2,3,1,0:T(8,128)} %fusion.9, f32[2,16,256,32]{2,3,1,0:T(8,128)} %fusion.11, f32[2,16,256,32]{2,3,1,0:T(8,128)} %fusion.13, f32[2,16,256,32]{2,3,1,0:T(8,128)} %fusion.15, f32[2,16,256,32]{2,3,1,0:T(8,128)} %fusion.17, ...), kind=kOutput, calls=%fused_computation.99 | convolution fusion | flops 52690944 | bytes 10510336 | tf_op jit(solution)/shard_map/kq,kdhw->qdhw/dot_general | solution.py:166
  137.5 1.1 copy.214
  139.8 1.1 fusion.132
  141.0 0.7 copy.213
  141.6 94.6 %all-reduce.7.cloned.1.call-done = (f32[27,32,32]{2,1,0:T(8,128)}, f32[27,32,32]{2,1,0:T(8,128)}) async-done(((f32[27,32,32]{2,1,0:T(8,128)}, f32[27,32,32]{2,1,0:T(8,128)}), (f32[27,32,32]{2,1,0:T(8,128)}, f32[27,32,32]{2,1,0:T(8,128)})) %all-reduce.7.cloned.1.call-update) | async-done | bytes 221200 | tf_op jit(solution)/shard_map/psum | solution.py:172
  236.3 1.8 copy.373
  238.1 1.8 copy.374
  (112 shorter events, 8.6 us)
Async XLA Ops:
  7.2 9.5 %copy-start.2 = (bf16[32,1,8,128]{3,2,1,0:T(8,128)(2,1)S(1)}, bf16[32,1,8,128]{3,2,1,0:T(8,128)(2,1)}, u32[]{:S(2)}) copy-start(bf16[32,1,8,128]{3,2,1,0:T(8,128)(2,1)} %param.7) | copy-start | bytes 196612
  7.2 9.4 %copy-start.7 = (bf16[27,32,32]{2,1,0:T(8,128)(2,1)S(1)}, bf16[27,32,32]{2,1,0:T(8,128)(2,1)}, u32[]{:S(2)}) copy-start(bf16[27,32,32]{2,1,0:T(8,128)(2,1)} %param.6) | copy-start | bytes 165892
  7.2 12.0 %copy-start.8 = (bf16[27,32,32]{2,1,0:T(8,128)(2,1)S(1)}, bf16[27,32,32]{2,1,0:T(8,128)(2,1)}, u32[]{:S(2)}) copy-start(bf16[27,32,32]{2,1,0:T(8,128)(2,1)} %param.5) | copy-start | bytes 165892
  7.2 229.1 %all-reduce.7.cloned.1.call-start = ((), (), s32[]{:S(2)}) async-start(), calls=%async_computation | async-start | bytes 1769472 | tf_op jit(solution)/shard_map/psum | solution.py:172
  8.2 12.4 %collective-permute-start.3 = (bf16[32,1,8,128]{3,0,2,1:T(8,128)(2,1)S(1)}, bf16[32,1,8,128]{3,0,2,1:T(8,128)(2,1)S(1)}, u32[]{:S(2)}, u32[]{:S(2)}) collective-permute-start(bf16[32,1,8,128]{3,0,2,1:T(8,128)(2,1)S(1)} %get-tuple-element.72), channel_id=1, source_target_pairs={{1,0},{2,1},{3,2},{4,3},{5,4},{6,5},{7,6},{8,7},{9,8},{10,9},{11,1... | collective-permute-start | bytes 196616 | tf_op jit(solution)/shard_map/ppermute | solution.py:23
  11.6 18.3 %collective-permute-start = (bf16[32,1,16,256]{3,0,2,1:T(8,128)(2,1)}, bf16[32,1,16,256]{3,0,2,1:T(8,128)(2,1)}, u32[]{:S(2)}, u32[]{:S(2)}) collective-permute-start(bf16[32,1,16,256]{3,0,2,1:T(8,128)(2,1)} %get-tuple-element.37), channel_id=1, source_target_pairs={{0,1},{1,2},{2,3},{3,4},{4,5},{5,6},{6,7},{7,8},{8,9},{9,10},{10,1... | collective-permute-start | bytes 786440 | tf_op jit(solution)/shard_map/ppermute | solution.py:14
  15.3 14.6 %collective-permute-start.1 = (bf16[32,1,16,256]{3,0,2,1:T(8,128)(2,1)S(1)}, bf16[32,1,16,256]{3,0,2,1:T(8,128)(2,1)}, u32[]{:S(2)}, u32[]{:S(2)}) collective-permute-start(bf16[32,1,16,256]{3,0,2,1:T(8,128)(2,1)S(1)} %get-tuple-element.38), channel_id=1, source_target_pairs={{1,0},{2,1},{3,2},{4,3},{5,4},{6,5},{7,6},{8,7},{9,8},{10,9},{11,1... | collective-permute-start | bytes 786440 | tf_op jit(solution)/shard_map/ppermute | solution.py:15
  42.8 12.2 %collective-permute-start.2 = (bf16[32,1,16,256]{3,0,2,1:T(8,128)(2,1)S(1)}, bf16[32,1,16,256]{3,0,2,1:T(8,128)(2,1)S(1)}, u32[]{:S(2)}, u32[]{:S(2)}) collective-permute-start(bf16[32,1,16,256]{3,0,2,1:T(8,128)(2,1)S(1)} %slice.469), channel_id=1, source_target_pairs={{0,1},{1,2},{2,3},{3,4},{4,5},{5,6},{6,7},{7,8},{8,9},{9,10},{10,1... | collective-permute-start | bytes 786440 | tf_op jit(solution)/shard_map/ppermute | solution.py:23
  49.2 63.4 %collective-permute-start.4 = (bf16[32,1,16,256]{3,0,2,1:T(8,128)(2,1)S(1)}, bf16[32,1,16,256]{3,0,2,1:T(8,128)(2,1)}, u32[]{:S(2)}, u32[]{:S(2)}) collective-permute-start(bf16[32,1,16,256]{3,0,2,1:T(8,128)(2,1)S(1)} %get-tuple-element.35), channel_id=1, source_target_pairs={{0,1},{1,2},{2,3},{3,4},{4,5},{5,6},{6,7},{7,8},{8,9},{9,10},{10,1... | collective-permute-start | bytes 786440 | tf_op jit(solution)/shard_map/ppermute | solution.py:14
  53.6 59.1 %collective-permute-start.5 = (bf16[32,1,16,256]{3,0,2,1:T(8,128)(2,1)S(1)}, bf16[32,1,16,256]{3,0,2,1:T(8,128)(2,1)}, u32[]{:S(2)}, u32[]{:S(2)}) collective-permute-start(bf16[32,1,16,256]{3,0,2,1:T(8,128)(2,1)S(1)} %get-tuple-element.36), channel_id=1, source_target_pairs={{1,0},{2,1},{3,2},{4,3},{5,4},{6,5},{7,6},{8,7},{9,8},{10,9},{11,1... | collective-permute-start | bytes 786440 | tf_op jit(solution)/shard_map/ppermute | solution.py:15
  115.7 0.9 copy-start.9
  126.2 1.4 copy-start.4
  126.2 1.4 copy-start.5
  126.2 1.4 copy-start.6
  127.7 1.1 copy-start
  127.7 1.1 copy-start.3
  130.6 0.8 copy-start.10
  133.3 5.3 %copy-start.1 = (bf16[96,3,18,128]{3,0,2,1:T(8,128)(2,1)S(1)}, bf16[96,3,18,128]{3,0,2,1:T(8,128)(2,1)}, u32[]{:S(2)}) copy-start(bf16[96,3,18,128]{3,0,2,1:T(8,128)(2,1)} %copy-done) | copy-start | bytes 3981316
  133.3 5.3 %copy-start.11 = (bf16[3,3,32,96]{3,2,1,0:T(8,128)(2,1)S(1)}, bf16[3,3,32,96]{3,2,1,0:T(8,128)(2,1)}, u32[]{:S(2)}) copy-start(bf16[3,3,32,96]{3,2,1,0:T(8,128)(2,1)} %reshape.196) | copy-start | bytes 165892
Sparse Core Ops, SparseCore 0:
  140.0 96.2 all-reduce.6
where the time goes:
time: 247 us
  waiting for transfers between devices  94.7 us (38%)
  local copies, waits for them, and re-layouts  84.6 us (34%)
  matrix products  30.3 us (12%)
  starting transfers between devices  16.6 us (7%)
  between operations  14.7 us (6%)
  other arithmetic  5.8 us (2%)
    psum x1, waiting for transfers between devices, on_device(): lax.psum((gather_terms(terms_one), gather_terms(terms_two)), 'slab')  94.6 us
    slice x5, local copies, waits for them, and re-layouts, column_stack(): pieces.append(field[..., first:first + stride * (count - 1) + 1:stride])  58.7 us
    dot_general x9, matrix products, on_device(): jnp.einsum('kq,kdhw->qdhw', rear_one[along_depth, along_rows], back_windo...  15.1 us
    unnamed x70, local copies, waits for them, and re-layouts  12.5 us
    ppermute x2, starting transfers between devices, extended_2(): before = lax.ppermute(last, axis, up)  8.1 us
    dot_general x9, matrix products, on_device(): jnp.einsum('odhw,kdhw->ok', grad_pre, window, preferred_element_type=jnp....  5.88 us
    ppermute x2, starting transfers between devices, passed_along(): return lax.ppermute(block, axis, route)  5.75 us
  transfers between devices with their start and end apart: 7, of which 1 were waited for; matrix products, arithmetic and copies ran while one was open for 31% of the time, Pallas kernels for 0%

commit v1 on v0

--- a/solution.py
+++ b/solution.py
@@ -33,6 +33,16 @@
         first = start(along_cols)
         pieces.append(field[..., first : first + stride * (count - 1) + 1 : stride])
     return jnp.concatenate(pieces, 0)
+
+
+def summed_over(terms, axis):
+    devices = lax.axis_size(axis)
+    flat = terms.reshape(-1)
+    room = -flat.shape[0] % devices
+    flat = jnp.pad(flat, (0, room)).reshape(devices, -1)
+    mine = lax.all_to_all(flat, axis, 0, 0, tiled=True).sum(0, keepdims=True)
+    whole = lax.all_to_all(jnp.broadcast_to(mine, flat.shape), axis, 0, 0, tiled=True)
+    return whole.reshape(-1)[: terms.size].reshape(terms.shape)
 
 
 def forward_kernel(weights):
@@ -82,8 +92,17 @@
     hidden = jax.nn.silu(preact).astype(jnp.bfloat16)
     upper_plane = passed_along(cotangent, "slab", -1)
     lower_plane = passed_along(hidden[:, planes - 1 :], "slab", 1)
-    stacked = pad_sides(jnp.concatenate([lower_plane, hidden], 1))
-    hidden_cols = column_stack(stacked, 2, half_cols, lambda along_cols: along_cols)
+    stacked = jnp.concatenate([lower_plane, hidden], 1)
+    stacked = jnp.pad(stacked, ((0, 0), (0, 0), (1, 1), (0, 0)))
+    picks = jnp.arange(columns)[:, None, None] == (
+        2 * jnp.arange(half_cols)[None, None, :] + jnp.arange(3)[None, :, None] - 1
+    )
+    hidden_cols = jnp.einsum(
+        "qdhp,pck->cqdhk", stacked, picks.astype(jnp.bfloat16), preferred_element_type=jnp.float32
+    )
+    hidden_cols = hidden_cols.astype(jnp.bfloat16).reshape(
+        3 * channels, planes + 1, height + 2, half_cols
+    )
     output = jnp.zeros((channels, half_planes, half_rows, half_cols), jnp.float32)
     terms_two = []
     for along_depth in range(3):
@@ -169,7 +188,9 @@
                 back_window,
                 preferred_element_type=jnp.float32,
             )
-    grad_one, grad_two = lax.psum((gather_terms(terms_one), gather_terms(terms_two)), "slab")
+    grad_one, grad_two = summed_over(
+        jnp.stack([gather_terms(terms_one), gather_terms(terms_two)]), "slab"
+    )
     return (output.astype(jnp.bfloat16), grad_volume.astype(jnp.bfloat16), grad_one, grad_two)
 
 

time: 247 us -> 162 us (0.66)
  waiting for transfers between devices: 94.7 us -> 3.2 us
  matrix products: 30.3 us -> 45.7 us
  local copies, waits for them, and re-layouts: 84.6 us -> 69.6 us
  starting transfers between devices: 16.6 us -> 31.4 us
  between operations: 14.7 us -> 1.41 us
  other arithmetic: 5.8 us -> 8.52 us
    psum x1 -> x0, waiting for transfers between devices: 94.6 us -> none  [on_device(): lax.psum((gather_terms(terms_one), gather_terms(terms_two)), 'slab')]
    slice x5 -> x2, local copies, waits for them, and re-layouts: 58.7 us -> 1.81 us  [column_stack(): pieces.append(field[..., first:first + stride * (count - 1) + 1:stride])]
    unnamed x70 -> x98, local copies, waits for them, and re-layouts: 12.5 us -> 33.8 us
    all_to_all x0 -> x2, starting transfers between devices: none -> 14.9 us  [the longest x1 8.9 us: summed_over(): mine = lax.all_to_all(flat, axis, 0, 0, tiled=True).sum(0, keepdims=True)]
    reshape x9, local copies, waits for them, and re-layouts: 0.79 us -> 10.8 us  [fold_term(): return term.reshape(size, 3, size).transpose(1, 0, 2)]
    dot_general x9, matrix products: 2.31 us -> 10.7 us  [on_device(): jnp.einsum('ok,kdhw->odhw', front_two[along_depth, along_rows], window, p...]
    dot_general x9, matrix products: 5.88 us -> 11.1 us  [on_device(): jnp.einsum('odhw,kdhw->ok', grad_pre, window, preferred_element_type=jnp....]
    another operation x0 -> x4, local copies, waits for them, and re-layouts: none -> 4.38 us  [the longest x3 2.42 us: on_device(): grad_one, grad_two = summed_over(jnp.stack([gather_terms(terms_one), gath...]
  transfers between devices with their start and end apart: 7 -> 8, of which waited for: 1 -> 1; matrix products, arithmetic and copies ran while one was open for 31% -> 47% of each run, Pallas kernels for 0% -> 0%
where the time goes in v1:
time: 162 us; the launch traced here: 160 us
  local copies, waits for them, and re-layouts  69.6 us (43%)
  matrix products  45.7 us (28%)
  starting transfers between devices  31.4 us (19%)
  other arithmetic  8.52 us (5%)
  waiting for transfers between devices  3.2 us (2%)
    unnamed x98, local copies, waits for them, and re-layouts  33.8 us
    dot_general x9, matrix products, on_device(): jnp.einsum('kq,kdhw->qdhw', rear_one[along_depth, along_rows], back_windo...  15.5 us
    dot_general x9, matrix products, on_device(): jnp.einsum('odhw,kdhw->ok', grad_pre, window, preferred_element_type=jnp....  11.1 us
    reshape x9, local copies, waits for them, and re-layouts, fold_term(): return term.reshape(size, 3, size).transpose(1, 0, 2)  10.8 us
    dot_general x9, matrix products, on_device(): jnp.einsum('ok,kdhw->odhw', front_two[along_depth, along_rows], window, p...  10.7 us
    ppermute x2, starting transfers between devices, extended_2(): before = lax.ppermute(last, axis, up)  8.92 us
    all_to_all x1, starting transfers between devices, summed_over(): mine = lax.all_to_all(flat, axis, 0, 0, tiled=True).sum(0, keepdims=True)  8.9 us
    all_to_all x1, starting transfers between devices, summed_over(): lax.all_to_all(jnp.broadcast_to(mine, flat.shape), axis, 0, 0, tiled=True)  5.96 us
  transfers between devices with their start and end apart: 8, of which 1 were waited for; matrix products, arithmetic and copies ran while one was open for 47% of the time, Pallas kernels for 0%

profile of v1, /device:TPU:0, one launch (start us, length us, event | category | flops | bytes accessed | tf_op | source)
XLA Modules:
  0.0 159.8 jit_solution(17442386256375201371)
XLA Ops:
  0.7 0.9 constant_dynamic-update-slice_fusion.7
  1.6 1.3 collective-permute-start.3
  2.9 1.3 copy.148
  4.3 3.7 %collective-permute-start = (bf16[32,1,16,256]{3,0,2,1:T(8,128)(2,1)S(1)}, bf16[32,1,16,256]{3,0,2,1:T(8,128)(2,1)}, u32[]{:S(2)}, u32[]{:S(2)}) collective-permute-start(bf16[32,1,16,256]{3,0,2,1:T(8,128)(2,1)S(1)} %get-tuple-element.37), channel_id=1, source_target_pairs={{0,1},{1,2},{2,3},{3,4},{4,5},{5,6},{6,7},{7,8},{8,9},{9,10},{10,1... | collective-permute-start | bytes 786440 | tf_op jit(solution)/shard_map/ppermute | solution.py:14
  8.0 1.3 collective-permute-start.1
  28.1 4.3 %copy.191 = f32[2,2,2,32,1,8,128]{3,2,6,1,5,0,4:T(2,128)} copy(f32[2,2,2,32,1,8,128]{6,3,5,2,1,0,4:T(8,128)S(1)} %bitcast.554) | data formatting | bytes 2097152 | tf_op jit(solution)/shard_map/reshape | solution.py:157
  32.4 3.6 %copy.192 = f32[32,2,16,256]{3,0,2,1:T(8,128)} copy(f32[32,2,16,256]{0,3,2,1:T(8,128)} %bitcast.542) | data formatting | bytes 2097152 | tf_op jit(solution)/shard_map/reshape | solution.py:158
  36.0 2.1 %select_maximum_fusion.2 = bf16[32,4,18,258]{3,0,2,1:T(8,128)(2,1)S(1)} fusion(bf16[32,1,16,256]{3,0,2,1:T(8,128)(2,1)} %collective-permute-done.1, bf16[32,2,16,256]{3,0,2,1:T(8,128)(2,1)S(1)} %copy.148, bf16[32,1,16,256]{3,0,2,1:T(8,128)(2,1)} %collective-permute-done), kind=kLoop, calls=%fused_computation.13 | loop fusion | flops 11294208 | bytes 2237440 | tf_op jit(solution)/shard_map/concatenate | solution.py:16
  43.6 1.7 %multiply_convert_fusion = (bf16[32,2,16,256]{3,0,2,1:T(8,128)(2,1)S(1)}, bf16[32,2,16,256]{3,0,2,1:T(8,128)(2,1)}) fusion(f32[32,2,16,256]{3,0,2,1:T(8,128)S(1)} %copy-done.5, f32[2,16,256,32]{2,3,1,0:T(8,128)S(1)} %fusion.28, f32[2,16,256,32]{2,3,1,0:T(8,128)S(1)} %fusion.32, f32[2,16,256,32]{2,3,1,0:T(8,128)S(1)} %fusion.36, ...), kind=kOutput, calls=%fused_computation.147 | convolution fusion | flops 55312384 | bytes 12066816 | tf_op jit(solution)/shard_map/ok,kdhw->odhw/dot_general | solution.py:86
  45.3 1.3 fusion.138
  46.5 1.3 fusion.141
  47.8 1.3 fusion.144
  49.0 1.3 fusion.147
  50.3 1.3 fusion.150
  51.5 1.3 fusion.153
  52.8 1.3 fusion.156
  55.5 1.4 reshape.265
  57.0 1.5 constant_dynamic-update-slice_fusion.16
  58.4 1.4 reshape.266
  59.9 1.4 reshape.267
  61.3 1.4 reshape.268
  62.7 1.4 reshape.269
  64.1 1.4 reshape.270
  65.6 1.4 reshape.271
  67.7 5.2 %collective-permute-start.4 = (bf16[32,1,16,256]{3,0,2,1:T(8,128)(2,1)}, bf16[32,1,16,256]{3,0,2,1:T(8,128)(2,1)}, u32[]{:S(2)}, u32[]{:S(2)}) collective-permute-start(bf16[32,1,16,256]{3,0,2,1:T(8,128)(2,1)} %get-tuple-element.35), channel_id=1, source_target_pairs={{0,1},{1,2},{2,3},{3,4},{4,5},{5,6},{6,7},{7,8},{8,9},{9,10},{10,1... | collective-permute-start | bytes 786440 | tf_op jit(solution)/shard_map/ppermute | solution.py:14
  72.9 1.3 collective-permute-start.5
  74.2 1.5 constant_dynamic-update-slice_fusion.15
  75.7 1.5 constant_dynamic-update-slice_fusion.14
  77.1 1.5 constant_dynamic-update-slice_fusion.13
  78.6 1.5 constant_dynamic-update-slice_fusion.12
  80.1 1.5 constant_dynamic-update-slice_fusion.11
  81.5 1.5 constant_dynamic-update-slice_fusion.10
  83.0 1.5 constant_dynamic-update-slice_fusion.9
  84.5 1.7 %fusion.162 = f32[32,96]{1,0:T(8,128)S(1)} fusion(bf16[32,2,16,256]{3,0,2,1:T(8,128)(2,1)} %copy-done, bf16[96,4,18,256]{3,0,2,1:T(8,128)(2,1)S(1)} %pad_maximum_fusion), kind=kOutput, calls=%fused_computation.146 | convolution fusion | flops 50331648 | bytes 2109440 | tf_op jit(solution)/shard_map/odhw,kdhw->ok/dot_general | solution.py:174
  86.9 1.9 %copy.203 = f32[9,3,32,32]{3,2,1,0:T(8,128)} copy(f32[9,3,32,32]{3,1,2,0:T(4,128)} %constant_dynamic-update-slice_fusion.8) | data formatting | bytes 221184 | tf_op jit(solution)/shard_map/stack | solution.py:66
  88.8 1.0 slice.461
  89.7 3.8 %collective-permute-start.2 = (bf16[32,1,16,256]{3,0,2,1:T(8,128)(2,1)S(1)}, bf16[32,1,16,256]{3,0,2,1:T(8,128)(2,1)S(1)}, u32[]{:S(2)}, u32[]{:S(2)}) collective-permute-start(bf16[32,1,16,256]{3,0,2,1:T(8,128)(2,1)S(1)} %slice.461), channel_id=1, source_target_pairs={{0,1},{1,2},{2,3},{3,4},{4,5},{5,6},{6,7},{7,8},{8,9},{9,10},{10,1... | collective-permute-start | bytes 786440 | tf_op jit(solution)/shard_map/ppermute | solution.py:23
  93.5 2.1 %select_maximum_fusion = bf16[32,4,18,258]{3,0,2,1:T(8,128)(2,1)S(1)} fusion(bf16[32,1,16,256]{3,0,2,1:T(8,128)(2,1)} %collective-permute-done.5, bf16[32,2,16,256]{3,0,2,1:T(8,128)(2,1)S(1)} %copy-done.1, bf16[32,1,16,256]{3,0,2,1:T(8,128)(2,1)} %collective-permute-done.4), kind=kLoop, calls=%fused_computation.11 | loop fusion | flops 11294208 | bytes 2237440 | tf_op jit(solution)/shard_map/concatenate | solution.py:16
  97.5 1.4 fusion.11
  98.9 1.3 fusion.13
  100.3 1.4 fusion.15
  101.7 1.4 fusion.17
  103.0 1.4 fusion.19
  104.4 1.4 fusion.5
  105.8 1.4 fusion.7
  107.1 1.4 fusion.9
  113.0 2.0 %copy.213 = f32[1,27,32,32]{3,2,1,0:T(8,128)} copy(f32[1,27,32,32]{2,3,1,0:T(8,128)} %bitcast.577) | data formatting | bytes 221184 | tf_op jit(solution)/shard_map/stack;reshape | solution.py:192
  115.0 2.1 %pad_maximum_fusion.2 = f32[2,27,32,32]{3,2,1,0:T(8,128)} fusion(f32[1,27,32,32]{3,2,1,0:T(8,128)} %copy.213, f32[1,27,32,32]{3,2,1,0:T(8,128)} %bitcast.553), kind=kLoop, calls=%fused_computation.156 | loop fusion | flops 55296 | bytes 442368 | tf_op jit(solution)/shard_map/stack | solution.py:192
  117.1 2.2 %all_to_all.13 = f32[16,1,3456]{2,1,0:T(1,128)} reshape(f32[2,27,32,32]{3,2,1,0:T(8,128)} %pad_maximum_fusion.2) | data formatting | bytes 442368 | tf_op jit(solution)/shard_map/all_to_all | solution.py:43
  119.4 8.9 %all-to-all-start = ((f32[16,1,3456]{2,1,0:T(1,128)}), f32[16,1,3456]{2,1,0:T(1,128)}, u32[]{:S(2)}, u32[]{:S(2)}) async-start(f32[16,1,3456]{2,1,0:T(1,128)} %all_to_all.13), calls=%async_computation | async-start | bytes 442368 | tf_op jit(solution)/shard_map/all_to_all | solution.py:43
  128.3 1.2 fusion.203
  129.5 1.1 convolution_add_fusion.7
  130.6 1.1 convolution_add_fusion.6
  131.7 1.1 convolution_add_fusion.5
  132.8 1.1 convolution_add_fusion.4
  134.0 1.8 %convolution_add_fusion.3 = f32[8,128,32]{1,2,0:T(8,128)} fusion(f32[8,128,32]{1,2,0:T(8,128)S(1)} %convolution_add_fusion.4, bf16[3,3,32,96]{3,2,1,0:T(8,128)(2,1)} %reshape.245, bf16[96,3,18,128]{3,0,2,1:T(8,128)(2,1)} %bitcast.538), kind=kOutput, calls=%fused_computation.99 | convolution fusion | flops 6324224 | bytes 466944 | tf_op jit(solution)/shard_map/ok,kdhw->odhw/dot_general | solution.py:116
  135.7 4.5 %fusion.116 = bf16[32,2,16,256]{3,0,2,1:T(8,128)(2,1)} fusion(f32[2,16,256,32]{2,3,1,0:T(8,128)} %fusion.5, f32[2,16,256,32]{2,3,1,0:T(8,128)} %fusion.7, f32[2,16,256,32]{2,3,1,0:T(8,128)} %fusion.9, f32[2,16,256,32]{2,3,1,0:T(8,128)S(1)} %copy-done.6, f32[2,16,256,32]{2,3,1,0:T(8,128)S(1)} %copy-done.7, f32[2,16,256,32]{2,3,1,0:T(8,128)} %fusion.15, ...), kind=kOutput, calls=%fused_computation.93 | convolution fusion | flops 52690944 | bytes 10510336 | tf_op jit(solution)/shard_map/kq,kdhw->qdhw/dot_general | solution.py:185
  140.2 1.1 reduce_sum.9
  142.1 6.0 %all-to-all-start.1 = ((f32[16,1,3456]{2,1,0:T(1,128)}), f32[16,1,3456]{2,1,0:T(1,128)S(1)}, u32[]{:S(2)}, u32[]{:S(2)}) async-start(f32[16,1,3456]{2,1,0:T(1,128)} %broadcast_in_dim.2), calls=%async_computation.1 | async-start | bytes 442368 | tf_op jit(solution)/shard_map/all_to_all | solution.py:44
  148.0 1.2 convolution_add_fusion.2
  149.2 2.1 %copy.216 = bf16[32,2,16,256]{3,2,1,0:T(8,128)(2,1)} copy(bf16[32,2,16,256]{3,0,2,1:T(8,128)(2,1)} %fusion.116) | data formatting | bytes 1048576
  151.3 1.1 convolution_add_fusion.1
  152.4 1.1 fusion.128
  154.2 3.2 %all-to-all-done.1 = f32[16,1,3456]{2,1,0:T(1,128)S(1)} async-done(((f32[16,1,3456]{2,1,0:T(1,128)}), f32[16,1,3456]{2,1,0:T(1,128)S(1)}, u32[]{:S(2)}, u32[]{:S(2)}) %all-to-all-start.1) | async-done | bytes 221216 | tf_op jit(solution)/shard_map/all_to_all | solution.py:44
  (147 shorter events, 37.0 us)
Async XLA Ops:
  0.6 8.7 %copy-start.3 = (bf16[32,1,8,128]{3,2,1,0:T(8,128)(2,1)S(1)}, bf16[32,1,8,128]{3,2,1,0:T(8,128)(2,1)}, u32[]{:S(2)}) copy-start(bf16[32,1,8,128]{3,2,1,0:T(8,128)(2,1)} %param.7) | copy-start | bytes 196612
  0.6 8.7 %copy-start.9 = (bf16[27,32,32]{2,1,0:T(8,128)(2,1)S(1)}, bf16[27,32,32]{2,1,0:T(8,128)(2,1)}, u32[]{:S(2)}) copy-start(bf16[27,32,32]{2,1,0:T(8,128)(2,1)} %param.6) | copy-start | bytes 165892
  0.7 22.3 %copy-start.10 = (bf16[27,32,32]{2,1,0:T(8,128)(2,1)S(1)}, bf16[27,32,32]{2,1,0:T(8,128)(2,1)}, u32[]{:S(2)}) copy-start(bf16[27,32,32]{2,1,0:T(8,128)(2,1)} %param.5) | copy-start | bytes 165892
  1.6 24.2 %collective-permute-start.3 = (bf16[32,1,8,128]{3,0,2,1:T(8,128)(2,1)S(1)}, bf16[32,1,8,128]{3,0,2,1:T(8,128)(2,1)S(1)}, u32[]{:S(2)}, u32[]{:S(2)}) collective-permute-start(bf16[32,1,8,128]{3,0,2,1:T(8,128)(2,1)S(1)} %get-tuple-element.72), channel_id=1, source_target_pairs={{1,0},{2,1},{3,2},{4,3},{5,4},{6,5},{7,6},{8,7},{9,8},{10,9},{11,1... | collective-permute-start | bytes 196616 | tf_op jit(solution)/shard_map/ppermute | solution.py:23
  4.3 31.7 %collective-permute-start = (bf16[32,1,16,256]{3,0,2,1:T(8,128)(2,1)S(1)}, bf16[32,1,16,256]{3,0,2,1:T(8,128)(2,1)}, u32[]{:S(2)}, u32[]{:S(2)}) collective-permute-start(bf16[32,1,16,256]{3,0,2,1:T(8,128)(2,1)S(1)} %get-tuple-element.37), channel_id=1, source_target_pairs={{0,1},{1,2},{2,3},{3,4},{4,5},{5,6},{6,7},{7,8},{8,9},{9,10},{10,1... | collective-permute-start | bytes 786440 | tf_op jit(solution)/shard_map/ppermute | solution.py:14
  8.0 28.0 %collective-permute-start.1 = (bf16[32,1,16,256]{3,0,2,1:T(8,128)(2,1)S(1)}, bf16[32,1,16,256]{3,0,2,1:T(8,128)(2,1)}, u32[]{:S(2)}, u32[]{:S(2)}) collective-permute-start(bf16[32,1,16,256]{3,0,2,1:T(8,128)(2,1)S(1)} %get-tuple-element.38), channel_id=1, source_target_pairs={{1,0},{2,1},{3,2},{4,3},{5,4},{6,5},{7,6},{8,7},{9,8},{10,9},{11,1... | collective-permute-start | bytes 786440 | tf_op jit(solution)/shard_map/ppermute | solution.py:15
  23.9 2.9 %copy-start.14 = (bf16[1,32,32]{1,2,0:T(8,128)(2,1)S(1)}, bf16[1,32,32]{1,2,0:T(8,128)(2,1)}, u32[]{:S(2)}) copy-start(bf16[1,32,32]{1,2,0:T(8,128)(2,1)} %copy.291) | copy-start | bytes 6148
  23.9 2.9 %copy-start.16 = (bf16[1,32,32]{1,2,0:T(8,128)(2,1)S(1)}, bf16[1,32,32]{1,2,0:T(8,128)(2,1)}, u32[]{:S(2)}) copy-start(bf16[1,32,32]{1,2,0:T(8,128)(2,1)} %copy.288) | copy-start | bytes 6148
  23.9 3.0 %copy-start.18 = (bf16[1,32,32]{1,2,0:T(8,128)(2,1)S(1)}, bf16[1,32,32]{1,2,0:T(8,128)(2,1)}, u32[]{:S(2)}) copy-start(bf16[1,32,32]{1,2,0:T(8,128)(2,1)} %copy.289) | copy-start | bytes 6148
  23.9 3.0 %copy-start.23 = (bf16[1,32,32]{1,2,0:T(8,128)(2,1)S(1)}, bf16[1,32,32]{1,2,0:T(8,128)(2,1)}, u32[]{:S(2)}) copy-start(bf16[1,32,32]{1,2,0:T(8,128)(2,1)} %copy.290) | copy-start | bytes 6148
  25.8 1.5 copy-start.19
  25.8 1.5 copy-start.21
  25.8 1.5 copy-start.24
  25.8 1.5 copy-start.25
  26.2 1.4 copy-start.15
  26.2 1.4 copy-start.17
  26.3 1.4 copy-start.20
  26.3 1.4 copy-start.22
  39.0 0.9 copy-start.13
  42.3 1.2 copy-start.5
  45.3 9.4 %copy-start = (bf16[32,2,16,256]{3,0,2,1:T(8,128)(2,1)}, bf16[32,2,16,256]{3,0,2,1:T(8,128)(2,1)S(1)}, u32[]{:S(2)}) copy-start(bf16[32,2,16,256]{3,0,2,1:T(8,128)(2,1)S(1)} %get-tuple-element.33) | copy-start | bytes 1572868
  67.7 25.8 %collective-permute-start.4 = (bf16[32,1,16,256]{3,0,2,1:T(8,128)(2,1)}, bf16[32,1,16,256]{3,0,2,1:T(8,128)(2,1)}, u32[]{:S(2)}, u32[]{:S(2)}) collective-permute-start(bf16[32,1,16,256]{3,0,2,1:T(8,128)(2,1)} %get-tuple-element.35), channel_id=1, source_target_pairs={{0,1},{1,2},{2,3},{3,4},{4,5},{5,6},{6,7},{7,8},{8,9},{9,10},{10,1... | collective-permute-start | bytes 786440 | tf_op jit(solution)/shard_map/ppermute | solution.py:14
  72.9 20.6 %collective-permute-start.5 = (bf16[32,1,16,256]{3,0,2,1:T(8,128)(2,1)}, bf16[32,1,16,256]{3,0,2,1:T(8,128)(2,1)}, u32[]{:S(2)}, u32[]{:S(2)}) collective-permute-start(bf16[32,1,16,256]{3,0,2,1:T(8,128)(2,1)} %get-tuple-element.36), channel_id=1, source_target_pairs={{1,0},{2,1},{3,2},{4,3},{5,4},{6,5},{7,6},{8,7},{9,8},{10,9},{11,1... | collective-permute-start | bytes 786440 | tf_op jit(solution)/shard_map/ppermute | solution.py:15
  86.1 7.4 %copy-start.1 = (bf16[32,2,16,256]{3,0,2,1:T(8,128)(2,1)S(1)}, bf16[32,2,16,256]{3,0,2,1:T(8,128)(2,1)}, u32[]{:S(2)}) copy-start(bf16[32,2,16,256]{3,0,2,1:T(8,128)(2,1)} %copy-done) | copy-start | bytes 1572868
  89.7 18.8 %collective-permute-start.2 = (bf16[32,1,16,256]{3,0,2,1:T(8,128)(2,1)S(1)}, bf16[32,1,16,256]{3,0,2,1:T(8,128)(2,1)S(1)}, u32[]{:S(2)}, u32[]{:S(2)}) collective-permute-start(bf16[32,1,16,256]{3,0,2,1:T(8,128)(2,1)S(1)} %slice.461), channel_id=1, source_target_pairs={{0,1},{1,2},{2,3},{3,4},{4,5},{5,6},{6,7},{7,8},{8,9},{9,10},{10,1... | collective-permute-start | bytes 786440 | tf_op jit(solution)/shard_map/ppermute | solution.py:23
  96.5 0.9 copy-start.11
  107.1 1.4 copy-start.8
  107.1 1.4 copy-start.26
  109.4 1.1 copy-start.2
  109.4 1.1 copy-start.4
  112.3 0.8 copy-start.12
  119.4 20.8 %all-to-all-start = ((f32[16,1,3456]{2,1,0:T(1,128)}), f32[16,1,3456]{2,1,0:T(1,128)}, u32[]{:S(2)}, u32[]{:S(2)}) async-start(f32[16,1,3456]{2,1,0:T(1,128)} %all_to_all.13), calls=%async_computation | async-start | bytes 442368 | tf_op jit(solution)/shard_map/all_to_all | solution.py:43
  128.3 7.5 %copy-start.6 = (f32[2,16,256,32]{2,3,1,0:T(8,128)S(1)}, f32[2,16,256,32]{2,3,1,0:T(8,128)}, u32[]{:S(2)}) copy-start(f32[2,16,256,32]{2,3,1,0:T(8,128)} %fusion.11) | copy-start | bytes 3145732
  128.3 7.4 %copy-start.7 = (f32[2,16,256,32]{2,3,1,0:T(8,128)S(1)}, f32[2,16,256,32]{2,3,1,0:T(8,128)}, u32[]{:S(2)}) copy-start(f32[2,16,256,32]{2,3,1,0:T(8,128)} %fusion.13) | copy-start | bytes 3145732
  142.1 15.3 %all-to-all-start.1 = ((f32[16,1,3456]{2,1,0:T(1,128)}), f32[16,1,3456]{2,1,0:T(1,128)S(1)}, u32[]{:S(2)}, u32[]{:S(2)}) async-start(f32[16,1,3456]{2,1,0:T(1,128)} %broadcast_in_dim.2), calls=%async_computation.1 | async-start | bytes 442368 | tf_op jit(solution)/shard_map/all_to_all | solution.py:44

commit v2 on v1

--- a/solution.py
+++ b/solution.py
@@ -1,4 +1,5 @@
 import jax
+import numpy as np
 import jax.numpy as jnp
 from jax import lax
 from jax.sharding import PartitionSpec as P
@@ -62,6 +63,13 @@
     return term.reshape(size, 3, size).transpose(1, 0, 2)
 
 
+def fold_terms(summed):
+    size = summed.shape[2]
+    folded = summed.reshape(2, 9, size, 3, size).transpose(0, 1, 3, 2, 4)
+    folded = folded.reshape(2, 27, size, size)
+    return folded[0], folded[1]
+
+
 def gather_terms(listed):
     stacked = jnp.stack(listed)
     return stacked.reshape(27, stacked.shape[2], stacked.shape[3])
@@ -74,7 +82,7 @@
     half_cols = columns // 2
     front_one = forward_kernel(weight_one)
     front_two = forward_kernel(weight_two)
-    rear_one = backward_kernel(weight_one)
+    rear_one = backward_kernel(weight_one).transpose(0, 1, 3, 2)
     padded = pad_sides(extended_2(volume, (("slab", 1),), 1))
     volume_cols = column_stack(padded, 1, columns, lambda along_cols: along_cols)
     preact = jnp.zeros((channels, planes, height, columns), jnp.float32)
@@ -120,21 +128,26 @@
                 preferred_element_type=jnp.float32,
             )
             terms_two.append(
-                fold_term(
-                    jnp.einsum(
-                        "odhw,kdhw->ok", cotangent, window, preferred_element_type=jnp.float32
-                    )
-                )
+                jnp.einsum("odhw,kdhw->ok", cotangent, window, preferred_element_type=jnp.float32)
             )
     extended = jnp.concatenate([cotangent, upper_plane], 1)
     extended = jnp.pad(extended, ((0, 0), (0, 0), (0, 1), (0, 1)))
     parity_taps = [[(1, 0)], [(2, 0), (0, 1)]]
+    order = []
+    for depth_parity in range(2):
+        for row_parity in range(2):
+            for col_parity in range(2):
+                for tap_depth, _ in parity_taps[depth_parity]:
+                    for tap_row, _ in parity_taps[row_parity]:
+                        for tap_col, _ in parity_taps[col_parity]:
+                            order.append(9 * tap_depth + 3 * tap_row + tap_col)
+    ordered_two = weight_two[np.array(order)]
+    taken = 0
     classes = []
     for depth_parity in range(2):
         for row_parity in range(2):
             for col_parity in range(2):
                 pieces = []
-                kernels = []
                 for tap_depth, skip_depth in parity_taps[depth_parity]:
                     for tap_row, skip_row in parity_taps[row_parity]:
                         for tap_col, skip_col in parity_taps[col_parity]:
@@ -146,9 +159,9 @@
                                     skip_col : skip_col + half_cols,
                                 ]
                             )
-                            kernels.append(weight_two[9 * tap_depth + 3 * tap_row + tap_col])
                 joined = jnp.concatenate(pieces, 0)
-                joined_kernel = jnp.concatenate(kernels, 0)
+                joined_kernel = ordered_two[taken : taken + len(pieces)].reshape(-1, channels)
+                taken += len(pieces)
                 classes.append(
                     jnp.einsum(
                         "kq,kdhw->qdhw", joined_kernel, joined, preferred_element_type=jnp.float32
@@ -170,11 +183,7 @@
                 :, along_depth : along_depth + planes, along_rows : along_rows + height, :
             ]
             terms_one.append(
-                fold_term(
-                    jnp.einsum(
-                        "odhw,kdhw->ok", grad_pre, window, preferred_element_type=jnp.float32
-                    )
-                )
+                jnp.einsum("odhw,kdhw->ok", grad_pre, window, preferred_element_type=jnp.float32)
             )
             back_window = rimmed_cols[
                 :,
@@ -183,14 +192,13 @@
                 :,
             ]
             grad_volume = grad_volume + jnp.einsum(
-                "kq,kdhw->qdhw",
+                "qk,kdhw->qdhw",
                 rear_one[along_depth, along_rows],
                 back_window,
                 preferred_element_type=jnp.float32,
             )
-    grad_one, grad_two = summed_over(
-        jnp.stack([gather_terms(terms_one), gather_terms(terms_two)]), "slab"
-    )
+    summed = summed_over(jnp.stack([jnp.stack(terms_one), jnp.stack(terms_two)]), "slab")
+    grad_one, grad_two = fold_terms(summed)
     return (output.astype(jnp.bfloat16), grad_volume.astype(jnp.bfloat16), grad_one, grad_two)
 
 

time: 162 us -> 112 us (0.69)
  local copies, waits for them, and re-layouts: 69.6 us -> 26.2 us
  matrix products: 45.7 us -> 39.1 us
  other arithmetic: 8.52 us -> 6.72 us
  starting transfers between devices: 31.4 us -> 33.1 us
    unnamed x98 -> x40, local copies, waits for them, and re-layouts: 33.8 us -> 6.65 us
    reshape x9 -> x1, local copies, waits for them, and re-layouts: 10.8 us -> 0.77 us  [backward_kernel(): return weights.reshape(3, 3, 3 * size, size)]
    another operation x6 -> x1, local copies, waits for them, and re-layouts: 6.88 us -> 0.71 us  [fold_terms(): folded = summed.reshape(2, 9, size, 3, size).transpose(0, 1, 3, 2, 4)]
    dot_general x9, matrix products: 11.1 us -> 5.75 us  [on_device(): jnp.einsum('odhw,kdhw->ok', grad_pre, window, preferred_element_type=jnp....]
    slice x3 -> x7, local copies, waits for them, and re-layouts: 0.25 us -> 3.22 us  [the longest x3 1.92 us: fold_terms(): return (folded[0], folded[1])]
    all_to_all x1, starting transfers between devices: 8.9 us -> 11.2 us  [summed_over(): mine = lax.all_to_all(flat, axis, 0, 0, tiled=True).sum(0, keepdims=True)]
  transfers between devices with their start and end apart: 8 -> 8, of which waited for: 1 -> 2; matrix products, arithmetic and copies ran while one was open for 47% -> 43% of each run, Pallas kernels for 0% -> 0%
where the time goes in v2:
time: 112 us; the launch traced here: 111 us
  matrix products  39.1 us (35%)
  starting transfers between devices  33.1 us (30%)
  local copies, waits for them, and re-layouts  26.2 us (23%)
  other arithmetic  6.72 us (6%)
  waiting for transfers between devices  4.73 us (4%)
  between operations  1.24 us (1%)
    dot_general x9, matrix products, on_device(): jnp.einsum('qk,kdhw->qdhw', rear_one[along_depth, along_rows], back_windo...  15.2 us
    all_to_all x1, starting transfers between devices, summed_over(): mine = lax.all_to_all(flat, axis, 0, 0, tiled=True).sum(0, keepdims=True)  11.2 us
    dot_general x9, matrix products, on_device(): jnp.einsum('ok,kdhw->odhw', front_two[along_depth, along_rows], window, p...  10.7 us
    ppermute x2, starting transfers between devices, extended_2(): before = lax.ppermute(last, axis, up)  7.39 us
    unnamed x40, local copies, waits for them, and re-layouts  6.65 us
    all_to_all x1, starting transfers between devices, summed_over(): lax.all_to_all(jnp.broadcast_to(mine, flat.shape), axis, 0, 0, tiled=True)  5.96 us
    ppermute x2, starting transfers between devices, passed_along(): return lax.ppermute(block, axis, route)  5.75 us
    dot_general x9, matrix products, on_device(): jnp.einsum('odhw,kdhw->ok', grad_pre, window, preferred_element_type=jnp....  5.75 us
  transfers between devices with their start and end apart: 8, of which 2 were waited for; matrix products, arithmetic and copies ran while one was open for 43% of the time, Pallas kernels for 0%

profile of v2, /device:TPU:0, one launch (start us, length us, event | category | flops | bytes accessed | tf_op | source)
XLA Modules:
  0.0 111.1 jit_solution(755232998653226458)
XLA Ops:
  0.7 0.9 constant_dynamic-update-slice_fusion.7
  1.6 1.3 %collective-permute-start.3 = (bf16[32,1,8,128]{3,0,2,1:T(8,128)(2,1)S(1)}, bf16[32,1,8,128]{3,0,2,1:T(8,128)(2,1)S(1)}, u32[]{:S(2)}, u32[]{:S(2)}) collective-permute-start(bf16[32,1,8,128]{3,0,2,1:T(8,128)(2,1)S(1)} %get-tuple-element.47), channel_id=1, source_target_pairs={{1,0},{2,1},{3,2},{4,3},{5,4},{6,5},{7,6},{8,7},{9,8},{10,9},{11,1... | collective-permute-start | bytes 196616 | tf_op jit(solution)/shard_map/ppermute | solution.py:24
  2.9 1.3 %copy.117 = bf16[32,2,16,256]{3,0,2,1:T(8,128)(2,1)S(1)} copy(bf16[32,2,16,256]{3,2,1,0:T(8,128)(2,1)} %param.6) | data formatting | bytes 1048576 | tf_op args[0]
  4.2 0.7 fusion.293
  5.0 3.8 %collective-permute-start = (bf16[32,1,16,256]{3,0,2,1:T(8,128)(2,1)}, bf16[32,1,16,256]{3,0,2,1:T(8,128)(2,1)}, u32[]{:S(2)}, u32[]{:S(2)}) collective-permute-start(bf16[32,1,16,256]{3,0,2,1:T(8,128)(2,1)} %get-tuple-element.32), channel_id=1, source_target_pairs={{0,1},{1,2},{2,3},{3,4},{4,5},{5,6},{6,7},{7,8},{8,9},{9,10},{10,1... | collective-permute-start | bytes 786440 | tf_op jit(solution)/shard_map/ppermute | solution.py:15
  8.7 1.3 %collective-permute-start.1 = (bf16[32,1,16,256]{3,0,2,1:T(8,128)(2,1)S(1)}, bf16[32,1,16,256]{3,0,2,1:T(8,128)(2,1)}, u32[]{:S(2)}, u32[]{:S(2)}) collective-permute-start(bf16[32,1,16,256]{3,0,2,1:T(8,128)(2,1)S(1)} %get-tuple-element.33), channel_id=1, source_target_pairs={{1,0},{2,1},{3,2},{4,3},{5,4},{6,5},{7,6},{8,7},{9,8},{10,9},{11,1... | collective-permute-start | bytes 786440 | tf_op jit(solution)/shard_map/ppermute | solution.py:16
  10.1 0.6 gather_fusion
  10.7 0.7 fusion.295
  11.3 0.6 fusion.294
  13.0 0.8 copy.144
  14.0 0.8 reshape.213
  16.8 4.3 %copy.141 = f32[2,2,2,32,1,8,128]{3,2,6,1,5,0,4:T(2,128)} copy(f32[2,2,2,32,1,8,128]{6,3,5,2,1,0,4:T(8,128)S(1)} %bitcast.525) | data formatting | bytes 2097152 | tf_op jit(solution)/shard_map/reshape | solution.py:170
  21.1 2.8 %copy.142 = f32[32,2,16,256]{3,0,2,1:T(8,128)S(1)} copy(f32[32,2,16,256]{0,3,2,1:T(8,128)} %bitcast.505) | data formatting | bytes 2097152 | tf_op jit(solution)/shard_map/reshape | solution.py:171
  23.9 2.1 %select_maximum_fusion.2 = bf16[32,4,18,258]{3,0,2,1:T(8,128)(2,1)S(1)} fusion(bf16[32,1,16,256]{3,0,2,1:T(8,128)(2,1)} %collective-permute-done.1, bf16[32,2,16,256]{3,0,2,1:T(8,128)(2,1)S(1)} %copy.117, bf16[32,1,16,256]{3,0,2,1:T(8,128)(2,1)} %collective-permute-done), kind=kLoop, calls=%fused_computation.14 | loop fusion | flops 11294208 | bytes 2237440 | tf_op jit(solution)/shard_map/concatenate | solution.py:17
  26.1 0.9 fusion.290
  30.1 0.9 multiply_convert_fusion
  31.0 0.6 fusion.132
  31.7 0.6 fusion.138
  32.3 0.6 fusion.144
  32.9 0.6 fusion.150
  33.6 0.6 fusion.156
  34.2 0.6 fusion.162
  34.9 0.6 fusion.168
  35.5 0.6 fusion.174
  36.2 4.5 %collective-permute-start.2 = (bf16[32,1,16,256]{3,0,2,1:T(8,128)(2,1)S(1)}, bf16[32,1,16,256]{3,0,2,1:T(8,128)(2,1)S(1)}, u32[]{:S(2)}, u32[]{:S(2)}) collective-permute-start(bf16[32,1,16,256]{3,0,2,1:T(8,128)(2,1)S(1)} %slice.393), channel_id=1, source_target_pairs={{0,1},{1,2},{2,3},{3,4},{4,5},{5,6},{6,7},{7,8},{8,9},{9,10},{10,1... | collective-permute-start | bytes 786440 | tf_op jit(solution)/shard_map/ppermute | solution.py:24
  40.7 3.6 %collective-permute-start.4 = (bf16[32,1,16,256]{3,0,2,1:T(8,128)(2,1)S(1)}, bf16[32,1,16,256]{3,0,2,1:T(8,128)(2,1)S(1)}, u32[]{:S(2)}, u32[]{:S(2)}) collective-permute-start(bf16[32,1,16,256]{3,0,2,1:T(8,128)(2,1)S(1)} %get-tuple-element.30), channel_id=1, source_target_pairs={{0,1},{1,2},{2,3},{3,4},{4,5},{5,6},{6,7},{7,8},{8,9},{9,10},{10,1... | collective-permute-start | bytes 786440 | tf_op jit(solution)/shard_map/ppermute | solution.py:15
  44.4 1.5 %collective-permute-start.5 = (bf16[32,1,16,256]{3,0,2,1:T(8,128)(2,1)S(1)}, bf16[32,1,16,256]{3,0,2,1:T(8,128)(2,1)S(1)}, u32[]{:S(2)}, u32[]{:S(2)}) collective-permute-start(bf16[32,1,16,256]{3,0,2,1:T(8,128)(2,1)S(1)} %get-tuple-element.31), channel_id=1, source_target_pairs={{1,0},{2,1},{3,2},{4,3},{5,4},{6,5},{7,6},{8,7},{9,8},{10,9},{11,1... | collective-permute-start | bytes 786440 | tf_op jit(solution)/shard_map/ppermute | solution.py:16
  45.8 0.6 fusion.180
  46.5 1.5 %collective-permute-done.5 = bf16[32,1,16,256]{3,0,2,1:T(8,128)(2,1)S(1)} collective-permute-done((bf16[32,1,16,256]{3,0,2,1:T(8,128)(2,1)S(1)}, bf16[32,1,16,256]{3,0,2,1:T(8,128)(2,1)S(1)}, u32[]{:S(2)}, u32[]{:S(2)}) %collective-permute-start.5) | collective-permute-done | bytes 262176 | tf_op jit(solution)/shard_map/ppermute | solution.py:16
  48.0 1.1 select_maximum_fusion
  49.1 0.9 fusion.289
  50.3 0.6 copy-done.6
  50.9 1.4 %fusion.11 = f32[2,16,256,32]{2,3,1,0:T(8,128)} fusion(bf16[96,4,18,256]{3,0,2,1:T(8,128)(2,1)S(1)} %pad_maximum_fusion.1, bf16[3,3,32,96]{3,2,1,0:T(8,128)(2,1)S(1)} %bitcast.535), kind=kOutput, calls=%fused_computation.25 | convolution fusion | flops 50331648 | bytes 2629632 | tf_op jit(solution)/shard_map/qk,kdhw->qdhw/dot_general | solution.py:194
  52.3 1.3 %fusion.13 = f32[2,16,256,32]{2,3,1,0:T(8,128)} fusion(bf16[96,4,18,256]{3,0,2,1:T(8,128)(2,1)S(1)} %pad_maximum_fusion.1, bf16[3,3,32,96]{3,2,1,0:T(8,128)(2,1)S(1)} %bitcast.536), kind=kOutput, calls=%fused_computation.27 | convolution fusion | flops 50331648 | bytes 2629632 | tf_op jit(solution)/shard_map/qk,kdhw->qdhw/dot_general | solution.py:194
  53.6 1.3 %fusion.15 = f32[2,16,256,32]{2,3,1,0:T(8,128)} fusion(bf16[96,4,18,256]{3,0,2,1:T(8,128)(2,1)S(1)} %pad_maximum_fusion.1, bf16[3,3,32,96]{3,2,1,0:T(8,128)(2,1)S(1)} %bitcast.537), kind=kOutput, calls=%fused_computation.29 | convolution fusion | flops 50331648 | bytes 2629632 | tf_op jit(solution)/shard_map/qk,kdhw->qdhw/dot_general | solution.py:194
  55.0 1.3 %fusion.17 = f32[2,16,256,32]{2,3,1,0:T(8,128)} fusion(bf16[96,4,18,256]{3,0,2,1:T(8,128)(2,1)S(1)} %pad_maximum_fusion.1, bf16[3,3,32,96]{3,2,1,0:T(8,128)(2,1)S(1)} %bitcast.538), kind=kOutput, calls=%fused_computation.31 | convolution fusion | flops 50331648 | bytes 2629632 | tf_op jit(solution)/shard_map/qk,kdhw->qdhw/dot_general | solution.py:194
  56.3 1.3 %fusion.19 = f32[2,16,256,32]{2,3,1,0:T(8,128)} fusion(bf16[96,4,18,256]{3,0,2,1:T(8,128)(2,1)S(1)} %pad_maximum_fusion.1, bf16[3,3,32,96]{3,2,1,0:T(8,128)(2,1)S(1)} %bitcast.539), kind=kOutput, calls=%fused_computation.33 | convolution fusion | flops 50331648 | bytes 2629632 | tf_op jit(solution)/shard_map/qk,kdhw->qdhw/dot_general | solution.py:194
  57.6 1.4 %fusion.5 = f32[2,16,256,32]{2,3,1,0:T(8,128)} fusion(bf16[96,4,18,256]{3,0,2,1:T(8,128)(2,1)S(1)} %pad_maximum_fusion.1, bf16[3,3,32,96]{3,2,1,0:T(8,128)(2,1)S(1)} %bitcast.540), kind=kOutput, calls=%fused_computation.19 | convolution fusion | flops 50331648 | bytes 2629632 | tf_op jit(solution)/shard_map/qk,kdhw->qdhw/dot_general | solution.py:194
  59.0 1.3 %fusion.7 = f32[2,16,256,32]{2,3,1,0:T(8,128)} fusion(bf16[96,4,18,256]{3,0,2,1:T(8,128)(2,1)S(1)} %pad_maximum_fusion.1, bf16[3,3,32,96]{3,2,1,0:T(8,128)(2,1)S(1)} %bitcast.541), kind=kOutput, calls=%fused_computation.21 | convolution fusion | flops 50331648 | bytes 2629632 | tf_op jit(solution)/shard_map/qk,kdhw->qdhw/dot_general | solution.py:194
  60.3 1.3 %fusion.9 = f32[2,16,256,32]{2,3,1,0:T(8,128)} fusion(bf16[96,4,18,256]{3,0,2,1:T(8,128)(2,1)S(1)} %pad_maximum_fusion.1, bf16[3,3,32,96]{3,2,1,0:T(8,128)(2,1)S(1)} %bitcast.542), kind=kOutput, calls=%fused_computation.23 | convolution fusion | flops 50331648 | bytes 2629632 | tf_op jit(solution)/shard_map/qk,kdhw->qdhw/dot_general | solution.py:194
  61.6 0.7 fusion.23
  62.6 0.6 copy-done.8
  64.8 0.8 pad_maximum_fusion.6
  65.5 2.0 %all_to_all.13 = f32[16,1,3456]{2,1,0:T(1,128)} reshape(f32[2,9,32,96]{3,2,1,0:T(8,128)} %pad_maximum_fusion.6) | data formatting | bytes 442368 | tf_op jit(solution)/shard_map/all_to_all | solution.py:44
  67.5 11.2 %all-to-all-start = ((f32[16,1,3456]{2,1,0:T(1,128)}), f32[16,1,3456]{2,1,0:T(1,128)}, u32[]{:S(2)}, u32[]{:S(2)}) async-start(f32[16,1,3456]{2,1,0:T(1,128)} %all_to_all.13), calls=%async_computation | async-start | bytes 442368 | tf_op jit(solution)/shard_map/all_to_all | solution.py:44
  78.8 1.2 %fusion.239 = f32[8,128,32]{1,2,0:T(8,128)S(1)} fusion(bf16[96,3,18,128]{3,0,2,1:T(8,128)(2,1)} %bitcast.515, bf16[3,3,32,96]{3,2,1,0:T(8,128)(2,1)} %reshape.213), kind=kOutput, calls=%fused_computation.213 | convolution fusion | flops 6291456 | bytes 335872 | tf_op jit(solution)/shard_map/ok,kdhw->odhw/dot_general | solution.py:124
  80.0 1.1 convolution_add_fusion.7
  81.1 1.1 convolution_add_fusion.6
  82.2 1.1 convolution_add_fusion.5
  83.3 1.1 convolution_add_fusion.4
  84.4 1.8 %convolution_add_fusion.3 = f32[8,128,32]{1,2,0:T(8,128)} fusion(f32[8,128,32]{1,2,0:T(8,128)S(1)} %convolution_add_fusion.4, bf16[96,3,18,128]{3,0,2,1:T(8,128)(2,1)} %bitcast.520, bf16[3,3,32,96]{3,2,1,0:T(8,128)(2,1)} %reshape.213), kind=kOutput, calls=%fused_computation.100 | convolution fusion | flops 6324224 | bytes 466944 | tf_op jit(solution)/shard_map/ok,kdhw->odhw/dot_general | solution.py:124
  86.2 4.5 %fusion.116 = bf16[32,2,16,256]{3,0,2,1:T(8,128)(2,1)} fusion(f32[2,16,256,32]{2,3,1,0:T(8,128)} %fusion.5, f32[2,16,256,32]{2,3,1,0:T(8,128)} %fusion.7, f32[2,16,256,32]{2,3,1,0:T(8,128)} %fusion.9, f32[2,16,256,32]{2,3,1,0:T(8,128)S(1)} %copy-done.1, f32[2,16,256,32]{2,3,1,0:T(8,128)S(1)} %copy-done.2, f32[2,16,256,32]{2,3,1,0:T(8,128)} %fusion.15, ...), kind=kOutput, calls=%fused_computation.94 | convolution fusion | flops 52690944 | bytes 10493952 | tf_op jit(solution)/shard_map/qk,kdhw->qdhw/dot_general | solution.py:194
  90.7 1.1 reduce_sum.9
  91.8 0.8 broadcast_in_dim.5
  92.6 6.0 %all-to-all-start.1 = ((f32[16,1,3456]{2,1,0:T(1,128)}), f32[16,1,3456]{2,1,0:T(1,128)S(1)}, u32[]{:S(2)}, u32[]{:S(2)}) async-start(f32[16,1,3456]{2,1,0:T(1,128)} %broadcast_in_dim.5), calls=%async_computation.1 | async-start | bytes 442368 | tf_op jit(solution)/shard_map/all_to_all | solution.py:45
  98.5 1.2 %convolution_add_fusion.2 = f32[8,128,32]{1,2,0:T(8,128)S(1)} fusion(f32[8,128,32]{1,2,0:T(8,128)} %convolution_add_fusion.3, bf16[96,3,18,128]{3,0,2,1:T(8,128)(2,1)} %bitcast.521, bf16[3,3,32,96]{3,2,1,0:T(8,128)(2,1)} %reshape.213), kind=kOutput, calls=%fused_computation.99 | convolution fusion | flops 6324224 | bytes 466944 | tf_op jit(solution)/shard_map/ok,kdhw->odhw/dot_general | solution.py:124
  99.7 2.1 %copy.158 = bf16[32,2,16,256]{3,2,1,0:T(8,128)(2,1)} copy(bf16[32,2,16,256]{3,0,2,1:T(8,128)(2,1)} %fusion.116) | data formatting | bytes 1048576
  101.8 1.1 convolution_add_fusion.1
  102.9 1.1 fusion.128
  104.0 0.7 copy.157
  104.7 3.2 %all-to-all-done.1 = f32[16,1,3456]{2,1,0:T(1,128)S(1)} async-done(((f32[16,1,3456]{2,1,0:T(1,128)}), f32[16,1,3456]{2,1,0:T(1,128)S(1)}, u32[]{:S(2)}, u32[]{:S(2)}) %all-to-all-start.1) | async-done | bytes 221216 | tf_op jit(solution)/shard_map/all_to_all | solution.py:45
  108.4 0.7 reshape_reshape_reshape.3
  109.4 0.8 copy.155
  110.2 0.8 copy.156
  (82 shorter events, 9.3 us)
Async XLA Ops:
  0.6 9.4 %copy-start.14 = (s32[27]{0:T(128)S(1)}, s32[27]{0:T(128)}, u32[]{:S(2)}) copy-start(s32[27]{0:T(128)} %constant.33) | copy-start | bytes 328
  0.6 11.3 %copy-start.7 = (bf16[32,1,8,128]{3,2,1,0:T(8,128)(2,1)S(1)}, bf16[32,1,8,128]{3,2,1,0:T(8,128)(2,1)}, u32[]{:S(2)}) copy-start(bf16[32,1,8,128]{3,2,1,0:T(8,128)(2,1)} %param.9) | copy-start | bytes 196612
  0.7 9.4 %copy-start.5 = (bf16[27,32,32]{2,1,0:T(8,128)(2,1)S(1)}, bf16[27,32,32]{2,1,0:T(8,128)(2,1)}, u32[]{:S(2)}) copy-start(bf16[27,32,32]{2,1,0:T(8,128)(2,1)} %param.8) | copy-start | bytes 165892
  0.7 12.0 %copy-start.4 = (bf16[27,32,32]{2,1,0:T(8,128)(2,1)S(1)}, bf16[27,32,32]{2,1,0:T(8,128)(2,1)}, u32[]{:S(2)}) copy-start(bf16[27,32,32]{2,1,0:T(8,128)(2,1)} %param.7) | copy-start | bytes 165892
  1.6 13.1 %collective-permute-start.3 = (bf16[32,1,8,128]{3,0,2,1:T(8,128)(2,1)S(1)}, bf16[32,1,8,128]{3,0,2,1:T(8,128)(2,1)S(1)}, u32[]{:S(2)}, u32[]{:S(2)}) collective-permute-start(bf16[32,1,8,128]{3,0,2,1:T(8,128)(2,1)S(1)} %get-tuple-element.47), channel_id=1, source_target_pairs={{1,0},{2,1},{3,2},{4,3},{5,4},{6,5},{7,6},{8,7},{9,8},{10,9},{11,1... | collective-permute-start | bytes 196616 | tf_op jit(solution)/shard_map/ppermute | solution.py:24
  5.0 18.9 %collective-permute-start = (bf16[32,1,16,256]{3,0,2,1:T(8,128)(2,1)}, bf16[32,1,16,256]{3,0,2,1:T(8,128)(2,1)}, u32[]{:S(2)}, u32[]{:S(2)}) collective-permute-start(bf16[32,1,16,256]{3,0,2,1:T(8,128)(2,1)} %get-tuple-element.32), channel_id=1, source_target_pairs={{0,1},{1,2},{2,3},{3,4},{4,5},{5,6},{6,7},{7,8},{8,9},{9,10},{10,1... | collective-permute-start | bytes 786440 | tf_op jit(solution)/shard_map/ppermute | solution.py:15
  8.7 15.2 %collective-permute-start.1 = (bf16[32,1,16,256]{3,0,2,1:T(8,128)(2,1)S(1)}, bf16[32,1,16,256]{3,0,2,1:T(8,128)(2,1)}, u32[]{:S(2)}, u32[]{:S(2)}) collective-permute-start(bf16[32,1,16,256]{3,0,2,1:T(8,128)(2,1)S(1)} %get-tuple-element.33), channel_id=1, source_target_pairs={{1,0},{2,1},{3,2},{4,3},{5,4},{6,5},{7,6},{8,7},{9,8},{10,9},{11,1... | collective-permute-start | bytes 786440 | tf_op jit(solution)/shard_map/ppermute | solution.py:16
  10.7 4.4 %copy-start.3 = (bf16[27,32,32]{2,1,0:T(8,128)(2,1)}, bf16[27,32,32]{2,1,0:T(8,128)(2,1)S(1)}, u32[]{:S(2)}) copy-start(bf16[27,32,32]{2,1,0:T(8,128)(2,1)S(1)} %gather_fusion) | copy-start | bytes 165892
  13.8 1.6 %copy-start.9 = (bf16[2,32,32]{2,1,0:T(8,128)(2,1)S(1)}, bf16[2,32,32]{2,1,0:T(8,128)(2,1)}, u32[]{:S(2)}) copy-start(bf16[2,32,32]{2,1,0:T(8,128)(2,1)} %get-tuple-element.45) | copy-start | bytes 12292
  13.8 2.0 %copy-start.12 = (bf16[4,32,32]{2,1,0:T(8,128)(2,1)S(1)}, bf16[4,32,32]{2,1,0:T(8,128)(2,1)}, u32[]{:S(2)}) copy-start(bf16[4,32,32]{2,1,0:T(8,128)(2,1)} %get-tuple-element.42) | copy-start | bytes 24580
  14.8 1.4 %copy-start.11 = (bf16[4,32,32]{2,1,0:T(8,128)(2,1)S(1)}, bf16[4,32,32]{2,1,0:T(8,128)(2,1)}, u32[]{:S(2)}) copy-start(bf16[4,32,32]{2,1,0:T(8,128)(2,1)} %get-tuple-element.41) | copy-start | bytes 24580
  15.2 1.2 %copy-start.10 = (bf16[4,32,32]{2,1,0:T(8,128)(2,1)S(1)}, bf16[4,32,32]{2,1,0:T(8,128)(2,1)}, u32[]{:S(2)}) copy-start(bf16[4,32,32]{2,1,0:T(8,128)(2,1)} %get-tuple-element.40) | copy-start | bytes 24580
  15.4 1.2 %slice-start = ((bf16[27,32,32]{2,1,0:T(8,128)(2,1)}), bf16[8,32,32]{2,1,0:T(8,128)(2,1)S(1)}, s32[]{:S(2)}) async-start(bf16[27,32,32]{2,1,0:T(8,128)(2,1)} %copy-done.3), calls=%async_computation.2 | async-start | bytes 131072 | tf_op jit(solution)/shard_map/slice | solution.py:163
  36.2 25.4 %collective-permute-start.2 = (bf16[32,1,16,256]{3,0,2,1:T(8,128)(2,1)S(1)}, bf16[32,1,16,256]{3,0,2,1:T(8,128)(2,1)S(1)}, u32[]{:S(2)}, u32[]{:S(2)}) collective-permute-start(bf16[32,1,16,256]{3,0,2,1:T(8,128)(2,1)S(1)} %slice.393), channel_id=1, source_target_pairs={{0,1},{1,2},{2,3},{3,4},{4,5},{5,6},{6,7},{7,8},{8,9},{9,10},{10,1... | collective-permute-start | bytes 786440 | tf_op jit(solution)/shard_map/ppermute | solution.py:24
  40.7 5.7 %collective-permute-start.4 = (bf16[32,1,16,256]{3,0,2,1:T(8,128)(2,1)S(1)}, bf16[32,1,16,256]{3,0,2,1:T(8,128)(2,1)S(1)}, u32[]{:S(2)}, u32[]{:S(2)}) collective-permute-start(bf16[32,1,16,256]{3,0,2,1:T(8,128)(2,1)S(1)} %get-tuple-element.30), channel_id=1, source_target_pairs={{0,1},{1,2},{2,3},{3,4},{4,5},{5,6},{6,7},{7,8},{8,9},{9,10},{10,1... | collective-permute-start | bytes 786440 | tf_op jit(solution)/shard_map/ppermute | solution.py:15
  44.4 3.7 %collective-permute-start.5 = (bf16[32,1,16,256]{3,0,2,1:T(8,128)(2,1)S(1)}, bf16[32,1,16,256]{3,0,2,1:T(8,128)(2,1)S(1)}, u32[]{:S(2)}, u32[]{:S(2)}) collective-permute-start(bf16[32,1,16,256]{3,0,2,1:T(8,128)(2,1)S(1)} %get-tuple-element.31), channel_id=1, source_target_pairs={{1,0},{2,1},{3,2},{4,3},{5,4},{6,5},{7,6},{8,7},{9,8},{10,9},{11,1... | collective-permute-start | bytes 786440 | tf_op jit(solution)/shard_map/ppermute | solution.py:16
  50.0 0.9 copy-start.6
  60.3 1.3 %copy-start.13 = (s32[3,128]{1,0:T(4,128)S(1)}, s32[3,128]{1,0:T(4,128)}, u32[]{:S(2)}) copy-start(s32[3,128]{1,0:T(4,128)} %add_add_fusion) | copy-start | bytes 4612
  62.3 0.8 copy-start.8
  62.6 2.0 %copy-start = (bf16[3,32,3,18,128]{4,1,0,3,2:T(8,128)(2,1)}, bf16[3,32,3,18,128]{4,1,0,3,2:T(8,128)(2,1)S(1)}, u32[]{:S(2)}) copy-start(bf16[3,32,3,18,128]{4,1,0,3,2:T(8,128)(2,1)S(1)} %copy.121) | copy-start | bytes 3981316
  67.5 23.2 %all-to-all-start = ((f32[16,1,3456]{2,1,0:T(1,128)}), f32[16,1,3456]{2,1,0:T(1,128)}, u32[]{:S(2)}, u32[]{:S(2)}) async-start(f32[16,1,3456]{2,1,0:T(1,128)} %all_to_all.13), calls=%async_computation | async-start | bytes 442368 | tf_op jit(solution)/shard_map/all_to_all | solution.py:44
  78.7 7.5 %copy-start.1 = (f32[2,16,256,32]{2,3,1,0:T(8,128)S(1)}, f32[2,16,256,32]{2,3,1,0:T(8,128)}, u32[]{:S(2)}) copy-start(f32[2,16,256,32]{2,3,1,0:T(8,128)} %fusion.11) | copy-start | bytes 3145732
  78.8 7.4 %copy-start.2 = (f32[2,16,256,32]{2,3,1,0:T(8,128)S(1)}, f32[2,16,256,32]{2,3,1,0:T(8,128)}, u32[]{:S(2)}) copy-start(f32[2,16,256,32]{2,3,1,0:T(8,128)} %fusion.13) | copy-start | bytes 3145732
  92.6 15.3 %all-to-all-start.1 = ((f32[16,1,3456]{2,1,0:T(1,128)}), f32[16,1,3456]{2,1,0:T(1,128)S(1)}, u32[]{:S(2)}, u32[]{:S(2)}) async-start(f32[16,1,3456]{2,1,0:T(1,128)} %broadcast_in_dim.5), calls=%async_computation.1 | async-start | bytes 442368 | tf_op jit(solution)/shard_map/all_to_all | solution.py:45

commit v3 on v2

--- a/solution.py
+++ b/solution.py
@@ -83,13 +83,17 @@
     front_one = forward_kernel(weight_one)
     front_two = forward_kernel(weight_two)
     rear_one = backward_kernel(weight_one).transpose(0, 1, 3, 2)
-    padded = pad_sides(extended_2(volume, (("slab", 1),), 1))
+    padded = pad_sides(extended_2(volume, (("slab", 1),), 2))
     volume_cols = column_stack(padded, 1, columns, lambda along_cols: along_cols)
-    preact = jnp.zeros((channels, planes, height, columns), jnp.float32)
+    cot_ext = extended_2(cotangent, (("slab", 1),), 1)
+    devices = lax.axis_size("slab")
+    place = lax.axis_index("slab") * planes + jnp.arange(-1, planes + 1)
+    inside = ((place >= 0) & (place < devices * planes))[None, :, None, None]
+    preact = jnp.zeros((channels, planes + 2, height, columns), jnp.float32)
     for along_depth in range(3):
         for along_rows in range(3):
             window = volume_cols[
-                :, along_depth : along_depth + planes, along_rows : along_rows + height, :
+                :, along_depth : along_depth + planes + 2, along_rows : along_rows + height, :
             ]
             preact = preact + jnp.einsum(
                 "ok,kdhw->odhw",
@@ -97,10 +101,8 @@
                 window,
                 preferred_element_type=jnp.float32,
             )
-    hidden = jax.nn.silu(preact).astype(jnp.bfloat16)
-    upper_plane = passed_along(cotangent, "slab", -1)
-    lower_plane = passed_along(hidden[:, planes - 1 :], "slab", 1)
-    stacked = jnp.concatenate([lower_plane, hidden], 1)
+    hidden = jnp.where(inside, jax.nn.silu(preact), 0.0).astype(jnp.bfloat16)
+    stacked = hidden[:, : planes + 1]
     stacked = jnp.pad(stacked, ((0, 0), (0, 0), (1, 1), (0, 0)))
     picks = jnp.arange(columns)[:, None, None] == (
         2 * jnp.arange(half_cols)[None, None, :] + jnp.arange(3)[None, :, None] - 1
@@ -130,8 +132,8 @@
             terms_two.append(
                 jnp.einsum("odhw,kdhw->ok", cotangent, window, preferred_element_type=jnp.float32)
             )
-    extended = jnp.concatenate([cotangent, upper_plane], 1)
-    extended = jnp.pad(extended, ((0, 0), (0, 0), (0, 1), (0, 1)))
+    extended = jnp.pad(cot_ext, ((0, 0), (0, 1), (0, 1), (0, 1)))
+    class_planes = half_planes + 2
     parity_taps = [[(1, 0)], [(2, 0), (0, 1)]]
     order = []
     for depth_parity in range(2):
@@ -154,7 +156,7 @@
                             pieces.append(
                                 extended[
                                     :,
-                                    skip_depth : skip_depth + half_planes,
+                                    skip_depth : skip_depth + class_planes,
                                     skip_row : skip_row + half_rows,
                                     skip_col : skip_col + half_cols,
                                 ]
@@ -167,20 +169,22 @@
                         "kq,kdhw->qdhw", joined_kernel, joined, preferred_element_type=jnp.float32
                     )
                 )
-    parity_grid = jnp.stack(classes).reshape(2, 2, 2, channels, half_planes, half_rows, half_cols)
+    parity_grid = jnp.stack(classes).reshape(2, 2, 2, channels, class_planes, half_rows, half_cols)
     grad_hidden = parity_grid.transpose(3, 4, 0, 5, 1, 6, 2).reshape(
-        channels, planes, height, columns
-    )
+        channels, 2 * class_planes, height, columns
+    )[:, 1 : planes + 3]
     sigma = jax.nn.sigmoid(preact)
-    grad_pre = (grad_hidden * (sigma * (1.0 + preact * (1.0 - sigma)))).astype(jnp.bfloat16)
-    rimmed = pad_sides(extended_2(grad_pre, (("slab", 1),), 1))
+    grad_rim = grad_hidden * (sigma * (1.0 + preact * (1.0 - sigma)))
+    grad_rim = jnp.where(inside, grad_rim, 0.0).astype(jnp.bfloat16)
+    grad_pre = grad_rim[:, 1 : planes + 1]
+    rimmed = pad_sides(grad_rim)
     rimmed_cols = column_stack(rimmed, 1, columns, lambda along_cols: 2 - along_cols)
     grad_volume = jnp.zeros((channels, planes, height, columns), jnp.float32)
     terms_one = []
     for along_depth in range(3):
         for along_rows in range(3):
             window = volume_cols[
-                :, along_depth : along_depth + planes, along_rows : along_rows + height, :
+                :, along_depth + 1 : along_depth + 1 + planes, along_rows : along_rows + height, :
             ]
             terms_one.append(
                 jnp.einsum("odhw,kdhw->ok", grad_pre, window, preferred_element_type=jnp.float32)

time: 112 us -> 112 us (level)
  local copies, waits for them, and re-layouts: 26.2 us -> 45.6 us
  matrix products: 39.1 us -> 24.7 us
  starting transfers between devices: 33.1 us -> 23 us
  waiting for transfers between devices: 4.73 us -> 9.96 us
    dot_general x9, matrix products: 15.2 us -> 3.23 us  [on_device(): jnp.einsum('qk,kdhw->qdhw', rear_one[along_depth, along_rows], back_windo...]
    dot_general x9, matrix products: 10.7 us -> 1.35 us  [on_device(): jnp.einsum('ok,kdhw->odhw', front_two[along_depth, along_rows], window, p...]
    reshape x1, local copies, waits for them, and re-layouts: 4.34 us -> 12.6 us  [on_device(): jnp.stack(classes)]
    slice x3 -> x1, local copies, waits for them, and re-layouts: 0.84 us -> 7.6 us  [on_device(): parity_grid.transpose(3, 4, 0, 5, 1, 6, 2)]
    dot_general x9, matrix products: 3.68 us -> 10 us  [on_device(): jnp.einsum('ok,kdhw->odhw', front_one[along_depth, along_rows], window, p...]
    ppermute x2 -> x0, starting transfers between devices: 5.75 us -> none  [passed_along(): return lax.ppermute(block, axis, route)]
    unnamed x40 -> x38, local copies, waits for them, and re-layouts: 6.65 us -> 12.3 us
    all_to_all x1, waiting for transfers between devices: 3.18 us -> 7.1 us  [summed_over(): lax.all_to_all(jnp.broadcast_to(mine, flat.shape), axis, 0, 0, tiled=True)]
  transfers between devices with their start and end apart: 8 -> 6, of which waited for: 2 -> 2; matrix products, arithmetic and copies ran while one was open for 43% -> 39% of each run, Pallas kernels for 0% -> 0%
where the time goes in v3:
time: 112 us; the launch traced here: 111 us
  local copies, waits for them, and re-layouts  45.6 us (41%)
  matrix products  24.7 us (22%)
  starting transfers between devices  23 us (21%)
  waiting for transfers between devices  9.96 us (9%)
  other arithmetic  6.84 us (6%)
  between operations  1.19 us (1%)
    reshape x1, local copies, waits for them, and re-layouts, on_device(): jnp.stack(classes)  12.6 us
    unnamed x38, local copies, waits for them, and re-layouts  12.3 us
    dot_general x9, matrix products, on_device(): jnp.einsum('ok,kdhw->odhw', front_one[along_depth, along_rows], window, p...  10 us
    ppermute x2, starting transfers between devices, extended_2(): before = lax.ppermute(last, axis, up)  8.48 us
    all_to_all x1, starting transfers between devices, summed_over(): mine = lax.all_to_all(flat, axis, 0, 0, tiled=True).sum(0, keepdims=True)  8.45 us
    slice x1, local copies, waits for them, and re-layouts, on_device(): parity_grid.transpose(3, 4, 0, 5, 1, 6, 2)  7.6 us
    all_to_all x1, waiting for transfers between devices, summed_over(): lax.all_to_all(jnp.broadcast_to(mine, flat.shape), axis, 0, 0, tiled=True)  7.1 us
    dot_general x9, matrix products, on_device(): jnp.einsum('odhw,kdhw->ok', grad_pre, window, preferred_element_type=jnp....  5.74 us
  transfers between devices with their start and end apart: 6, of which 2 were waited for; matrix products, arithmetic and copies ran while one was open for 39% of the time, Pallas kernels for 0%

profile of v3, /device:TPU:0, one launch (start us, length us, event | category | flops | bytes accessed | tf_op | source)
XLA Modules:
  0.0 111.4 jit_solution(4646513925318622365)
XLA Ops:
  0.7 0.9 copy.103
  1.6 2.5 %collective-permute-start.2 = (bf16[32,1,8,128]{3,0,2,1:T(8,128)(2,1)S(1)}, bf16[32,1,8,128]{3,0,2,1:T(8,128)(2,1)S(1)}, u32[]{:S(2)}, u32[]{:S(2)}) collective-permute-start(bf16[32,1,8,128]{3,0,2,1:T(8,128)(2,1)S(1)} %copy.103), channel_id=1, source_target_pairs={{0,1},{1,2},{2,3},{3,4},{4,5},{5,6},{6,7},{7,8},{8,9},{9,10},{10,1... | collective-permute-start | bytes 196616 | tf_op jit(solution)/shard_map/ppermute | solution.py:15
  4.1 1.3 %collective-permute-start.3 = (bf16[32,1,8,128]{3,0,2,1:T(8,128)(2,1)S(1)}, bf16[32,1,8,128]{3,0,2,1:T(8,128)(2,1)S(1)}, u32[]{:S(2)}, u32[]{:S(2)}) collective-permute-start(bf16[32,1,8,128]{3,0,2,1:T(8,128)(2,1)S(1)} %copy.103), channel_id=1, source_target_pairs={{1,0},{2,1},{3,2},{4,3},{5,4},{6,5},{7,6},{8,7},{9,8},{10,9},{11,1... | collective-permute-start | bytes 196616 | tf_op jit(solution)/shard_map/ppermute | solution.py:16
  5.4 2.1 %copy.96 = bf16[32,2,16,256]{3,0,2,1:T(8,128)(2,1)} copy(bf16[32,2,16,256]{3,2,1,0:T(8,128)(2,1)} %param.6) | data formatting | bytes 1048576 | tf_op args[0]
  7.6 6.0 %collective-permute-start = (bf16[32,2,16,256]{3,0,2,1:T(8,128)(2,1)}, bf16[32,2,16,256]{3,0,2,1:T(8,128)(2,1)}, u32[]{:S(2)}, u32[]{:S(2)}) collective-permute-start(bf16[32,2,16,256]{3,0,2,1:T(8,128)(2,1)} %copy.96), channel_id=1, source_target_pairs={{0,1},{1,2},{2,3},{3,4},{4,5},{5,6},{6,7},{7,8},{8,9},{9,10},{10,1... | collective-permute-start | bytes 1572872 | tf_op jit(solution)/shard_map/ppermute | solution.py:15
  13.5 1.3 %collective-permute-start.1 = (bf16[32,2,16,256]{3,0,2,1:T(8,128)(2,1)}, bf16[32,2,16,256]{3,0,2,1:T(8,128)(2,1)}, u32[]{:S(2)}, u32[]{:S(2)}) collective-permute-start(bf16[32,2,16,256]{3,0,2,1:T(8,128)(2,1)} %copy.96), channel_id=1, source_target_pairs={{1,0},{2,1},{3,2},{4,3},{5,4},{6,5},{7,6},{8,7},{9,8},{10,9},{11,1... | collective-permute-start | bytes 1572872 | tf_op jit(solution)/shard_map/ppermute | solution.py:16
  14.8 0.7 pad_clamp_fusion
  15.5 1.5 %gather_fusion = bf16[27,32,32]{2,1,0:T(8,128)(2,1)S(1)} fusion(bf16[27,32,32]{2,1,0:T(8,128)(2,1)} %param.8, s32[1024]{0:T(1024)S(1)} %pad_clamp_fusion), kind=kCustom, calls=%fused_computation | custom fusion | bytes 110700 | tf_op jit(solution)/shard_map/gather | solution.py:146
  17.0 0.6 fusion.244
  17.6 0.6 fusion.243
  18.9 0.8 reshape.183
  20.7 0.4 fusion.186
  23.0 0.4 fusion.95
  23.4 12.6 %copy.113 = f32[2,2,2,32,3,8,128]{3,2,6,1,5,0,4:T(2,128)} copy(f32[2,2,2,32,3,8,128]{6,3,5,4,2,1,0:T(8,128)S(1)} %bitcast.503) | data formatting | bytes 6291456 | tf_op jit(solution)/shard_map/reshape | solution.py:172
  35.9 7.6 %slice.431 = f32[32,4,16,256]{0,3,2,1:T(8,128)} slice(f32[32,6,16,256]{0,3,2,1:T(8,128)} %bitcast.483), slice={[0:32], [1:5], [0:16], [0:256]} | slice | bytes 4194304 | tf_op jit(solution)/shard_map/slice | solution.py:173
  43.5 5.1 %copy.191 = f32[32,4,16,256]{3,0,2,1:T(8,128)S(1)} copy(f32[32,4,16,256]{0,3,2,1:T(8,128)} %slice.431) | data formatting | bytes 4194304
  48.7 2.8 %select_maximum_fusion = bf16[32,6,18,258]{3,0,2,1:T(8,128)(2,1)S(1)} fusion(bf16[32,2,16,256]{3,0,2,1:T(8,128)(2,1)} %collective-permute-done.1, bf16[32,2,16,256]{3,0,2,1:T(8,128)(2,1)} %copy.96, bf16[32,2,16,256]{3,0,2,1:T(8,128)(2,1)} %collective-permute-done), kind=kLoop, calls=%fused_computation.28 | loop fusion | flops 16941312 | bytes 3356160 | tf_op jit(solution)/shard_map/concatenate | solution.py:17
  51.4 1.4 %fusion.241 = (bf16[32,6,18,256]{3,0,2,1:T(8,128)(2,1)S(1)}, bf16[32,6,18,256]{3,0,2,1:T(8,128)(2,1)S(1)}, bf16[32,6,18,256]{3,0,2,1:T(8,128)(2,1)S(1)}) fusion(bf16[32,6,18,258]{3,0,2,1:T(8,128)(2,1)S(1)} %select_maximum_fusion), kind=kLoop, calls=%fused_computation.284 | loop fusion | bytes 10616832 | tf_op jit(solution)/shard_map/slice | solution.py:35
  52.9 0.4 pad_maximum_fusion
  53.3 0.6 fusion.11
  53.8 0.6 fusion.13
  54.4 0.6 fusion.15
  54.9 0.6 fusion.17
  55.5 0.6 fusion.19
  56.0 0.6 fusion.5
  56.6 0.6 fusion.7
  57.2 1.9 %fusion.9 = f32[4,16,256,32]{2,3,1,0:T(8,128)} fusion(bf16[96,6,18,256]{3,0,2,1:T(8,128)(2,1)S(1)} %pad_maximum_fusion, bf16[3,3,32,96]{3,2,1,0:T(8,128)(2,1)S(1)} %reshape.179), kind=kOutput, calls=%fused_computation.16 | convolution fusion | flops 100663296 | bytes 5251072 | tf_op jit(solution)/shard_map/ok,kdhw->odhw/dot_general | solution.py:98
  59.0 4.3 %select_convert_fusion = (bf16[32,4,16,256]{3,0,2,1:T(8,128)(2,1)S(1)}, f32[32,4,16,256]{3,0,2,1:T(8,128)}, f32[32,4,16,256]{3,0,2,1:T(8,128)}) fusion(f32[32,4,16,256]{3,0,2,1:T(8,128)S(1)} %copy.191, pred[4]{0:T(512)(128)(4,1)S(1)} %compare_and_fusion, bf16[96,6,18,256]{3,0,2,1:T(8,128)(2,1)S(1)} %pad_maximum_fusion, ...), kind=kOutput, calls=%fused_computation.34 | convolution fusion | flops 110100480 | bytes 27271680 | tf_op jit(solution)/shard_map/ok,kdhw->odhw/dot_general | solution.py:98
  63.3 0.6 fusion.117
  63.9 2.4 %pad_slice_fusion.2 = (bf16[32,4,18,256]{3,0,2,1:T(8,128)(2,1)S(1)}, bf16[32,4,18,256]{3,0,2,1:T(8,128)(2,1)}, bf16[32,4,18,256]{3,0,2,1:T(8,128)(2,1)}) fusion(bf16[32,4,16,256]{3,0,2,1:T(8,128)(2,1)S(1)} %get-tuple-element.23), kind=kLoop, calls=%fused_computation.38 | loop fusion | bytes 4587520 | tf_op jit(solution)/shard_map/slice | solution.py:35
  66.4 0.6 fusion.123
  67.0 0.6 fusion.129
  67.6 0.6 fusion.135
  68.3 0.6 fusion.141
  68.9 0.6 fusion.147
  69.6 0.6 fusion.153
  70.2 0.6 fusion.159
  70.9 0.6 fusion.165
  71.8 0.6 copy-done.1
  72.5 0.5 fusion.63
  73.0 0.7 fusion.64
  75.6 1.0 all_to_all.13
  76.6 8.5 %all-to-all-start = ((f32[16,1,3456]{2,1,0:T(1,128)}), f32[16,1,3456]{2,1,0:T(1,128)S(1)}, u32[]{:S(2)}, u32[]{:S(2)}) async-start(f32[16,1,3456]{2,1,0:T(1,128)} %all_to_all.13), calls=%async_computation | async-start | bytes 442368 | tf_op jit(solution)/shard_map/all_to_all | solution.py:44
  85.0 1.8 %pad_maximum_fusion.1 = bf16[96,4,18,256]{3,0,2,1:T(8,128)(2,1)S(1)} fusion(bf16[32,4,18,256]{3,0,2,1:T(8,128)(2,1)} %get-tuple-element.29, bf16[32,4,18,256]{3,0,2,1:T(8,128)(2,1)} %get-tuple-element.28, bf16[32,4,18,256]{3,0,2,1:T(8,128)(2,1)S(1)} %get-tuple-element.27), kind=kLoop, calls=%fused_computation.9 | loop fusion | flops 10616832 | bytes 7077888 | tf_op jit(solution)/shard_map/concatenate | solution.py:36
  86.8 0.3 fusion.58
  87.2 0.4 fusion.65
  87.5 0.4 fusion.68
  87.9 0.4 fusion.71
  88.3 0.4 fusion.74
  88.6 0.4 fusion.77
  89.0 0.4 fusion.80
  89.4 0.4 fusion.83
  89.7 0.5 copy-done.5
  91.2 0.4 fusion.92
  91.5 2.9 %all-to-all-done = f32[16,1,3456]{2,1,0:T(1,128)S(1)} async-done(((f32[16,1,3456]{2,1,0:T(1,128)}), f32[16,1,3456]{2,1,0:T(1,128)S(1)}, u32[]{:S(2)}, u32[]{:S(2)}) %all-to-all-start) | async-done | bytes 221216 | tf_op jit(solution)/shard_map/all_to_all | solution.py:44
  94.5 0.8 broadcast_in_dim.32
  95.3 3.5 %all-to-all-start.1 = ((f32[16,1,3456]{2,1,0:T(1,128)}), f32[16,1,3456]{2,1,0:T(1,128)S(1)}, u32[]{:S(2)}, u32[]{:S(2)}) async-start(f32[16,1,3456]{2,1,0:T(1,128)} %broadcast_in_dim.32), calls=%async_computation.1 | async-start | bytes 442368 | tf_op jit(solution)/shard_map/all_to_all | solution.py:45
  99.0 1.1 copy.130
  100.4 0.7 copy.129
  101.1 7.1 %all-to-all-done.1 = f32[16,1,3456]{2,1,0:T(1,128)S(1)} async-done(((f32[16,1,3456]{2,1,0:T(1,128)}), f32[16,1,3456]{2,1,0:T(1,128)S(1)}, u32[]{:S(2)}, u32[]{:S(2)}) %all-to-all-start.1) | async-done | bytes 221216 | tf_op jit(solution)/shard_map/all_to_all | solution.py:45
  108.2 0.5 reduce.1
  108.7 0.7 reshape_reshape_reshape.3
  109.7 0.8 copy.127
  110.6 0.8 copy.128
  (73 shorter events, 7.3 us)
Async XLA Ops:
  0.6 18.1 %copy-start.4 = (bf16[27,32,32]{2,1,0:T(8,128)(2,1)S(1)}, bf16[27,32,32]{2,1,0:T(8,128)(2,1)}, u32[]{:S(2)}) copy-start(bf16[27,32,32]{2,1,0:T(8,128)(2,1)} %param.8) | copy-start | bytes 165892
  0.6 17.6 %copy-start.3 = (bf16[27,32,32]{2,1,0:T(8,128)(2,1)S(1)}, bf16[27,32,32]{2,1,0:T(8,128)(2,1)}, u32[]{:S(2)}) copy-start(bf16[27,32,32]{2,1,0:T(8,128)(2,1)} %param.7) | copy-start | bytes 165892
  1.6 18.2 %copy-start.6 = (bf16[32,1,8,128]{3,2,1,0:T(8,128)(2,1)S(1)}, bf16[32,1,8,128]{3,2,1,0:T(8,128)(2,1)}, u32[]{:S(2)}) copy-start(bf16[32,1,8,128]{3,2,1,0:T(8,128)(2,1)} %param.9) | copy-start | bytes 196612
  1.6 18.2 %collective-permute-start.2 = (bf16[32,1,8,128]{3,0,2,1:T(8,128)(2,1)S(1)}, bf16[32,1,8,128]{3,0,2,1:T(8,128)(2,1)S(1)}, u32[]{:S(2)}, u32[]{:S(2)}) collective-permute-start(bf16[32,1,8,128]{3,0,2,1:T(8,128)(2,1)S(1)} %copy.103), channel_id=1, source_target_pairs={{0,1},{1,2},{2,3},{3,4},{4,5},{5,6},{6,7},{7,8},{8,9},{9,10},{10,1... | collective-permute-start | bytes 196616 | tf_op jit(solution)/shard_map/ppermute | solution.py:15
  4.1 15.7 %collective-permute-start.3 = (bf16[32,1,8,128]{3,0,2,1:T(8,128)(2,1)S(1)}, bf16[32,1,8,128]{3,0,2,1:T(8,128)(2,1)S(1)}, u32[]{:S(2)}, u32[]{:S(2)}) collective-permute-start(bf16[32,1,8,128]{3,0,2,1:T(8,128)(2,1)S(1)} %copy.103), channel_id=1, source_target_pairs={{1,0},{2,1},{3,2},{4,3},{5,4},{6,5},{7,6},{8,7},{9,8},{10,9},{11,1... | collective-permute-start | bytes 196616 | tf_op jit(solution)/shard_map/ppermute | solution.py:16
  7.6 41.1 %collective-permute-start = (bf16[32,2,16,256]{3,0,2,1:T(8,128)(2,1)}, bf16[32,2,16,256]{3,0,2,1:T(8,128)(2,1)}, u32[]{:S(2)}, u32[]{:S(2)}) collective-permute-start(bf16[32,2,16,256]{3,0,2,1:T(8,128)(2,1)} %copy.96), channel_id=1, source_target_pairs={{0,1},{1,2},{2,3},{3,4},{4,5},{5,6},{6,7},{7,8},{8,9},{9,10},{10,1... | collective-permute-start | bytes 1572872 | tf_op jit(solution)/shard_map/ppermute | solution.py:15
  13.5 35.1 %collective-permute-start.1 = (bf16[32,2,16,256]{3,0,2,1:T(8,128)(2,1)}, bf16[32,2,16,256]{3,0,2,1:T(8,128)(2,1)}, u32[]{:S(2)}, u32[]{:S(2)}) collective-permute-start(bf16[32,2,16,256]{3,0,2,1:T(8,128)(2,1)} %copy.96), channel_id=1, source_target_pairs={{1,0},{2,1},{3,2},{4,3},{5,4},{6,5},{7,6},{8,7},{9,8},{10,9},{11,1... | collective-permute-start | bytes 1572872 | tf_op jit(solution)/shard_map/ppermute | solution.py:16
  17.0 3.3 %copy-start.2 = (bf16[27,32,32]{2,1,0:T(8,128)(2,1)}, bf16[27,32,32]{2,1,0:T(8,128)(2,1)S(1)}, u32[]{:S(2)}) copy-start(bf16[27,32,32]{2,1,0:T(8,128)(2,1)S(1)} %gather_fusion) | copy-start | bytes 165892
  20.1 1.0 copy-start.8
  20.5 1.1 copy-start.11
  21.3 0.8 copy-start.10
  21.9 0.8 copy-start.9
  22.1 0.8 slice-start
  70.2 1.6 %copy-start = (f32[32,4,16,256]{3,0,2,1:T(8,128)S(1)}, f32[32,4,16,256]{3,0,2,1:T(8,128)}, u32[]{:S(2)}) copy-start(f32[32,4,16,256]{3,0,2,1:T(8,128)} %get-tuple-element.24) | copy-start | bytes 6291460
  70.2 2.3 %copy-start.1 = (f32[32,4,16,256]{3,0,2,1:T(8,128)S(1)}, f32[32,4,16,256]{3,0,2,1:T(8,128)}, u32[]{:S(2)}) copy-start(f32[32,4,16,256]{3,0,2,1:T(8,128)} %get-tuple-element.49) | copy-start | bytes 6291460
  73.0 0.9 copy-start.7
  76.6 17.8 %all-to-all-start = ((f32[16,1,3456]{2,1,0:T(1,128)}), f32[16,1,3456]{2,1,0:T(1,128)S(1)}, u32[]{:S(2)}, u32[]{:S(2)}) async-start(f32[16,1,3456]{2,1,0:T(1,128)} %all_to_all.13), calls=%async_computation | async-start | bytes 442368 | tf_op jit(solution)/shard_map/all_to_all | solution.py:44
  89.3 0.9 copy-start.5
  95.3 12.9 %all-to-all-start.1 = ((f32[16,1,3456]{2,1,0:T(1,128)}), f32[16,1,3456]{2,1,0:T(1,128)S(1)}, u32[]{:S(2)}, u32[]{:S(2)}) async-start(f32[16,1,3456]{2,1,0:T(1,128)} %broadcast_in_dim.32), calls=%async_computation.1 | async-start | bytes 442368 | tf_op jit(solution)/shard_map/all_to_all | solution.py:45

commit v4 on v3

--- a/solution.py
+++ b/solution.py
@@ -132,47 +132,26 @@
             terms_two.append(
                 jnp.einsum("odhw,kdhw->ok", cotangent, window, preferred_element_type=jnp.float32)
             )
-    extended = jnp.pad(cot_ext, ((0, 0), (0, 1), (0, 1), (0, 1)))
-    class_planes = half_planes + 2
-    parity_taps = [[(1, 0)], [(2, 0), (0, 1)]]
-    order = []
-    for depth_parity in range(2):
-        for row_parity in range(2):
-            for col_parity in range(2):
-                for tap_depth, _ in parity_taps[depth_parity]:
-                    for tap_row, _ in parity_taps[row_parity]:
-                        for tap_col, _ in parity_taps[col_parity]:
-                            order.append(9 * tap_depth + 3 * tap_row + tap_col)
-    ordered_two = weight_two[np.array(order)]
-    taken = 0
-    classes = []
-    for depth_parity in range(2):
-        for row_parity in range(2):
-            for col_parity in range(2):
-                pieces = []
-                for tap_depth, skip_depth in parity_taps[depth_parity]:
-                    for tap_row, skip_row in parity_taps[row_parity]:
-                        for tap_col, skip_col in parity_taps[col_parity]:
-                            pieces.append(
-                                extended[
-                                    :,
-                                    skip_depth : skip_depth + class_planes,
-                                    skip_row : skip_row + half_rows,
-                                    skip_col : skip_col + half_cols,
-                                ]
-                            )
-                joined = jnp.concatenate(pieces, 0)
-                joined_kernel = ordered_two[taken : taken + len(pieces)].reshape(-1, channels)
-                taken += len(pieces)
-                classes.append(
-                    jnp.einsum(
-                        "kq,kdhw->qdhw", joined_kernel, joined, preferred_element_type=jnp.float32
-                    )
-                )
-    parity_grid = jnp.stack(classes).reshape(2, 2, 2, channels, class_planes, half_rows, half_cols)
-    grad_hidden = parity_grid.transpose(3, 4, 0, 5, 1, 6, 2).reshape(
-        channels, 2 * class_planes, height, columns
-    )[:, 1 : planes + 3]
+    rear_two = backward_kernel(weight_two).transpose(0, 1, 3, 2)
+    spread = lax.pad(
+        cot_ext, jnp.zeros((), cot_ext.dtype), ((0, 0, 0), (0, 1, 1), (1, 2, 1), (1, 2, 1))
+    )
+    spread_cols = column_stack(spread, 1, columns, lambda along_cols: 2 - along_cols)
+    grad_hidden = jnp.zeros((channels, planes + 2, height, columns), jnp.float32)
+    for along_depth in range(3):
+        for along_rows in range(3):
+            back_window = spread_cols[
+                :,
+                2 - along_depth : 2 - along_depth + planes + 2,
+                2 - along_rows : 2 - along_rows + height,
+                :,
+            ]
+            grad_hidden = grad_hidden + jnp.einsum(
+                "qk,kdhw->qdhw",
+                rear_two[along_depth, along_rows],
+                back_window,
+                preferred_element_type=jnp.float32,
+            )
     sigma = jax.nn.sigmoid(preact)
     grad_rim = grad_hidden * (sigma * (1.0 + preact * (1.0 - sigma)))
     grad_rim = jnp.where(inside, grad_rim, 0.0).astype(jnp.bfloat16)

time: 112 us -> 128 us (1.14)
  matrix products: 24.7 us -> 53.1 us
  local copies, waits for them, and re-layouts: 45.6 us -> 28.2 us
  other arithmetic: 6.84 us -> 10.5 us
  starting transfers between devices: 23 us -> 25 us
    dot_general x9, matrix products: 10 us -> 23.8 us  [on_device(): jnp.einsum('ok,kdhw->odhw', front_one[along_depth, along_rows], window, p...]
    reshape x1 -> x0, local copies, waits for them, and re-layouts: 12.6 us -> none  [on_device(): jnp.stack(classes)]
    slice x5 -> x0, local copies, waits for them, and re-layouts: 8.96 us -> none  [the longest x1 7.6 us: on_device(): parity_grid.transpose(3, 4, 0, 5, 1, 6, 2)]
    pad x0 -> x1, local copies, waits for them, and re-layouts: none -> 8.52 us  [on_device(): lax.pad(cot_ext, jnp.zeros((), cot_ext.dtype), ((0, 0, 0), (0, 1, 1), (1,...]
    unnamed x38 -> x18, local copies, waits for them, and re-layouts: 12.3 us -> 5.37 us
    dot_general x8 -> x9, matrix products: 2.08 us -> 8.95 us  [on_device(): jnp.einsum('qk,kdhw->qdhw', rear_two[along_depth, along_rows], back_windo...]
    dot_general x9, matrix products: 3.23 us -> 7.54 us  [on_device(): jnp.einsum('qk,kdhw->qdhw', rear_one[along_depth, along_rows], back_windo...]
    dot_general x9, matrix products: 1.35 us -> 4.75 us  [on_device(): jnp.einsum('ok,kdhw->odhw', front_two[along_depth, along_rows], window, p...]
  transfers between devices with their start and end apart: 6 -> 6, of which waited for: 2 -> 2; matrix products, arithmetic and copies ran while one was open for 39% -> 23% of each run, Pallas kernels for 0% -> 0%
where the time goes in v4:
time: 128 us
  matrix products  53.1 us (41%)
  local copies, waits for them, and re-layouts  28.2 us (22%)
  starting transfers between devices  25 us (20%)
  other arithmetic  10.5 us (8%)
  waiting for transfers between devices  9.89 us (8%)
    dot_general x9, matrix products, on_device(): jnp.einsum('ok,kdhw->odhw', front_one[along_depth, along_rows], window, p...  23.8 us
    all_to_all x1, starting transfers between devices, summed_over(): mine = lax.all_to_all(flat, axis, 0, 0, tiled=True).sum(0, keepdims=True)  10 us
    dot_general x9, matrix products, on_device(): jnp.einsum('qk,kdhw->qdhw', rear_two[along_depth, along_rows], back_windo...  8.95 us
    pad x1, local copies, waits for them, and re-layouts, on_device(): lax.pad(cot_ext, jnp.zeros((), cot_ext.dtype), ((0, 0, 0), (0, 1, 1), (1,...  8.52 us
    ppermute x2, starting transfers between devices, extended_2(): before = lax.ppermute(last, axis, up)  8.2 us
    dot_general x9, matrix products, on_device(): jnp.einsum('qk,kdhw->qdhw', rear_one[along_depth, along_rows], back_windo...  7.54 us
    dot_general x9, matrix products, on_device(): jnp.einsum('odhw,kdhw->ok', grad_pre, window, preferred_element_type=jnp....  5.81 us
    slice x3, local copies, waits for them, and re-layouts, column_stack(): pieces.append(field[..., first:first + stride * (count - 1) + 1:stride])  5.53 us
  transfers between devices with their start and end apart: 6, of which 2 were waited for; matrix products, arithmetic and copies ran while one was open for 23% of the time, Pallas kernels for 0%

profile of v4, /device:TPU:0, one launch (start us, length us, event | category | flops | bytes accessed | tf_op | source)
XLA Modules:
  0.0 127.7 jit_solution(14446615661789568523)
XLA Ops:
  0.7 1.4 %copy.77 = bf16[32,2,16,256]{3,0,2,1:T(8,128)(2,1)S(1)} copy(bf16[32,2,16,256]{3,2,1,0:T(8,128)(2,1)} %param.4) | data formatting | bytes 1048576 | tf_op args[0]
  2.0 1.3 %collective-permute-start.1 = (bf16[32,2,16,256]{3,0,2,1:T(8,128)(2,1)S(1)}, bf16[32,2,16,256]{3,0,2,1:T(8,128)(2,1)}, u32[]{:S(2)}, u32[]{:S(2)}) collective-permute-start(bf16[32,2,16,256]{3,0,2,1:T(8,128)(2,1)S(1)} %copy.77), channel_id=1, source_target_pairs={{1,0},{2,1},{3,2},{4,3},{5,4},{6,5},{7,6},{8,7},{9,8},{10,9},{11,1... | collective-permute-start | bytes 1572872 | tf_op jit(solution)/shard_map/ppermute | solution.py:16
  3.3 3.8 %collective-permute-start = (bf16[32,2,16,256]{3,0,2,1:T(8,128)(2,1)S(1)}, bf16[32,2,16,256]{3,0,2,1:T(8,128)(2,1)}, u32[]{:S(2)}, u32[]{:S(2)}) collective-permute-start(bf16[32,2,16,256]{3,0,2,1:T(8,128)(2,1)S(1)} %copy.77), channel_id=1, source_target_pairs={{0,1},{1,2},{2,3},{3,4},{4,5},{5,6},{6,7},{7,8},{8,9},{9,10},{10,1... | collective-permute-start | bytes 1572872 | tf_op jit(solution)/shard_map/ppermute | solution.py:15
  7.2 0.8 copy.83
  8.0 1.3 %collective-permute-start.3 = (bf16[32,1,8,128]{3,0,2,1:T(8,128)(2,1)S(1)}, bf16[32,1,8,128]{3,0,2,1:T(8,128)(2,1)S(1)}, u32[]{:S(2)}, u32[]{:S(2)}) collective-permute-start(bf16[32,1,8,128]{3,0,2,1:T(8,128)(2,1)S(1)} %copy.83), channel_id=1, source_target_pairs={{1,0},{2,1},{3,2},{4,3},{5,4},{6,5},{7,6},{8,7},{9,8},{10,9},{11,1... | collective-permute-start | bytes 196616 | tf_op jit(solution)/shard_map/ppermute | solution.py:16
  9.3 4.4 %collective-permute-start.2 = (bf16[32,1,8,128]{3,0,2,1:T(8,128)(2,1)S(1)}, bf16[32,1,8,128]{3,0,2,1:T(8,128)(2,1)S(1)}, u32[]{:S(2)}, u32[]{:S(2)}) collective-permute-start(bf16[32,1,8,128]{3,0,2,1:T(8,128)(2,1)S(1)} %copy.83), channel_id=1, source_target_pairs={{0,1},{1,2},{2,3},{3,4},{4,5},{5,6},{6,7},{7,8},{8,9},{9,10},{10,1... | collective-permute-start | bytes 196616 | tf_op jit(solution)/shard_map/ppermute | solution.py:15
  13.7 1.1 copy.166
  15.2 0.8 reshape.156
  16.1 0.8 copy.89
  16.9 8.5 %pad.17 = bf16[32,6,18,258]{3,0,2,1:T(8,128)(2,1)S(1)} pad(bf16[32,3,8,128]{3,0,2,1:T(8,128)(2,1)S(1)} %pad_maximum_fusion.4, bf16[]{:T(256)} %constant.4.clone.1), padding=0_0_0x0_1_1x1_2_1x1_2_1 | pad | bytes 1979906 | tf_op jit(solution)/shard_map/pad | solution.py:136
  25.5 1.4 %fusion.234 = (bf16[32,6,18,256]{3,0,2,1:T(8,128)(2,1)S(1)}, bf16[32,6,18,256]{3,0,2,1:T(8,128)(2,1)S(1)}, bf16[32,6,18,256]{3,0,2,1:T(8,128)(2,1)S(1)}) fusion(bf16[32,6,18,258]{3,0,2,1:T(8,128)(2,1)S(1)} %pad.17), kind=kLoop, calls=%fused_computation.251 | loop fusion | bytes 10616832 | tf_op jit(solution)/shard_map/slice | solution.py:35
  27.3 0.6 fusion.3
  27.8 0.6 fusion.5
  28.4 0.6 fusion.7
  28.9 0.6 fusion.9
  29.5 0.6 fusion.11
  30.1 0.6 fusion.13
  30.6 0.6 fusion.15
  31.2 1.9 %fusion.17 = f32[4,16,256,32]{2,3,1,0:T(8,128)} fusion(bf16[96,6,18,256]{3,0,2,1:T(8,128)(2,1)S(1)} %pad_maximum_fusion.1, bf16[3,3,32,96]{3,2,1,0:T(8,128)(2,1)S(1)} %bitcast.523), kind=kOutput, calls=%fused_computation.24 | convolution fusion | flops 100663296 | bytes 5251072 | tf_op jit(solution)/shard_map/qk,kdhw->qdhw/dot_general | solution.py:149
  33.1 2.7 %select_maximum_fusion = bf16[32,6,18,258]{3,0,2,1:T(8,128)(2,1)S(1)} fusion(bf16[32,2,16,256]{3,0,2,1:T(8,128)(2,1)} %collective-permute-done.1, bf16[32,2,16,256]{3,0,2,1:T(8,128)(2,1)S(1)} %copy.77, bf16[32,2,16,256]{3,0,2,1:T(8,128)(2,1)} %collective-permute-done), kind=kLoop, calls=%fused_computation.46 | loop fusion | flops 16941312 | bytes 3356160 | tf_op jit(solution)/shard_map/concatenate | solution.py:17
  35.8 3.2 %fusion.235 = (bf16[32,6,18,256]{3,0,2,1:T(8,128)(2,1)S(1)}, bf16[32,6,18,256]{3,0,2,1:T(8,128)(2,1)}, bf16[32,6,18,256]{3,0,2,1:T(8,128)(2,1)}) fusion(bf16[32,6,18,258]{3,0,2,1:T(8,128)(2,1)S(1)} %select_maximum_fusion), kind=kLoop, calls=%fused_computation.252 | loop fusion | bytes 10616832 | tf_op jit(solution)/shard_map/slice | solution.py:35
  39.0 3.0 %pad_maximum_fusion = bf16[96,6,18,256]{3,0,2,1:T(8,128)(2,1)S(1)} fusion(bf16[32,6,18,256]{3,0,2,1:T(8,128)(2,1)} %get-tuple-element.25, bf16[32,6,18,256]{3,0,2,1:T(8,128)(2,1)} %get-tuple-element.24, bf16[32,6,18,256]{3,0,2,1:T(8,128)(2,1)S(1)} %get-tuple-element.23), kind=kLoop, calls=%fused_computation.4 | loop fusion | flops 15925248 | bytes 10616832 | tf_op jit(solution)/shard_map/concatenate | solution.py:36
  42.0 1.9 %fusion.23 = f32[4,16,256,32]{2,3,1,0:T(8,128)} fusion(bf16[96,6,18,256]{3,0,2,1:T(8,128)(2,1)S(1)} %pad_maximum_fusion, bf16[3,3,32,96]{3,2,1,0:T(8,128)(2,1)S(1)} %reshape.152), kind=kOutput, calls=%fused_computation.30 | convolution fusion | flops 100663296 | bytes 5251072 | tf_op jit(solution)/shard_map/ok,kdhw->odhw/dot_general | solution.py:98
  43.9 1.9 %fusion.25 = f32[4,16,256,32]{2,3,1,0:T(8,128)} fusion(bf16[96,6,18,256]{3,0,2,1:T(8,128)(2,1)S(1)} %pad_maximum_fusion, bf16[3,3,32,96]{3,2,1,0:T(8,128)(2,1)S(1)} %reshape.152), kind=kOutput, calls=%fused_computation.32 | convolution fusion | flops 100663296 | bytes 5251072 | tf_op jit(solution)/shard_map/ok,kdhw->odhw/dot_general | solution.py:98
  45.8 1.9 %fusion.27 = f32[4,16,256,32]{2,3,1,0:T(8,128)} fusion(bf16[96,6,18,256]{3,0,2,1:T(8,128)(2,1)S(1)} %pad_maximum_fusion, bf16[3,3,32,96]{3,2,1,0:T(8,128)(2,1)S(1)} %reshape.152), kind=kOutput, calls=%fused_computation.34 | convolution fusion | flops 100663296 | bytes 5251072 | tf_op jit(solution)/shard_map/ok,kdhw->odhw/dot_general | solution.py:98
  47.7 1.9 %fusion.29 = f32[4,16,256,32]{2,3,1,0:T(8,128)} fusion(bf16[96,6,18,256]{3,0,2,1:T(8,128)(2,1)S(1)} %pad_maximum_fusion, bf16[3,3,32,96]{3,2,1,0:T(8,128)(2,1)S(1)} %reshape.152), kind=kOutput, calls=%fused_computation.36 | convolution fusion | flops 100663296 | bytes 5251072 | tf_op jit(solution)/shard_map/ok,kdhw->odhw/dot_general | solution.py:98
  49.6 1.9 %fusion.31 = f32[4,16,256,32]{2,3,1,0:T(8,128)} fusion(bf16[96,6,18,256]{3,0,2,1:T(8,128)(2,1)S(1)} %pad_maximum_fusion, bf16[3,3,32,96]{3,2,1,0:T(8,128)(2,1)S(1)} %reshape.152), kind=kOutput, calls=%fused_computation.38 | convolution fusion | flops 100663296 | bytes 5251072 | tf_op jit(solution)/shard_map/ok,kdhw->odhw/dot_general | solution.py:98
  51.5 1.9 %fusion.33 = f32[4,16,256,32]{2,3,1,0:T(8,128)} fusion(bf16[96,6,18,256]{3,0,2,1:T(8,128)(2,1)S(1)} %pad_maximum_fusion, bf16[3,3,32,96]{3,2,1,0:T(8,128)(2,1)S(1)} %reshape.152), kind=kOutput, calls=%fused_computation.40 | convolution fusion | flops 100663296 | bytes 5251072 | tf_op jit(solution)/shard_map/ok,kdhw->odhw/dot_general | solution.py:98
  53.4 1.9 %fusion.37 = f32[4,16,256,32]{2,3,1,0:T(8,128)} fusion(bf16[96,6,18,256]{3,0,2,1:T(8,128)(2,1)S(1)} %pad_maximum_fusion, bf16[3,3,32,96]{3,2,1,0:T(8,128)(2,1)S(1)} %reshape.152), kind=kOutput, calls=%fused_computation.44 | convolution fusion | flops 100663296 | bytes 5251072 | tf_op jit(solution)/shard_map/ok,kdhw->odhw/dot_general | solution.py:98
  55.3 1.9 %fusion.35 = f32[4,16,256,32]{2,3,1,0:T(8,128)} fusion(bf16[96,6,18,256]{3,0,2,1:T(8,128)(2,1)S(1)} %pad_maximum_fusion, bf16[3,3,32,96]{3,2,1,0:T(8,128)(2,1)S(1)} %reshape.152), kind=kOutput, calls=%fused_computation.42 | convolution fusion | flops 100663296 | bytes 5251072 | tf_op jit(solution)/shard_map/ok,kdhw->odhw/dot_general | solution.py:98
  57.1 8.7 %add_divide_fusion = (f32[32,4,16,256]{3,0,2,1:T(8,128)}, f32[32,4,16,256]{3,0,2,1:T(8,128)S(1)}) fusion(bf16[96,6,18,256]{3,0,2,1:T(8,128)(2,1)S(1)} %pad_maximum_fusion, bf16[3,3,32,96]{3,2,1,0:T(8,128)(2,1)S(1)} %reshape.152, f32[4,16,256,32]{2,3,1,0:T(8,128)} %fusion.23, f32[4,16,256,32]{2,3,1,0:T(8,128)} %fusion.25, f32[4,16,256,32]{2,3,1,0:T(8,128)} %fusion.27, ...), kind=kOutput, calls=%fused_computation.55 | convolution fusion | flops 106430464 | bytes 24125440 | tf_op jit(solution)/shard_map/ok,kdhw->odhw/dot_general | solution.py:98
  65.8 3.2 %fusion.43 = bf16[32,4,16,256]{3,0,2,1:T(8,128)(2,1)S(1)} fusion(f32[4,16,256,32]{2,3,1,0:T(8,128)S(1)} %fusion.3, f32[4,16,256,32]{2,3,1,0:T(8,128)S(1)} %fusion.5, f32[4,16,256,32]{2,3,1,0:T(8,128)S(1)} %fusion.7, f32[4,16,256,32]{2,3,1,0:T(8,128)S(1)} %fusion.9, f32[32,4,16,256]{3,0,2,1:T(8,128)S(1)} %get-tuple-element.32, ...), kind=kOutput, calls=%fused_computation.53 | convolution fusion | flops 110100480 | bytes 23077376 | tf_op jit(solution)/shard_map/qk,kdhw->qdhw/dot_general | solution.py:149
  69.0 1.0 pad_slice_fusion.2
  70.0 0.6 fusion.131
  70.6 1.0 copy-done.1
  72.1 0.7 fusion.86
  74.0 0.8 convolution_add_fusion.2
  77.8 1.3 %fusion.102 = f32[2,16,256,32]{2,3,1,0:T(8,128)} fusion(f32[2,16,256,32]{2,3,1,0:T(8,128)S(1)} %fusion.99, bf16[96,4,18,256]{3,0,2,1:T(8,128)(2,1)S(1)} %pad_maximum_fusion.2, bf16[3,3,32,96]{3,2,1,0:T(8,128)(2,1)S(1)} %bitcast.515), kind=kOutput, calls=%fused_computation.105 | convolution fusion | flops 50593792 | bytes 3678208 | tf_op jit(solution)/shard_map/qk,kdhw->qdhw/dot_general | solution.py:177
  80.7 0.7 fusion.137
  81.4 0.6 fusion.143
  82.1 0.6 fusion.149
  82.7 0.6 fusion.155
  83.4 0.6 fusion.161
  84.0 0.6 fusion.167
  84.6 0.6 fusion.173
  85.3 0.6 fusion.179
  85.9 0.8 pad_maximum_fusion.3
  86.7 2.0 %all_to_all.13 = f32[16,1,3456]{2,1,0:T(1,128)} reshape(f32[2,9,32,96]{3,2,1,0:T(8,128)} %pad_maximum_fusion.3) | data formatting | bytes 442368 | tf_op jit(solution)/shard_map/all_to_all | solution.py:44
  88.7 10.0 %all-to-all-start = ((f32[16,1,3456]{2,1,0:T(1,128)}), f32[16,1,3456]{2,1,0:T(1,128)}, u32[]{:S(2)}, u32[]{:S(2)}) async-start(f32[16,1,3456]{2,1,0:T(1,128)} %all_to_all.13), calls=%async_computation | async-start | bytes 442368 | tf_op jit(solution)/shard_map/all_to_all | solution.py:44
  98.7 1.8 %convolution_add_fusion.1 = f32[8,128,32]{1,2,0:T(8,128)} fusion(f32[8,128,32]{1,2,0:T(8,128)} %convolution_add_fusion.2, bf16[96,3,18,128]{3,0,2,1:T(8,128)(2,1)} %bitcast.496, bf16[3,3,32,96]{3,2,1,0:T(8,128)(2,1)} %reshape.156), kind=kOutput, calls=%fused_computation.111 | convolution fusion | flops 6324224 | bytes 466944 | tf_op jit(solution)/shard_map/ok,kdhw->odhw/dot_general | solution.py:126
  100.5 2.6 %fusion.105 = f32[2,16,256,32]{2,3,1,0:T(8,128)} fusion(f32[2,16,256,32]{2,3,1,0:T(8,128)} %fusion.102, bf16[96,4,18,256]{3,0,2,1:T(8,128)(2,1)S(1)} %pad_maximum_fusion.2, bf16[3,3,32,96]{3,2,1,0:T(8,128)(2,1)} %bitcast.507), kind=kOutput, calls=%fused_computation.106 | convolution fusion | flops 50593792 | bytes 3678208 | tf_op jit(solution)/shard_map/qk,kdhw->qdhw/dot_general | solution.py:177
  103.1 5.0 %all-to-all-done = f32[16,1,3456]{2,1,0:T(1,128)} async-done(((f32[16,1,3456]{2,1,0:T(1,128)}), f32[16,1,3456]{2,1,0:T(1,128)}, u32[]{:S(2)}, u32[]{:S(2)}) %all-to-all-start) | async-done | bytes 221216 | tf_op jit(solution)/shard_map/all_to_all | solution.py:44
  108.1 1.1 reduce_sum.9
  109.2 0.8 broadcast_in_dim.28
  110.0 4.2 %all-to-all-start.1 = ((f32[16,1,3456]{2,1,0:T(1,128)}), f32[16,1,3456]{2,1,0:T(1,128)}, u32[]{:S(2)}, u32[]{:S(2)}) async-start(f32[16,1,3456]{2,1,0:T(1,128)} %broadcast_in_dim.28), calls=%async_computation.1 | async-start | bytes 442368 | tf_op jit(solution)/shard_map/all_to_all | solution.py:45
  114.2 1.2 fusion.118
  115.4 0.7 copy.102
  116.0 1.6 %fusion.114 = bf16[32,2,16,256]{3,0,2,1:T(8,128)(2,1)S(1)} fusion(f32[2,16,256,32]{2,3,1,0:T(8,128)} %fusion.105, bf16[96,4,18,256]{3,0,2,1:T(8,128)(2,1)S(1)} %pad_maximum_fusion.2, bf16[3,3,32,96]{3,2,1,0:T(8,128)(2,1)} %bitcast.508), kind=kOutput, calls=%fused_computation.109 | convolution fusion | flops 50855936 | bytes 3153920 | tf_op jit(solution)/shard_map/qk,kdhw->qdhw/dot_general | solution.py:177
  117.6 1.1 copy.103
  118.7 4.9 %all-to-all-done.1 = f32[16,1,3456]{2,1,0:T(1,128)} async-done(((f32[16,1,3456]{2,1,0:T(1,128)}), f32[16,1,3456]{2,1,0:T(1,128)}, u32[]{:S(2)}, u32[]{:S(2)}) %all-to-all-start.1) | async-done | bytes 221216 | tf_op jit(solution)/shard_map/all_to_all | solution.py:45
  123.6 1.5 %reduce.1 = f32[16,3456]{1,0:T(8,128)S(1)} reduce(f32[16,1,3456]{2,1,0:T(1,128)} %all-to-all-done.1, f32[]{:T(128)} %constant.35), dimensions={1}, to_apply=%all_to_all.12.reduce_sub_computation | reduce | bytes 442372 | tf_op jit(solution)/shard_map/all_to_all | solution.py:45
  125.0 0.7 reshape_reshape_reshape.3
  126.0 0.8 copy.100
  126.9 0.8 copy.101
  (50 shorter events, 7.5 us)
Async XLA Ops:
  0.6 15.5 %copy-start.3 = (bf16[27,32,32]{2,1,0:T(8,128)(2,1)S(1)}, bf16[27,32,32]{2,1,0:T(8,128)(2,1)}, u32[]{:S(2)}) copy-start(bf16[27,32,32]{2,1,0:T(8,128)(2,1)} %param.5) | copy-start | bytes 165892
  0.6 14.4 %copy-start.2 = (bf16[27,32,32]{2,1,0:T(8,128)(2,1)S(1)}, bf16[27,32,32]{2,1,0:T(8,128)(2,1)}, u32[]{:S(2)}) copy-start(bf16[27,32,32]{2,1,0:T(8,128)(2,1)} %param.6) | copy-start | bytes 165892
  2.0 31.0 %collective-permute-start.1 = (bf16[32,2,16,256]{3,0,2,1:T(8,128)(2,1)S(1)}, bf16[32,2,16,256]{3,0,2,1:T(8,128)(2,1)}, u32[]{:S(2)}, u32[]{:S(2)}) collective-permute-start(bf16[32,2,16,256]{3,0,2,1:T(8,128)(2,1)S(1)} %copy.77), channel_id=1, source_target_pairs={{1,0},{2,1},{3,2},{4,3},{5,4},{6,5},{7,6},{8,7},{9,8},{10,9},{11,1... | collective-permute-start | bytes 1572872 | tf_op jit(solution)/shard_map/ppermute | solution.py:16
  3.3 29.7 %collective-permute-start = (bf16[32,2,16,256]{3,0,2,1:T(8,128)(2,1)S(1)}, bf16[32,2,16,256]{3,0,2,1:T(8,128)(2,1)}, u32[]{:S(2)}, u32[]{:S(2)}) collective-permute-start(bf16[32,2,16,256]{3,0,2,1:T(8,128)(2,1)S(1)} %copy.77), channel_id=1, source_target_pairs={{0,1},{1,2},{2,3},{3,4},{4,5},{5,6},{6,7},{7,8},{8,9},{9,10},{10,1... | collective-permute-start | bytes 1572872 | tf_op jit(solution)/shard_map/ppermute | solution.py:15
  8.0 8.9 %collective-permute-start.3 = (bf16[32,1,8,128]{3,0,2,1:T(8,128)(2,1)S(1)}, bf16[32,1,8,128]{3,0,2,1:T(8,128)(2,1)S(1)}, u32[]{:S(2)}, u32[]{:S(2)}) collective-permute-start(bf16[32,1,8,128]{3,0,2,1:T(8,128)(2,1)S(1)} %copy.83), channel_id=1, source_target_pairs={{1,0},{2,1},{3,2},{4,3},{5,4},{6,5},{7,6},{8,7},{9,8},{10,9},{11,1... | collective-permute-start | bytes 196616 | tf_op jit(solution)/shard_map/ppermute | solution.py:16
  9.3 7.6 %collective-permute-start.2 = (bf16[32,1,8,128]{3,0,2,1:T(8,128)(2,1)S(1)}, bf16[32,1,8,128]{3,0,2,1:T(8,128)(2,1)S(1)}, u32[]{:S(2)}, u32[]{:S(2)}) collective-permute-start(bf16[32,1,8,128]{3,0,2,1:T(8,128)(2,1)S(1)} %copy.83), channel_id=1, source_target_pairs={{0,1},{1,2},{2,3},{3,4},{4,5},{5,6},{6,7},{7,8},{8,9},{9,10},{10,1... | collective-permute-start | bytes 196616 | tf_op jit(solution)/shard_map/ppermute | solution.py:15
  70.0 1.6 %copy-start.1 = (f32[32,4,16,256]{3,0,2,1:T(8,128)S(1)}, f32[32,4,16,256]{3,0,2,1:T(8,128)}, u32[]{:S(2)}) copy-start(f32[32,4,16,256]{3,0,2,1:T(8,128)} %get-tuple-element.31) | copy-start | bytes 6291460
  72.1 0.9 copy-start.5
  73.0 7.6 %copy-start = (bf16[3,32,3,18,128]{4,1,0,3,2:T(8,128)(2,1)}, bf16[3,32,3,18,128]{4,1,0,3,2:T(8,128)(2,1)S(1)}, u32[]{:S(2)}) copy-start(bf16[3,32,3,18,128]{4,1,0,3,2:T(8,128)(2,1)S(1)} %copy.81) | copy-start | bytes 3981316
  74.8 0.9 copy-start.4
  77.8 1.3 %copy-start.6 = (bf16[32,1,8,128]{3,2,1,0:T(8,128)(2,1)S(1)}, bf16[32,1,8,128]{3,2,1,0:T(8,128)(2,1)}, u32[]{:S(2)}) copy-start(bf16[32,1,8,128]{3,2,1,0:T(8,128)(2,1)} %param.7) | copy-start | bytes 196612
  88.7 19.4 %all-to-all-start = ((f32[16,1,3456]{2,1,0:T(1,128)}), f32[16,1,3456]{2,1,0:T(1,128)}, u32[]{:S(2)}, u32[]{:S(2)}) async-start(f32[16,1,3456]{2,1,0:T(1,128)} %all_to_all.13), calls=%async_computation | async-start | bytes 442368 | tf_op jit(solution)/shard_map/all_to_all | solution.py:44
  110.0 13.6 %all-to-all-start.1 = ((f32[16,1,3456]{2,1,0:T(1,128)}), f32[16,1,3456]{2,1,0:T(1,128)}, u32[]{:S(2)}, u32[]{:S(2)}) async-start(f32[16,1,3456]{2,1,0:T(1,128)} %broadcast_in_dim.28), calls=%async_computation.1 | async-start | bytes 442368 | tf_op jit(solution)/shard_map/all_to_all | solution.py:45

commit v5 on v3

--- a/solution.py
+++ b/solution.py
@@ -133,13 +133,14 @@
                 jnp.einsum("odhw,kdhw->ok", cotangent, window, preferred_element_type=jnp.float32)
             )
     extended = jnp.pad(cot_ext, ((0, 0), (0, 1), (0, 1), (0, 1)))
-    class_planes = half_planes + 2
+    class_planes = half_planes + 1
     parity_taps = [[(1, 0)], [(2, 0), (0, 1)]]
+    depth_taps = [[(2, 0), (0, 1)], [(1, 1)]]
     order = []
     for depth_parity in range(2):
         for row_parity in range(2):
             for col_parity in range(2):
-                for tap_depth, _ in parity_taps[depth_parity]:
+                for tap_depth, _ in depth_taps[depth_parity]:
                     for tap_row, _ in parity_taps[row_parity]:
                         for tap_col, _ in parity_taps[col_parity]:
                             order.append(9 * tap_depth + 3 * tap_row + tap_col)
@@ -150,7 +151,7 @@
         for row_parity in range(2):
             for col_parity in range(2):
                 pieces = []
-                for tap_depth, skip_depth in parity_taps[depth_parity]:
+                for tap_depth, skip_depth in depth_taps[depth_parity]:
                     for tap_row, skip_row in parity_taps[row_parity]:
                         for tap_col, skip_col in parity_taps[col_parity]:
                             pieces.append(
@@ -172,7 +173,7 @@
     parity_grid = jnp.stack(classes).reshape(2, 2, 2, channels, class_planes, half_rows, half_cols)
     grad_hidden = parity_grid.transpose(3, 4, 0, 5, 1, 6, 2).reshape(
         channels, 2 * class_planes, height, columns
-    )[:, 1 : planes + 3]
+    )
     sigma = jax.nn.sigmoid(preact)
     grad_rim = grad_hidden * (sigma * (1.0 + preact * (1.0 - sigma)))
     grad_rim = jnp.where(inside, grad_rim, 0.0).astype(jnp.bfloat16)

time: 112 us -> 101 us (0.902)
  local copies, waits for them, and re-layouts: 45.6 us -> 33.3 us
    slice x1, local copies, waits for them, and re-layouts: 7.6 us -> 0.24 us  [on_device(): extended[:, skip_depth:skip_depth + class_planes, skip_row:skip_row + hal...]
    unnamed x38 -> x40, local copies, waits for them, and re-layouts: 12.3 us -> 6.49 us
    reshape x0 -> x1, local copies, waits for them, and re-layouts: none -> 5.12 us  [on_device(): parity_grid.transpose(3, 4, 0, 5, 1, 6, 2)]
    reshape x1, local copies, waits for them, and re-layouts: 12.6 us -> 8.51 us  [on_device(): jnp.stack(classes)]
    concatenate x1 -> x2, other arithmetic: 2.78 us -> 2.69 us  [extended_2(): shard = jnp.concatenate([before, shard, after], axis=dim)]
  transfers between devices with their start and end apart: 6 -> 6, of which waited for: 2 -> 2; matrix products, arithmetic and copies ran while one was open for 39% -> 32% of each run, Pallas kernels for 0% -> 0%
where the time goes in v5:
time: 101 us; the launch traced here: 99.9 us
  local copies, waits for them, and re-layouts  33.3 us (33%)
  matrix products  24.5 us (24%)
  starting transfers between devices  23 us (23%)
  waiting for transfers between devices  9.94 us (10%)
  other arithmetic  7.92 us (8%)
  between operations  1.2 us (1%)
    dot_general x9, matrix products, on_device(): jnp.einsum('ok,kdhw->odhw', front_one[along_depth, along_rows], window, p...  10.1 us
    all_to_all x1, starting transfers between devices, summed_over(): mine = lax.all_to_all(flat, axis, 0, 0, tiled=True).sum(0, keepdims=True)  9.21 us
    reshape x1, local copies, waits for them, and re-layouts, on_device(): jnp.stack(classes)  8.51 us
    ppermute x2, starting transfers between devices, extended_2(): before = lax.ppermute(last, axis, up)  7.72 us
    all_to_all x1, waiting for transfers between devices, summed_over(): lax.all_to_all(jnp.broadcast_to(mine, flat.shape), axis, 0, 0, tiled=True)  7.09 us
    unnamed x40, local copies, waits for them, and re-layouts  6.49 us
    dot_general x9, matrix products, on_device(): jnp.einsum('odhw,kdhw->ok', grad_pre, window, preferred_element_type=jnp....  5.75 us
    reshape x1, local copies, waits for them, and re-layouts, on_device(): parity_grid.transpose(3, 4, 0, 5, 1, 6, 2)  5.12 us
  transfers between devices with their start and end apart: 6, of which 2 were waited for; matrix products, arithmetic and copies ran while one was open for 32% of the time, Pallas kernels for 0%

profile of v5, /device:TPU:0, one launch (start us, length us, event | category | flops | bytes accessed | tf_op | source)
XLA Modules:
  0.0 99.9 jit_solution(8197863189230346800)
XLA Ops:
  0.7 0.9 copy.113
  1.6 2.5 %collective-permute-start.2 = (bf16[32,1,8,128]{3,0,2,1:T(8,128)(2,1)S(1)}, bf16[32,1,8,128]{3,0,2,1:T(8,128)(2,1)S(1)}, u32[]{:S(2)}, u32[]{:S(2)}) collective-permute-start(bf16[32,1,8,128]{3,0,2,1:T(8,128)(2,1)S(1)} %copy.113), channel_id=1, source_target_pairs={{0,1},{1,2},{2,3},{3,4},{4,5},{5,6},{6,7},{7,8},{8,9},{9,10},{10,1... | collective-permute-start | bytes 196616 | tf_op jit(solution)/shard_map/ppermute | solution.py:15
  4.1 1.3 %collective-permute-start.3 = (bf16[32,1,8,128]{3,0,2,1:T(8,128)(2,1)S(1)}, bf16[32,1,8,128]{3,0,2,1:T(8,128)(2,1)S(1)}, u32[]{:S(2)}, u32[]{:S(2)}) collective-permute-start(bf16[32,1,8,128]{3,0,2,1:T(8,128)(2,1)S(1)} %copy.113), channel_id=1, source_target_pairs={{1,0},{2,1},{3,2},{4,3},{5,4},{6,5},{7,6},{8,7},{9,8},{10,9},{11,1... | collective-permute-start | bytes 196616 | tf_op jit(solution)/shard_map/ppermute | solution.py:16
  5.4 1.3 %copy.106 = bf16[32,2,16,256]{3,0,2,1:T(8,128)(2,1)S(1)} copy(bf16[32,2,16,256]{3,2,1,0:T(8,128)(2,1)} %param.6) | data formatting | bytes 1048576 | tf_op args[0]
  6.8 5.2 %collective-permute-start = (bf16[32,2,16,256]{3,0,2,1:T(8,128)(2,1)S(1)}, bf16[32,2,16,256]{3,0,2,1:T(8,128)(2,1)S(1)}, u32[]{:S(2)}, u32[]{:S(2)}) collective-permute-start(bf16[32,2,16,256]{3,0,2,1:T(8,128)(2,1)S(1)} %copy.106), channel_id=1, source_target_pairs={{0,1},{1,2},{2,3},{3,4},{4,5},{5,6},{6,7},{7,8},{8,9},{9,10},{10,1... | collective-permute-start | bytes 1572872 | tf_op jit(solution)/shard_map/ppermute | solution.py:15
  12.0 1.3 %collective-permute-start.1 = (bf16[32,2,16,256]{3,0,2,1:T(8,128)(2,1)S(1)}, bf16[32,2,16,256]{3,0,2,1:T(8,128)(2,1)}, u32[]{:S(2)}, u32[]{:S(2)}) collective-permute-start(bf16[32,2,16,256]{3,0,2,1:T(8,128)(2,1)S(1)} %copy.106), channel_id=1, source_target_pairs={{1,0},{2,1},{3,2},{4,3},{5,4},{6,5},{7,6},{8,7},{9,8},{10,9},{11,1... | collective-permute-start | bytes 1572872 | tf_op jit(solution)/shard_map/ppermute | solution.py:16
  13.3 0.7 pad_clamp_fusion
  13.9 1.5 %gather_fusion = bf16[27,32,32]{2,1,0:T(8,128)(2,1)S(1)} fusion(bf16[27,32,32]{2,1,0:T(8,128)(2,1)} %param.8, s32[1024]{0:T(1024)S(1)} %pad_clamp_fusion), kind=kCustom, calls=%fused_computation | custom fusion | bytes 110700 | tf_op jit(solution)/shard_map/gather | solution.py:147
  15.5 0.7 fusion.262
  16.3 0.8 reshape.179
  17.1 0.6 add_add_fusion
  18.0 0.8 reshape.183
  18.8 0.6 compare_and_fusion
  22.5 8.5 %copy.125 = f32[2,2,2,32,2,8,128]{3,2,6,1,5,0,4:T(2,128)} copy(f32[2,2,2,32,2,8,128]{6,3,5,4,2,1,0:T(8,128)S(1)} %bitcast.503) | data formatting | bytes 4194304 | tf_op jit(solution)/shard_map/reshape | solution.py:173
  31.0 5.1 %copy.126 = f32[32,4,16,256]{3,0,2,1:T(8,128)S(1)} copy(f32[32,4,16,256]{0,3,2,1:T(8,128)} %bitcast.483) | data formatting | bytes 4194304 | tf_op jit(solution)/shard_map/reshape | solution.py:174
  36.1 2.6 %select_maximum_fusion = bf16[32,6,18,258]{3,0,2,1:T(8,128)(2,1)S(1)} fusion(bf16[32,2,16,256]{3,0,2,1:T(8,128)(2,1)} %collective-permute-done.1, bf16[32,2,16,256]{3,0,2,1:T(8,128)(2,1)S(1)} %copy.106, bf16[32,2,16,256]{3,0,2,1:T(8,128)(2,1)S(1)} %collective-permute-done), kind=kLoop, calls=%fused_computation.28 | loop fusion | flops 16941312 | bytes 3356160 | tf_op jit(solution)/shard_map/concatenate | solution.py:17
  38.8 1.4 %fusion.259 = (bf16[32,6,18,256]{3,0,2,1:T(8,128)(2,1)S(1)}, bf16[32,6,18,256]{3,0,2,1:T(8,128)(2,1)S(1)}, bf16[32,6,18,256]{3,0,2,1:T(8,128)(2,1)S(1)}) fusion(bf16[32,6,18,258]{3,0,2,1:T(8,128)(2,1)S(1)} %select_maximum_fusion), kind=kLoop, calls=%fused_computation.299 | loop fusion | bytes 10616832 | tf_op jit(solution)/shard_map/slice | solution.py:35
  40.2 0.4 pad_maximum_fusion
  40.6 0.5 copy-done.7
  41.1 0.6 fusion.11
  41.6 0.6 fusion.13
  42.2 0.6 fusion.15
  42.7 0.6 fusion.17
  43.3 0.6 fusion.19
  43.8 0.6 fusion.5
  44.4 0.6 fusion.7
  45.0 1.9 %fusion.9 = f32[4,16,256,32]{2,3,1,0:T(8,128)} fusion(bf16[96,6,18,256]{3,0,2,1:T(8,128)(2,1)S(1)} %pad_maximum_fusion, bf16[3,3,32,96]{3,2,1,0:T(8,128)(2,1)S(1)} %copy-done.7), kind=kOutput, calls=%fused_computation.16 | convolution fusion | flops 100663296 | bytes 5251072 | tf_op jit(solution)/shard_map/ok,kdhw->odhw/dot_general | solution.py:98
  46.8 4.3 %select_convert_fusion = (bf16[32,4,16,256]{3,0,2,1:T(8,128)(2,1)S(1)}, f32[32,4,16,256]{3,0,2,1:T(8,128)}, f32[32,4,16,256]{3,0,2,1:T(8,128)}) fusion(f32[32,4,16,256]{3,0,2,1:T(8,128)S(1)} %copy.126, pred[4]{0:T(512)(128)(4,1)S(1)} %copy-done.13, bf16[96,6,18,256]{3,0,2,1:T(8,128)(2,1)S(1)} %pad_maximum_fusion, bf16[3,3,32,96]{3,2,1,0:T(8,128)(2,1)S(1)} %copy-done.7, ...), kind=kOutput, calls=%fused_computation.34 | convolution fusion | flops 110100480 | bytes 27271680 | tf_op jit(solution)/shard_map/ok,kdhw->odhw/dot_general | solution.py:98
  51.1 0.6 fusion.122
  51.8 2.4 %pad_slice_fusion.2 = (bf16[32,4,18,256]{3,0,2,1:T(8,128)(2,1)S(1)}, bf16[32,4,18,256]{3,0,2,1:T(8,128)(2,1)}, bf16[32,4,18,256]{3,0,2,1:T(8,128)(2,1)}) fusion(bf16[32,4,16,256]{3,0,2,1:T(8,128)(2,1)S(1)} %get-tuple-element.23), kind=kLoop, calls=%fused_computation.38 | loop fusion | bytes 4587520 | tf_op jit(solution)/shard_map/slice | solution.py:35
  54.2 0.6 fusion.128
  54.8 0.6 fusion.134
  55.5 0.6 fusion.140
  56.1 0.6 fusion.146
  56.7 0.6 fusion.152
  57.4 0.6 fusion.158
  58.1 0.6 fusion.164
  58.7 0.6 fusion.170
  59.7 0.6 copy-done.1
  60.3 0.5 fusion.63
  60.8 0.7 fusion.64
  63.4 1.0 %all_to_all.13 = f32[16,1,3456]{2,1,0:T(1,128)} reshape(f32[2,9,32,96]{3,2,1,0:T(8,128)S(1)} %pad_maximum_fusion.8) | data formatting | bytes 442368 | tf_op jit(solution)/shard_map/all_to_all | solution.py:44
  64.4 9.2 %all-to-all-start = ((f32[16,1,3456]{2,1,0:T(1,128)}), f32[16,1,3456]{2,1,0:T(1,128)S(1)}, u32[]{:S(2)}, u32[]{:S(2)}) async-start(f32[16,1,3456]{2,1,0:T(1,128)} %all_to_all.13), calls=%async_computation | async-start | bytes 442368 | tf_op jit(solution)/shard_map/all_to_all | solution.py:44
  73.6 1.8 %pad_maximum_fusion.1 = bf16[96,4,18,256]{3,0,2,1:T(8,128)(2,1)S(1)} fusion(bf16[32,4,18,256]{3,0,2,1:T(8,128)(2,1)} %get-tuple-element.29, bf16[32,4,18,256]{3,0,2,1:T(8,128)(2,1)} %get-tuple-element.28, bf16[32,4,18,256]{3,0,2,1:T(8,128)(2,1)S(1)} %get-tuple-element.27), kind=kLoop, calls=%fused_computation.9 | loop fusion | flops 10616832 | bytes 7077888 | tf_op jit(solution)/shard_map/concatenate | solution.py:36
  75.4 0.3 fusion.58
  75.7 0.4 fusion.65
  76.1 0.4 fusion.68
  76.5 0.4 fusion.71
  76.8 0.4 fusion.74
  77.2 0.4 fusion.77
  77.6 0.4 fusion.80
  77.9 0.4 fusion.83
  78.3 0.5 copy-done.8
  79.8 0.4 fusion.92
  80.1 2.8 %all-to-all-done = f32[16,1,3456]{2,1,0:T(1,128)S(1)} async-done(((f32[16,1,3456]{2,1,0:T(1,128)}), f32[16,1,3456]{2,1,0:T(1,128)S(1)}, u32[]{:S(2)}, u32[]{:S(2)}) %all-to-all-start) | async-done | bytes 221216 | tf_op jit(solution)/shard_map/all_to_all | solution.py:44
  83.1 0.8 broadcast_in_dim.32
  83.9 3.5 %all-to-all-start.1 = ((f32[16,1,3456]{2,1,0:T(1,128)}), f32[16,1,3456]{2,1,0:T(1,128)S(1)}, u32[]{:S(2)}, u32[]{:S(2)}) async-start(f32[16,1,3456]{2,1,0:T(1,128)} %broadcast_in_dim.32), calls=%async_computation.1 | async-start | bytes 442368 | tf_op jit(solution)/shard_map/all_to_all | solution.py:45
  87.6 1.1 %copy.142 = bf16[32,2,16,256]{3,2,1,0:T(8,128)(2,1)} copy(bf16[32,2,16,256]{3,0,2,1:T(8,128)(2,1)S(1)} %fusion.92) | data formatting | bytes 1048576
  89.0 0.7 copy.141
  89.7 7.1 %all-to-all-done.1 = f32[16,1,3456]{2,1,0:T(1,128)S(1)} async-done(((f32[16,1,3456]{2,1,0:T(1,128)}), f32[16,1,3456]{2,1,0:T(1,128)S(1)}, u32[]{:S(2)}, u32[]{:S(2)}) %all-to-all-start.1) | async-done | bytes 221216 | tf_op jit(solution)/shard_map/all_to_all | solution.py:45
  96.8 0.5 reduce.1
  97.3 0.7 reshape_reshape_reshape.3
  98.3 0.8 copy.139
  99.1 0.8 copy.140
  (77 shorter events, 7.4 us)
Async XLA Ops:
  0.6 17.2 %copy-start.5 = (bf16[27,32,32]{2,1,0:T(8,128)(2,1)S(1)}, bf16[27,32,32]{2,1,0:T(8,128)(2,1)}, u32[]{:S(2)}) copy-start(bf16[27,32,32]{2,1,0:T(8,128)(2,1)} %param.8) | copy-start | bytes 165892
  0.6 15.5 %copy-start.4 = (bf16[27,32,32]{2,1,0:T(8,128)(2,1)S(1)}, bf16[27,32,32]{2,1,0:T(8,128)(2,1)}, u32[]{:S(2)}) copy-start(bf16[27,32,32]{2,1,0:T(8,128)(2,1)} %param.7) | copy-start | bytes 165892
  1.6 17.9 %copy-start.6 = (bf16[32,1,8,128]{3,2,1,0:T(8,128)(2,1)S(1)}, bf16[32,1,8,128]{3,2,1,0:T(8,128)(2,1)}, u32[]{:S(2)}) copy-start(bf16[32,1,8,128]{3,2,1,0:T(8,128)(2,1)} %param.9) | copy-start | bytes 196612
  1.6 17.8 %collective-permute-start.2 = (bf16[32,1,8,128]{3,0,2,1:T(8,128)(2,1)S(1)}, bf16[32,1,8,128]{3,0,2,1:T(8,128)(2,1)S(1)}, u32[]{:S(2)}, u32[]{:S(2)}) collective-permute-start(bf16[32,1,8,128]{3,0,2,1:T(8,128)(2,1)S(1)} %copy.113), channel_id=1, source_target_pairs={{0,1},{1,2},{2,3},{3,4},{4,5},{5,6},{6,7},{7,8},{8,9},{9,10},{10,1... | collective-permute-start | bytes 196616 | tf_op jit(solution)/shard_map/ppermute | solution.py:15
  4.1 15.4 %collective-permute-start.3 = (bf16[32,1,8,128]{3,0,2,1:T(8,128)(2,1)S(1)}, bf16[32,1,8,128]{3,0,2,1:T(8,128)(2,1)S(1)}, u32[]{:S(2)}, u32[]{:S(2)}) collective-permute-start(bf16[32,1,8,128]{3,0,2,1:T(8,128)(2,1)S(1)} %copy.113), channel_id=1, source_target_pairs={{1,0},{2,1},{3,2},{4,3},{5,4},{6,5},{7,6},{8,7},{9,8},{10,9},{11,1... | collective-permute-start | bytes 196616 | tf_op jit(solution)/shard_map/ppermute | solution.py:16
  6.8 29.3 %collective-permute-start = (bf16[32,2,16,256]{3,0,2,1:T(8,128)(2,1)S(1)}, bf16[32,2,16,256]{3,0,2,1:T(8,128)(2,1)S(1)}, u32[]{:S(2)}, u32[]{:S(2)}) collective-permute-start(bf16[32,2,16,256]{3,0,2,1:T(8,128)(2,1)S(1)} %copy.106), channel_id=1, source_target_pairs={{0,1},{1,2},{2,3},{3,4},{4,5},{5,6},{6,7},{7,8},{8,9},{9,10},{10,1... | collective-permute-start | bytes 1572872 | tf_op jit(solution)/shard_map/ppermute | solution.py:15
  12.0 24.2 %collective-permute-start.1 = (bf16[32,2,16,256]{3,0,2,1:T(8,128)(2,1)S(1)}, bf16[32,2,16,256]{3,0,2,1:T(8,128)(2,1)}, u32[]{:S(2)}, u32[]{:S(2)}) collective-permute-start(bf16[32,2,16,256]{3,0,2,1:T(8,128)(2,1)S(1)} %copy.106), channel_id=1, source_target_pairs={{1,0},{2,1},{3,2},{4,3},{5,4},{6,5},{7,6},{8,7},{9,8},{10,9},{11,1... | collective-permute-start | bytes 1572872 | tf_op jit(solution)/shard_map/ppermute | solution.py:16
  15.4 4.4 %copy-start.2 = (bf16[27,32,32]{2,1,0:T(8,128)(2,1)}, bf16[27,32,32]{2,1,0:T(8,128)(2,1)S(1)}, u32[]{:S(2)}) copy-start(bf16[27,32,32]{2,1,0:T(8,128)(2,1)S(1)} %gather_fusion) | copy-start | bytes 165892
  19.5 1.1 %copy-start.11 = (bf16[4,32,32]{2,1,0:T(8,128)(2,1)S(1)}, bf16[4,32,32]{2,1,0:T(8,128)(2,1)}, u32[]{:S(2)}) copy-start(bf16[4,32,32]{2,1,0:T(8,128)(2,1)} %get-tuple-element.38) | copy-start | bytes 24580
  19.8 1.1 %copy-start.10 = (bf16[4,32,32]{2,1,0:T(8,128)(2,1)S(1)}, bf16[4,32,32]{2,1,0:T(8,128)(2,1)}, u32[]{:S(2)}) copy-start(bf16[4,32,32]{2,1,0:T(8,128)(2,1)} %get-tuple-element.37) | copy-start | bytes 24580
  20.4 0.8 slice-start
  20.6 0.9 copy-start.3
  20.9 1.3 %copy-start.9 = (bf16[4,32,32]{2,1,0:T(8,128)(2,1)S(1)}, bf16[4,32,32]{2,1,0:T(8,128)(2,1)}, u32[]{:S(2)}) copy-start(bf16[4,32,32]{2,1,0:T(8,128)(2,1)} %get-tuple-element.36) | copy-start | bytes 24580
  40.2 0.9 copy-start.7
  45.0 1.9 %copy-start.13 = (pred[4]{0:T(512)(128)(4,1)S(1)}, pred[4]{0:T(512)(128)(4,1)}, u32[]{:S(2)}) copy-start(pred[4]{0:T(512)(128)(4,1)} %compare_and_fusion) | copy-start | bytes 16
  58.0 1.6 %copy-start = (f32[32,4,16,256]{3,0,2,1:T(8,128)S(1)}, f32[32,4,16,256]{3,0,2,1:T(8,128)}, u32[]{:S(2)}) copy-start(f32[32,4,16,256]{3,0,2,1:T(8,128)} %get-tuple-element.24) | copy-start | bytes 6291460
  58.0 2.3 %copy-start.1 = (f32[32,4,16,256]{3,0,2,1:T(8,128)S(1)}, f32[32,4,16,256]{3,0,2,1:T(8,128)}, u32[]{:S(2)}) copy-start(f32[32,4,16,256]{3,0,2,1:T(8,128)} %get-tuple-element.49) | copy-start | bytes 6291460
  59.4 1.5 %copy-start.12 = (s32[3,128]{1,0:T(4,128)S(1)}, s32[3,128]{1,0:T(4,128)}, u32[]{:S(2)}) copy-start(s32[3,128]{1,0:T(4,128)} %add_add_fusion) | copy-start | bytes 4612
  64.4 18.6 %all-to-all-start = ((f32[16,1,3456]{2,1,0:T(1,128)}), f32[16,1,3456]{2,1,0:T(1,128)S(1)}, u32[]{:S(2)}, u32[]{:S(2)}) async-start(f32[16,1,3456]{2,1,0:T(1,128)} %all_to_all.13), calls=%async_computation | async-start | bytes 442368 | tf_op jit(solution)/shard_map/all_to_all | solution.py:44
  77.9 0.9 copy-start.8
  83.9 12.9 %all-to-all-start.1 = ((f32[16,1,3456]{2,1,0:T(1,128)}), f32[16,1,3456]{2,1,0:T(1,128)S(1)}, u32[]{:S(2)}, u32[]{:S(2)}) async-start(f32[16,1,3456]{2,1,0:T(1,128)} %broadcast_in_dim.32), calls=%async_computation.1 | async-start | bytes 442368 | tf_op jit(solution)/shard_map/all_to_all | solution.py:45

commit v6 on v5

--- a/solution.py
+++ b/solution.py
@@ -170,12 +170,12 @@
                         "kq,kdhw->qdhw", joined_kernel, joined, preferred_element_type=jnp.float32
                     )
                 )
-    parity_grid = jnp.stack(classes).reshape(2, 2, 2, channels, class_planes, half_rows, half_cols)
+    parity_grid = jnp.stack(classes).astype(jnp.bfloat16).reshape(2, 2, 2, channels, class_planes, half_rows, half_cols)
     grad_hidden = parity_grid.transpose(3, 4, 0, 5, 1, 6, 2).reshape(
         channels, 2 * class_planes, height, columns
     )
     sigma = jax.nn.sigmoid(preact)
-    grad_rim = grad_hidden * (sigma * (1.0 + preact * (1.0 - sigma)))
+    grad_rim = grad_hidden.astype(jnp.float32) * (sigma * (1.0 + preact * (1.0 - sigma)))
     grad_rim = jnp.where(inside, grad_rim, 0.0).astype(jnp.bfloat16)
     grad_pre = grad_rim[:, 1 : planes + 1]
     rimmed = pad_sides(grad_rim)

time: 101 us -> 96.4 us (0.954)
  local copies, waits for them, and re-layouts: 33.3 us -> 29.6 us
  other arithmetic: 7.92 us -> 6.76 us
    reshape x2 -> x0, local copies, waits for them, and re-layouts: 13.6 us -> none  [the longest x1 8.51 us: on_device(): jnp.stack(classes)]
    convert_element_type x0 -> x2, local copies, waits for them, and re-layouts: none -> 12.9 us  [on_device(): grad_hidden.astype(jnp.float32) * (sigma * (1.0 + preact * (1.0 - sigma)))]
    reshape x4, local copies, waits for them, and re-layouts: 1.91 us -> 0.64 us  [forward_kernel(): weights.reshape(3, 3, 3, size, size).transpose(0, 1, 3, 2, 4)]
    unnamed x40 -> x26, local copies, waits for them, and re-layouts: 6.49 us -> 5.46 us
  transfers between devices with their start and end apart: 6 -> 6, of which waited for: 2 -> 2; matrix products, arithmetic and copies ran while one was open for 32% -> 29% of each run, Pallas kernels for 0% -> 0%
where the time goes in v6:
time: 96.4 us; the launch traced here: 95.8 us
  local copies, waits for them, and re-layouts  29.6 us (31%)
  matrix products  24.6 us (26%)
  starting transfers between devices  23 us (24%)
  waiting for transfers between devices  10.5 us (11%)
  other arithmetic  6.76 us (7%)
  between operations  1.22 us (1%)
    convert_element_type x2, local copies, waits for them, and re-layouts, on_device(): grad_hidden.astype(jnp.float32) * (sigma * (1.0 + preact * (1.0 - sigma)))  12.9 us
    dot_general x9, matrix products, on_device(): jnp.einsum('ok,kdhw->odhw', front_one[along_depth, along_rows], window, p...  10.1 us
    all_to_all x1, starting transfers between devices, summed_over(): mine = lax.all_to_all(flat, axis, 0, 0, tiled=True).sum(0, keepdims=True)  9.21 us
    ppermute x2, starting transfers between devices, extended_2(): before = lax.ppermute(last, axis, up)  7.72 us
    all_to_all x1, waiting for transfers between devices, summed_over(): lax.all_to_all(jnp.broadcast_to(mine, flat.shape), axis, 0, 0, tiled=True)  7.1 us
    dot_general x9, matrix products, on_device(): jnp.einsum('odhw,kdhw->ok', grad_pre, window, preferred_element_type=jnp....  5.75 us
    unnamed x26, local copies, waits for them, and re-layouts  5.46 us
    slice x2, local copies, waits for them, and re-layouts, column_stack(): pieces.append(field[..., first:first + stride * (count - 1) + 1:stride])  3.82 us
  transfers between devices with their start and end apart: 6, of which 2 were waited for; matrix products, arithmetic and copies ran while one was open for 29% of the time, Pallas kernels for 0%

profile of v6, /device:TPU:0, one launch (start us, length us, event | category | flops | bytes accessed | tf_op | source)
XLA Modules:
  0.0 95.8 jit_solution(4933964099639402754)
XLA Ops:
  0.7 0.9 copy.113
  1.6 2.5 %collective-permute-start.2 = (bf16[32,1,8,128]{3,0,2,1:T(8,128)(2,1)S(1)}, bf16[32,1,8,128]{3,0,2,1:T(8,128)(2,1)S(1)}, u32[]{:S(2)}, u32[]{:S(2)}) collective-permute-start(bf16[32,1,8,128]{3,0,2,1:T(8,128)(2,1)S(1)} %copy.113), channel_id=1, source_target_pairs={{0,1},{1,2},{2,3},{3,4},{4,5},{5,6},{6,7},{7,8},{8,9},{9,10},{10,1... | collective-permute-start | bytes 196616 | tf_op jit(solution)/shard_map/ppermute | solution.py:15
  4.1 1.3 %collective-permute-start.3 = (bf16[32,1,8,128]{3,0,2,1:T(8,128)(2,1)S(1)}, bf16[32,1,8,128]{3,0,2,1:T(8,128)(2,1)S(1)}, u32[]{:S(2)}, u32[]{:S(2)}) collective-permute-start(bf16[32,1,8,128]{3,0,2,1:T(8,128)(2,1)S(1)} %copy.113), channel_id=1, source_target_pairs={{1,0},{2,1},{3,2},{4,3},{5,4},{6,5},{7,6},{8,7},{9,8},{10,9},{11,1... | collective-permute-start | bytes 196616 | tf_op jit(solution)/shard_map/ppermute | solution.py:16
  5.4 1.3 %copy.106 = bf16[32,2,16,256]{3,0,2,1:T(8,128)(2,1)S(1)} copy(bf16[32,2,16,256]{3,2,1,0:T(8,128)(2,1)} %param.6) | data formatting | bytes 1048576 | tf_op args[0]
  6.8 5.2 %collective-permute-start = (bf16[32,2,16,256]{3,0,2,1:T(8,128)(2,1)S(1)}, bf16[32,2,16,256]{3,0,2,1:T(8,128)(2,1)S(1)}, u32[]{:S(2)}, u32[]{:S(2)}) collective-permute-start(bf16[32,2,16,256]{3,0,2,1:T(8,128)(2,1)S(1)} %copy.106), channel_id=1, source_target_pairs={{0,1},{1,2},{2,3},{3,4},{4,5},{5,6},{6,7},{7,8},{8,9},{9,10},{10,1... | collective-permute-start | bytes 1572872 | tf_op jit(solution)/shard_map/ppermute | solution.py:15
  12.0 1.3 %collective-permute-start.1 = (bf16[32,2,16,256]{3,0,2,1:T(8,128)(2,1)S(1)}, bf16[32,2,16,256]{3,0,2,1:T(8,128)(2,1)}, u32[]{:S(2)}, u32[]{:S(2)}) collective-permute-start(bf16[32,2,16,256]{3,0,2,1:T(8,128)(2,1)S(1)} %copy.106), channel_id=1, source_target_pairs={{1,0},{2,1},{3,2},{4,3},{5,4},{6,5},{7,6},{8,7},{9,8},{10,9},{11,1... | collective-permute-start | bytes 1572872 | tf_op jit(solution)/shard_map/ppermute | solution.py:16
  13.3 0.7 pad_clamp_fusion
  13.9 1.5 %gather_fusion = bf16[27,32,32]{2,1,0:T(8,128)(2,1)S(1)} fusion(bf16[27,32,32]{2,1,0:T(8,128)(2,1)} %param.8, s32[1024]{0:T(1024)S(1)} %pad_clamp_fusion), kind=kCustom, calls=%fused_computation | custom fusion | bytes 110700 | tf_op jit(solution)/shard_map/gather | solution.py:147
  16.5 0.2 fusion.269
  17.6 0.2 fusion.101
  17.8 0.3 fusion.103
  18.2 0.3 fusion.105
  19.2 0.3 fusion.107
  19.5 7.8 %copy.125 = f32[2,2,2,32,2,8,128]{3,2,6,1,5,0,4:T(2,128)} copy(bf16[2,2,2,32,2,8,128]{6,3,5,4,2,1,0:T(8,128)(2,1)S(1)} %bitcast.506) | data formatting | bytes 3145728 | tf_op jit(solution)/shard_map/convert_element_type | solution.py:178
  27.3 5.1 %copy.126 = f32[32,4,16,256]{3,0,2,1:T(8,128)S(1)} copy(f32[32,4,16,256]{0,3,2,1:T(8,128)} %bitcast.484) | data formatting | bytes 4194304 | tf_op jit(solution)/shard_map/convert_element_type | solution.py:178
  32.4 2.6 %select_maximum_fusion = bf16[32,6,18,258]{3,0,2,1:T(8,128)(2,1)S(1)} fusion(bf16[32,2,16,256]{3,0,2,1:T(8,128)(2,1)} %collective-permute-done.1, bf16[32,2,16,256]{3,0,2,1:T(8,128)(2,1)S(1)} %copy.106, bf16[32,2,16,256]{3,0,2,1:T(8,128)(2,1)S(1)} %collective-permute-done), kind=kLoop, calls=%fused_computation.28 | loop fusion | flops 16941312 | bytes 3356160 | tf_op jit(solution)/shard_map/concatenate | solution.py:17
  35.1 1.4 %fusion.267 = (bf16[32,6,18,256]{3,0,2,1:T(8,128)(2,1)S(1)}, bf16[32,6,18,256]{3,0,2,1:T(8,128)(2,1)S(1)}, bf16[32,6,18,256]{3,0,2,1:T(8,128)(2,1)S(1)}) fusion(bf16[32,6,18,258]{3,0,2,1:T(8,128)(2,1)S(1)} %select_maximum_fusion), kind=kLoop, calls=%fused_computation.307 | loop fusion | bytes 10616832 | tf_op jit(solution)/shard_map/slice | solution.py:35
  36.5 0.4 pad_maximum_fusion
  36.9 0.6 fusion.11
  37.4 0.6 fusion.13
  38.0 0.6 fusion.15
  38.6 0.6 fusion.17
  39.1 0.6 fusion.19
  39.7 0.6 fusion.5
  40.2 0.6 fusion.7
  40.8 1.9 %fusion.9 = f32[4,16,256,32]{2,3,1,0:T(8,128)} fusion(bf16[96,6,18,256]{3,0,2,1:T(8,128)(2,1)S(1)} %pad_maximum_fusion, bf16[3,3,32,96]{3,2,1,0:T(8,128)(2,1)S(1)} %reshape.181), kind=kOutput, calls=%fused_computation.16 | convolution fusion | flops 100663296 | bytes 5251072 | tf_op jit(solution)/shard_map/ok,kdhw->odhw/dot_general | solution.py:98
  42.7 4.3 %select_convert_fusion = (bf16[32,4,16,256]{3,0,2,1:T(8,128)(2,1)S(1)}, f32[32,4,16,256]{3,0,2,1:T(8,128)}, f32[32,4,16,256]{3,0,2,1:T(8,128)}) fusion(f32[32,4,16,256]{3,0,2,1:T(8,128)S(1)} %copy.126, pred[4]{0:T(512)(128)(4,1)S(1)} %compare_and_fusion, bf16[96,6,18,256]{3,0,2,1:T(8,128)(2,1)S(1)} %pad_maximum_fusion, ...), kind=kOutput, calls=%fused_computation.34 | convolution fusion | flops 110100480 | bytes 27271680 | tf_op jit(solution)/shard_map/ok,kdhw->odhw/dot_general | solution.py:98
  47.0 0.6 fusion.130
  47.6 2.4 %pad_slice_fusion.2 = (bf16[32,4,18,256]{3,0,2,1:T(8,128)(2,1)S(1)}, bf16[32,4,18,256]{3,0,2,1:T(8,128)(2,1)}, bf16[32,4,18,256]{3,0,2,1:T(8,128)(2,1)}) fusion(bf16[32,4,16,256]{3,0,2,1:T(8,128)(2,1)S(1)} %get-tuple-element.23), kind=kLoop, calls=%fused_computation.38 | loop fusion | bytes 4587520 | tf_op jit(solution)/shard_map/slice | solution.py:35
  50.0 0.6 fusion.136
  50.6 0.6 fusion.142
  51.3 0.6 fusion.148
  51.9 0.6 fusion.154
  52.6 0.6 fusion.160
  53.2 0.6 fusion.166
  53.9 0.6 fusion.172
  54.5 0.6 fusion.178
  55.2 0.3 copy-done
  55.5 0.6 copy-done.1
  56.1 0.5 fusion.63
  56.6 0.7 fusion.64
  59.2 1.0 %all_to_all.13 = f32[16,1,3456]{2,1,0:T(1,128)} reshape(f32[2,9,32,96]{3,2,1,0:T(8,128)S(1)} %pad_maximum_fusion.8) | data formatting | bytes 442368 | tf_op jit(solution)/shard_map/all_to_all | solution.py:44
  60.2 9.2 %all-to-all-start = ((f32[16,1,3456]{2,1,0:T(1,128)}), f32[16,1,3456]{2,1,0:T(1,128)S(1)}, u32[]{:S(2)}, u32[]{:S(2)}) async-start(f32[16,1,3456]{2,1,0:T(1,128)} %all_to_all.13), calls=%async_computation | async-start | bytes 442368 | tf_op jit(solution)/shard_map/all_to_all | solution.py:44
  69.4 1.8 %pad_maximum_fusion.1 = bf16[96,4,18,256]{3,0,2,1:T(8,128)(2,1)S(1)} fusion(bf16[32,4,18,256]{3,0,2,1:T(8,128)(2,1)} %get-tuple-element.29, bf16[32,4,18,256]{3,0,2,1:T(8,128)(2,1)} %get-tuple-element.28, bf16[32,4,18,256]{3,0,2,1:T(8,128)(2,1)S(1)} %get-tuple-element.27), kind=kLoop, calls=%fused_computation.9 | loop fusion | flops 10616832 | bytes 7077888 | tf_op jit(solution)/shard_map/concatenate | solution.py:36
  71.2 0.3 fusion.58
  71.6 0.4 fusion.65
  71.9 0.4 fusion.68
  72.3 0.4 fusion.71
  72.7 0.4 fusion.74
  73.0 0.4 fusion.77
  73.4 0.4 fusion.80
  73.7 0.4 fusion.83
  75.1 0.4 fusion.92
  75.4 3.4 %all-to-all-done = f32[16,1,3456]{2,1,0:T(1,128)S(1)} async-done(((f32[16,1,3456]{2,1,0:T(1,128)}), f32[16,1,3456]{2,1,0:T(1,128)S(1)}, u32[]{:S(2)}, u32[]{:S(2)}) %all-to-all-start) | async-done | bytes 221216 | tf_op jit(solution)/shard_map/all_to_all | solution.py:44
  78.9 0.8 broadcast_in_dim.32
  79.7 3.5 %all-to-all-start.1 = ((f32[16,1,3456]{2,1,0:T(1,128)}), f32[16,1,3456]{2,1,0:T(1,128)S(1)}, u32[]{:S(2)}, u32[]{:S(2)}) async-start(f32[16,1,3456]{2,1,0:T(1,128)} %broadcast_in_dim.32), calls=%async_computation.1 | async-start | bytes 442368 | tf_op jit(solution)/shard_map/all_to_all | solution.py:45
  83.4 1.1 %copy.142 = bf16[32,2,16,256]{3,2,1,0:T(8,128)(2,1)} copy(bf16[32,2,16,256]{3,0,2,1:T(8,128)(2,1)S(1)} %fusion.92) | data formatting | bytes 1048576
  84.8 0.7 copy.141
  85.5 7.1 %all-to-all-done.1 = f32[16,1,3456]{2,1,0:T(1,128)S(1)} async-done(((f32[16,1,3456]{2,1,0:T(1,128)}), f32[16,1,3456]{2,1,0:T(1,128)S(1)}, u32[]{:S(2)}, u32[]{:S(2)}) %all-to-all-start.1) | async-done | bytes 221216 | tf_op jit(solution)/shard_map/all_to_all | solution.py:45
  92.6 0.5 reduce.1
  93.1 0.7 reshape_reshape_reshape.3
  93.8 0.3 fusion.268
  94.1 0.8 copy.139
  95.0 0.8 copy.140
  (63 shorter events, 5.9 us)
Async XLA Ops:
  0.6 15.4 %copy-start.5 = (bf16[27,32,32]{2,1,0:T(8,128)(2,1)S(1)}, bf16[27,32,32]{2,1,0:T(8,128)(2,1)}, u32[]{:S(2)}) copy-start(bf16[27,32,32]{2,1,0:T(8,128)(2,1)} %param.8) | copy-start | bytes 165892
  0.6 14.9 %copy-start.4 = (bf16[27,32,32]{2,1,0:T(8,128)(2,1)S(1)}, bf16[27,32,32]{2,1,0:T(8,128)(2,1)}, u32[]{:S(2)}) copy-start(bf16[27,32,32]{2,1,0:T(8,128)(2,1)} %param.7) | copy-start | bytes 165892
  1.6 14.8 %copy-start.6 = (bf16[32,1,8,128]{3,2,1,0:T(8,128)(2,1)S(1)}, bf16[32,1,8,128]{3,2,1,0:T(8,128)(2,1)}, u32[]{:S(2)}) copy-start(bf16[32,1,8,128]{3,2,1,0:T(8,128)(2,1)} %param.9) | copy-start | bytes 196612
  1.6 14.8 %collective-permute-start.2 = (bf16[32,1,8,128]{3,0,2,1:T(8,128)(2,1)S(1)}, bf16[32,1,8,128]{3,0,2,1:T(8,128)(2,1)S(1)}, u32[]{:S(2)}, u32[]{:S(2)}) collective-permute-start(bf16[32,1,8,128]{3,0,2,1:T(8,128)(2,1)S(1)} %copy.113), channel_id=1, source_target_pairs={{0,1},{1,2},{2,3},{3,4},{4,5},{5,6},{6,7},{7,8},{8,9},{9,10},{10,1... | collective-permute-start | bytes 196616 | tf_op jit(solution)/shard_map/ppermute | solution.py:15
  4.1 12.3 %collective-permute-start.3 = (bf16[32,1,8,128]{3,0,2,1:T(8,128)(2,1)S(1)}, bf16[32,1,8,128]{3,0,2,1:T(8,128)(2,1)S(1)}, u32[]{:S(2)}, u32[]{:S(2)}) collective-permute-start(bf16[32,1,8,128]{3,0,2,1:T(8,128)(2,1)S(1)} %copy.113), channel_id=1, source_target_pairs={{1,0},{2,1},{3,2},{4,3},{5,4},{6,5},{7,6},{8,7},{9,8},{10,9},{11,1... | collective-permute-start | bytes 196616 | tf_op jit(solution)/shard_map/ppermute | solution.py:16
  6.8 25.6 %collective-permute-start = (bf16[32,2,16,256]{3,0,2,1:T(8,128)(2,1)S(1)}, bf16[32,2,16,256]{3,0,2,1:T(8,128)(2,1)S(1)}, u32[]{:S(2)}, u32[]{:S(2)}) collective-permute-start(bf16[32,2,16,256]{3,0,2,1:T(8,128)(2,1)S(1)} %copy.106), channel_id=1, source_target_pairs={{0,1},{1,2},{2,3},{3,4},{4,5},{5,6},{6,7},{7,8},{8,9},{9,10},{10,1... | collective-permute-start | bytes 1572872 | tf_op jit(solution)/shard_map/ppermute | solution.py:15
  12.0 20.4 %collective-permute-start.1 = (bf16[32,2,16,256]{3,0,2,1:T(8,128)(2,1)S(1)}, bf16[32,2,16,256]{3,0,2,1:T(8,128)(2,1)}, u32[]{:S(2)}, u32[]{:S(2)}) collective-permute-start(bf16[32,2,16,256]{3,0,2,1:T(8,128)(2,1)S(1)} %copy.106), channel_id=1, source_target_pairs={{1,0},{2,1},{3,2},{4,3},{5,4},{6,5},{7,6},{8,7},{9,8},{10,9},{11,1... | collective-permute-start | bytes 1572872 | tf_op jit(solution)/shard_map/ppermute | solution.py:16
  15.4 1.3 %copy-start.2 = (bf16[27,32,32]{2,1,0:T(8,128)(2,1)}, bf16[27,32,32]{2,1,0:T(8,128)(2,1)S(1)}, u32[]{:S(2)}) copy-start(bf16[27,32,32]{2,1,0:T(8,128)(2,1)S(1)} %gather_fusion) | copy-start | bytes 165892
  17.3 0.8 slice-start
  17.5 0.9 copy-start.3
  53.9 1.6 %copy-start = (f32[32,4,16,256]{3,0,2,1:T(8,128)S(1)}, f32[32,4,16,256]{3,0,2,1:T(8,128)}, u32[]{:S(2)}) copy-start(f32[32,4,16,256]{3,0,2,1:T(8,128)} %get-tuple-element.24) | copy-start | bytes 6291460
  53.9 2.3 %copy-start.1 = (f32[32,4,16,256]{3,0,2,1:T(8,128)S(1)}, f32[32,4,16,256]{3,0,2,1:T(8,128)}, u32[]{:S(2)}) copy-start(f32[32,4,16,256]{3,0,2,1:T(8,128)} %get-tuple-element.49) | copy-start | bytes 6291460
  60.2 18.6 %all-to-all-start = ((f32[16,1,3456]{2,1,0:T(1,128)}), f32[16,1,3456]{2,1,0:T(1,128)S(1)}, u32[]{:S(2)}, u32[]{:S(2)}) async-start(f32[16,1,3456]{2,1,0:T(1,128)} %all_to_all.13), calls=%async_computation | async-start | bytes 442368 | tf_op jit(solution)/shard_map/all_to_all | solution.py:44
  79.7 12.9 %all-to-all-start.1 = ((f32[16,1,3456]{2,1,0:T(1,128)}), f32[16,1,3456]{2,1,0:T(1,128)S(1)}, u32[]{:S(2)}, u32[]{:S(2)}) async-start(f32[16,1,3456]{2,1,0:T(1,128)} %broadcast_in_dim.32), calls=%async_computation.1 | async-start | bytes 442368 | tf_op jit(solution)/shard_map/all_to_all | solution.py:45

commit v7 on v4

--- a/solution.py
+++ b/solution.py
@@ -132,26 +132,49 @@
             terms_two.append(
                 jnp.einsum("odhw,kdhw->ok", cotangent, window, preferred_element_type=jnp.float32)
             )
-    rear_two = backward_kernel(weight_two).transpose(0, 1, 3, 2)
-    spread = lax.pad(
-        cot_ext, jnp.zeros((), cot_ext.dtype), ((0, 0, 0), (0, 1, 1), (1, 2, 1), (1, 2, 1))
-    )
-    spread_cols = column_stack(spread, 1, columns, lambda along_cols: 2 - along_cols)
-    grad_hidden = jnp.zeros((channels, planes + 2, height, columns), jnp.float32)
-    for along_depth in range(3):
-        for along_rows in range(3):
-            back_window = spread_cols[
-                :,
-                2 - along_depth : 2 - along_depth + planes + 2,
-                2 - along_rows : 2 - along_rows + height,
-                :,
-            ]
-            grad_hidden = grad_hidden + jnp.einsum(
-                "qk,kdhw->qdhw",
-                rear_two[along_depth, along_rows],
-                back_window,
-                preferred_element_type=jnp.float32,
-            )
+    extended = jnp.pad(cot_ext, ((0, 0), (0, 0), (0, 1), (0, 0)))
+    spread = jnp.arange(half_cols)[:, None, None] * 2 + jnp.arange(3)[None, :, None] - 1
+    spread = (spread == jnp.arange(columns)[None, None, :]).astype(jnp.bfloat16)
+    widened = jnp.einsum("odrj,jcw->codrw", extended, spread, preferred_element_type=jnp.float32)
+    widened = widened.astype(jnp.bfloat16)
+    class_planes = half_planes + 1
+    row_taps = [[(1, 0)], [(2, 0), (0, 1)]]
+    depth_taps = [[(2, 0), (0, 1)], [(1, 1)]]
+    order = []
+    for depth_slot in range(2):
+        for row_parity in range(2):
+            for tap_depth, _ in depth_taps[depth_slot]:
+                for tap_row, _ in row_taps[row_parity]:
+                    for tap_col in range(3):
+                        order.append(9 * tap_depth + 3 * tap_row + tap_col)
+    ordered_two = weight_two[np.array(order)]
+    taken = 0
+    classes = []
+    for depth_slot in range(2):
+        for row_parity in range(2):
+            pieces = []
+            for tap_depth, skip_depth in depth_taps[depth_slot]:
+                for tap_row, skip_row in row_taps[row_parity]:
+                    for tap_col in range(3):
+                        pieces.append(
+                            widened[
+                                tap_col,
+                                :,
+                                skip_depth : skip_depth + class_planes,
+                                skip_row : skip_row + half_rows,
+                                :,
+                            ]
+                        )
+            joined = jnp.concatenate(pieces, 0)
+            joined_kernel = ordered_two[taken : taken + len(pieces)].reshape(-1, channels)
+            taken += len(pieces)
+            classes.append(
+                jnp.einsum("kq,kdhw->qdhw", joined_kernel, joined, preferred_element_type=jnp.float32)
+            )
+    parity_grid = jnp.stack(classes).reshape(2, 2, channels, class_planes, half_rows, columns)
+    grad_hidden = parity_grid.transpose(2, 3, 0, 4, 1, 5).reshape(
+        channels, 2 * class_planes, height, columns
+    )
     sigma = jax.nn.sigmoid(preact)
     grad_rim = grad_hidden * (sigma * (1.0 + preact * (1.0 - sigma)))
     grad_rim = jnp.where(inside, grad_rim, 0.0).astype(jnp.bfloat16)

time: 128 us -> 83.5 us (0.65)
  matrix products: 53.1 us -> 22.5 us
  local copies, waits for them, and re-layouts: 28.2 us -> 16.7 us
  other arithmetic: 10.5 us -> 5.96 us
    dot_general x9, matrix products: 23.8 us -> 7.54 us  [on_device(): jnp.einsum('ok,kdhw->odhw', front_one[along_depth, along_rows], window, p...]
    pad x1 -> x0, local copies, waits for them, and re-layouts: 8.52 us -> none  [on_device(): lax.pad(cot_ext, jnp.zeros((), cot_ext.dtype), ((0, 0, 0), (0, 1, 1), (1,...]
    dot_general x9 -> x5, matrix products: 8.95 us -> 2.37 us  [the longest x4 1.78 us: on_device(): jnp.einsum('kq,kdhw->qdhw', joined_kernel, joined, preferred_element_type...]
    dot_general x9, matrix products: 7.54 us -> 3.22 us  [on_device(): jnp.einsum('qk,kdhw->qdhw', rear_one[along_depth, along_rows], back_windo...]
    dot_general x9, matrix products: 4.75 us -> 1.35 us  [on_device(): jnp.einsum('ok,kdhw->odhw', front_two[along_depth, along_rows], window, p...]
    all_to_all x1, starting transfers between devices: 10 us -> 12.4 us  [summed_over(): mine = lax.all_to_all(flat, axis, 0, 0, tiled=True).sum(0, keepdims=True)]
    all_to_all x1, waiting for transfers between devices: 4.85 us -> 7.1 us  [summed_over(): lax.all_to_all(jnp.broadcast_to(mine, flat.shape), axis, 0, 0, tiled=True)]
    concatenate x3 -> x2, other arithmetic: 3.9 us -> 2.18 us  [column_stack(): return jnp.concatenate(pieces, 0)]
  transfers between devices with their start and end apart: 6 -> 6, of which waited for: 2 -> 2; matrix products, arithmetic and copies ran while one was open for 23% -> 19% of each run, Pallas kernels for 0% -> 0%
where the time goes in v7:
time: 83.5 us; the launch traced here: 83 us
  starting transfers between devices  26.1 us (31%)
  matrix products  22.5 us (27%)
  local copies, waits for them, and re-layouts  16.7 us (20%)
  waiting for transfers between devices  10.5 us (13%)
  other arithmetic  5.96 us (7%)
  between operations  1.21 us (1%)
    all_to_all x1, starting transfers between devices, summed_over(): mine = lax.all_to_all(flat, axis, 0, 0, tiled=True).sum(0, keepdims=True)  12.4 us
    ppermute x2, starting transfers between devices, extended_2(): before = lax.ppermute(last, axis, up)  7.58 us
    dot_general x9, matrix products, on_device(): jnp.einsum('ok,kdhw->odhw', front_one[along_depth, along_rows], window, p...  7.54 us
    all_to_all x1, waiting for transfers between devices, summed_over(): lax.all_to_all(jnp.broadcast_to(mine, flat.shape), axis, 0, 0, tiled=True)  7.1 us
    dot_general x9, matrix products, on_device(): jnp.einsum('odhw,kdhw->ok', grad_pre, window, preferred_element_type=jnp....  5.75 us
    unnamed x26, local copies, waits for them, and re-layouts  5.44 us
    slice x2, local copies, waits for them, and re-layouts, column_stack(): pieces.append(field[..., first:first + stride * (count - 1) + 1:stride])  3.83 us
    all_to_all x1, starting transfers between devices, summed_over(): lax.all_to_all(jnp.broadcast_to(mine, flat.shape), axis, 0, 0, tiled=True)  3.53 us
  transfers between devices with their start and end apart: 6, of which 2 were waited for; matrix products, arithmetic and copies ran while one was open for 19% of the time, Pallas kernels for 0%

profile of v7, /device:TPU:0, one launch (start us, length us, event | category | flops | bytes accessed | tf_op | source)
XLA Modules:
  0.0 83.0 jit_solution(5328839461036063229)
XLA Ops:
  0.7 0.9 %copy.97 = bf16[32,1,8,128]{3,0,2,1:T(8,128)(2,1)S(1)} copy(bf16[32,1,8,128]{3,2,1,0:T(8,128)(2,1)} %param.9) | data formatting | bytes 131072 | tf_op args[3]
  1.6 2.4 %collective-permute-start.2 = (bf16[32,1,8,128]{3,0,2,1:T(8,128)(2,1)S(1)}, bf16[32,1,8,128]{3,0,2,1:T(8,128)(2,1)S(1)}, u32[]{:S(2)}, u32[]{:S(2)}) collective-permute-start(bf16[32,1,8,128]{3,0,2,1:T(8,128)(2,1)S(1)} %copy.97), channel_id=1, source_target_pairs={{0,1},{1,2},{2,3},{3,4},{4,5},{5,6},{6,7},{7,8},{8,9},{9,10},{10,1... | collective-permute-start | bytes 196616 | tf_op jit(solution)/shard_map/ppermute | solution.py:15
  4.0 1.3 %collective-permute-start.3 = (bf16[32,1,8,128]{3,0,2,1:T(8,128)(2,1)S(1)}, bf16[32,1,8,128]{3,0,2,1:T(8,128)(2,1)S(1)}, u32[]{:S(2)}, u32[]{:S(2)}) collective-permute-start(bf16[32,1,8,128]{3,0,2,1:T(8,128)(2,1)S(1)} %copy.97), channel_id=1, source_target_pairs={{1,0},{2,1},{3,2},{4,3},{5,4},{6,5},{7,6},{8,7},{9,8},{10,9},{11,1... | collective-permute-start | bytes 196616 | tf_op jit(solution)/shard_map/ppermute | solution.py:16
  5.3 1.3 %copy.90 = bf16[32,2,16,256]{3,0,2,1:T(8,128)(2,1)S(1)} copy(bf16[32,2,16,256]{3,2,1,0:T(8,128)(2,1)} %param.6) | data formatting | bytes 1048576 | tf_op args[0]
  6.6 5.2 %collective-permute-start = (bf16[32,2,16,256]{3,0,2,1:T(8,128)(2,1)S(1)}, bf16[32,2,16,256]{3,0,2,1:T(8,128)(2,1)S(1)}, u32[]{:S(2)}, u32[]{:S(2)}) collective-permute-start(bf16[32,2,16,256]{3,0,2,1:T(8,128)(2,1)S(1)} %copy.90), channel_id=1, source_target_pairs={{0,1},{1,2},{2,3},{3,4},{4,5},{5,6},{6,7},{7,8},{8,9},{9,10},{10,1... | collective-permute-start | bytes 1572872 | tf_op jit(solution)/shard_map/ppermute | solution.py:15
  11.8 1.3 %collective-permute-start.1 = (bf16[32,2,16,256]{3,0,2,1:T(8,128)(2,1)S(1)}, bf16[32,2,16,256]{3,0,2,1:T(8,128)(2,1)S(1)}, u32[]{:S(2)}, u32[]{:S(2)}) collective-permute-start(bf16[32,2,16,256]{3,0,2,1:T(8,128)(2,1)S(1)} %copy.90), channel_id=1, source_target_pairs={{1,0},{2,1},{3,2},{4,3},{5,4},{6,5},{7,6},{8,7},{9,8},{10,9},{11,1... | collective-permute-start | bytes 1572872 | tf_op jit(solution)/shard_map/ppermute | solution.py:16
  13.1 0.7 pad_clamp_fusion
  13.8 1.5 %gather_fusion = bf16[27,32,32]{2,1,0:T(8,128)(2,1)S(1)} fusion(bf16[27,32,32]{2,1,0:T(8,128)(2,1)} %param.8, s32[1024]{0:T(1024)S(1)} %pad_clamp_fusion), kind=kCustom, calls=%fused_computation | custom fusion | bytes 110700 | tf_op jit(solution)/shard_map/gather | solution.py:150
  16.2 0.6 fusion.64
  17.5 0.4 convolution_bitcast_fusion
  18.0 0.4 convolution_bitcast_fusion.3
  18.4 0.3 convolution_bitcast_fusion.1
  18.9 0.6 convolution_bitcast_fusion.2
  19.5 0.2 pad_maximum_fusion.2
  19.9 1.7 %select_maximum_fusion = bf16[32,6,18,258]{3,0,2,1:T(8,128)(2,1)S(1)} fusion(bf16[32,2,16,256]{3,0,2,1:T(8,128)(2,1)S(1)} %collective-permute-done.1, bf16[32,2,16,256]{3,0,2,1:T(8,128)(2,1)S(1)} %copy.90, bf16[32,2,16,256]{3,0,2,1:T(8,128)(2,1)S(1)} %collective-permute-done), kind=kLoop, calls=%fused_computation.28 | loop fusion | flops 16941312 | bytes 3356160 | tf_op jit(solution)/shard_map/concatenate | solution.py:17
  21.6 1.4 %fusion.254 = (bf16[32,6,18,256]{3,0,2,1:T(8,128)(2,1)S(1)}, bf16[32,6,18,256]{3,0,2,1:T(8,128)(2,1)S(1)}, bf16[32,6,18,256]{3,0,2,1:T(8,128)(2,1)S(1)}) fusion(bf16[32,6,18,258]{3,0,2,1:T(8,128)(2,1)S(1)} %select_maximum_fusion), kind=kLoop, calls=%fused_computation.290 | loop fusion | bytes 10616832 | tf_op jit(solution)/shard_map/slice | solution.py:35
  23.0 0.4 pad_maximum_fusion
  23.4 0.6 fusion.11
  24.0 0.6 fusion.13
  24.5 0.6 fusion.15
  25.1 0.6 fusion.17
  25.6 0.6 fusion.19
  26.2 0.6 fusion.5
  26.7 0.6 fusion.7
  27.3 0.6 fusion.9
  27.9 3.1 %select_convert_fusion = (bf16[32,4,16,256]{3,0,2,1:T(8,128)(2,1)S(1)}, f32[32,4,16,256]{3,0,2,1:T(8,128)}, f32[32,4,16,256]{3,0,2,1:T(8,128)}) fusion(f32[32,4,16,256]{3,0,2,1:T(8,128)S(1)} %bitcast.523, pred[4]{0:T(512)(128)(4,1)S(1)} %compare_and_fusion, bf16[96,6,18,256]{3,0,2,1:T(8,128)(2,1)S(1)} %pad_maximum_fusion, ...), kind=kOutput, calls=%fused_computation.35 | convolution fusion | flops 110100480 | bytes 27271680 | tf_op jit(solution)/shard_map/ok,kdhw->odhw/dot_general | solution.py:98
  31.0 0.6 fusion.110
  31.6 2.4 %pad_slice_fusion.2 = (bf16[32,4,18,256]{3,0,2,1:T(8,128)(2,1)S(1)}, bf16[32,4,18,256]{3,0,2,1:T(8,128)(2,1)}, bf16[32,4,18,256]{3,0,2,1:T(8,128)(2,1)}) fusion(bf16[32,4,16,256]{3,0,2,1:T(8,128)(2,1)S(1)} %get-tuple-element.23), kind=kLoop, calls=%fused_computation.39 | loop fusion | bytes 4587520 | tf_op jit(solution)/shard_map/slice | solution.py:35
  34.0 0.6 fusion.116
  34.6 0.6 fusion.122
  35.3 0.6 fusion.128
  35.9 0.6 fusion.134
  36.6 0.6 fusion.140
  37.2 0.6 fusion.146
  37.9 0.6 fusion.152
  38.5 0.6 fusion.158
  39.2 0.3 copy-done
  39.5 0.6 copy-done.1
  40.1 0.5 fusion.63
  40.7 0.7 fusion.65
  41.3 0.2 copy.94
  43.2 1.0 %all_to_all.13 = f32[16,1,3456]{2,1,0:T(1,128)} reshape(f32[2,9,32,96]{3,2,1,0:T(8,128)S(1)} %pad_maximum_fusion.3) | data formatting | bytes 442368 | tf_op jit(solution)/shard_map/all_to_all | solution.py:44
  44.2 12.4 %all-to-all-start = ((f32[16,1,3456]{2,1,0:T(1,128)}), f32[16,1,3456]{2,1,0:T(1,128)S(1)}, u32[]{:S(2)}, u32[]{:S(2)}) async-start(f32[16,1,3456]{2,1,0:T(1,128)} %all_to_all.13), calls=%async_computation | async-start | bytes 442368 | tf_op jit(solution)/shard_map/all_to_all | solution.py:44
  56.6 1.8 %pad_maximum_fusion.1 = bf16[96,4,18,256]{3,0,2,1:T(8,128)(2,1)S(1)} fusion(bf16[32,4,18,256]{3,0,2,1:T(8,128)(2,1)} %get-tuple-element.53, bf16[32,4,18,256]{3,0,2,1:T(8,128)(2,1)} %get-tuple-element.52, bf16[32,4,18,256]{3,0,2,1:T(8,128)(2,1)S(1)} %get-tuple-element.51), kind=kLoop, calls=%fused_computation.9 | loop fusion | flops 10616832 | bytes 7077888 | tf_op jit(solution)/shard_map/concatenate | solution.py:36
  58.4 0.3 fusion.58
  58.8 0.4 fusion.66
  59.1 0.4 fusion.69
  59.5 0.4 fusion.72
  59.8 0.4 fusion.75
  60.2 0.4 fusion.78
  60.6 0.4 fusion.81
  60.9 0.4 fusion.84
  62.2 0.4 fusion.93
  62.6 3.4 %all-to-all-done = f32[16,1,3456]{2,1,0:T(1,128)S(1)} async-done(((f32[16,1,3456]{2,1,0:T(1,128)}), f32[16,1,3456]{2,1,0:T(1,128)S(1)}, u32[]{:S(2)}, u32[]{:S(2)}) %all-to-all-start) | async-done | bytes 221216 | tf_op jit(solution)/shard_map/all_to_all | solution.py:44
  66.1 0.8 broadcast_in_dim.35
  66.9 3.5 %all-to-all-start.1 = ((f32[16,1,3456]{2,1,0:T(1,128)}), f32[16,1,3456]{2,1,0:T(1,128)S(1)}, u32[]{:S(2)}, u32[]{:S(2)}) async-start(f32[16,1,3456]{2,1,0:T(1,128)} %broadcast_in_dim.35), calls=%async_computation.1 | async-start | bytes 442368 | tf_op jit(solution)/shard_map/all_to_all | solution.py:45
  70.6 1.1 %copy.119 = bf16[32,2,16,256]{3,2,1,0:T(8,128)(2,1)} copy(bf16[32,2,16,256]{3,0,2,1:T(8,128)(2,1)S(1)} %fusion.93) | data formatting | bytes 1048576
  72.0 0.7 copy.118
  72.7 7.1 %all-to-all-done.1 = f32[16,1,3456]{2,1,0:T(1,128)S(1)} async-done(((f32[16,1,3456]{2,1,0:T(1,128)}), f32[16,1,3456]{2,1,0:T(1,128)S(1)}, u32[]{:S(2)}, u32[]{:S(2)}) %all-to-all-start.1) | async-done | bytes 221216 | tf_op jit(solution)/shard_map/all_to_all | solution.py:45
  79.8 0.5 reduce.1
  80.3 0.7 reshape_reshape_reshape.3
  81.0 0.3 fusion.255
  81.3 0.8 copy.116
  82.1 0.8 copy.117
  (62 shorter events, 4.9 us)
Async XLA Ops:
  0.6 15.2 %copy-start.4 = (bf16[27,32,32]{2,1,0:T(8,128)(2,1)S(1)}, bf16[27,32,32]{2,1,0:T(8,128)(2,1)}, u32[]{:S(2)}) copy-start(bf16[27,32,32]{2,1,0:T(8,128)(2,1)} %param.8) | copy-start | bytes 165892
  0.6 14.7 %copy-start.3 = (bf16[27,32,32]{2,1,0:T(8,128)(2,1)S(1)}, bf16[27,32,32]{2,1,0:T(8,128)(2,1)}, u32[]{:S(2)}) copy-start(bf16[27,32,32]{2,1,0:T(8,128)(2,1)} %param.7) | copy-start | bytes 165892
  1.6 14.6 %collective-permute-start.2 = (bf16[32,1,8,128]{3,0,2,1:T(8,128)(2,1)S(1)}, bf16[32,1,8,128]{3,0,2,1:T(8,128)(2,1)S(1)}, u32[]{:S(2)}, u32[]{:S(2)}) collective-permute-start(bf16[32,1,8,128]{3,0,2,1:T(8,128)(2,1)S(1)} %copy.97), channel_id=1, source_target_pairs={{0,1},{1,2},{2,3},{3,4},{4,5},{5,6},{6,7},{7,8},{8,9},{9,10},{10,1... | collective-permute-start | bytes 196616 | tf_op jit(solution)/shard_map/ppermute | solution.py:15
  4.0 12.2 %collective-permute-start.3 = (bf16[32,1,8,128]{3,0,2,1:T(8,128)(2,1)S(1)}, bf16[32,1,8,128]{3,0,2,1:T(8,128)(2,1)S(1)}, u32[]{:S(2)}, u32[]{:S(2)}) collective-permute-start(bf16[32,1,8,128]{3,0,2,1:T(8,128)(2,1)S(1)} %copy.97), channel_id=1, source_target_pairs={{1,0},{2,1},{3,2},{4,3},{5,4},{6,5},{7,6},{8,7},{9,8},{10,9},{11,1... | collective-permute-start | bytes 196616 | tf_op jit(solution)/shard_map/ppermute | solution.py:16
  6.6 13.3 %collective-permute-start = (bf16[32,2,16,256]{3,0,2,1:T(8,128)(2,1)S(1)}, bf16[32,2,16,256]{3,0,2,1:T(8,128)(2,1)S(1)}, u32[]{:S(2)}, u32[]{:S(2)}) collective-permute-start(bf16[32,2,16,256]{3,0,2,1:T(8,128)(2,1)S(1)} %copy.90), channel_id=1, source_target_pairs={{0,1},{1,2},{2,3},{3,4},{4,5},{5,6},{6,7},{7,8},{8,9},{9,10},{10,1... | collective-permute-start | bytes 1572872 | tf_op jit(solution)/shard_map/ppermute | solution.py:15
  11.8 8.1 %collective-permute-start.1 = (bf16[32,2,16,256]{3,0,2,1:T(8,128)(2,1)S(1)}, bf16[32,2,16,256]{3,0,2,1:T(8,128)(2,1)S(1)}, u32[]{:S(2)}, u32[]{:S(2)}) collective-permute-start(bf16[32,2,16,256]{3,0,2,1:T(8,128)(2,1)S(1)} %copy.90), channel_id=1, source_target_pairs={{1,0},{2,1},{3,2},{4,3},{5,4},{6,5},{7,6},{8,7},{9,8},{10,9},{11,1... | collective-permute-start | bytes 1572872 | tf_op jit(solution)/shard_map/ppermute | solution.py:16
  15.3 1.5 %copy-start.2 = (bf16[27,32,32]{2,1,0:T(8,128)(2,1)}, bf16[27,32,32]{2,1,0:T(8,128)(2,1)S(1)}, u32[]{:S(2)}) copy-start(bf16[27,32,32]{2,1,0:T(8,128)(2,1)S(1)} %gather_fusion) | copy-start | bytes 165892
  17.5 0.9 %slice-start.1 = ((bf16[27,32,32]{2,1,0:T(8,128)(2,1)}), bf16[3,32,32]{2,1,0:T(8,128)(2,1)S(1)}, s32[]{:S(2)}) async-start(bf16[27,32,32]{2,1,0:T(8,128)(2,1)} %copy-done.2), calls=%async_computation.3 | async-start | bytes 49152 | tf_op jit(solution)/shard_map/slice | solution.py:169
  18.0 0.9 %slice-start = ((bf16[27,32,32]{2,1,0:T(8,128)(2,1)}), bf16[12,32,32]{2,1,0:T(8,128)(2,1)S(1)}, s32[]{:S(2)}) async-start(bf16[27,32,32]{2,1,0:T(8,128)(2,1)} %copy-done.2), calls=%async_computation.2 | async-start | bytes 196608 | tf_op jit(solution)/shard_map/slice | solution.py:169
  37.9 1.6 %copy-start = (f32[32,4,16,256]{3,0,2,1:T(8,128)S(1)}, f32[32,4,16,256]{3,0,2,1:T(8,128)}, u32[]{:S(2)}) copy-start(f32[32,4,16,256]{3,0,2,1:T(8,128)} %get-tuple-element.24) | copy-start | bytes 6291460
  37.9 2.3 %copy-start.1 = (f32[32,4,16,256]{3,0,2,1:T(8,128)S(1)}, f32[32,4,16,256]{3,0,2,1:T(8,128)}, u32[]{:S(2)}) copy-start(f32[32,4,16,256]{3,0,2,1:T(8,128)} %get-tuple-element.56) | copy-start | bytes 6291460
  40.6 0.9 %copy-start.5 = (bf16[32,1,8,128]{3,2,1,0:T(8,128)(2,1)S(1)}, bf16[32,1,8,128]{3,2,1,0:T(8,128)(2,1)}, u32[]{:S(2)}) copy-start(bf16[32,1,8,128]{3,2,1,0:T(8,128)(2,1)} %param.9) | copy-start | bytes 196612
  44.2 21.7 %all-to-all-start = ((f32[16,1,3456]{2,1,0:T(1,128)}), f32[16,1,3456]{2,1,0:T(1,128)S(1)}, u32[]{:S(2)}, u32[]{:S(2)}) async-start(f32[16,1,3456]{2,1,0:T(1,128)} %all_to_all.13), calls=%async_computation | async-start | bytes 442368 | tf_op jit(solution)/shard_map/all_to_all | solution.py:44
  66.9 12.9 %all-to-all-start.1 = ((f32[16,1,3456]{2,1,0:T(1,128)}), f32[16,1,3456]{2,1,0:T(1,128)S(1)}, u32[]{:S(2)}, u32[]{:S(2)}) async-start(f32[16,1,3456]{2,1,0:T(1,128)} %broadcast_in_dim.35), calls=%async_computation.1 | async-start | bytes 442368 | tf_op jit(solution)/shard_map/all_to_all | solution.py:45

commit v8 on v7

--- a/solution.py
+++ b/solution.py
@@ -203,8 +203,8 @@
                 back_window,
                 preferred_element_type=jnp.float32,
             )
-    summed = summed_over(jnp.stack([jnp.stack(terms_one), jnp.stack(terms_two)]), "slab")
-    grad_one, grad_two = fold_terms(summed)
+    folded = fold_terms(jnp.stack([jnp.stack(terms_one), jnp.stack(terms_two)]))
+    grad_one, grad_two = summed_over(jnp.stack(folded), "slab")
     return (output.astype(jnp.bfloat16), grad_volume.astype(jnp.bfloat16), grad_one, grad_two)
 
 

time: 83.5 us -> 92.8 us (1.11)
  local copies, waits for them, and re-layouts: 16.7 us -> 24.8 us
  other arithmetic: 5.96 us -> 8.83 us
  starting transfers between devices: 26.1 us -> 24.8 us
    another operation x1 -> x7, local copies, waits for them, and re-layouts: 0.71 us -> 5.93 us  [the longest x4 3.84 us: on_device(): grad_one, grad_two = summed_over(jnp.stack(folded), 'slab')]
    another operation x1 -> x2, other arithmetic: 0.05 us -> 2.21 us  [the longest x1 1.31 us: on_device(): grad_one, grad_two = summed_over(jnp.stack(folded), 'slab')]
    all_to_all x1, starting transfers between devices: 12.4 us -> 11.1 us  [summed_over(): mine = lax.all_to_all(flat, axis, 0, 0, tiled=True).sum(0, keepdims=True)]
    all_to_all x1, local copies, waits for them, and re-layouts: 1 us -> 2.24 us  [summed_over(): mine = lax.all_to_all(flat, axis, 0, 0, tiled=True).sum(0, keepdims=True)]
    concatenate x0 -> x1, other arithmetic: none -> 1.18 us
    slice x3 -> x5, local copies, waits for them, and re-layouts: 1.92 us -> 2.13 us  [fold_terms(): return (folded[0], folded[1])]
    unnamed x26 -> x30, local copies, waits for them, and re-layouts: 5.44 us -> 5.58 us
where the time goes in v8:
time: 92.8 us; the launch traced here: 92.1 us
  local copies, waits for them, and re-layouts  24.8 us (27%)
  starting transfers between devices  24.8 us (27%)
  matrix products  22.5 us (24%)
  waiting for transfers between devices  9.91 us (11%)
  other arithmetic  8.83 us (10%)
  between operations  1.23 us (1%)
    all_to_all x1, starting transfers between devices, summed_over(): mine = lax.all_to_all(flat, axis, 0, 0, tiled=True).sum(0, keepdims=True)  11.1 us
    ppermute x2, starting transfers between devices, extended_2(): before = lax.ppermute(last, axis, up)  7.58 us
    dot_general x9, matrix products, on_device(): jnp.einsum('ok,kdhw->odhw', front_one[along_depth, along_rows], window, p...  7.51 us
    all_to_all x1, waiting for transfers between devices, summed_over(): lax.all_to_all(jnp.broadcast_to(mine, flat.shape), axis, 0, 0, tiled=True)  7.09 us
    dot_general x9, matrix products, on_device(): jnp.einsum('odhw,kdhw->ok', grad_pre, window, preferred_element_type=jnp....  5.8 us
    unnamed x30, local copies, waits for them, and re-layouts  5.58 us
    another operation x4, local copies, waits for them, and re-layouts, on_device(): grad_one, grad_two = summed_over(jnp.stack(folded), 'slab')  3.84 us
    slice x2, local copies, waits for them, and re-layouts, column_stack(): pieces.append(field[..., first:first + stride * (count - 1) + 1:stride])  3.8 us
  transfers between devices with their start and end apart: 6, of which 2 were waited for; matrix products, arithmetic and copies ran while one was open for 19% of the time, Pallas kernels for 0%

profile of v8, /device:TPU:0, one launch (start us, length us, event | category | flops | bytes accessed | tf_op | source)
XLA Modules:
  0.0 92.1 jit_solution(5213681457001723378)
XLA Ops:
  0.7 0.9 copy.130
  1.6 2.4 %collective-permute-start.2 = (bf16[32,1,8,128]{3,0,2,1:T(8,128)(2,1)S(1)}, bf16[32,1,8,128]{3,0,2,1:T(8,128)(2,1)S(1)}, u32[]{:S(2)}, u32[]{:S(2)}) collective-permute-start(bf16[32,1,8,128]{3,0,2,1:T(8,128)(2,1)S(1)} %copy.130), channel_id=1, source_target_pairs={{0,1},{1,2},{2,3},{3,4},{4,5},{5,6},{6,7},{7,8},{8,9},{9,10},{10,1... | collective-permute-start | bytes 196616 | tf_op jit(solution)/shard_map/ppermute | solution.py:15
  4.0 1.3 %collective-permute-start.3 = (bf16[32,1,8,128]{3,0,2,1:T(8,128)(2,1)S(1)}, bf16[32,1,8,128]{3,0,2,1:T(8,128)(2,1)S(1)}, u32[]{:S(2)}, u32[]{:S(2)}) collective-permute-start(bf16[32,1,8,128]{3,0,2,1:T(8,128)(2,1)S(1)} %copy.130), channel_id=1, source_target_pairs={{1,0},{2,1},{3,2},{4,3},{5,4},{6,5},{7,6},{8,7},{9,8},{10,9},{11,1... | collective-permute-start | bytes 196616 | tf_op jit(solution)/shard_map/ppermute | solution.py:16
  5.3 1.3 %copy.123 = bf16[32,2,16,256]{3,0,2,1:T(8,128)(2,1)S(1)} copy(bf16[32,2,16,256]{3,2,1,0:T(8,128)(2,1)} %param.6) | data formatting | bytes 1048576 | tf_op args[0]
  6.6 5.2 %collective-permute-start = (bf16[32,2,16,256]{3,0,2,1:T(8,128)(2,1)S(1)}, bf16[32,2,16,256]{3,0,2,1:T(8,128)(2,1)S(1)}, u32[]{:S(2)}, u32[]{:S(2)}) collective-permute-start(bf16[32,2,16,256]{3,0,2,1:T(8,128)(2,1)S(1)} %copy.123), channel_id=1, source_target_pairs={{0,1},{1,2},{2,3},{3,4},{4,5},{5,6},{6,7},{7,8},{8,9},{9,10},{10,1... | collective-permute-start | bytes 1572872 | tf_op jit(solution)/shard_map/ppermute | solution.py:15
  11.8 1.3 %collective-permute-start.1 = (bf16[32,2,16,256]{3,0,2,1:T(8,128)(2,1)S(1)}, bf16[32,2,16,256]{3,0,2,1:T(8,128)(2,1)S(1)}, u32[]{:S(2)}, u32[]{:S(2)}) collective-permute-start(bf16[32,2,16,256]{3,0,2,1:T(8,128)(2,1)S(1)} %copy.123), channel_id=1, source_target_pairs={{1,0},{2,1},{3,2},{4,3},{5,4},{6,5},{7,6},{8,7},{9,8},{10,9},{11,1... | collective-permute-start | bytes 1572872 | tf_op jit(solution)/shard_map/ppermute | solution.py:16
  13.1 0.7 pad_clamp_fusion
  13.8 1.5 %gather_fusion = bf16[27,32,32]{2,1,0:T(8,128)(2,1)S(1)} fusion(bf16[27,32,32]{2,1,0:T(8,128)(2,1)} %param.8, s32[1024]{0:T(1024)S(1)} %pad_clamp_fusion), kind=kCustom, calls=%fused_computation | custom fusion | bytes 110700 | tf_op jit(solution)/shard_map/gather | solution.py:150
  15.7 0.8 copy.138
  16.6 0.8 reshape.205
  17.5 0.6 fusion.64
  18.8 0.4 convolution_bitcast_fusion
  19.2 0.4 convolution_bitcast_fusion.3
  20.1 0.6 convolution_bitcast_fusion.2
  21.1 1.7 %select_maximum_fusion = bf16[32,6,18,258]{3,0,2,1:T(8,128)(2,1)S(1)} fusion(bf16[32,2,16,256]{3,0,2,1:T(8,128)(2,1)S(1)} %collective-permute-done.1, bf16[32,2,16,256]{3,0,2,1:T(8,128)(2,1)S(1)} %copy.123, bf16[32,2,16,256]{3,0,2,1:T(8,128)(2,1)S(1)} %collective-permute-done), kind=kLoop, calls=%fused_computation.28 | loop fusion | flops 16941312 | bytes 3356160 | tf_op jit(solution)/shard_map/concatenate | solution.py:17
  22.8 1.4 %fusion.256 = (bf16[32,6,18,256]{3,0,2,1:T(8,128)(2,1)S(1)}, bf16[32,6,18,256]{3,0,2,1:T(8,128)(2,1)S(1)}, bf16[32,6,18,256]{3,0,2,1:T(8,128)(2,1)S(1)}) fusion(bf16[32,6,18,258]{3,0,2,1:T(8,128)(2,1)S(1)} %select_maximum_fusion), kind=kLoop, calls=%fused_computation.300 | loop fusion | bytes 10616832 | tf_op jit(solution)/shard_map/slice | solution.py:35
  24.2 0.4 pad_maximum_fusion
  24.6 0.6 fusion.11
  25.2 0.6 fusion.13
  25.8 0.6 fusion.15
  26.3 0.6 fusion.17
  26.9 0.6 fusion.19
  27.4 0.6 fusion.5
  28.0 0.6 fusion.7
  28.5 0.6 fusion.9
  29.1 3.1 %select_convert_fusion = (bf16[32,4,16,256]{3,0,2,1:T(8,128)(2,1)S(1)}, f32[32,4,16,256]{3,0,2,1:T(8,128)}, f32[32,4,16,256]{3,0,2,1:T(8,128)}) fusion(f32[32,4,16,256]{3,0,2,1:T(8,128)S(1)} %bitcast.524, pred[4]{0:T(512)(128)(4,1)S(1)} %compare_and_fusion, bf16[96,6,18,256]{3,0,2,1:T(8,128)(2,1)S(1)} %pad_maximum_fusion, ...), kind=kOutput, calls=%fused_computation.35 | convolution fusion | flops 110100480 | bytes 27271680 | tf_op jit(solution)/shard_map/ok,kdhw->odhw/dot_general | solution.py:98
  32.2 0.6 fusion.110
  32.8 2.4 %pad_slice_fusion.2 = (bf16[32,4,18,256]{3,0,2,1:T(8,128)(2,1)S(1)}, bf16[32,4,18,256]{3,0,2,1:T(8,128)(2,1)}, bf16[32,4,18,256]{3,0,2,1:T(8,128)(2,1)}) fusion(bf16[32,4,16,256]{3,0,2,1:T(8,128)(2,1)S(1)} %get-tuple-element.29), kind=kLoop, calls=%fused_computation.39 | loop fusion | bytes 4587520 | tf_op jit(solution)/shard_map/slice | solution.py:35
  35.2 0.6 copy-done.1
  35.8 0.5 fusion.63
  36.3 0.7 fusion.65
  38.9 0.6 fusion.116
  39.5 0.6 fusion.122
  40.2 0.6 fusion.128
  40.8 0.6 fusion.134
  41.5 0.6 fusion.140
  42.1 0.6 fusion.146
  42.8 0.6 fusion.152
  43.4 0.6 fusion.158
  44.1 0.9 fusion.176
  45.0 1.1 %copy.148 = f32[2,9,32,32]{2,3,1,0:T(8,128)S(1)} copy(f32[2,9,32,32]{3,2,1,0:T(8,128)} %get-tuple-element.60) | data formatting | bytes 147456 | tf_op jit(solution)/shard_map/slice.9
  46.1 0.9 copy.149
  47.1 1.2 %pad_maximum_fusion.5 = f32[2,9,96,32]{2,3,1,0:T(8,128)S(1)} fusion(f32[2,9,32,32]{2,3,1,0:T(8,128)S(1)} %copy.150, f32[2,9,32,32]{2,3,1,0:T(8,128)} %copy.149, f32[2,9,32,32]{2,3,1,0:T(8,128)S(1)} %copy.148), kind=kLoop, calls=%fused_computation.166 | loop fusion | flops 110592 | bytes 442368 | tf_op jit(solution)/shard_map/concatenate
  48.4 1.0 %slice.401 = f32[1,27,32,32]{2,1,3,0:T(8,128)} reshape(f32[1,9,96,32]{2,1,3,0:T(8,128)S(1)} %copy.151) | data formatting | bytes 221184 | tf_op jit(solution)/shard_map/slice | solution.py:70
  49.5 1.0 %slice.403 = f32[1,27,32,32]{2,1,3,0:T(8,128)} reshape(f32[1,9,96,32]{2,1,3,0:T(8,128)S(1)} %copy.152) | data formatting | bytes 221184 | tf_op jit(solution)/shard_map/slice | solution.py:70
  50.4 1.3 %pad_maximum_fusion.3 = f32[2,27,32,32]{2,1,3,0:T(8,128)S(1)} fusion(f32[1,27,32,32]{2,1,3,0:T(8,128)} %slice.403, f32[1,27,32,32]{2,1,3,0:T(8,128)} %slice.401), kind=kLoop, calls=%fused_computation.143 | loop fusion | flops 55296 | bytes 442368 | tf_op jit(solution)/shard_map/stack | solution.py:207
  51.7 1.4 %copy.153 = f32[2,27,32,32]{3,2,1,0:T(8,128)} copy(f32[2,27,32,32]{2,1,3,0:T(8,128)S(1)} %pad_maximum_fusion.3) | data formatting | bytes 442368 | tf_op jit(solution)/shard_map/stack | solution.py:207
  53.2 2.2 %all_to_all.13 = f32[16,1,3456]{2,1,0:T(1,128)} reshape(f32[2,27,32,32]{3,2,1,0:T(8,128)} %copy.153) | data formatting | bytes 442368 | tf_op jit(solution)/shard_map/all_to_all | solution.py:44
  55.4 11.1 %all-to-all-start = ((f32[16,1,3456]{2,1,0:T(1,128)}), f32[16,1,3456]{2,1,0:T(1,128)S(1)}, u32[]{:S(2)}, u32[]{:S(2)}) async-start(f32[16,1,3456]{2,1,0:T(1,128)} %all_to_all.13), calls=%async_computation | async-start | bytes 442368 | tf_op jit(solution)/shard_map/all_to_all | solution.py:44
  66.6 1.8 %pad_maximum_fusion.1 = bf16[96,4,18,256]{3,0,2,1:T(8,128)(2,1)S(1)} fusion(bf16[32,4,18,256]{3,0,2,1:T(8,128)(2,1)} %get-tuple-element.57, bf16[32,4,18,256]{3,0,2,1:T(8,128)(2,1)} %get-tuple-element.56, bf16[32,4,18,256]{3,0,2,1:T(8,128)(2,1)S(1)} %get-tuple-element.55), kind=kLoop, calls=%fused_computation.9 | loop fusion | flops 10616832 | bytes 7077888 | tf_op jit(solution)/shard_map/concatenate | solution.py:36
  68.7 0.4 fusion.66
  70.2 0.4 fusion.78
  70.9 0.4 fusion.84
  71.3 0.5 copy-done.6
  72.7 0.4 fusion.93
  73.1 2.8 %all-to-all-done = f32[16,1,3456]{2,1,0:T(1,128)S(1)} async-done(((f32[16,1,3456]{2,1,0:T(1,128)}), f32[16,1,3456]{2,1,0:T(1,128)S(1)}, u32[]{:S(2)}, u32[]{:S(2)}) %all-to-all-start) | async-done | bytes 221216 | tf_op jit(solution)/shard_map/all_to_all | solution.py:44
  76.0 0.8 broadcast_in_dim.35
  76.8 3.5 %all-to-all-start.1 = ((f32[16,1,3456]{2,1,0:T(1,128)}), f32[16,1,3456]{2,1,0:T(1,128)S(1)}, u32[]{:S(2)}, u32[]{:S(2)}) async-start(f32[16,1,3456]{2,1,0:T(1,128)} %broadcast_in_dim.35), calls=%async_computation.1 | async-start | bytes 442368 | tf_op jit(solution)/shard_map/all_to_all | solution.py:45
  80.5 1.1 %copy.156 = bf16[32,2,16,256]{3,2,1,0:T(8,128)(2,1)} copy(bf16[32,2,16,256]{3,0,2,1:T(8,128)(2,1)S(1)} %fusion.93) | data formatting | bytes 1048576
  81.9 0.7 copy.155
  82.6 7.1 %all-to-all-done.1 = f32[16,1,3456]{2,1,0:T(1,128)S(1)} async-done(((f32[16,1,3456]{2,1,0:T(1,128)}), f32[16,1,3456]{2,1,0:T(1,128)S(1)}, u32[]{:S(2)}, u32[]{:S(2)}) %all-to-all-start.1) | async-done | bytes 221216 | tf_op jit(solution)/shard_map/all_to_all | solution.py:45
  89.7 0.6 slice_reduce_fusion
  90.3 0.9 unstack.13
  91.2 0.9 unstack.15
  (75 shorter events, 7.5 us)
Async XLA Ops:
  0.6 15.9 %copy-start.4 = (bf16[27,32,32]{2,1,0:T(8,128)(2,1)S(1)}, bf16[27,32,32]{2,1,0:T(8,128)(2,1)}, u32[]{:S(2)}) copy-start(bf16[27,32,32]{2,1,0:T(8,128)(2,1)} %param.8) | copy-start | bytes 165892
  0.6 14.7 %copy-start.3 = (bf16[27,32,32]{2,1,0:T(8,128)(2,1)S(1)}, bf16[27,32,32]{2,1,0:T(8,128)(2,1)}, u32[]{:S(2)}) copy-start(bf16[27,32,32]{2,1,0:T(8,128)(2,1)} %param.7) | copy-start | bytes 165892
  1.6 15.9 %collective-permute-start.2 = (bf16[32,1,8,128]{3,0,2,1:T(8,128)(2,1)S(1)}, bf16[32,1,8,128]{3,0,2,1:T(8,128)(2,1)S(1)}, u32[]{:S(2)}, u32[]{:S(2)}) collective-permute-start(bf16[32,1,8,128]{3,0,2,1:T(8,128)(2,1)S(1)} %copy.130), channel_id=1, source_target_pairs={{0,1},{1,2},{2,3},{3,4},{4,5},{5,6},{6,7},{7,8},{8,9},{9,10},{10,1... | collective-permute-start | bytes 196616 | tf_op jit(solution)/shard_map/ppermute | solution.py:15
  4.0 13.5 %collective-permute-start.3 = (bf16[32,1,8,128]{3,0,2,1:T(8,128)(2,1)S(1)}, bf16[32,1,8,128]{3,0,2,1:T(8,128)(2,1)S(1)}, u32[]{:S(2)}, u32[]{:S(2)}) collective-permute-start(bf16[32,1,8,128]{3,0,2,1:T(8,128)(2,1)S(1)} %copy.130), channel_id=1, source_target_pairs={{1,0},{2,1},{3,2},{4,3},{5,4},{6,5},{7,6},{8,7},{9,8},{10,9},{11,1... | collective-permute-start | bytes 196616 | tf_op jit(solution)/shard_map/ppermute | solution.py:16
  6.6 14.5 %collective-permute-start = (bf16[32,2,16,256]{3,0,2,1:T(8,128)(2,1)S(1)}, bf16[32,2,16,256]{3,0,2,1:T(8,128)(2,1)S(1)}, u32[]{:S(2)}, u32[]{:S(2)}) collective-permute-start(bf16[32,2,16,256]{3,0,2,1:T(8,128)(2,1)S(1)} %copy.123), channel_id=1, source_target_pairs={{0,1},{1,2},{2,3},{3,4},{4,5},{5,6},{6,7},{7,8},{8,9},{9,10},{10,1... | collective-permute-start | bytes 1572872 | tf_op jit(solution)/shard_map/ppermute | solution.py:15
  11.8 9.3 %collective-permute-start.1 = (bf16[32,2,16,256]{3,0,2,1:T(8,128)(2,1)S(1)}, bf16[32,2,16,256]{3,0,2,1:T(8,128)(2,1)S(1)}, u32[]{:S(2)}, u32[]{:S(2)}) collective-permute-start(bf16[32,2,16,256]{3,0,2,1:T(8,128)(2,1)S(1)} %copy.123), channel_id=1, source_target_pairs={{1,0},{2,1},{3,2},{4,3},{5,4},{6,5},{7,6},{8,7},{9,8},{10,9},{11,1... | collective-permute-start | bytes 1572872 | tf_op jit(solution)/shard_map/ppermute | solution.py:16
  15.3 2.8 %copy-start.2 = (bf16[27,32,32]{2,1,0:T(8,128)(2,1)}, bf16[27,32,32]{2,1,0:T(8,128)(2,1)S(1)}, u32[]{:S(2)}) copy-start(bf16[27,32,32]{2,1,0:T(8,128)(2,1)S(1)} %gather_fusion) | copy-start | bytes 165892
  18.8 0.9 slice-start.1
  19.2 0.9 slice-start
  32.8 2.4 %copy-start = (f32[32,4,16,256]{3,0,2,1:T(8,128)S(1)}, f32[32,4,16,256]{3,0,2,1:T(8,128)}, u32[]{:S(2)}) copy-start(f32[32,4,16,256]{3,0,2,1:T(8,128)} %get-tuple-element.30) | copy-start | bytes 6291460
  32.8 3.0 %copy-start.1 = (f32[32,4,16,256]{3,0,2,1:T(8,128)S(1)}, f32[32,4,16,256]{3,0,2,1:T(8,128)}, u32[]{:S(2)}) copy-start(f32[32,4,16,256]{3,0,2,1:T(8,128)} %get-tuple-element.65) | copy-start | bytes 6291460
  36.3 0.9 %copy-start.7 = (bf16[32,1,8,128]{3,2,1,0:T(8,128)(2,1)S(1)}, bf16[32,1,8,128]{3,2,1,0:T(8,128)(2,1)}, u32[]{:S(2)}) copy-start(bf16[32,1,8,128]{3,2,1,0:T(8,128)(2,1)} %param.9) | copy-start | bytes 196612
  55.4 20.5 %all-to-all-start = ((f32[16,1,3456]{2,1,0:T(1,128)}), f32[16,1,3456]{2,1,0:T(1,128)S(1)}, u32[]{:S(2)}, u32[]{:S(2)}) async-start(f32[16,1,3456]{2,1,0:T(1,128)} %all_to_all.13), calls=%async_computation | async-start | bytes 442368 | tf_op jit(solution)/shard_map/all_to_all | solution.py:44
  66.5 1.8 %copy-start.5 = (bf16[3,3,96,32]{2,3,1,0:T(8,128)(2,1)S(1)}, bf16[3,3,96,32]{2,3,1,0:T(8,128)(2,1)}, u32[]{:S(2)}) copy-start(bf16[3,3,96,32]{2,3,1,0:T(8,128)(2,1)} %copy.138) | copy-start | bytes 165892
  70.9 0.9 copy-start.6
  76.8 12.9 %all-to-all-start.1 = ((f32[16,1,3456]{2,1,0:T(1,128)}), f32[16,1,3456]{2,1,0:T(1,128)S(1)}, u32[]{:S(2)}, u32[]{:S(2)}) async-start(f32[16,1,3456]{2,1,0:T(1,128)} %broadcast_in_dim.35), calls=%async_computation.1 | async-start | bytes 442368 | tf_op jit(solution)/shard_map/all_to_all | solution.py:45

commit v9 on v7

--- a/solution.py
+++ b/solution.py
@@ -113,25 +113,25 @@
     hidden_cols = hidden_cols.astype(jnp.bfloat16).reshape(
         3 * channels, planes + 1, height + 2, half_cols
     )
-    output = jnp.zeros((channels, half_planes, half_rows, half_cols), jnp.float32)
-    terms_two = []
-    for along_depth in range(3):
-        for along_rows in range(3):
-            window = hidden_cols[
+    windows = jnp.stack(
+        [
+            hidden_cols[
                 :,
                 along_depth : along_depth + planes - 1 : 2,
                 along_rows : along_rows + height - 1 : 2,
                 :,
             ]
-            output = output + jnp.einsum(
-                "ok,kdhw->odhw",
-                front_two[along_depth, along_rows],
-                window,
-                preferred_element_type=jnp.float32,
-            )
-            terms_two.append(
-                jnp.einsum("odhw,kdhw->ok", cotangent, window, preferred_element_type=jnp.float32)
-            )
+            for along_depth in range(3)
+            for along_rows in range(3)
+        ]
+    )
+    output = jnp.einsum(
+        "tok,tkdhw->odhw",
+        front_two.reshape(9, channels, 3 * channels),
+        windows,
+        preferred_element_type=jnp.float32,
+    )
+    terms_two = jnp.einsum("odhw,tkdhw->tok", cotangent, windows, preferred_element_type=jnp.float32)
     extended = jnp.pad(cot_ext, ((0, 0), (0, 0), (0, 1), (0, 0)))
     spread = jnp.arange(half_cols)[:, None, None] * 2 + jnp.arange(3)[None, :, None] - 1
     spread = (spread == jnp.arange(columns)[None, None, :]).astype(jnp.bfloat16)
@@ -203,7 +203,7 @@
                 back_window,
                 preferred_element_type=jnp.float32,
             )
-    summed = summed_over(jnp.stack([jnp.stack(terms_one), jnp.stack(terms_two)]), "slab")
+    summed = summed_over(jnp.stack([jnp.stack(terms_one), terms_two]), "slab")
     grad_one, grad_two = fold_terms(summed)
     return (output.astype(jnp.bfloat16), grad_volume.astype(jnp.bfloat16), grad_one, grad_two)
 

time: 83.5 us -> 87.2 us (1.044)
  local copies, waits for them, and re-layouts: 16.7 us -> 19.8 us
  other arithmetic: 5.96 us -> 8.22 us
  waiting for transfers between devices: 10.5 us -> 8.85 us
    dot_general x9, matrix products: 3.22 us -> 5.5 us  [on_device(): jnp.einsum('qk,kdhw->qdhw', rear_one[along_depth, along_rows], back_windo...]
    dot_general x18 -> x2, matrix products: 2.96 us -> 1.14 us  [the longest x1 0.7 us: on_device(): jnp.einsum('odhw,tkdhw->tok', cotangent, windows, preferred_element_type=...]
    all_to_all x1, waiting for transfers between devices: 7.1 us -> 5.41 us  [summed_over(): lax.all_to_all(jnp.broadcast_to(mine, flat.shape), axis, 0, 0, tiled=True)]
    unnamed x26 -> x42, local copies, waits for them, and re-layouts: 5.44 us -> 6.89 us
    all_to_all x1, starting transfers between devices: 12.4 us -> 11.2 us  [summed_over(): mine = lax.all_to_all(flat, axis, 0, 0, tiled=True).sum(0, keepdims=True)]
    all_to_all x1, other arithmetic: 0.52 us -> 1.46 us  [summed_over(): lax.all_to_all(jnp.broadcast_to(mine, flat.shape), axis, 0, 0, tiled=True)]
    reduce_sum x1, other arithmetic: 0.14 us -> 1.08 us  [summed_over(): mine = lax.all_to_all(flat, axis, 0, 0, tiled=True).sum(0, keepdims=True)]
  transfers between devices with their start and end apart: 6 -> 6, of which waited for: 2 -> 2; matrix products, arithmetic and copies ran while one was open for 19% -> 22% of each run, Pallas kernels for 0% -> 0%
where the time goes in v9:
time: 87.2 us; the launch traced here: 86.5 us
  starting transfers between devices  25.5 us (29%)
  matrix products  22.9 us (26%)
  local copies, waits for them, and re-layouts  19.8 us (23%)
  waiting for transfers between devices  8.85 us (10%)
  other arithmetic  8.22 us (9%)
  between operations  1.22 us (1%)
    all_to_all x1, starting transfers between devices, summed_over(): mine = lax.all_to_all(flat, axis, 0, 0, tiled=True).sum(0, keepdims=True)  11.2 us
    ppermute x2, starting transfers between devices, extended_2(): before = lax.ppermute(last, axis, up)  7.58 us
    dot_general x9, matrix products, on_device(): jnp.einsum('ok,kdhw->odhw', front_one[along_depth, along_rows], window, p...  7.53 us
    unnamed x42, local copies, waits for them, and re-layouts  6.89 us
    dot_general x9, matrix products, on_device(): jnp.einsum('odhw,kdhw->ok', grad_pre, window, preferred_element_type=jnp....  5.74 us
    dot_general x9, matrix products, on_device(): jnp.einsum('qk,kdhw->qdhw', rear_one[along_depth, along_rows], back_windo...  5.5 us
    all_to_all x1, waiting for transfers between devices, summed_over(): lax.all_to_all(jnp.broadcast_to(mine, flat.shape), axis, 0, 0, tiled=True)  5.41 us
    all_to_all x1, starting transfers between devices, summed_over(): lax.all_to_all(jnp.broadcast_to(mine, flat.shape), axis, 0, 0, tiled=True)  4.18 us
  transfers between devices with their start and end apart: 6, of which 2 were waited for; matrix products, arithmetic and copies ran while one was open for 22% of the time, Pallas kernels for 0%

profile of v9, /device:TPU:0, one launch (start us, length us, event | category | flops | bytes accessed | tf_op | source)
XLA Modules:
  0.0 86.5 jit_solution(9942910560274470681)
XLA Ops:
  0.7 0.9 %copy.83 = bf16[32,1,8,128]{3,0,2,1:T(8,128)(2,1)S(1)} copy(bf16[32,1,8,128]{3,2,1,0:T(8,128)(2,1)} %param.9) | data formatting | bytes 131072 | tf_op args[3]
  1.6 2.4 %collective-permute-start.2 = (bf16[32,1,8,128]{3,0,2,1:T(8,128)(2,1)S(1)}, bf16[32,1,8,128]{3,0,2,1:T(8,128)(2,1)S(1)}, u32[]{:S(2)}, u32[]{:S(2)}) collective-permute-start(bf16[32,1,8,128]{3,0,2,1:T(8,128)(2,1)S(1)} %copy.83), channel_id=1, source_target_pairs={{0,1},{1,2},{2,3},{3,4},{4,5},{5,6},{6,7},{7,8},{8,9},{9,10},{10,1... | collective-permute-start | bytes 196616 | tf_op jit(solution)/shard_map/ppermute | solution.py:15
  4.0 1.3 %collective-permute-start.3 = (bf16[32,1,8,128]{3,0,2,1:T(8,128)(2,1)S(1)}, bf16[32,1,8,128]{3,0,2,1:T(8,128)(2,1)S(1)}, u32[]{:S(2)}, u32[]{:S(2)}) collective-permute-start(bf16[32,1,8,128]{3,0,2,1:T(8,128)(2,1)S(1)} %copy.83), channel_id=1, source_target_pairs={{1,0},{2,1},{3,2},{4,3},{5,4},{6,5},{7,6},{8,7},{9,8},{10,9},{11,1... | collective-permute-start | bytes 196616 | tf_op jit(solution)/shard_map/ppermute | solution.py:16
  5.3 1.3 %copy.76 = bf16[32,2,16,256]{3,0,2,1:T(8,128)(2,1)S(1)} copy(bf16[32,2,16,256]{3,2,1,0:T(8,128)(2,1)} %param.6) | data formatting | bytes 1048576 | tf_op args[0]
  6.6 5.2 %collective-permute-start = (bf16[32,2,16,256]{3,0,2,1:T(8,128)(2,1)S(1)}, bf16[32,2,16,256]{3,0,2,1:T(8,128)(2,1)S(1)}, u32[]{:S(2)}, u32[]{:S(2)}) collective-permute-start(bf16[32,2,16,256]{3,0,2,1:T(8,128)(2,1)S(1)} %copy.76), channel_id=1, source_target_pairs={{0,1},{1,2},{2,3},{3,4},{4,5},{5,6},{6,7},{7,8},{8,9},{9,10},{10,1... | collective-permute-start | bytes 1572872 | tf_op jit(solution)/shard_map/ppermute | solution.py:15
  11.8 1.3 %collective-permute-start.1 = (bf16[32,2,16,256]{3,0,2,1:T(8,128)(2,1)S(1)}, bf16[32,2,16,256]{3,0,2,1:T(8,128)(2,1)S(1)}, u32[]{:S(2)}, u32[]{:S(2)}) collective-permute-start(bf16[32,2,16,256]{3,0,2,1:T(8,128)(2,1)S(1)} %copy.76), channel_id=1, source_target_pairs={{1,0},{2,1},{3,2},{4,3},{5,4},{6,5},{7,6},{8,7},{9,8},{10,9},{11,1... | collective-permute-start | bytes 1572872 | tf_op jit(solution)/shard_map/ppermute | solution.py:16
  13.1 0.7 pad_clamp_fusion
  13.8 1.5 %gather_fusion = bf16[27,32,32]{2,1,0:T(8,128)(2,1)S(1)} fusion(bf16[27,32,32]{2,1,0:T(8,128)(2,1)} %param.8, s32[1024]{0:T(1024)S(1)} %pad_clamp_fusion), kind=kCustom, calls=%fused_computation | custom fusion | bytes 110700 | tf_op jit(solution)/shard_map/gather | solution.py:150
  15.7 0.8 copy.91
  16.6 0.8 reshape.167
  17.5 0.6 fusion.68
  18.8 0.4 convolution_bitcast_fusion
  19.2 0.4 convolution_bitcast_fusion.3
  20.1 0.6 convolution_bitcast_fusion.2
  21.1 1.7 %select_maximum_fusion = bf16[32,6,18,258]{3,0,2,1:T(8,128)(2,1)S(1)} fusion(bf16[32,2,16,256]{3,0,2,1:T(8,128)(2,1)S(1)} %collective-permute-done.1, bf16[32,2,16,256]{3,0,2,1:T(8,128)(2,1)S(1)} %copy.76, bf16[32,2,16,256]{3,0,2,1:T(8,128)(2,1)S(1)} %collective-permute-done), kind=kLoop, calls=%fused_computation.28 | loop fusion | flops 16941312 | bytes 3356160 | tf_op jit(solution)/shard_map/concatenate | solution.py:17
  22.8 1.4 %fusion.214 = (bf16[32,6,18,256]{3,0,2,1:T(8,128)(2,1)S(1)}, bf16[32,6,18,256]{3,0,2,1:T(8,128)(2,1)S(1)}, bf16[32,6,18,256]{3,0,2,1:T(8,128)(2,1)S(1)}) fusion(bf16[32,6,18,258]{3,0,2,1:T(8,128)(2,1)S(1)} %select_maximum_fusion), kind=kLoop, calls=%fused_computation.225 | loop fusion | bytes 10616832 | tf_op jit(solution)/shard_map/slice | solution.py:35
  24.2 0.4 pad_maximum_fusion
  24.6 0.6 fusion.11
  25.2 0.6 fusion.13
  25.7 0.6 fusion.15
  26.3 0.6 fusion.17
  26.9 0.6 fusion.19
  27.4 0.6 fusion.5
  28.0 0.6 fusion.7
  28.5 0.6 fusion.9
  29.1 3.1 %select_convert_fusion = (bf16[32,4,16,256]{3,0,2,1:T(8,128)(2,1)S(1)}, f32[32,4,16,256]{3,0,2,1:T(8,128)}, f32[32,4,16,256]{3,0,2,1:T(8,128)}) fusion(f32[32,4,16,256]{3,0,2,1:T(8,128)S(1)} %bitcast.407, pred[4]{0:T(512)(128)(4,1)S(1)} %compare_and_fusion, bf16[96,6,18,256]{3,0,2,1:T(8,128)(2,1)S(1)} %pad_maximum_fusion, ...), kind=kOutput, calls=%fused_computation.35 | convolution fusion | flops 110100480 | bytes 27271680 | tf_op jit(solution)/shard_map/ok,kdhw->odhw/dot_general | solution.py:98
  32.2 0.6 fusion.115
  32.8 2.8 %pad_slice_fusion.2 = (bf16[32,4,18,256]{3,0,2,1:T(8,128)(2,1)}, bf16[32,4,18,256]{3,0,2,1:T(8,128)(2,1)}, bf16[32,4,18,256]{3,0,2,1:T(8,128)(2,1)}) fusion(bf16[32,4,16,256]{3,0,2,1:T(8,128)(2,1)S(1)} %get-tuple-element.23), kind=kLoop, calls=%fused_computation.39 | loop fusion | bytes 4587520 | tf_op jit(solution)/shard_map/slice | solution.py:35
  35.6 0.6 fusion.121
  36.2 0.6 fusion.127
  36.8 0.6 fusion.133
  37.5 0.6 fusion.139
  38.1 0.6 fusion.145
  38.8 0.6 fusion.151
  39.4 0.6 fusion.157
  40.1 0.6 fusion.163
  41.0 0.6 copy-done.3
  41.7 0.5 fusion.67
  42.2 0.7 fusion.69
  43.4 1.2 %copy-done = bf16[9,96,1,8,128]{4,1,0,3,2:T(8,128)(2,1)} copy-done((bf16[9,96,1,8,128]{4,1,0,3,2:T(8,128)(2,1)}, bf16[9,96,1,8,128]{4,1,0,3,2:T(8,128)(2,1)S(1)}, u32[]{:S(2)}) %copy-start) | copy-done | bytes 1769496
  44.6 0.7 fusion.100
  45.4 1.0 %all_to_all.13 = f32[16,1,3456]{2,1,0:T(1,128)} reshape(f32[2,9,32,96]{3,2,1,0:T(8,128)S(1)} %pad_maximum_fusion.3) | data formatting | bytes 442368 | tf_op jit(solution)/shard_map/all_to_all | solution.py:44
  46.4 11.2 %all-to-all-start = ((f32[16,1,3456]{2,1,0:T(1,128)}), f32[16,1,3456]{2,1,0:T(1,128)}, u32[]{:S(2)}, u32[]{:S(2)}) async-start(f32[16,1,3456]{2,1,0:T(1,128)} %all_to_all.13), calls=%async_computation | async-start | bytes 442368 | tf_op jit(solution)/shard_map/all_to_all | solution.py:44
  57.6 2.1 %pad_maximum_fusion.1 = bf16[96,4,18,256]{3,0,2,1:T(8,128)(2,1)S(1)} fusion(bf16[32,4,18,256]{3,0,2,1:T(8,128)(2,1)} %get-tuple-element.53, bf16[32,4,18,256]{3,0,2,1:T(8,128)(2,1)} %get-tuple-element.52, bf16[32,4,18,256]{3,0,2,1:T(8,128)(2,1)} %get-tuple-element.51), kind=kLoop, calls=%fused_computation.9 | loop fusion | flops 10616832 | bytes 7077888 | tf_op jit(solution)/shard_map/concatenate | solution.py:36
  60.1 0.4 fusion.70
  60.5 0.3 fusion.73
  60.8 0.3 fusion.76
  61.2 0.3 fusion.79
  61.5 0.4 fusion.82
  61.9 0.3 fusion.85
  62.2 1.3 %fusion.88 = f32[2,16,256,32]{2,3,1,0:T(8,128)} fusion(f32[2,16,256,32]{2,3,1,0:T(8,128)S(1)} %fusion.85, bf16[96,4,18,256]{3,0,2,1:T(8,128)(2,1)S(1)} %pad_maximum_fusion.1, bf16[3,3,32,96]{3,2,1,0:T(8,128)(2,1)S(1)} %bitcast.435), kind=kOutput, calls=%fused_computation.93 | convolution fusion | flops 50593792 | bytes 3678208 | tf_op jit(solution)/shard_map/qk,kdhw->qdhw/dot_general | solution.py:200
  63.6 3.4 %all-to-all-done = f32[16,1,3456]{2,1,0:T(1,128)} async-done(((f32[16,1,3456]{2,1,0:T(1,128)}), f32[16,1,3456]{2,1,0:T(1,128)}, u32[]{:S(2)}, u32[]{:S(2)}) %all-to-all-start) | async-done | bytes 221216 | tf_op jit(solution)/shard_map/all_to_all | solution.py:44
  67.0 1.1 %reduce_sum.9 = f32[3456]{0:T(1024)S(1)} reduce(f32[16,1,3456]{2,1,0:T(1,128)} %all-to-all-done, f32[]{:T(128)} %constant.8.clone.1), dimensions={0,1}, to_apply=%region_0.1 | reduce | flops 51840 | bytes 235012 | tf_op jit(solution)/shard_map/reduce_sum | solution.py:44
  68.1 0.8 broadcast_in_dim.35
  68.9 4.2 %all-to-all-start.1 = ((f32[16,1,3456]{2,1,0:T(1,128)}), f32[16,1,3456]{2,1,0:T(1,128)}, u32[]{:S(2)}, u32[]{:S(2)}) async-start(f32[16,1,3456]{2,1,0:T(1,128)} %broadcast_in_dim.35), calls=%async_computation.1 | async-start | bytes 442368 | tf_op jit(solution)/shard_map/all_to_all | solution.py:45
  73.1 1.7 %fusion.97 = bf16[32,2,16,256]{3,0,2,1:T(8,128)(2,1)S(1)} fusion(f32[2,16,256,32]{2,3,1,0:T(8,128)} %fusion.88, bf16[96,4,18,256]{3,0,2,1:T(8,128)(2,1)S(1)} %pad_maximum_fusion.1, bf16[3,3,32,96]{3,2,1,0:T(8,128)(2,1)} %bitcast.427), kind=kOutput, calls=%fused_computation.96 | convolution fusion | flops 50855936 | bytes 3153920 | tf_op jit(solution)/shard_map/qk,kdhw->qdhw/dot_general | solution.py:200
  74.8 1.1 %copy.97 = bf16[32,2,16,256]{3,2,1,0:T(8,128)(2,1)} copy(bf16[32,2,16,256]{3,0,2,1:T(8,128)(2,1)S(1)} %fusion.97) | data formatting | bytes 1048576
  75.9 0.4 fusion.109
  76.4 0.7 copy.96
  77.0 5.4 %all-to-all-done.1 = f32[16,1,3456]{2,1,0:T(1,128)} async-done(((f32[16,1,3456]{2,1,0:T(1,128)}), f32[16,1,3456]{2,1,0:T(1,128)}, u32[]{:S(2)}, u32[]{:S(2)}) %all-to-all-start.1) | async-done | bytes 221216 | tf_op jit(solution)/shard_map/all_to_all | solution.py:45
  82.4 1.5 %reduce.1 = f32[16,3456]{1,0:T(8,128)S(1)} reduce(f32[16,1,3456]{2,1,0:T(1,128)} %all-to-all-done.1, f32[]{:T(128)} %constant.47), dimensions={1}, to_apply=%all_to_all.12.reduce_sub_computation | reduce | bytes 442372 | tf_op jit(solution)/shard_map/all_to_all | solution.py:45
  83.9 0.7 reshape_reshape_reshape.3
  84.9 0.8 copy.94
  85.7 0.8 copy.95
  (63 shorter events, 3.5 us)
Async XLA Ops:
  0.6 15.9 %copy-start.6 = (bf16[27,32,32]{2,1,0:T(8,128)(2,1)S(1)}, bf16[27,32,32]{2,1,0:T(8,128)(2,1)}, u32[]{:S(2)}) copy-start(bf16[27,32,32]{2,1,0:T(8,128)(2,1)} %param.8) | copy-start | bytes 165892
  0.6 14.7 %copy-start.5 = (bf16[27,32,32]{2,1,0:T(8,128)(2,1)S(1)}, bf16[27,32,32]{2,1,0:T(8,128)(2,1)}, u32[]{:S(2)}) copy-start(bf16[27,32,32]{2,1,0:T(8,128)(2,1)} %param.7) | copy-start | bytes 165892
  1.6 15.9 %collective-permute-start.2 = (bf16[32,1,8,128]{3,0,2,1:T(8,128)(2,1)S(1)}, bf16[32,1,8,128]{3,0,2,1:T(8,128)(2,1)S(1)}, u32[]{:S(2)}, u32[]{:S(2)}) collective-permute-start(bf16[32,1,8,128]{3,0,2,1:T(8,128)(2,1)S(1)} %copy.83), channel_id=1, source_target_pairs={{0,1},{1,2},{2,3},{3,4},{4,5},{5,6},{6,7},{7,8},{8,9},{9,10},{10,1... | collective-permute-start | bytes 196616 | tf_op jit(solution)/shard_map/ppermute | solution.py:15
  4.0 13.5 %collective-permute-start.3 = (bf16[32,1,8,128]{3,0,2,1:T(8,128)(2,1)S(1)}, bf16[32,1,8,128]{3,0,2,1:T(8,128)(2,1)S(1)}, u32[]{:S(2)}, u32[]{:S(2)}) collective-permute-start(bf16[32,1,8,128]{3,0,2,1:T(8,128)(2,1)S(1)} %copy.83), channel_id=1, source_target_pairs={{1,0},{2,1},{3,2},{4,3},{5,4},{6,5},{7,6},{8,7},{9,8},{10,9},{11,1... | collective-permute-start | bytes 196616 | tf_op jit(solution)/shard_map/ppermute | solution.py:16
  6.6 14.5 %collective-permute-start = (bf16[32,2,16,256]{3,0,2,1:T(8,128)(2,1)S(1)}, bf16[32,2,16,256]{3,0,2,1:T(8,128)(2,1)S(1)}, u32[]{:S(2)}, u32[]{:S(2)}) collective-permute-start(bf16[32,2,16,256]{3,0,2,1:T(8,128)(2,1)S(1)} %copy.76), channel_id=1, source_target_pairs={{0,1},{1,2},{2,3},{3,4},{4,5},{5,6},{6,7},{7,8},{8,9},{9,10},{10,1... | collective-permute-start | bytes 1572872 | tf_op jit(solution)/shard_map/ppermute | solution.py:15
  11.8 9.3 %collective-permute-start.1 = (bf16[32,2,16,256]{3,0,2,1:T(8,128)(2,1)S(1)}, bf16[32,2,16,256]{3,0,2,1:T(8,128)(2,1)S(1)}, u32[]{:S(2)}, u32[]{:S(2)}) collective-permute-start(bf16[32,2,16,256]{3,0,2,1:T(8,128)(2,1)S(1)} %copy.76), channel_id=1, source_target_pairs={{1,0},{2,1},{3,2},{4,3},{5,4},{6,5},{7,6},{8,7},{9,8},{10,9},{11,1... | collective-permute-start | bytes 1572872 | tf_op jit(solution)/shard_map/ppermute | solution.py:16
  15.3 2.7 %copy-start.4 = (bf16[27,32,32]{2,1,0:T(8,128)(2,1)}, bf16[27,32,32]{2,1,0:T(8,128)(2,1)S(1)}, u32[]{:S(2)}) copy-start(bf16[27,32,32]{2,1,0:T(8,128)(2,1)S(1)} %gather_fusion) | copy-start | bytes 165892
  18.8 0.9 %slice-start.1 = ((bf16[27,32,32]{2,1,0:T(8,128)(2,1)}), bf16[3,32,32]{2,1,0:T(8,128)(2,1)S(1)}, s32[]{:S(2)}) async-start(bf16[27,32,32]{2,1,0:T(8,128)(2,1)} %copy-done.4), calls=%async_computation.3 | async-start | bytes 49152 | tf_op jit(solution)/shard_map/slice | solution.py:169
  19.2 0.9 %slice-start = ((bf16[27,32,32]{2,1,0:T(8,128)(2,1)}), bf16[12,32,32]{2,1,0:T(8,128)(2,1)S(1)}, s32[]{:S(2)}) async-start(bf16[27,32,32]{2,1,0:T(8,128)(2,1)} %copy-done.4), calls=%async_computation.2 | async-start | bytes 196608 | tf_op jit(solution)/shard_map/slice | solution.py:169
  39.4 1.6 %copy-start.2 = (f32[32,4,16,256]{3,0,2,1:T(8,128)S(1)}, f32[32,4,16,256]{3,0,2,1:T(8,128)}, u32[]{:S(2)}) copy-start(f32[32,4,16,256]{3,0,2,1:T(8,128)} %get-tuple-element.24) | copy-start | bytes 6291460
  39.4 2.3 %copy-start.3 = (f32[32,4,16,256]{3,0,2,1:T(8,128)S(1)}, f32[32,4,16,256]{3,0,2,1:T(8,128)}, u32[]{:S(2)}) copy-start(f32[32,4,16,256]{3,0,2,1:T(8,128)} %get-tuple-element.56) | copy-start | bytes 6291460
  43.1 1.6 %copy-start.9 = (bf16[32,1,8,128]{3,2,1,0:T(8,128)(2,1)S(1)}, bf16[32,1,8,128]{3,2,1,0:T(8,128)(2,1)}, u32[]{:S(2)}) copy-start(bf16[32,1,8,128]{3,2,1,0:T(8,128)(2,1)} %param.9) | copy-start | bytes 196612
  43.4 1.2 %copy-start = (bf16[9,96,1,8,128]{4,1,0,3,2:T(8,128)(2,1)}, bf16[9,96,1,8,128]{4,1,0,3,2:T(8,128)(2,1)S(1)}, u32[]{:S(2)}) copy-start(bf16[9,96,1,8,128]{4,1,0,3,2:T(8,128)(2,1)S(1)} %bitcast_dynamic-update-slice_fusion) | copy-start | bytes 5308420
  46.4 20.6 %all-to-all-start = ((f32[16,1,3456]{2,1,0:T(1,128)}), f32[16,1,3456]{2,1,0:T(1,128)}, u32[]{:S(2)}, u32[]{:S(2)}) async-start(f32[16,1,3456]{2,1,0:T(1,128)} %all_to_all.13), calls=%async_computation | async-start | bytes 442368 | tf_op jit(solution)/shard_map/all_to_all | solution.py:44
  57.6 2.2 %copy-start.7 = (bf16[3,3,96,32]{2,3,1,0:T(8,128)(2,1)S(1)}, bf16[3,3,96,32]{2,3,1,0:T(8,128)(2,1)}, u32[]{:S(2)}) copy-start(bf16[3,3,96,32]{2,3,1,0:T(8,128)(2,1)} %copy.91) | copy-start | bytes 165892
  68.9 13.6 %all-to-all-start.1 = ((f32[16,1,3456]{2,1,0:T(1,128)}), f32[16,1,3456]{2,1,0:T(1,128)}, u32[]{:S(2)}, u32[]{:S(2)}) async-start(f32[16,1,3456]{2,1,0:T(1,128)} %broadcast_in_dim.35), calls=%async_computation.1 | async-start | bytes 442368 | tf_op jit(solution)/shard_map/all_to_all | solution.py:45
  73.1 2.8 %copy-start.1 = (bf16[9,96,1,8,128]{4,1,0,3,2:T(8,128)(2,1)S(1)}, bf16[9,96,1,8,128]{4,1,0,3,2:T(8,128)(2,1)}, u32[]{:S(2)}) copy-start(bf16[9,96,1,8,128]{4,1,0,3,2:T(8,128)(2,1)} %copy-done) | copy-start | bytes 5308420
  73.1 2.8 %copy-start.8 = (bf16[9,32,96,1]{2,1,0,3:T(8,128)(2,1)S(1)}, bf16[9,32,96,1]{2,1,0,3:T(8,128)(2,1)}, u32[]{:S(2)}) copy-start(bf16[9,32,96,1]{2,1,0,3:T(8,128)(2,1)} %reshape.167) | copy-start | bytes 165892

commit v10 on v7

--- a/solution.py
+++ b/solution.py
@@ -18,12 +18,6 @@
     return shard
 
 
-def passed_along(block, axis, distance):
-    devices = range(lax.axis_size(axis))
-    route = [(i - distance, i) for i in devices if i - distance in devices]
-    return lax.ppermute(block, axis, route)
-
-
 def pad_sides(field):
     return jnp.pad(field, ((0, 0), (0, 0), (1, 1), (1, 1)))
 
@@ -58,11 +52,6 @@
     return weights.reshape(3, 3, 3 * size, size)
 
 
-def fold_term(term):
-    size = term.shape[0]
-    return term.reshape(size, 3, size).transpose(1, 0, 2)
-
-
 def fold_terms(summed):
     size = summed.shape[2]
     folded = summed.reshape(2, 9, size, 3, size).transpose(0, 1, 3, 2, 4)
@@ -70,12 +59,7 @@
     return folded[0], folded[1]
 
 
-def gather_terms(listed):
-    stacked = jnp.stack(listed)
-    return stacked.reshape(27, stacked.shape[2], stacked.shape[3])
-
-
-def on_device(volume, weight_one, weight_two, cotangent):
+def layer(volume, weight_one, weight_two, cotangent):
     channels, planes, height, columns = volume.shape
     half_planes = planes // 2
     half_rows = height // 2
@@ -221,6 +205,4 @@
         P("grp", None, None),
         P("grp", None, None),
     )
-    return jax.shard_map(
-        on_device, mesh=mesh, in_specs=in_specs, out_specs=out_specs, check_vma=False
-    )
+    return jax.shard_map(layer, mesh=mesh, in_specs=in_specs, out_specs=out_specs, check_vma=False)

time: 83.5 us -> 83.5 us (level)
  no operation moved by 1% of the time
where the time goes in v10:
time: 83.5 us; the launch traced here: 83 us
  starting transfers between devices  26.1 us (31%)
  matrix products  22.5 us (27%)
  local copies, waits for them, and re-layouts  16.7 us (20%)
  waiting for transfers between devices  10.5 us (13%)
  other arithmetic  5.96 us (7%)
  between operations  1.21 us (1%)
    all_to_all x1, starting transfers between devices, summed_over(): mine = lax.all_to_all(flat, axis, 0, 0, tiled=True).sum(0, keepdims=True)  12.4 us
    ppermute x2, starting transfers between devices, extended_2(): before = lax.ppermute(last, axis, up)  7.58 us
    dot_general x9, matrix products, layer(): jnp.einsum('ok,kdhw->odhw', front_one[along_depth, along_rows], window, p...  7.54 us
    all_to_all x1, waiting for transfers between devices, summed_over(): lax.all_to_all(jnp.broadcast_to(mine, flat.shape), axis, 0, 0, tiled=True)  7.1 us
    dot_general x9, matrix products, layer(): jnp.einsum('odhw,kdhw->ok', grad_pre, window, preferred_element_type=jnp....  5.75 us
    unnamed x26, local copies, waits for them, and re-layouts  5.44 us
    slice x2, local copies, waits for them, and re-layouts, column_stack(): pieces.append(field[..., first:first + stride * (count - 1) + 1:stride])  3.83 us
    all_to_all x1, starting transfers between devices, summed_over(): lax.all_to_all(jnp.broadcast_to(mine, flat.shape), axis, 0, 0, tiled=True)  3.53 us
  transfers between devices with their start and end apart: 6, of which 2 were waited for; matrix products, arithmetic and copies ran while one was open for 19% of the time, Pallas kernels for 0%

profile of v10, /device:TPU:0, one launch (start us, length us, event | category | flops | bytes accessed | tf_op | source)
XLA Modules:
  0.0 83.0 jit_solution(5328839461036063229)
XLA Ops:
  0.7 0.9 %copy.97 = bf16[32,1,8,128]{3,0,2,1:T(8,128)(2,1)S(1)} copy(bf16[32,1,8,128]{3,2,1,0:T(8,128)(2,1)} %param.9) | data formatting | bytes 131072 | tf_op args[3]
  1.6 2.4 %collective-permute-start.2 = (bf16[32,1,8,128]{3,0,2,1:T(8,128)(2,1)S(1)}, bf16[32,1,8,128]{3,0,2,1:T(8,128)(2,1)S(1)}, u32[]{:S(2)}, u32[]{:S(2)}) collective-permute-start(bf16[32,1,8,128]{3,0,2,1:T(8,128)(2,1)S(1)} %copy.97), channel_id=1, source_target_pairs={{0,1},{1,2},{2,3},{3,4},{4,5},{5,6},{6,7},{7,8},{8,9},{9,10},{10,1... | collective-permute-start | bytes 196616 | tf_op jit(solution)/shard_map/ppermute | solution.py:15
  4.0 1.3 %collective-permute-start.3 = (bf16[32,1,8,128]{3,0,2,1:T(8,128)(2,1)S(1)}, bf16[32,1,8,128]{3,0,2,1:T(8,128)(2,1)S(1)}, u32[]{:S(2)}, u32[]{:S(2)}) collective-permute-start(bf16[32,1,8,128]{3,0,2,1:T(8,128)(2,1)S(1)} %copy.97), channel_id=1, source_target_pairs={{1,0},{2,1},{3,2},{4,3},{5,4},{6,5},{7,6},{8,7},{9,8},{10,9},{11,1... | collective-permute-start | bytes 196616 | tf_op jit(solution)/shard_map/ppermute | solution.py:16
  5.3 1.3 %copy.90 = bf16[32,2,16,256]{3,0,2,1:T(8,128)(2,1)S(1)} copy(bf16[32,2,16,256]{3,2,1,0:T(8,128)(2,1)} %param.6) | data formatting | bytes 1048576 | tf_op args[0]
  6.6 5.2 %collective-permute-start = (bf16[32,2,16,256]{3,0,2,1:T(8,128)(2,1)S(1)}, bf16[32,2,16,256]{3,0,2,1:T(8,128)(2,1)S(1)}, u32[]{:S(2)}, u32[]{:S(2)}) collective-permute-start(bf16[32,2,16,256]{3,0,2,1:T(8,128)(2,1)S(1)} %copy.90), channel_id=1, source_target_pairs={{0,1},{1,2},{2,3},{3,4},{4,5},{5,6},{6,7},{7,8},{8,9},{9,10},{10,1... | collective-permute-start | bytes 1572872 | tf_op jit(solution)/shard_map/ppermute | solution.py:15
  11.8 1.3 %collective-permute-start.1 = (bf16[32,2,16,256]{3,0,2,1:T(8,128)(2,1)S(1)}, bf16[32,2,16,256]{3,0,2,1:T(8,128)(2,1)S(1)}, u32[]{:S(2)}, u32[]{:S(2)}) collective-permute-start(bf16[32,2,16,256]{3,0,2,1:T(8,128)(2,1)S(1)} %copy.90), channel_id=1, source_target_pairs={{1,0},{2,1},{3,2},{4,3},{5,4},{6,5},{7,6},{8,7},{9,8},{10,9},{11,1... | collective-permute-start | bytes 1572872 | tf_op jit(solution)/shard_map/ppermute | solution.py:16
  13.1 0.7 pad_clamp_fusion
  13.8 1.5 %gather_fusion = bf16[27,32,32]{2,1,0:T(8,128)(2,1)S(1)} fusion(bf16[27,32,32]{2,1,0:T(8,128)(2,1)} %param.8, s32[1024]{0:T(1024)S(1)} %pad_clamp_fusion), kind=kCustom, calls=%fused_computation | custom fusion | bytes 110700 | tf_op jit(solution)/shard_map/gather | solution.py:134
  16.2 0.6 fusion.64
  17.5 0.4 convolution_bitcast_fusion
  18.0 0.4 convolution_bitcast_fusion.3
  18.4 0.3 convolution_bitcast_fusion.1
  18.9 0.6 convolution_bitcast_fusion.2
  19.5 0.2 pad_maximum_fusion.2
  19.9 1.7 %select_maximum_fusion = bf16[32,6,18,258]{3,0,2,1:T(8,128)(2,1)S(1)} fusion(bf16[32,2,16,256]{3,0,2,1:T(8,128)(2,1)S(1)} %collective-permute-done.1, bf16[32,2,16,256]{3,0,2,1:T(8,128)(2,1)S(1)} %copy.90, bf16[32,2,16,256]{3,0,2,1:T(8,128)(2,1)S(1)} %collective-permute-done), kind=kLoop, calls=%fused_computation.28 | loop fusion | flops 16941312 | bytes 3356160 | tf_op jit(solution)/shard_map/concatenate | solution.py:17
  21.6 1.4 %fusion.254 = (bf16[32,6,18,256]{3,0,2,1:T(8,128)(2,1)S(1)}, bf16[32,6,18,256]{3,0,2,1:T(8,128)(2,1)S(1)}, bf16[32,6,18,256]{3,0,2,1:T(8,128)(2,1)S(1)}) fusion(bf16[32,6,18,258]{3,0,2,1:T(8,128)(2,1)S(1)} %select_maximum_fusion), kind=kLoop, calls=%fused_computation.290 | loop fusion | bytes 10616832 | tf_op jit(solution)/shard_map/slice | solution.py:29
  23.0 0.4 pad_maximum_fusion
  23.4 0.6 fusion.11
  24.0 0.6 fusion.13
  24.5 0.6 fusion.15
  25.1 0.6 fusion.17
  25.6 0.6 fusion.19
  26.2 0.6 fusion.5
  26.7 0.6 fusion.7
  27.3 0.6 fusion.9
  27.9 3.1 %select_convert_fusion = (bf16[32,4,16,256]{3,0,2,1:T(8,128)(2,1)S(1)}, f32[32,4,16,256]{3,0,2,1:T(8,128)}, f32[32,4,16,256]{3,0,2,1:T(8,128)}) fusion(f32[32,4,16,256]{3,0,2,1:T(8,128)S(1)} %bitcast.523, pred[4]{0:T(512)(128)(4,1)S(1)} %compare_and_fusion, bf16[96,6,18,256]{3,0,2,1:T(8,128)(2,1)S(1)} %pad_maximum_fusion, ...), kind=kOutput, calls=%fused_computation.35 | convolution fusion | flops 110100480 | bytes 27271680 | tf_op jit(solution)/shard_map/ok,kdhw->odhw/dot_general | solution.py:82
  31.0 0.6 fusion.110
  31.6 2.4 %pad_slice_fusion.2 = (bf16[32,4,18,256]{3,0,2,1:T(8,128)(2,1)S(1)}, bf16[32,4,18,256]{3,0,2,1:T(8,128)(2,1)}, bf16[32,4,18,256]{3,0,2,1:T(8,128)(2,1)}) fusion(bf16[32,4,16,256]{3,0,2,1:T(8,128)(2,1)S(1)} %get-tuple-element.23), kind=kLoop, calls=%fused_computation.39 | loop fusion | bytes 4587520 | tf_op jit(solution)/shard_map/slice | solution.py:29
  34.0 0.6 fusion.116
  34.6 0.6 fusion.122
  35.3 0.6 fusion.128
  35.9 0.6 fusion.134
  36.6 0.6 fusion.140
  37.2 0.6 fusion.146
  37.9 0.6 fusion.152
  38.5 0.6 fusion.158
  39.2 0.3 copy-done
  39.5 0.6 copy-done.1
  40.1 0.5 fusion.63
  40.7 0.7 fusion.65
  41.3 0.2 copy.94
  43.2 1.0 %all_to_all.13 = f32[16,1,3456]{2,1,0:T(1,128)} reshape(f32[2,9,32,96]{3,2,1,0:T(8,128)S(1)} %pad_maximum_fusion.3) | data formatting | bytes 442368 | tf_op jit(solution)/shard_map/all_to_all | solution.py:38
  44.2 12.4 %all-to-all-start = ((f32[16,1,3456]{2,1,0:T(1,128)}), f32[16,1,3456]{2,1,0:T(1,128)S(1)}, u32[]{:S(2)}, u32[]{:S(2)}) async-start(f32[16,1,3456]{2,1,0:T(1,128)} %all_to_all.13), calls=%async_computation | async-start | bytes 442368 | tf_op jit(solution)/shard_map/all_to_all | solution.py:38
  56.6 1.8 %pad_maximum_fusion.1 = bf16[96,4,18,256]{3,0,2,1:T(8,128)(2,1)S(1)} fusion(bf16[32,4,18,256]{3,0,2,1:T(8,128)(2,1)} %get-tuple-element.53, bf16[32,4,18,256]{3,0,2,1:T(8,128)(2,1)} %get-tuple-element.52, bf16[32,4,18,256]{3,0,2,1:T(8,128)(2,1)S(1)} %get-tuple-element.51), kind=kLoop, calls=%fused_computation.9 | loop fusion | flops 10616832 | bytes 7077888 | tf_op jit(solution)/shard_map/concatenate | solution.py:30
  58.4 0.3 fusion.58
  58.8 0.4 fusion.66
  59.1 0.4 fusion.69
  59.5 0.4 fusion.72
  59.8 0.4 fusion.75
  60.2 0.4 fusion.78
  60.6 0.4 fusion.81
  60.9 0.4 fusion.84
  62.2 0.4 fusion.93
  62.6 3.4 %all-to-all-done = f32[16,1,3456]{2,1,0:T(1,128)S(1)} async-done(((f32[16,1,3456]{2,1,0:T(1,128)}), f32[16,1,3456]{2,1,0:T(1,128)S(1)}, u32[]{:S(2)}, u32[]{:S(2)}) %all-to-all-start) | async-done | bytes 221216 | tf_op jit(solution)/shard_map/all_to_all | solution.py:38
  66.1 0.8 broadcast_in_dim.35
  66.9 3.5 %all-to-all-start.1 = ((f32[16,1,3456]{2,1,0:T(1,128)}), f32[16,1,3456]{2,1,0:T(1,128)S(1)}, u32[]{:S(2)}, u32[]{:S(2)}) async-start(f32[16,1,3456]{2,1,0:T(1,128)} %broadcast_in_dim.35), calls=%async_computation.1 | async-start | bytes 442368 | tf_op jit(solution)/shard_map/all_to_all | solution.py:39
  70.6 1.1 %copy.119 = bf16[32,2,16,256]{3,2,1,0:T(8,128)(2,1)} copy(bf16[32,2,16,256]{3,0,2,1:T(8,128)(2,1)S(1)} %fusion.93) | data formatting | bytes 1048576
  72.0 0.7 copy.118
  72.7 7.1 %all-to-all-done.1 = f32[16,1,3456]{2,1,0:T(1,128)S(1)} async-done(((f32[16,1,3456]{2,1,0:T(1,128)}), f32[16,1,3456]{2,1,0:T(1,128)S(1)}, u32[]{:S(2)}, u32[]{:S(2)}) %all-to-all-start.1) | async-done | bytes 221216 | tf_op jit(solution)/shard_map/all_to_all | solution.py:39
  79.8 0.5 reduce.1
  80.3 0.7 reshape_reshape_reshape.3
  81.0 0.3 fusion.255
  81.3 0.8 copy.116
  82.1 0.8 copy.117
  (62 shorter events, 4.9 us)
Async XLA Ops:
  0.6 15.2 %copy-start.4 = (bf16[27,32,32]{2,1,0:T(8,128)(2,1)S(1)}, bf16[27,32,32]{2,1,0:T(8,128)(2,1)}, u32[]{:S(2)}) copy-start(bf16[27,32,32]{2,1,0:T(8,128)(2,1)} %param.8) | copy-start | bytes 165892
  0.6 14.7 %copy-start.3 = (bf16[27,32,32]{2,1,0:T(8,128)(2,1)S(1)}, bf16[27,32,32]{2,1,0:T(8,128)(2,1)}, u32[]{:S(2)}) copy-start(bf16[27,32,32]{2,1,0:T(8,128)(2,1)} %param.7) | copy-start | bytes 165892
  1.6 14.6 %collective-permute-start.2 = (bf16[32,1,8,128]{3,0,2,1:T(8,128)(2,1)S(1)}, bf16[32,1,8,128]{3,0,2,1:T(8,128)(2,1)S(1)}, u32[]{:S(2)}, u32[]{:S(2)}) collective-permute-start(bf16[32,1,8,128]{3,0,2,1:T(8,128)(2,1)S(1)} %copy.97), channel_id=1, source_target_pairs={{0,1},{1,2},{2,3},{3,4},{4,5},{5,6},{6,7},{7,8},{8,9},{9,10},{10,1... | collective-permute-start | bytes 196616 | tf_op jit(solution)/shard_map/ppermute | solution.py:15
  4.0 12.2 %collective-permute-start.3 = (bf16[32,1,8,128]{3,0,2,1:T(8,128)(2,1)S(1)}, bf16[32,1,8,128]{3,0,2,1:T(8,128)(2,1)S(1)}, u32[]{:S(2)}, u32[]{:S(2)}) collective-permute-start(bf16[32,1,8,128]{3,0,2,1:T(8,128)(2,1)S(1)} %copy.97), channel_id=1, source_target_pairs={{1,0},{2,1},{3,2},{4,3},{5,4},{6,5},{7,6},{8,7},{9,8},{10,9},{11,1... | collective-permute-start | bytes 196616 | tf_op jit(solution)/shard_map/ppermute | solution.py:16
  6.6 13.3 %collective-permute-start = (bf16[32,2,16,256]{3,0,2,1:T(8,128)(2,1)S(1)}, bf16[32,2,16,256]{3,0,2,1:T(8,128)(2,1)S(1)}, u32[]{:S(2)}, u32[]{:S(2)}) collective-permute-start(bf16[32,2,16,256]{3,0,2,1:T(8,128)(2,1)S(1)} %copy.90), channel_id=1, source_target_pairs={{0,1},{1,2},{2,3},{3,4},{4,5},{5,6},{6,7},{7,8},{8,9},{9,10},{10,1... | collective-permute-start | bytes 1572872 | tf_op jit(solution)/shard_map/ppermute | solution.py:15
  11.8 8.1 %collective-permute-start.1 = (bf16[32,2,16,256]{3,0,2,1:T(8,128)(2,1)S(1)}, bf16[32,2,16,256]{3,0,2,1:T(8,128)(2,1)S(1)}, u32[]{:S(2)}, u32[]{:S(2)}) collective-permute-start(bf16[32,2,16,256]{3,0,2,1:T(8,128)(2,1)S(1)} %copy.90), channel_id=1, source_target_pairs={{1,0},{2,1},{3,2},{4,3},{5,4},{6,5},{7,6},{8,7},{9,8},{10,9},{11,1... | collective-permute-start | bytes 1572872 | tf_op jit(solution)/shard_map/ppermute | solution.py:16
  15.3 1.5 %copy-start.2 = (bf16[27,32,32]{2,1,0:T(8,128)(2,1)}, bf16[27,32,32]{2,1,0:T(8,128)(2,1)S(1)}, u32[]{:S(2)}) copy-start(bf16[27,32,32]{2,1,0:T(8,128)(2,1)S(1)} %gather_fusion) | copy-start | bytes 165892
  17.5 0.9 %slice-start.1 = ((bf16[27,32,32]{2,1,0:T(8,128)(2,1)}), bf16[3,32,32]{2,1,0:T(8,128)(2,1)S(1)}, s32[]{:S(2)}) async-start(bf16[27,32,32]{2,1,0:T(8,128)(2,1)} %copy-done.2), calls=%async_computation.3 | async-start | bytes 49152 | tf_op jit(solution)/shard_map/slice | solution.py:153
  18.0 0.9 %slice-start = ((bf16[27,32,32]{2,1,0:T(8,128)(2,1)}), bf16[12,32,32]{2,1,0:T(8,128)(2,1)S(1)}, s32[]{:S(2)}) async-start(bf16[27,32,32]{2,1,0:T(8,128)(2,1)} %copy-done.2), calls=%async_computation.2 | async-start | bytes 196608 | tf_op jit(solution)/shard_map/slice | solution.py:153
  37.9 1.6 %copy-start = (f32[32,4,16,256]{3,0,2,1:T(8,128)S(1)}, f32[32,4,16,256]{3,0,2,1:T(8,128)}, u32[]{:S(2)}) copy-start(f32[32,4,16,256]{3,0,2,1:T(8,128)} %get-tuple-element.24) | copy-start | bytes 6291460
  37.9 2.3 %copy-start.1 = (f32[32,4,16,256]{3,0,2,1:T(8,128)S(1)}, f32[32,4,16,256]{3,0,2,1:T(8,128)}, u32[]{:S(2)}) copy-start(f32[32,4,16,256]{3,0,2,1:T(8,128)} %get-tuple-element.56) | copy-start | bytes 6291460
  40.6 0.9 %copy-start.5 = (bf16[32,1,8,128]{3,2,1,0:T(8,128)(2,1)S(1)}, bf16[32,1,8,128]{3,2,1,0:T(8,128)(2,1)}, u32[]{:S(2)}) copy-start(bf16[32,1,8,128]{3,2,1,0:T(8,128)(2,1)} %param.9) | copy-start | bytes 196612
  44.2 21.7 %all-to-all-start = ((f32[16,1,3456]{2,1,0:T(1,128)}), f32[16,1,3456]{2,1,0:T(1,128)S(1)}, u32[]{:S(2)}, u32[]{:S(2)}) async-start(f32[16,1,3456]{2,1,0:T(1,128)} %all_to_all.13), calls=%async_computation | async-start | bytes 442368 | tf_op jit(solution)/shard_map/all_to_all | solution.py:38
  66.9 12.9 %all-to-all-start.1 = ((f32[16,1,3456]{2,1,0:T(1,128)}), f32[16,1,3456]{2,1,0:T(1,128)S(1)}, u32[]{:S(2)}, u32[]{:S(2)}) async-start(f32[16,1,3456]{2,1,0:T(1,128)} %broadcast_in_dim.35), calls=%async_computation.1 | async-start | bytes 442368 | tf_op jit(solution)/shard_map/all_to_all | solution.py:39

commit v11 on v10

--- a/solution.py
+++ b/solution.py
@@ -5,17 +5,36 @@
 from jax.sharding import PartitionSpec as P
 
 
-def extended_2(shard, sides, width):
-    for axis, dim in sides:
-        devices, length = (lax.axis_size(axis), shard.shape[dim])
-        up = [(i, (i + 1) % devices) for i in range(devices - 1)]
-        down = [(j, i) for i, j in up]
-        last = lax.slice_in_dim(shard, length - width, length, axis=dim)
-        initial = lax.slice_in_dim(shard, 0, width, axis=dim)
-        before = lax.ppermute(last, axis, up)
-        after = lax.ppermute(initial, axis, down)
-        shard = jnp.concatenate([before, shard, after], axis=dim)
-    return shard
+def passed_along(block, axis, distance):
+    devices = range(lax.axis_size(axis))
+    route = [(i - distance, i) for i in devices if i - distance in devices]
+    return lax.ppermute(block, axis, route)
+
+
+def borders(volume, cotangent, axis):
+    channels, planes = volume.shape[:2]
+    half_planes = cotangent.shape[1]
+    vol_shape = (channels, 2) + volume.shape[2:]
+    cot_shape = (channels, 1) + cotangent.shape[2:]
+    vol_size = vol_shape[1] * vol_shape[2] * vol_shape[3]
+    upward = jnp.concatenate(
+        [
+            volume[:, planes - 2 :].reshape(channels, -1),
+            cotangent[:, half_planes - 1 :].reshape(channels, -1),
+        ],
+        1,
+    )
+    downward = jnp.concatenate(
+        [volume[:, :2].reshape(channels, -1), cotangent[:, :1].reshape(channels, -1)], 1
+    )
+    below = passed_along(upward, axis, 1)
+    above = passed_along(downward, axis, -1)
+    return (
+        below[:, :vol_size].reshape(vol_shape),
+        above[:, :vol_size].reshape(vol_shape),
+        below[:, vol_size:].reshape(cot_shape),
+        above[:, vol_size:].reshape(cot_shape),
+    )
 
 
 def pad_sides(field):
@@ -67,9 +86,10 @@
     front_one = forward_kernel(weight_one)
     front_two = forward_kernel(weight_two)
     rear_one = backward_kernel(weight_one).transpose(0, 1, 3, 2)
-    padded = pad_sides(extended_2(volume, (("slab", 1),), 2))
+    vol_below, vol_above, cot_below, cot_above = borders(volume, cotangent, "slab")
+    padded = pad_sides(jnp.concatenate([vol_below, volume, vol_above], 1))
     volume_cols = column_stack(padded, 1, columns, lambda along_cols: along_cols)
-    cot_ext = extended_2(cotangent, (("slab", 1),), 1)
+    cot_ext = jnp.concatenate([cot_below, cotangent, cot_above], 1)
     devices = lax.axis_size("slab")
     place = lax.axis_index("slab") * planes + jnp.arange(-1, planes + 1)
     inside = ((place >= 0) & (place < devices * planes))[None, :, None, None]
@@ -163,18 +183,20 @@
     grad_rim = grad_hidden * (sigma * (1.0 + preact * (1.0 - sigma)))
     grad_rim = jnp.where(inside, grad_rim, 0.0).astype(jnp.bfloat16)
     grad_pre = grad_rim[:, 1 : planes + 1]
+    terms_one = []
+    for along_depth in range(3):
+        for along_rows in range(3):
+            window = volume_cols[
+                :, along_depth + 1 : along_depth + 1 + planes, along_rows : along_rows + height, :
+            ]
+            terms_one.append(
+                jnp.einsum("odhw,kdhw->ok", grad_pre, window, preferred_element_type=jnp.float32)
+            )
     rimmed = pad_sides(grad_rim)
     rimmed_cols = column_stack(rimmed, 1, columns, lambda along_cols: 2 - along_cols)
     grad_volume = jnp.zeros((channels, planes, height, columns), jnp.float32)
-    terms_one = []
-    for along_depth in range(3):
-        for along_rows in range(3):
-            window = volume_cols[
-                :, along_depth + 1 : along_depth + 1 + planes, along_rows : along_rows + height, :
-            ]
-            terms_one.append(
-                jnp.einsum("odhw,kdhw->ok", grad_pre, window, preferred_element_type=jnp.float32)
-            )
+    for along_depth in range(3):
+        for along_rows in range(3):
             back_window = rimmed_cols[
                 :,
                 2 - along_depth : 2 - along_depth + planes,
@@ -187,9 +209,10 @@
                 back_window,
                 preferred_element_type=jnp.float32,
             )
+    grad_volume = grad_volume.astype(jnp.bfloat16)
     summed = summed_over(jnp.stack([jnp.stack(terms_one), jnp.stack(terms_two)]), "slab")
     grad_one, grad_two = fold_terms(summed)
-    return (output.astype(jnp.bfloat16), grad_volume.astype(jnp.bfloat16), grad_one, grad_two)
+    return (output.astype(jnp.bfloat16), grad_volume, grad_one, grad_two)
 
 
 def solution(mesh):

time: 83.5 us -> 86.5 us (1.036)
  local copies, waits for them, and re-layouts: 16.7 us -> 20.4 us
  starting transfers between devices: 26.1 us -> 23.1 us
  waiting for transfers between devices: 10.5 us -> 13.4 us
    ppermute x4 -> x2, starting transfers between devices: 10.2 us -> 3.71 us  [passed_along(): return lax.ppermute(block, axis, route)]
    all_to_all x1, starting transfers between devices: 12.4 us -> 15.9 us  [summed_over(): mine = lax.all_to_all(flat, axis, 0, 0, tiled=True).sum(0, keepdims=True)]
    ppermute x4 -> x2, waiting for transfers between devices: 0.01 us -> 2.97 us  [passed_along(): return lax.ppermute(block, axis, route)]
    unnamed x26 -> x44, local copies, waits for them, and re-layouts: 5.44 us -> 7.63 us
    gather x1, local copies, waits for them, and re-layouts: 1.52 us -> 0.59 us  [layer(): ordered_two = weight_two[np.array(order)]]
  transfers between devices with their start and end apart: 6 -> 4, of which waited for: 2 -> 3; matrix products, arithmetic and copies ran while one was open for 19% -> 11% of each run, Pallas kernels for 0% -> 0%
where the time goes in v11:
time: 86.5 us; the launch traced here: 86.1 us
  starting transfers between devices  23.1 us (27%)
  matrix products  22.5 us (26%)
  local copies, waits for them, and re-layouts  20.4 us (24%)
  waiting for transfers between devices  13.4 us (15%)
  other arithmetic  5.26 us (6%)
  between operations  1.32 us (2%)
    all_to_all x1, starting transfers between devices, summed_over(): mine = lax.all_to_all(flat, axis, 0, 0, tiled=True).sum(0, keepdims=True)  15.9 us
    unnamed x44, local copies, waits for them, and re-layouts  7.63 us
    dot_general x9, matrix products, layer(): jnp.einsum('ok,kdhw->odhw', front_one[along_depth, along_rows], window, p...  7.57 us
    all_to_all x1, waiting for transfers between devices, summed_over(): lax.all_to_all(jnp.broadcast_to(mine, flat.shape), axis, 0, 0, tiled=True)  7.1 us
    dot_general x9, matrix products, layer(): jnp.einsum('odhw,kdhw->ok', grad_pre, window, preferred_element_type=jnp....  5.75 us
    slice x2, local copies, waits for them, and re-layouts, column_stack(): pieces.append(field[..., first:first + stride * (count - 1) + 1:stride])  3.81 us
    ppermute x2, starting transfers between devices, passed_along(): return lax.ppermute(block, axis, route)  3.71 us
    all_to_all x1, starting transfers between devices, summed_over(): lax.all_to_all(jnp.broadcast_to(mine, flat.shape), axis, 0, 0, tiled=True)  3.53 us
  transfers between devices with their start and end apart: 4, of which 3 were waited for; matrix products, arithmetic and copies ran while one was open for 11% of the time, Pallas kernels for 0%

profile of v11, /device:TPU:0, one launch (start us, length us, event | category | flops | bytes accessed | tf_op | source)
XLA Modules:
  0.0 86.1 jit_solution(12417663479280660272)
XLA Ops:
  0.7 1.4 %copy.163 = bf16[4,8,32,256]{3,1,2,0:T(8,128)(2,1)S(1)} copy(bf16[4,8,32,256]{3,2,1,0:T(8,128)(2,1)} %bitcast.566) | data formatting | bytes 1048576
  2.1 0.9 constant_dynamic-update-slice_fusion.1
  3.0 0.6 constant_dynamic-update-slice_fusion
  3.6 2.4 %collective-permute-start = (bf16[32,9216]{1,0:T(8,128)(2,1)}, bf16[32,9216]{1,0:T(8,128)(2,1)S(1)}, u32[]{:S(2)}, u32[]{:S(2)}) collective-permute-start(bf16[32,9216]{1,0:T(8,128)(2,1)} %constant_dynamic-update-slice_fusion), channel_id=1, source_target_pairs={{0,1},{1,2},{2,3},{3,4},{4,5},{5,6},{6,7},{7,8},{8,9},{9,10},{10,1... | collective-permute-start | bytes 1769480 | tf_op jit(solution)/shard_map/ppermute | solution.py:11
  6.0 1.3 %collective-permute-start.1 = (bf16[32,9216]{1,0:T(8,128)(2,1)}, bf16[32,9216]{1,0:T(8,128)(2,1)S(1)}, u32[]{:S(2)}, u32[]{:S(2)}) collective-permute-start(bf16[32,9216]{1,0:T(8,128)(2,1)} %constant_dynamic-update-slice_fusion), channel_id=1, source_target_pairs={{1,0},{2,1},{3,2},{4,3},{5,4},{6,5},{7,6},{8,7},{9,8},{10,9},{11,1... | collective-permute-start | bytes 1769480 | tf_op jit(solution)/shard_map/ppermute | solution.py:11
  7.4 0.6 gather_fusion
  9.3 3.0 %collective-permute-done.1 = bf16[32,9216]{1,0:T(8,128)(2,1)S(1)} collective-permute-done((bf16[32,9216]{1,0:T(8,128)(2,1)}, bf16[32,9216]{1,0:T(8,128)(2,1)S(1)}, u32[]{:S(2)}, u32[]{:S(2)}) %collective-permute-start.1) | collective-permute-done | bytes 589856 | tf_op jit(solution)/shard_map/ppermute | solution.py:11
  12.3 0.6 fusion.64
  12.9 0.7 fusion.179
  13.6 0.8 slice_bitcast_fusion.8
  14.5 0.3 copy.86
  15.3 1.7 %select_maximum_fusion = bf16[32,6,18,258]{3,0,2,1:T(8,128)(2,1)S(1)} fusion(bf16[32,2,16,256]{3,0,2,1:T(8,128)(2,1)S(1)} %copy.88, bf16[32,2,16,256]{3,0,2,1:T(8,128)(2,1)S(1)} %copy.87, bf16[32,2,16,256]{3,0,2,1:T(8,128)(2,1)S(1)} %copy.86), kind=kLoop, calls=%fused_computation.28 | loop fusion | flops 16941312 | bytes 3356160 | tf_op jit(solution)/shard_map/concatenate | solution.py:90
  17.0 1.4 %fusion.254 = (bf16[32,6,18,256]{3,0,2,1:T(8,128)(2,1)S(1)}, bf16[32,6,18,256]{3,0,2,1:T(8,128)(2,1)S(1)}, bf16[32,6,18,256]{3,0,2,1:T(8,128)(2,1)S(1)}) fusion(bf16[32,6,18,258]{3,0,2,1:T(8,128)(2,1)S(1)} %select_maximum_fusion), kind=kLoop, calls=%fused_computation.294 | loop fusion | bytes 10616832 | tf_op jit(solution)/shard_map/slice | solution.py:48
  18.4 0.4 pad_maximum_fusion
  18.8 0.6 fusion.11
  19.4 0.6 fusion.13
  19.9 0.6 fusion.15
  20.5 0.6 fusion.17
  21.0 0.6 fusion.3
  21.6 0.6 fusion.5
  22.1 0.6 fusion.7
  22.7 0.6 fusion.9
  23.3 0.8 copy-done.2
  24.6 0.6 slice-done
  25.2 0.6 convolution_bitcast_fusion.2
  25.9 0.4 convolution_bitcast_fusion
  26.3 0.4 convolution_bitcast_fusion.3
  27.5 3.1 %select_convert_fusion = (bf16[32,4,16,256]{3,0,2,1:T(8,128)(2,1)S(1)}, f32[32,4,16,256]{3,0,2,1:T(8,128)}, f32[32,4,16,256]{3,0,2,1:T(8,128)}) fusion(f32[32,4,16,256]{3,0,2,1:T(8,128)S(1)} %bitcast.546, pred[4]{0:T(512)(128)(4,1)S(1)} %compare_and_fusion, f32[4,16,256,32]{2,3,1,0:T(8,128)S(1)} %fusion.3, f32[4,16,256,32]{2,3,1,0:T(8,128)S(1)} %fusion.5, ...), kind=kOutput, calls=%fused_computation.35 | convolution fusion | flops 110100480 | bytes 27271680 | tf_op jit(solution)/shard_map/ok,kdhw->odhw/dot_general | solution.py:102
  30.6 0.6 fusion.110
  31.2 2.4 %pad_slice_fusion.2 = (bf16[32,4,18,256]{3,0,2,1:T(8,128)(2,1)S(1)}, bf16[32,4,18,256]{3,0,2,1:T(8,128)(2,1)}, bf16[32,4,18,256]{3,0,2,1:T(8,128)(2,1)}) fusion(bf16[32,4,16,256]{3,0,2,1:T(8,128)(2,1)S(1)} %get-tuple-element.23), kind=kLoop, calls=%fused_computation.39 | loop fusion | bytes 4587520 | tf_op jit(solution)/shard_map/slice | solution.py:48
  33.6 0.6 fusion.116
  34.3 0.6 fusion.122
  34.9 0.6 fusion.128
  35.6 0.6 fusion.134
  36.2 0.6 fusion.140
  36.9 0.6 fusion.146
  37.5 0.6 fusion.152
  38.2 0.6 fusion.158
  38.8 0.3 copy-done
  39.1 0.6 copy-done.1
  39.8 0.5 fusion.63
  40.3 0.7 fusion.65
  42.9 1.0 %all_to_all.13 = f32[16,1,3456]{2,1,0:T(1,128)} reshape(f32[2,9,32,96]{3,2,1,0:T(8,128)S(1)} %pad_maximum_fusion.3) | data formatting | bytes 442368 | tf_op jit(solution)/shard_map/all_to_all | solution.py:57
  43.9 15.9 %all-to-all-start = ((f32[16,1,3456]{2,1,0:T(1,128)}), f32[16,1,3456]{2,1,0:T(1,128)S(1)}, u32[]{:S(2)}, u32[]{:S(2)}) async-start(f32[16,1,3456]{2,1,0:T(1,128)} %all_to_all.13), calls=%async_computation | async-start | bytes 442368 | tf_op jit(solution)/shard_map/all_to_all | solution.py:57
  59.8 1.8 %pad_maximum_fusion.1 = bf16[96,4,18,256]{3,0,2,1:T(8,128)(2,1)S(1)} fusion(bf16[32,4,18,256]{3,0,2,1:T(8,128)(2,1)} %get-tuple-element.53, bf16[32,4,18,256]{3,0,2,1:T(8,128)(2,1)} %get-tuple-element.52, bf16[32,4,18,256]{3,0,2,1:T(8,128)(2,1)S(1)} %get-tuple-element.51), kind=kLoop, calls=%fused_computation.9 | loop fusion | flops 10616832 | bytes 7077888 | tf_op jit(solution)/shard_map/concatenate | solution.py:49
  61.5 0.3 fusion.58
  61.9 0.4 fusion.66
  62.2 0.4 fusion.69
  62.6 0.4 fusion.72
  63.0 0.4 fusion.75
  63.3 0.4 fusion.78
  63.7 0.4 fusion.81
  64.1 0.4 fusion.84
  65.4 0.4 fusion.93
  65.7 3.4 %all-to-all-done = f32[16,1,3456]{2,1,0:T(1,128)S(1)} async-done(((f32[16,1,3456]{2,1,0:T(1,128)}), f32[16,1,3456]{2,1,0:T(1,128)S(1)}, u32[]{:S(2)}, u32[]{:S(2)}) %all-to-all-start) | async-done | bytes 221216 | tf_op jit(solution)/shard_map/all_to_all | solution.py:57
  69.3 0.8 broadcast_in_dim.35
  70.1 3.5 %all-to-all-start.1 = ((f32[16,1,3456]{2,1,0:T(1,128)}), f32[16,1,3456]{2,1,0:T(1,128)S(1)}, u32[]{:S(2)}, u32[]{:S(2)}) async-start(f32[16,1,3456]{2,1,0:T(1,128)} %broadcast_in_dim.35), calls=%async_computation.1 | async-start | bytes 442368 | tf_op jit(solution)/shard_map/all_to_all | solution.py:58
  73.7 1.1 %copy.115 = bf16[32,2,16,256]{3,2,1,0:T(8,128)(2,1)} copy(bf16[32,2,16,256]{3,0,2,1:T(8,128)(2,1)S(1)} %fusion.93) | data formatting | bytes 1048576
  75.2 0.7 copy.114
  75.8 7.1 %all-to-all-done.1 = f32[16,1,3456]{2,1,0:T(1,128)S(1)} async-done(((f32[16,1,3456]{2,1,0:T(1,128)}), f32[16,1,3456]{2,1,0:T(1,128)S(1)}, u32[]{:S(2)}, u32[]{:S(2)}) %all-to-all-start.1) | async-done | bytes 221216 | tf_op jit(solution)/shard_map/all_to_all | solution.py:58
  82.9 0.5 reduce.1
  83.4 0.7 reshape_reshape_reshape.3
  84.5 0.8 copy.112
  85.3 0.8 copy.113
  (83 shorter events, 6.6 us)
Async XLA Ops:
  0.6 6.7 %copy-start.10 = (s32[27]{0:T(128)S(1)}, s32[27]{0:T(128)}, u32[]{:S(2)}) copy-start(s32[27]{0:T(128)} %constant.46) | copy-start | bytes 328
  0.6 7.4 %copy-start.3 = (bf16[32,2,16,256]{3,2,1,0:T(8,128)(2,1)S(1)}, bf16[32,2,16,256]{3,2,1,0:T(8,128)(2,1)}, u32[]{:S(2)}) copy-start(bf16[32,2,16,256]{3,2,1,0:T(8,128)(2,1)} %param.6) | copy-start | bytes 1572868
  0.7 2.3 %copy-start.7 = (bf16[32,1,8,128]{3,2,1,0:T(8,128)(2,1)S(1)}, bf16[32,1,8,128]{3,2,1,0:T(8,128)(2,1)}, u32[]{:S(2)}) copy-start(bf16[32,1,8,128]{3,2,1,0:T(8,128)(2,1)} %param.9) | copy-start | bytes 196612
  0.7 6.8 %copy-start.6 = (bf16[27,32,32]{2,1,0:T(8,128)(2,1)S(1)}, bf16[27,32,32]{2,1,0:T(8,128)(2,1)}, u32[]{:S(2)}) copy-start(bf16[27,32,32]{2,1,0:T(8,128)(2,1)} %param.8) | copy-start | bytes 165892
  0.7 7.7 %copy-start.5 = (bf16[27,32,32]{2,1,0:T(8,128)(2,1)S(1)}, bf16[27,32,32]{2,1,0:T(8,128)(2,1)}, u32[]{:S(2)}) copy-start(bf16[27,32,32]{2,1,0:T(8,128)(2,1)} %param.7) | copy-start | bytes 165892
  3.6 5.6 %collective-permute-start = (bf16[32,9216]{1,0:T(8,128)(2,1)}, bf16[32,9216]{1,0:T(8,128)(2,1)S(1)}, u32[]{:S(2)}, u32[]{:S(2)}) collective-permute-start(bf16[32,9216]{1,0:T(8,128)(2,1)} %constant_dynamic-update-slice_fusion), channel_id=1, source_target_pairs={{0,1},{1,2},{2,3},{3,4},{4,5},{5,6},{6,7},{7,8},{8,9},{9,10},{10,1... | collective-permute-start | bytes 1769480 | tf_op jit(solution)/shard_map/ppermute | solution.py:11
  6.0 6.2 %collective-permute-start.1 = (bf16[32,9216]{1,0:T(8,128)(2,1)}, bf16[32,9216]{1,0:T(8,128)(2,1)S(1)}, u32[]{:S(2)}, u32[]{:S(2)}) collective-permute-start(bf16[32,9216]{1,0:T(8,128)(2,1)} %constant_dynamic-update-slice_fusion), channel_id=1, source_target_pairs={{1,0},{2,1},{3,2},{4,3},{5,4},{6,5},{7,6},{8,7},{9,8},{10,9},{11,1... | collective-permute-start | bytes 1769480 | tf_op jit(solution)/shard_map/ppermute | solution.py:11
  8.0 4.2 %copy-start.4 = (bf16[27,32,32]{2,1,0:T(8,128)(2,1)}, bf16[27,32,32]{2,1,0:T(8,128)(2,1)S(1)}, u32[]{:S(2)}) copy-start(bf16[27,32,32]{2,1,0:T(8,128)(2,1)S(1)} %gather_fusion) | copy-start | bytes 165892
  22.7 1.4 %copy-start.2 = (bf16[192,2,8,256]{3,0,2,1:T(8,128)(2,1)S(1)}, bf16[192,2,8,256]{3,0,2,1:T(8,128)(2,1)}, u32[]{:S(2)}) copy-start(bf16[192,2,8,256]{3,0,2,1:T(8,128)(2,1)} %get-tuple-element.38) | copy-start | bytes 4718596
  24.4 0.9 %slice-start = ((bf16[27,32,32]{2,1,0:T(8,128)(2,1)}), bf16[12,32,32]{2,1,0:T(8,128)(2,1)S(1)}, s32[]{:S(2)}) async-start(bf16[27,32,32]{2,1,0:T(8,128)(2,1)} %copy-done.4), calls=%async_computation.2 | async-start | bytes 196608 | tf_op jit(solution)/shard_map/slice | solution.py:173
  25.9 0.9 %slice-start.1 = ((bf16[27,32,32]{2,1,0:T(8,128)(2,1)}), bf16[3,32,32]{2,1,0:T(8,128)(2,1)S(1)}, s32[]{:S(2)}) async-start(bf16[27,32,32]{2,1,0:T(8,128)(2,1)} %copy-done.4), calls=%async_computation.3 | async-start | bytes 49152 | tf_op jit(solution)/shard_map/slice | solution.py:173
  25.9 1.0 %copy-start.9 = (bf16[32,2,8,256]{3,0,2,1:T(8,128)(2,1)S(1)}, bf16[32,2,8,256]{3,0,2,1:T(8,128)(2,1)}, u32[]{:S(2)}) copy-start(bf16[32,2,8,256]{3,0,2,1:T(8,128)(2,1)} %get-tuple-element.48) | copy-start | bytes 786436
  37.5 1.6 %copy-start = (f32[32,4,16,256]{3,0,2,1:T(8,128)S(1)}, f32[32,4,16,256]{3,0,2,1:T(8,128)}, u32[]{:S(2)}) copy-start(f32[32,4,16,256]{3,0,2,1:T(8,128)} %get-tuple-element.24) | copy-start | bytes 6291460
  37.5 2.3 %copy-start.1 = (f32[32,4,16,256]{3,0,2,1:T(8,128)S(1)}, f32[32,4,16,256]{3,0,2,1:T(8,128)}, u32[]{:S(2)}) copy-start(f32[32,4,16,256]{3,0,2,1:T(8,128)} %get-tuple-element.56) | copy-start | bytes 6291460
  40.3 0.9 %copy-start.8 = (bf16[32,1,8,128]{3,2,1,0:T(8,128)(2,1)S(1)}, bf16[32,1,8,128]{3,2,1,0:T(8,128)(2,1)}, u32[]{:S(2)}) copy-start(bf16[32,1,8,128]{3,2,1,0:T(8,128)(2,1)} %param.9) | copy-start | bytes 196612
  43.9 25.2 %all-to-all-start = ((f32[16,1,3456]{2,1,0:T(1,128)}), f32[16,1,3456]{2,1,0:T(1,128)S(1)}, u32[]{:S(2)}, u32[]{:S(2)}) async-start(f32[16,1,3456]{2,1,0:T(1,128)} %all_to_all.13), calls=%async_computation | async-start | bytes 442368 | tf_op jit(solution)/shard_map/all_to_all | solution.py:57
  70.1 12.9 %all-to-all-start.1 = ((f32[16,1,3456]{2,1,0:T(1,128)}), f32[16,1,3456]{2,1,0:T(1,128)S(1)}, u32[]{:S(2)}, u32[]{:S(2)}) async-start(f32[16,1,3456]{2,1,0:T(1,128)} %broadcast_in_dim.35), calls=%async_computation.1 | async-start | bytes 442368 | tf_op jit(solution)/shard_map/all_to_all | solution.py:58

commit v12 on v10

--- a/solution.py
+++ b/solution.py
@@ -163,18 +163,21 @@
     grad_rim = grad_hidden * (sigma * (1.0 + preact * (1.0 - sigma)))
     grad_rim = jnp.where(inside, grad_rim, 0.0).astype(jnp.bfloat16)
     grad_pre = grad_rim[:, 1 : planes + 1]
+    volume_minor = volume_cols[:, 1 : planes + 3].transpose(1, 2, 3, 0)
+    terms_one = []
+    for along_depth in range(3):
+        for along_rows in range(3):
+            window = volume_minor[
+                along_depth : along_depth + planes, along_rows : along_rows + height
+            ]
+            terms_one.append(
+                jnp.einsum("odhw,dhwk->ok", grad_pre, window, preferred_element_type=jnp.float32)
+            )
     rimmed = pad_sides(grad_rim)
     rimmed_cols = column_stack(rimmed, 1, columns, lambda along_cols: 2 - along_cols)
     grad_volume = jnp.zeros((channels, planes, height, columns), jnp.float32)
-    terms_one = []
-    for along_depth in range(3):
-        for along_rows in range(3):
-            window = volume_cols[
-                :, along_depth + 1 : along_depth + 1 + planes, along_rows : along_rows + height, :
-            ]
-            terms_one.append(
-                jnp.einsum("odhw,kdhw->ok", grad_pre, window, preferred_element_type=jnp.float32)
-            )
+    for along_depth in range(3):
+        for along_rows in range(3):
             back_window = rimmed_cols[
                 :,
                 2 - along_depth : 2 - along_depth + planes,
@@ -187,9 +190,10 @@
                 back_window,
                 preferred_element_type=jnp.float32,
             )
+    grad_volume = grad_volume.astype(jnp.bfloat16)
     summed = summed_over(jnp.stack([jnp.stack(terms_one), jnp.stack(terms_two)]), "slab")
     grad_one, grad_two = fold_terms(summed)
-    return (output.astype(jnp.bfloat16), grad_volume.astype(jnp.bfloat16), grad_one, grad_two)
+    return (output.astype(jnp.bfloat16), grad_volume, grad_one, grad_two)
 
 
 def solution(mesh):

time: 83.5 us -> 86.6 us (1.037)
  matrix products: 22.5 us -> 25.4 us
  local copies, waits for them, and re-layouts: 16.7 us -> 18.2 us
  starting transfers between devices: 26.1 us -> 24.8 us
    dot_general x9, matrix products: 7.54 us -> 10.4 us  [layer(): jnp.einsum('ok,kdhw->odhw', front_one[along_depth, along_rows], window, p...]
    reshape x1, local copies, waits for them, and re-layouts: 0.14 us -> 1.47 us  [layer(): jnp.stack(classes).reshape(2, 2, channels, class_planes, half_rows, columns)]
    all_to_all x1, starting transfers between devices: 12.4 us -> 11.1 us  [summed_over(): mine = lax.all_to_all(flat, axis, 0, 0, tiled=True).sum(0, keepdims=True)]
  transfers between devices with their start and end apart: 6 -> 6, of which waited for: 2 -> 2; matrix products, arithmetic and copies ran while one was open for 19% -> 20% of each run, Pallas kernels for 0% -> 0%
where the time goes in v12:
time: 86.6 us; the launch traced here: 86 us
  matrix products  25.4 us (29%)
  starting transfers between devices  24.8 us (29%)
  local copies, waits for them, and re-layouts  18.2 us (21%)
  waiting for transfers between devices  10.5 us (12%)
  other arithmetic  5.94 us (7%)
  between operations  1.19 us (1%)
    all_to_all x1, starting transfers between devices, summed_over(): mine = lax.all_to_all(flat, axis, 0, 0, tiled=True).sum(0, keepdims=True)  11.1 us
    dot_general x9, matrix products, layer(): jnp.einsum('ok,kdhw->odhw', front_one[along_depth, along_rows], window, p...  10.4 us
    ppermute x2, starting transfers between devices, extended_2(): before = lax.ppermute(last, axis, up)  7.58 us
    all_to_all x1, waiting for transfers between devices, summed_over(): lax.all_to_all(jnp.broadcast_to(mine, flat.shape), axis, 0, 0, tiled=True)  7.09 us
    dot_general x9, matrix products, layer(): jnp.einsum('odhw,dhwk->ok', grad_pre, window, preferred_element_type=jnp....  5.77 us
    unnamed x26, local copies, waits for them, and re-layouts  5.44 us
    slice x2, local copies, waits for them, and re-layouts, column_stack(): pieces.append(field[..., first:first + stride * (count - 1) + 1:stride])  3.75 us
    all_to_all x1, starting transfers between devices, summed_over(): lax.all_to_all(jnp.broadcast_to(mine, flat.shape), axis, 0, 0, tiled=True)  3.53 us
  transfers between devices with their start and end apart: 6, of which 2 were waited for; matrix products, arithmetic and copies ran while one was open for 20% of the time, Pallas kernels for 0%

profile of v12, /device:TPU:0, one launch (start us, length us, event | category | flops | bytes accessed | tf_op | source)
XLA Modules:
  0.0 86.0 jit_solution(2115867472784119749)
XLA Ops:
  0.7 0.9 %copy.97 = bf16[32,1,8,128]{3,0,2,1:T(8,128)(2,1)S(1)} copy(bf16[32,1,8,128]{3,2,1,0:T(8,128)(2,1)} %param.9) | data formatting | bytes 131072 | tf_op args[3]
  1.6 2.4 %collective-permute-start.2 = (bf16[32,1,8,128]{3,0,2,1:T(8,128)(2,1)S(1)}, bf16[32,1,8,128]{3,0,2,1:T(8,128)(2,1)S(1)}, u32[]{:S(2)}, u32[]{:S(2)}) collective-permute-start(bf16[32,1,8,128]{3,0,2,1:T(8,128)(2,1)S(1)} %copy.97), channel_id=1, source_target_pairs={{0,1},{1,2},{2,3},{3,4},{4,5},{5,6},{6,7},{7,8},{8,9},{9,10},{10,1... | collective-permute-start | bytes 196616 | tf_op jit(solution)/shard_map/ppermute | solution.py:15
  4.0 1.3 %collective-permute-start.3 = (bf16[32,1,8,128]{3,0,2,1:T(8,128)(2,1)S(1)}, bf16[32,1,8,128]{3,0,2,1:T(8,128)(2,1)S(1)}, u32[]{:S(2)}, u32[]{:S(2)}) collective-permute-start(bf16[32,1,8,128]{3,0,2,1:T(8,128)(2,1)S(1)} %copy.97), channel_id=1, source_target_pairs={{1,0},{2,1},{3,2},{4,3},{5,4},{6,5},{7,6},{8,7},{9,8},{10,9},{11,1... | collective-permute-start | bytes 196616 | tf_op jit(solution)/shard_map/ppermute | solution.py:16
  5.3 1.3 %copy.90 = bf16[32,2,16,256]{3,0,2,1:T(8,128)(2,1)S(1)} copy(bf16[32,2,16,256]{3,2,1,0:T(8,128)(2,1)} %param.6) | data formatting | bytes 1048576 | tf_op args[0]
  6.6 5.2 %collective-permute-start = (bf16[32,2,16,256]{3,0,2,1:T(8,128)(2,1)S(1)}, bf16[32,2,16,256]{3,0,2,1:T(8,128)(2,1)S(1)}, u32[]{:S(2)}, u32[]{:S(2)}) collective-permute-start(bf16[32,2,16,256]{3,0,2,1:T(8,128)(2,1)S(1)} %copy.90), channel_id=1, source_target_pairs={{0,1},{1,2},{2,3},{3,4},{4,5},{5,6},{6,7},{7,8},{8,9},{9,10},{10,1... | collective-permute-start | bytes 1572872 | tf_op jit(solution)/shard_map/ppermute | solution.py:15
  11.8 1.3 %collective-permute-start.1 = (bf16[32,2,16,256]{3,0,2,1:T(8,128)(2,1)S(1)}, bf16[32,2,16,256]{3,0,2,1:T(8,128)(2,1)S(1)}, u32[]{:S(2)}, u32[]{:S(2)}) collective-permute-start(bf16[32,2,16,256]{3,0,2,1:T(8,128)(2,1)S(1)} %copy.90), channel_id=1, source_target_pairs={{1,0},{2,1},{3,2},{4,3},{5,4},{6,5},{7,6},{8,7},{9,8},{10,9},{11,1... | collective-permute-start | bytes 1572872 | tf_op jit(solution)/shard_map/ppermute | solution.py:16
  13.1 0.7 pad_clamp_fusion
  13.8 1.5 %gather_fusion = bf16[27,32,32]{2,1,0:T(8,128)(2,1)S(1)} fusion(bf16[27,32,32]{2,1,0:T(8,128)(2,1)} %param.8, s32[1024]{0:T(1024)S(1)} %pad_clamp_fusion), kind=kCustom, calls=%fused_computation | custom fusion | bytes 110700 | tf_op jit(solution)/shard_map/gather | solution.py:134
  16.2 0.6 fusion.64
  17.5 0.4 convolution_bitcast_fusion
  18.0 0.4 convolution_bitcast_fusion.3
  18.4 0.3 convolution_bitcast_fusion.1
  18.9 0.6 convolution_bitcast_fusion.2
  19.7 1.5 %copy.103 = f32[2,2,32,2,8,256]{5,2,1,4,0,3:T(8,128)} copy(f32[2,2,32,2,8,256]{5,2,4,3,1,0:T(8,128)S(1)} %bitcast.524) | data formatting | bytes 4194304 | tf_op jit(solution)/shard_map/reshape | solution.py:158
  21.2 1.7 %select_maximum_fusion = bf16[32,6,18,258]{3,0,2,1:T(8,128)(2,1)S(1)} fusion(bf16[32,2,16,256]{3,0,2,1:T(8,128)(2,1)S(1)} %collective-permute-done.1, bf16[32,2,16,256]{3,0,2,1:T(8,128)(2,1)S(1)} %copy.90, bf16[32,2,16,256]{3,0,2,1:T(8,128)(2,1)S(1)} %collective-permute-done), kind=kLoop, calls=%fused_computation.29 | loop fusion | flops 16941312 | bytes 3356160 | tf_op jit(solution)/shard_map/concatenate | solution.py:17
  22.9 1.4 %fusion.254 = (bf16[32,6,18,256]{3,0,2,1:T(8,128)(2,1)S(1)}, bf16[32,6,18,256]{3,0,2,1:T(8,128)(2,1)S(1)}, bf16[32,6,18,256]{3,0,2,1:T(8,128)(2,1)S(1)}) fusion(bf16[32,6,18,258]{3,0,2,1:T(8,128)(2,1)S(1)} %select_maximum_fusion), kind=kLoop, calls=%fused_computation.291 | loop fusion | bytes 10616832 | tf_op jit(solution)/shard_map/slice | solution.py:29
  24.3 0.4 pad_maximum_fusion
  24.7 0.6 fusion.11
  25.3 0.6 fusion.13
  25.8 0.6 fusion.15
  26.4 0.6 fusion.17
  26.9 0.6 fusion.19
  27.5 0.6 fusion.5
  28.1 0.6 fusion.7
  28.6 1.9 %fusion.9 = f32[4,16,256,32]{2,3,1,0:T(8,128)} fusion(bf16[96,6,18,256]{3,0,2,1:T(8,128)(2,1)S(1)} %pad_maximum_fusion, bf16[3,3,32,96]{3,2,1,0:T(8,128)(2,1)S(1)} %reshape.195), kind=kOutput, calls=%fused_computation.17 | convolution fusion | flops 100663296 | bytes 5251072 | tf_op jit(solution)/shard_map/ok,kdhw->odhw/dot_general | solution.py:82
  30.5 0.2 slice_bitcast_fusion
  30.8 4.6 %select_convert_fusion = (bf16[32,4,16,256]{3,0,2,1:T(8,128)(2,1)S(1)}, f32[32,4,16,256]{3,0,2,1:T(8,128)}, f32[32,4,16,256]{3,0,2,1:T(8,128)}) fusion(f32[32,4,16,256]{3,0,2,1:T(8,128)} %bitcast.525, pred[4]{0:T(512)(128)(4,1)S(1)} %compare_and_fusion, bf16[96,6,18,256]{3,0,2,1:T(8,128)(2,1)S(1)} %pad_maximum_fusion, ...), kind=kOutput, calls=%fused_computation.36 | convolution fusion | flops 110100480 | bytes 27271680 | tf_op jit(solution)/shard_map/ok,kdhw->odhw/dot_general | solution.py:82
  35.4 2.4 %pad_slice_fusion.2 = (bf16[32,4,18,256]{3,0,2,1:T(8,128)(2,1)S(1)}, bf16[32,4,18,256]{3,0,2,1:T(8,128)(2,1)}, bf16[32,4,18,256]{3,0,2,1:T(8,128)(2,1)}) fusion(bf16[32,4,16,256]{3,0,2,1:T(8,128)(2,1)S(1)} %get-tuple-element.23), kind=kLoop, calls=%fused_computation.40 | loop fusion | bytes 4587520 | tf_op jit(solution)/shard_map/slice | solution.py:29
  37.7 0.6 fusion.110
  38.4 0.6 fusion.116
  39.0 0.6 fusion.122
  39.7 0.6 fusion.128
  40.3 0.6 fusion.134
  41.0 0.6 fusion.140
  41.6 0.6 fusion.146
  42.3 0.6 fusion.152
  42.9 0.6 fusion.158
  43.6 0.3 copy-done
  43.9 0.6 copy-done.1
  44.5 0.5 fusion.63
  45.0 0.7 fusion.65
  47.6 1.0 %all_to_all.13 = f32[16,1,3456]{2,1,0:T(1,128)} reshape(f32[2,9,32,96]{3,2,1,0:T(8,128)S(1)} %pad_maximum_fusion.3) | data formatting | bytes 442368 | tf_op jit(solution)/shard_map/all_to_all | solution.py:38
  48.6 11.1 %all-to-all-start = ((f32[16,1,3456]{2,1,0:T(1,128)}), f32[16,1,3456]{2,1,0:T(1,128)S(1)}, u32[]{:S(2)}, u32[]{:S(2)}) async-start(f32[16,1,3456]{2,1,0:T(1,128)} %all_to_all.13), calls=%async_computation | async-start | bytes 442368 | tf_op jit(solution)/shard_map/all_to_all | solution.py:38
  59.7 1.8 %pad_maximum_fusion.1 = bf16[96,4,18,256]{3,0,2,1:T(8,128)(2,1)S(1)} fusion(bf16[32,4,18,256]{3,0,2,1:T(8,128)(2,1)} %get-tuple-element.53, bf16[32,4,18,256]{3,0,2,1:T(8,128)(2,1)} %get-tuple-element.52, bf16[32,4,18,256]{3,0,2,1:T(8,128)(2,1)S(1)} %get-tuple-element.51), kind=kLoop, calls=%fused_computation.10 | loop fusion | flops 10616832 | bytes 7077888 | tf_op jit(solution)/shard_map/concatenate | solution.py:30
  61.5 0.3 fusion.58
  61.8 0.4 fusion.66
  62.2 0.4 fusion.69
  62.5 0.4 fusion.72
  62.9 0.4 fusion.75
  63.3 0.4 fusion.78
  63.6 0.4 fusion.81
  64.0 0.4 fusion.84
  65.3 0.4 fusion.93
  65.7 3.4 %all-to-all-done = f32[16,1,3456]{2,1,0:T(1,128)S(1)} async-done(((f32[16,1,3456]{2,1,0:T(1,128)}), f32[16,1,3456]{2,1,0:T(1,128)S(1)}, u32[]{:S(2)}, u32[]{:S(2)}) %all-to-all-start) | async-done | bytes 221216 | tf_op jit(solution)/shard_map/all_to_all | solution.py:38
  69.2 0.8 broadcast_in_dim.35
  70.0 3.5 %all-to-all-start.1 = ((f32[16,1,3456]{2,1,0:T(1,128)}), f32[16,1,3456]{2,1,0:T(1,128)S(1)}, u32[]{:S(2)}, u32[]{:S(2)}) async-start(f32[16,1,3456]{2,1,0:T(1,128)} %broadcast_in_dim.35), calls=%async_computation.1 | async-start | bytes 442368 | tf_op jit(solution)/shard_map/all_to_all | solution.py:39
  73.7 1.1 %copy.119 = bf16[32,2,16,256]{3,2,1,0:T(8,128)(2,1)} copy(bf16[32,2,16,256]{3,0,2,1:T(8,128)(2,1)S(1)} %fusion.93) | data formatting | bytes 1048576
  75.1 0.7 copy.118
  75.8 7.1 %all-to-all-done.1 = f32[16,1,3456]{2,1,0:T(1,128)S(1)} async-done(((f32[16,1,3456]{2,1,0:T(1,128)}), f32[16,1,3456]{2,1,0:T(1,128)S(1)}, u32[]{:S(2)}, u32[]{:S(2)}) %all-to-all-start.1) | async-done | bytes 221216 | tf_op jit(solution)/shard_map/all_to_all | solution.py:39
  82.9 0.5 reduce.1
  83.4 0.7 reshape_reshape_reshape.3
  84.1 0.3 fusion.255
  84.4 0.8 copy.116
  85.2 0.8 copy.117
  (63 shorter events, 5.2 us)
Async XLA Ops:
  0.6 15.2 %copy-start.4 = (bf16[27,32,32]{2,1,0:T(8,128)(2,1)S(1)}, bf16[27,32,32]{2,1,0:T(8,128)(2,1)}, u32[]{:S(2)}) copy-start(bf16[27,32,32]{2,1,0:T(8,128)(2,1)} %param.8) | copy-start | bytes 165892
  0.6 14.7 %copy-start.3 = (bf16[27,32,32]{2,1,0:T(8,128)(2,1)S(1)}, bf16[27,32,32]{2,1,0:T(8,128)(2,1)}, u32[]{:S(2)}) copy-start(bf16[27,32,32]{2,1,0:T(8,128)(2,1)} %param.7) | copy-start | bytes 165892
  1.6 14.6 %collective-permute-start.2 = (bf16[32,1,8,128]{3,0,2,1:T(8,128)(2,1)S(1)}, bf16[32,1,8,128]{3,0,2,1:T(8,128)(2,1)S(1)}, u32[]{:S(2)}, u32[]{:S(2)}) collective-permute-start(bf16[32,1,8,128]{3,0,2,1:T(8,128)(2,1)S(1)} %copy.97), channel_id=1, source_target_pairs={{0,1},{1,2},{2,3},{3,4},{4,5},{5,6},{6,7},{7,8},{8,9},{9,10},{10,1... | collective-permute-start | bytes 196616 | tf_op jit(solution)/shard_map/ppermute | solution.py:15
  4.0 12.2 %collective-permute-start.3 = (bf16[32,1,8,128]{3,0,2,1:T(8,128)(2,1)S(1)}, bf16[32,1,8,128]{3,0,2,1:T(8,128)(2,1)S(1)}, u32[]{:S(2)}, u32[]{:S(2)}) collective-permute-start(bf16[32,1,8,128]{3,0,2,1:T(8,128)(2,1)S(1)} %copy.97), channel_id=1, source_target_pairs={{1,0},{2,1},{3,2},{4,3},{5,4},{6,5},{7,6},{8,7},{9,8},{10,9},{11,1... | collective-permute-start | bytes 196616 | tf_op jit(solution)/shard_map/ppermute | solution.py:16
  6.6 14.6 %collective-permute-start = (bf16[32,2,16,256]{3,0,2,1:T(8,128)(2,1)S(1)}, bf16[32,2,16,256]{3,0,2,1:T(8,128)(2,1)S(1)}, u32[]{:S(2)}, u32[]{:S(2)}) collective-permute-start(bf16[32,2,16,256]{3,0,2,1:T(8,128)(2,1)S(1)} %copy.90), channel_id=1, source_target_pairs={{0,1},{1,2},{2,3},{3,4},{4,5},{5,6},{6,7},{7,8},{8,9},{9,10},{10,1... | collective-permute-start | bytes 1572872 | tf_op jit(solution)/shard_map/ppermute | solution.py:15
  11.8 9.4 %collective-permute-start.1 = (bf16[32,2,16,256]{3,0,2,1:T(8,128)(2,1)S(1)}, bf16[32,2,16,256]{3,0,2,1:T(8,128)(2,1)S(1)}, u32[]{:S(2)}, u32[]{:S(2)}) collective-permute-start(bf16[32,2,16,256]{3,0,2,1:T(8,128)(2,1)S(1)} %copy.90), channel_id=1, source_target_pairs={{1,0},{2,1},{3,2},{4,3},{5,4},{6,5},{7,6},{8,7},{9,8},{10,9},{11,1... | collective-permute-start | bytes 1572872 | tf_op jit(solution)/shard_map/ppermute | solution.py:16
  15.3 1.5 %copy-start.2 = (bf16[27,32,32]{2,1,0:T(8,128)(2,1)}, bf16[27,32,32]{2,1,0:T(8,128)(2,1)S(1)}, u32[]{:S(2)}) copy-start(bf16[27,32,32]{2,1,0:T(8,128)(2,1)S(1)} %gather_fusion) | copy-start | bytes 165892
  17.5 0.9 %slice-start.1 = ((bf16[27,32,32]{2,1,0:T(8,128)(2,1)}), bf16[3,32,32]{2,1,0:T(8,128)(2,1)S(1)}, s32[]{:S(2)}) async-start(bf16[27,32,32]{2,1,0:T(8,128)(2,1)} %copy-done.2), calls=%async_computation.3 | async-start | bytes 49152 | tf_op jit(solution)/shard_map/slice | solution.py:153
  18.0 0.9 %slice-start = ((bf16[27,32,32]{2,1,0:T(8,128)(2,1)}), bf16[12,32,32]{2,1,0:T(8,128)(2,1)S(1)}, s32[]{:S(2)}) async-start(bf16[27,32,32]{2,1,0:T(8,128)(2,1)} %copy-done.2), calls=%async_computation.2 | async-start | bytes 196608 | tf_op jit(solution)/shard_map/slice | solution.py:153
  42.2 1.6 %copy-start = (f32[32,4,16,256]{3,0,2,1:T(8,128)S(1)}, f32[32,4,16,256]{3,0,2,1:T(8,128)}, u32[]{:S(2)}) copy-start(f32[32,4,16,256]{3,0,2,1:T(8,128)} %get-tuple-element.24) | copy-start | bytes 6291460
  42.2 2.3 %copy-start.1 = (f32[32,4,16,256]{3,0,2,1:T(8,128)S(1)}, f32[32,4,16,256]{3,0,2,1:T(8,128)}, u32[]{:S(2)}) copy-start(f32[32,4,16,256]{3,0,2,1:T(8,128)} %get-tuple-element.56) | copy-start | bytes 6291460
  45.0 0.9 %copy-start.5 = (bf16[32,1,8,128]{3,2,1,0:T(8,128)(2,1)S(1)}, bf16[32,1,8,128]{3,2,1,0:T(8,128)(2,1)}, u32[]{:S(2)}) copy-start(bf16[32,1,8,128]{3,2,1,0:T(8,128)(2,1)} %param.9) | copy-start | bytes 196612
  48.6 20.4 %all-to-all-start = ((f32[16,1,3456]{2,1,0:T(1,128)}), f32[16,1,3456]{2,1,0:T(1,128)S(1)}, u32[]{:S(2)}, u32[]{:S(2)}) async-start(f32[16,1,3456]{2,1,0:T(1,128)} %all_to_all.13), calls=%async_computation | async-start | bytes 442368 | tf_op jit(solution)/shard_map/all_to_all | solution.py:38
  70.0 12.9 %all-to-all-start.1 = ((f32[16,1,3456]{2,1,0:T(1,128)}), f32[16,1,3456]{2,1,0:T(1,128)S(1)}, u32[]{:S(2)}, u32[]{:S(2)}) async-start(f32[16,1,3456]{2,1,0:T(1,128)} %broadcast_in_dim.35), calls=%async_computation.1 | async-start | bytes 442368 | tf_op jit(solution)/shard_map/all_to_all | solution.py:39

commit v13 on v12

--- a/solution.py
+++ b/solution.py
@@ -32,12 +32,16 @@
 
 def summed_over(terms, axis):
     devices = lax.axis_size(axis)
-    flat = terms.reshape(-1)
-    room = -flat.shape[0] % devices
-    flat = jnp.pad(flat, (0, room)).reshape(devices, -1)
-    mine = lax.all_to_all(flat, axis, 0, 0, tiled=True).sum(0, keepdims=True)
-    whole = lax.all_to_all(jnp.broadcast_to(mine, flat.shape), axis, 0, 0, tiled=True)
-    return whole.reshape(-1)[: terms.size].reshape(terms.shape)
+    width = terms.shape[-1]
+    rows = terms.size // width
+    lanes = -width % 128
+    room = -rows % (8 * devices)
+    flat = jnp.pad(terms.reshape(rows, width), ((0, room), (0, lanes)))
+    flat = flat.reshape(devices, -1, width + lanes)
+    mine = lax.all_to_all(flat, axis, 0, 0).sum(0, keepdims=True)
+    whole = lax.all_to_all(jnp.broadcast_to(mine, flat.shape), axis, 0, 0)
+    whole = whole.reshape(-1, width + lanes)[:rows, :width]
+    return whole.reshape(terms.shape)
 
 
 def forward_kernel(weights):
@@ -163,15 +167,14 @@
     grad_rim = grad_hidden * (sigma * (1.0 + preact * (1.0 - sigma)))
     grad_rim = jnp.where(inside, grad_rim, 0.0).astype(jnp.bfloat16)
     grad_pre = grad_rim[:, 1 : planes + 1]
-    volume_minor = volume_cols[:, 1 : planes + 3].transpose(1, 2, 3, 0)
     terms_one = []
     for along_depth in range(3):
         for along_rows in range(3):
-            window = volume_minor[
-                along_depth : along_depth + planes, along_rows : along_rows + height
+            window = volume_cols[
+                :, along_depth + 1 : along_depth + 1 + planes, along_rows : along_rows + height, :
             ]
             terms_one.append(
-                jnp.einsum("odhw,dhwk->ok", grad_pre, window, preferred_element_type=jnp.float32)
+                jnp.einsum("odhw,kdhw->ok", grad_pre, window, preferred_element_type=jnp.float32)
             )
     rimmed = pad_sides(grad_rim)
     rimmed_cols = column_stack(rimmed, 1, columns, lambda along_cols: 2 - along_cols)

time: 86.6 us -> 85.8 us (level)
  waiting for transfers between devices: 10.5 us -> 13.9 us
  matrix products: 25.4 us -> 22.6 us
  local copies, waits for them, and re-layouts: 18.2 us -> 16.1 us
  starting transfers between devices: 24.8 us -> 25.9 us
    all_to_all x2, waiting for transfers between devices: 10.5 us -> 13.9 us  [the longest x1 8.65 us: summed_over(): whole = lax.all_to_all(jnp.broadcast_to(mine, flat.shape), axis, 0, 0)]
    dot_general x9, matrix products: 10.4 us -> 7.59 us  [layer(): jnp.einsum('ok,kdhw->odhw', front_one[along_depth, along_rows], window, p...]
    reshape x1, local copies, waits for them, and re-layouts: 1.47 us -> 0.14 us  [layer(): jnp.stack(classes).reshape(2, 2, channels, class_planes, half_rows, columns)]
    all_to_all x2, starting transfers between devices: 14.6 us -> 15.7 us  [the longest x1 12.2 us: summed_over(): mine = lax.all_to_all(flat, axis, 0, 0).sum(0, keepdims=True)]
    all_to_all x1 -> x0, local copies, waits for them, and re-layouts: 1 us -> none  [summed_over(): mine = lax.all_to_all(flat, axis, 0, 0, tiled=True).sum(0, keepdims=True)]
  transfers between devices with their start and end apart: 6 -> 6, of which waited for: 2 -> 2; matrix products, arithmetic and copies ran while one was open for 20% -> 18% of each run, Pallas kernels for 0% -> 0%
where the time goes in v13:
time: 85.8 us; the launch traced here: 85.2 us
  starting transfers between devices  25.9 us (30%)
  matrix products  22.6 us (26%)
  local copies, waits for them, and re-layouts  16.1 us (19%)
  waiting for transfers between devices  13.9 us (16%)
  other arithmetic  5.51 us (6%)
  between operations  1.21 us (1%)
    all_to_all x1, starting transfers between devices, summed_over(): mine = lax.all_to_all(flat, axis, 0, 0).sum(0, keepdims=True)  12.2 us
    all_to_all x1, waiting for transfers between devices, summed_over(): whole = lax.all_to_all(jnp.broadcast_to(mine, flat.shape), axis, 0, 0)  8.65 us
    dot_general x9, matrix products, layer(): jnp.einsum('ok,kdhw->odhw', front_one[along_depth, along_rows], window, p...  7.59 us
    ppermute x2, starting transfers between devices, extended_2(): before = lax.ppermute(last, axis, up)  7.58 us
    dot_general x9, matrix products, layer(): jnp.einsum('odhw,kdhw->ok', grad_pre, window, preferred_element_type=jnp....  5.75 us
    unnamed x26, local copies, waits for them, and re-layouts  5.44 us
    all_to_all x1, waiting for transfers between devices, summed_over(): mine = lax.all_to_all(flat, axis, 0, 0).sum(0, keepdims=True)  5.25 us
    slice x2, local copies, waits for them, and re-layouts, column_stack(): pieces.append(field[..., first:first + stride * (count - 1) + 1:stride])  3.82 us
  transfers between devices with their start and end apart: 6, of which 2 were waited for; matrix products, arithmetic and copies ran while one was open for 18% of the time, Pallas kernels for 0%

profile of v13, /device:TPU:0, one launch (start us, length us, event | category | flops | bytes accessed | tf_op | source)
XLA Modules:
  0.0 85.2 jit_solution(2374970168873255439)
XLA Ops:
  0.7 0.9 %copy.68 = bf16[32,1,8,128]{3,0,2,1:T(8,128)(2,1)S(1)} copy(bf16[32,1,8,128]{3,2,1,0:T(8,128)(2,1)} %param.9) | data formatting | bytes 131072 | tf_op args[3]
  1.6 2.4 %collective-permute-start.2 = (bf16[32,1,8,128]{3,0,2,1:T(8,128)(2,1)S(1)}, bf16[32,1,8,128]{3,0,2,1:T(8,128)(2,1)S(1)}, u32[]{:S(2)}, u32[]{:S(2)}) collective-permute-start(bf16[32,1,8,128]{3,0,2,1:T(8,128)(2,1)S(1)} %copy.68), channel_id=1, source_target_pairs={{0,1},{1,2},{2,3},{3,4},{4,5},{5,6},{6,7},{7,8},{8,9},{9,10},{10,1... | collective-permute-start | bytes 196616 | tf_op jit(solution)/shard_map/ppermute | solution.py:15
  4.0 1.3 %collective-permute-start.3 = (bf16[32,1,8,128]{3,0,2,1:T(8,128)(2,1)S(1)}, bf16[32,1,8,128]{3,0,2,1:T(8,128)(2,1)S(1)}, u32[]{:S(2)}, u32[]{:S(2)}) collective-permute-start(bf16[32,1,8,128]{3,0,2,1:T(8,128)(2,1)S(1)} %copy.68), channel_id=1, source_target_pairs={{1,0},{2,1},{3,2},{4,3},{5,4},{6,5},{7,6},{8,7},{9,8},{10,9},{11,1... | collective-permute-start | bytes 196616 | tf_op jit(solution)/shard_map/ppermute | solution.py:16
  5.3 1.3 %copy.61 = bf16[32,2,16,256]{3,0,2,1:T(8,128)(2,1)S(1)} copy(bf16[32,2,16,256]{3,2,1,0:T(8,128)(2,1)} %param.6) | data formatting | bytes 1048576 | tf_op args[0]
  6.6 5.2 %collective-permute-start = (bf16[32,2,16,256]{3,0,2,1:T(8,128)(2,1)S(1)}, bf16[32,2,16,256]{3,0,2,1:T(8,128)(2,1)S(1)}, u32[]{:S(2)}, u32[]{:S(2)}) collective-permute-start(bf16[32,2,16,256]{3,0,2,1:T(8,128)(2,1)S(1)} %copy.61), channel_id=1, source_target_pairs={{0,1},{1,2},{2,3},{3,4},{4,5},{5,6},{6,7},{7,8},{8,9},{9,10},{10,1... | collective-permute-start | bytes 1572872 | tf_op jit(solution)/shard_map/ppermute | solution.py:15
  11.8 1.3 %collective-permute-start.1 = (bf16[32,2,16,256]{3,0,2,1:T(8,128)(2,1)S(1)}, bf16[32,2,16,256]{3,0,2,1:T(8,128)(2,1)S(1)}, u32[]{:S(2)}, u32[]{:S(2)}) collective-permute-start(bf16[32,2,16,256]{3,0,2,1:T(8,128)(2,1)S(1)} %copy.61), channel_id=1, source_target_pairs={{1,0},{2,1},{3,2},{4,3},{5,4},{6,5},{7,6},{8,7},{9,8},{10,9},{11,1... | collective-permute-start | bytes 1572872 | tf_op jit(solution)/shard_map/ppermute | solution.py:16
  13.1 0.7 pad_clamp_fusion
  13.8 1.5 %gather_fusion = bf16[27,32,32]{2,1,0:T(8,128)(2,1)S(1)} fusion(bf16[27,32,32]{2,1,0:T(8,128)(2,1)} %param.8, s32[1024]{0:T(1024)S(1)} %pad_clamp_fusion), kind=kCustom, calls=%fused_computation | custom fusion | bytes 110700 | tf_op jit(solution)/shard_map/gather | solution.py:138
  16.2 0.6 fusion.64
  17.5 0.4 convolution_bitcast_fusion
  18.0 0.4 convolution_bitcast_fusion.3
  18.4 0.3 convolution_bitcast_fusion.1
  18.9 0.6 convolution_bitcast_fusion.2
  19.5 0.2 pad_maximum_fusion.2
  19.9 1.9 %select_maximum_fusion = bf16[32,6,18,258]{3,0,2,1:T(8,128)(2,1)S(1)} fusion(bf16[32,2,16,256]{3,0,2,1:T(8,128)(2,1)S(1)} %collective-permute-done.1, bf16[32,2,16,256]{3,0,2,1:T(8,128)(2,1)S(1)} %copy.61, bf16[32,2,16,256]{3,0,2,1:T(8,128)(2,1)S(1)} %collective-permute-done), kind=kLoop, calls=%fused_computation.28 | loop fusion | flops 16941312 | bytes 3356160 | tf_op jit(solution)/shard_map/concatenate | solution.py:17
  21.8 1.4 %fusion.254 = (bf16[32,6,18,256]{3,0,2,1:T(8,128)(2,1)S(1)}, bf16[32,6,18,256]{3,0,2,1:T(8,128)(2,1)S(1)}, bf16[32,6,18,256]{3,0,2,1:T(8,128)(2,1)S(1)}) fusion(bf16[32,6,18,258]{3,0,2,1:T(8,128)(2,1)S(1)} %select_maximum_fusion), kind=kLoop, calls=%fused_computation.290 | loop fusion | bytes 10616832 | tf_op jit(solution)/shard_map/slice | solution.py:29
  23.2 0.4 pad_maximum_fusion
  23.6 0.6 fusion.11
  24.1 0.6 fusion.13
  24.7 0.6 fusion.15
  25.3 0.6 fusion.17
  25.8 0.6 fusion.19
  26.4 0.6 fusion.5
  26.9 0.6 fusion.7
  27.5 0.6 fusion.9
  28.1 3.1 %select_convert_fusion = (bf16[32,4,16,256]{3,0,2,1:T(8,128)(2,1)S(1)}, f32[32,4,16,256]{3,0,2,1:T(8,128)}, f32[32,4,16,256]{3,0,2,1:T(8,128)}) fusion(f32[32,4,16,256]{3,0,2,1:T(8,128)S(1)} %bitcast.524, pred[4]{0:T(512)(128)(4,1)S(1)} %compare_and_fusion, bf16[96,6,18,256]{3,0,2,1:T(8,128)(2,1)S(1)} %pad_maximum_fusion, ...), kind=kOutput, calls=%fused_computation.35 | convolution fusion | flops 110100480 | bytes 27271680 | tf_op jit(solution)/shard_map/ok,kdhw->odhw/dot_general | solution.py:86
  31.2 0.6 fusion.110
  31.8 2.4 %pad_slice_fusion.2 = (bf16[32,4,18,256]{3,0,2,1:T(8,128)(2,1)S(1)}, bf16[32,4,18,256]{3,0,2,1:T(8,128)(2,1)}, bf16[32,4,18,256]{3,0,2,1:T(8,128)(2,1)}) fusion(bf16[32,4,16,256]{3,0,2,1:T(8,128)(2,1)S(1)} %get-tuple-element.19), kind=kLoop, calls=%fused_computation.39 | loop fusion | bytes 4587520 | tf_op jit(solution)/shard_map/slice | solution.py:29
  34.2 0.6 fusion.116
  34.8 0.6 fusion.122
  35.5 0.6 fusion.128
  36.1 0.6 fusion.134
  36.8 0.6 fusion.140
  37.4 0.6 fusion.146
  38.1 0.6 fusion.152
  38.7 0.6 fusion.158
  39.4 0.3 copy-done
  39.7 0.6 copy-done.1
  40.3 0.5 fusion.63
  40.9 0.7 fusion.65
  41.5 0.2 copy.65
  42.7 0.2 fusion.101
  43.4 0.7 pad.24
  44.2 12.2 %all-to-all-start = ((f32[16,40,128]{2,1,0:T(8,128)}), f32[16,40,128]{2,1,0:T(8,128)S(1)}, u32[]{:S(2)}, u32[]{:S(2)}) async-start(f32[16,40,128]{2,1,0:T(8,128)} %bitcast.185), calls=%async_computation | async-start | bytes 655360 | tf_op jit(solution)/shard_map/all_to_all | solution.py:41
  56.4 1.8 %pad_maximum_fusion.1 = bf16[96,4,18,256]{3,0,2,1:T(8,128)(2,1)S(1)} fusion(bf16[32,4,18,256]{3,0,2,1:T(8,128)(2,1)} %get-tuple-element.49, bf16[32,4,18,256]{3,0,2,1:T(8,128)(2,1)} %get-tuple-element.48, bf16[32,4,18,256]{3,0,2,1:T(8,128)(2,1)S(1)} %get-tuple-element.47), kind=kLoop, calls=%fused_computation.9 | loop fusion | flops 10616832 | bytes 7077888 | tf_op jit(solution)/shard_map/concatenate | solution.py:30
  58.2 0.3 fusion.58
  58.5 0.4 fusion.66
  58.9 0.4 fusion.69
  59.2 0.4 fusion.72
  59.6 0.4 fusion.75
  60.0 0.4 fusion.78
  60.3 0.4 fusion.81
  61.5 0.4 fusion.84
  61.9 0.4 fusion.93
  62.2 5.3 %all-to-all-done = f32[16,40,128]{2,1,0:T(8,128)S(1)} async-done(((f32[16,40,128]{2,1,0:T(8,128)}), f32[16,40,128]{2,1,0:T(8,128)S(1)}, u32[]{:S(2)}, u32[]{:S(2)}) %all-to-all-start) | async-done | bytes 327712 | tf_op jit(solution)/shard_map/all_to_all | solution.py:41
  67.5 0.7 broadcast_in_dim.35
  68.2 3.5 %all-to-all-start.1 = ((f32[16,40,128]{2,1,0:T(8,128)}), f32[16,40,128]{2,1,0:T(8,128)S(1)}, u32[]{:S(2)}, u32[]{:S(2)}) async-start(f32[16,40,128]{2,1,0:T(8,128)} %broadcast_in_dim.35), calls=%async_computation.1 | async-start | bytes 655360 | tf_op jit(solution)/shard_map/all_to_all | solution.py:42
  71.9 1.1 %copy.89 = bf16[32,2,16,256]{3,2,1,0:T(8,128)(2,1)} copy(bf16[32,2,16,256]{3,0,2,1:T(8,128)(2,1)S(1)} %fusion.93) | data formatting | bytes 1048576
  73.5 0.7 copy.88
  74.2 8.6 %all-to-all-done.1 = f32[16,40,128]{2,1,0:T(8,128)S(1)} async-done(((f32[16,40,128]{2,1,0:T(8,128)}), f32[16,40,128]{2,1,0:T(8,128)S(1)}, u32[]{:S(2)}, u32[]{:S(2)}) %all-to-all-start.1) | async-done | bytes 327712 | tf_op jit(solution)/shard_map/all_to_all | solution.py:42
  82.8 0.4 reshape_reshape.3
  83.3 0.3 fusion.255
  83.6 0.8 copy.86
  84.4 0.8 copy.87
  (62 shorter events, 4.6 us)
Async XLA Ops:
  0.6 15.2 %copy-start.4 = (bf16[27,32,32]{2,1,0:T(8,128)(2,1)S(1)}, bf16[27,32,32]{2,1,0:T(8,128)(2,1)}, u32[]{:S(2)}) copy-start(bf16[27,32,32]{2,1,0:T(8,128)(2,1)} %param.8) | copy-start | bytes 165892
  0.6 14.7 %copy-start.3 = (bf16[27,32,32]{2,1,0:T(8,128)(2,1)S(1)}, bf16[27,32,32]{2,1,0:T(8,128)(2,1)}, u32[]{:S(2)}) copy-start(bf16[27,32,32]{2,1,0:T(8,128)(2,1)} %param.7) | copy-start | bytes 165892
  1.6 14.6 %collective-permute-start.2 = (bf16[32,1,8,128]{3,0,2,1:T(8,128)(2,1)S(1)}, bf16[32,1,8,128]{3,0,2,1:T(8,128)(2,1)S(1)}, u32[]{:S(2)}, u32[]{:S(2)}) collective-permute-start(bf16[32,1,8,128]{3,0,2,1:T(8,128)(2,1)S(1)} %copy.68), channel_id=1, source_target_pairs={{0,1},{1,2},{2,3},{3,4},{4,5},{5,6},{6,7},{7,8},{8,9},{9,10},{10,1... | collective-permute-start | bytes 196616 | tf_op jit(solution)/shard_map/ppermute | solution.py:15
  4.0 12.2 %collective-permute-start.3 = (bf16[32,1,8,128]{3,0,2,1:T(8,128)(2,1)S(1)}, bf16[32,1,8,128]{3,0,2,1:T(8,128)(2,1)S(1)}, u32[]{:S(2)}, u32[]{:S(2)}) collective-permute-start(bf16[32,1,8,128]{3,0,2,1:T(8,128)(2,1)S(1)} %copy.68), channel_id=1, source_target_pairs={{1,0},{2,1},{3,2},{4,3},{5,4},{6,5},{7,6},{8,7},{9,8},{10,9},{11,1... | collective-permute-start | bytes 196616 | tf_op jit(solution)/shard_map/ppermute | solution.py:16
  6.6 13.3 %collective-permute-start = (bf16[32,2,16,256]{3,0,2,1:T(8,128)(2,1)S(1)}, bf16[32,2,16,256]{3,0,2,1:T(8,128)(2,1)S(1)}, u32[]{:S(2)}, u32[]{:S(2)}) collective-permute-start(bf16[32,2,16,256]{3,0,2,1:T(8,128)(2,1)S(1)} %copy.61), channel_id=1, source_target_pairs={{0,1},{1,2},{2,3},{3,4},{4,5},{5,6},{6,7},{7,8},{8,9},{9,10},{10,1... | collective-permute-start | bytes 1572872 | tf_op jit(solution)/shard_map/ppermute | solution.py:15
  11.8 8.1 %collective-permute-start.1 = (bf16[32,2,16,256]{3,0,2,1:T(8,128)(2,1)S(1)}, bf16[32,2,16,256]{3,0,2,1:T(8,128)(2,1)S(1)}, u32[]{:S(2)}, u32[]{:S(2)}) collective-permute-start(bf16[32,2,16,256]{3,0,2,1:T(8,128)(2,1)S(1)} %copy.61), channel_id=1, source_target_pairs={{1,0},{2,1},{3,2},{4,3},{5,4},{6,5},{7,6},{8,7},{9,8},{10,9},{11,1... | collective-permute-start | bytes 1572872 | tf_op jit(solution)/shard_map/ppermute | solution.py:16
  15.3 1.5 %copy-start.2 = (bf16[27,32,32]{2,1,0:T(8,128)(2,1)}, bf16[27,32,32]{2,1,0:T(8,128)(2,1)S(1)}, u32[]{:S(2)}) copy-start(bf16[27,32,32]{2,1,0:T(8,128)(2,1)S(1)} %gather_fusion) | copy-start | bytes 165892
  17.5 0.9 %slice-start.1 = ((bf16[27,32,32]{2,1,0:T(8,128)(2,1)}), bf16[3,32,32]{2,1,0:T(8,128)(2,1)S(1)}, s32[]{:S(2)}) async-start(bf16[27,32,32]{2,1,0:T(8,128)(2,1)} %copy-done.2), calls=%async_computation.3 | async-start | bytes 49152 | tf_op jit(solution)/shard_map/slice | solution.py:157
  18.0 0.9 %slice-start = ((bf16[27,32,32]{2,1,0:T(8,128)(2,1)}), bf16[12,32,32]{2,1,0:T(8,128)(2,1)S(1)}, s32[]{:S(2)}) async-start(bf16[27,32,32]{2,1,0:T(8,128)(2,1)} %copy-done.2), calls=%async_computation.2 | async-start | bytes 196608 | tf_op jit(solution)/shard_map/slice | solution.py:157
  38.1 1.6 %copy-start = (f32[32,4,16,256]{3,0,2,1:T(8,128)S(1)}, f32[32,4,16,256]{3,0,2,1:T(8,128)}, u32[]{:S(2)}) copy-start(f32[32,4,16,256]{3,0,2,1:T(8,128)} %get-tuple-element.20) | copy-start | bytes 6291460
  38.1 2.3 %copy-start.1 = (f32[32,4,16,256]{3,0,2,1:T(8,128)S(1)}, f32[32,4,16,256]{3,0,2,1:T(8,128)}, u32[]{:S(2)}) copy-start(f32[32,4,16,256]{3,0,2,1:T(8,128)} %get-tuple-element.52) | copy-start | bytes 6291460
  40.8 0.9 %copy-start.5 = (bf16[32,1,8,128]{3,2,1,0:T(8,128)(2,1)S(1)}, bf16[32,1,8,128]{3,2,1,0:T(8,128)(2,1)}, u32[]{:S(2)}) copy-start(bf16[32,1,8,128]{3,2,1,0:T(8,128)(2,1)} %param.9) | copy-start | bytes 196612
  44.2 23.3 %all-to-all-start = ((f32[16,40,128]{2,1,0:T(8,128)}), f32[16,40,128]{2,1,0:T(8,128)S(1)}, u32[]{:S(2)}, u32[]{:S(2)}) async-start(f32[16,40,128]{2,1,0:T(8,128)} %bitcast.185), calls=%async_computation | async-start | bytes 655360 | tf_op jit(solution)/shard_map/all_to_all | solution.py:41
  68.2 14.6 %all-to-all-start.1 = ((f32[16,40,128]{2,1,0:T(8,128)}), f32[16,40,128]{2,1,0:T(8,128)S(1)}, u32[]{:S(2)}, u32[]{:S(2)}) async-start(f32[16,40,128]{2,1,0:T(8,128)} %broadcast_in_dim.35), calls=%async_computation.1 | async-start | bytes 655360 | tf_op jit(solution)/shard_map/all_to_all | solution.py:42

commit v14 on v12

--- a/solution.py
+++ b/solution.py
@@ -50,13 +50,6 @@
 def backward_kernel(weights):
     size = weights.shape[1]
     return weights.reshape(3, 3, 3 * size, size)
-
-
-def fold_terms(summed):
-    size = summed.shape[2]
-    folded = summed.reshape(2, 9, size, 3, size).transpose(0, 1, 3, 2, 4)
-    folded = folded.reshape(2, 27, size, size)
-    return folded[0], folded[1]
 
 
 def layer(volume, weight_one, weight_two, cotangent):
@@ -114,7 +107,12 @@
                 preferred_element_type=jnp.float32,
             )
             terms_two.append(
-                jnp.einsum("odhw,kdhw->ok", cotangent, window, preferred_element_type=jnp.float32)
+                jnp.einsum(
+                    "odhw,cqdhw->coq",
+                    cotangent,
+                    window.reshape((3, channels) + window.shape[1:]),
+                    preferred_element_type=jnp.float32,
+                )
             )
     extended = jnp.pad(cot_ext, ((0, 0), (0, 0), (0, 1), (0, 0)))
     spread = jnp.arange(half_cols)[:, None, None] * 2 + jnp.arange(3)[None, :, None] - 1
@@ -163,15 +161,19 @@
     grad_rim = grad_hidden * (sigma * (1.0 + preact * (1.0 - sigma)))
     grad_rim = jnp.where(inside, grad_rim, 0.0).astype(jnp.bfloat16)
     grad_pre = grad_rim[:, 1 : planes + 1]
-    volume_minor = volume_cols[:, 1 : planes + 3].transpose(1, 2, 3, 0)
     terms_one = []
     for along_depth in range(3):
         for along_rows in range(3):
-            window = volume_minor[
-                along_depth : along_depth + planes, along_rows : along_rows + height
+            window = volume_cols[
+                :, along_depth + 1 : along_depth + 1 + planes, along_rows : along_rows + height, :
             ]
             terms_one.append(
-                jnp.einsum("odhw,dhwk->ok", grad_pre, window, preferred_element_type=jnp.float32)
+                jnp.einsum(
+                    "odhw,cqdhw->coq",
+                    grad_pre,
+                    window.reshape((3, channels) + window.shape[1:]),
+                    preferred_element_type=jnp.float32,
+                )
             )
     rimmed = pad_sides(grad_rim)
     rimmed_cols = column_stack(rimmed, 1, columns, lambda along_cols: 2 - along_cols)
@@ -192,7 +194,8 @@
             )
     grad_volume = grad_volume.astype(jnp.bfloat16)
     summed = summed_over(jnp.stack([jnp.stack(terms_one), jnp.stack(terms_two)]), "slab")
-    grad_one, grad_two = fold_terms(summed)
+    folded = summed.reshape(2, 27, channels, channels)
+    grad_one, grad_two = folded[0], folded[1]
     return (output.astype(jnp.bfloat16), grad_volume, grad_one, grad_two)
 
 

time: 86.6 us -> 92.3 us (1.066)
  local copies, waits for them, and re-layouts: 18.2 us -> 26.6 us
  matrix products: 25.4 us -> 21.6 us
  starting transfers between devices: 24.8 us -> 26.1 us
    slice x3, local copies, waits for them, and re-layouts: 1.92 us -> 5.85 us  [the longest x1 5.05 us: layer(): volume_cols[:, along_depth + 1:along_depth + 1 + planes, along_rows:along...]
    dot_general x9, matrix products: 10.4 us -> 7.53 us  [layer(): jnp.einsum('ok,kdhw->odhw', front_one[along_depth, along_rows], window, p...]
    unnamed x26 -> x44, local copies, waits for them, and re-layouts: 5.44 us -> 7.97 us
    squeeze x0 -> x2, local copies, waits for them, and re-layouts: none -> 1.84 us  [layer(): grad_one, grad_two = (folded[0], folded[1])]
    reshape x1, local copies, waits for them, and re-layouts: 1.47 us -> 0.14 us  [layer(): jnp.stack(classes).reshape(2, 2, channels, class_planes, half_rows, columns)]
    all_to_all x1, starting transfers between devices: 11.1 us -> 12.4 us  [summed_over(): mine = lax.all_to_all(flat, axis, 0, 0, tiled=True).sum(0, keepdims=True)]
    all_to_all x1, local copies, waits for them, and re-layouts: 1 us -> 2.24 us  [summed_over(): mine = lax.all_to_all(flat, axis, 0, 0, tiled=True).sum(0, keepdims=True)]
  transfers between devices with their start and end apart: 6 -> 6, of which waited for: 2 -> 2; matrix products, arithmetic and copies ran while one was open for 20% -> 17% of each run, Pallas kernels for 0% -> 0%
where the time goes in v14:
time: 92.3 us; the launch traced here: 91.7 us
  local copies, waits for them, and re-layouts  26.6 us (29%)
  starting transfers between devices  26.1 us (28%)
  matrix products  21.6 us (23%)
  waiting for transfers between devices  10.5 us (11%)
  other arithmetic  5.5 us (6%)
  between operations  1.4 us (2%)
    all_to_all x1, starting transfers between devices, summed_over(): mine = lax.all_to_all(flat, axis, 0, 0, tiled=True).sum(0, keepdims=True)  12.4 us
    unnamed x44, local copies, waits for them, and re-layouts  7.97 us
    ppermute x2, starting transfers between devices, extended_2(): before = lax.ppermute(last, axis, up)  7.58 us
    dot_general x9, matrix products, layer(): jnp.einsum('ok,kdhw->odhw', front_one[along_depth, along_rows], window, p...  7.53 us
    all_to_all x1, waiting for transfers between devices, summed_over(): lax.all_to_all(jnp.broadcast_to(mine, flat.shape), axis, 0, 0, tiled=True)  7.09 us
    slice x1, local copies, waits for them, and re-layouts, layer(): volume_cols[:, along_depth + 1:along_depth + 1 + planes, along_rows:along...  5.05 us
    dot_general x9, matrix products, layer(): jnp.einsum('odhw,cqdhw->coq', grad_pre, window.reshape((3, channels) + wi...  4.79 us
    slice x2, local copies, waits for them, and re-layouts, column_stack(): pieces.append(field[..., first:first + stride * (count - 1) + 1:stride])  3.69 us
  transfers between devices with their start and end apart: 6, of which 2 were waited for; matrix products, arithmetic and copies ran while one was open for 17% of the time, Pallas kernels for 0%

profile of v14, /device:TPU:0, one launch (start us, length us, event | category | flops | bytes accessed | tf_op | source)
XLA Modules:
  0.0 91.7 jit_solution(14697325162370300551)
XLA Ops:
  0.7 0.9 copy.105
  1.6 2.4 %collective-permute-start.2 = (bf16[32,1,8,128]{3,0,2,1:T(8,128)(2,1)S(1)}, bf16[32,1,8,128]{3,0,2,1:T(8,128)(2,1)S(1)}, u32[]{:S(2)}, u32[]{:S(2)}) collective-permute-start(bf16[32,1,8,128]{3,0,2,1:T(8,128)(2,1)S(1)} %copy.105), channel_id=1, source_target_pairs={{0,1},{1,2},{2,3},{3,4},{4,5},{5,6},{6,7},{7,8},{8,9},{9,10},{10,1... | collective-permute-start | bytes 196616 | tf_op jit(solution)/shard_map/ppermute | solution.py:15
  4.0 1.3 %collective-permute-start.3 = (bf16[32,1,8,128]{3,0,2,1:T(8,128)(2,1)S(1)}, bf16[32,1,8,128]{3,0,2,1:T(8,128)(2,1)S(1)}, u32[]{:S(2)}, u32[]{:S(2)}) collective-permute-start(bf16[32,1,8,128]{3,0,2,1:T(8,128)(2,1)S(1)} %copy.105), channel_id=1, source_target_pairs={{1,0},{2,1},{3,2},{4,3},{5,4},{6,5},{7,6},{8,7},{9,8},{10,9},{11,1... | collective-permute-start | bytes 196616 | tf_op jit(solution)/shard_map/ppermute | solution.py:16
  5.3 1.3 %copy.98 = bf16[32,2,16,256]{3,0,2,1:T(8,128)(2,1)S(1)} copy(bf16[32,2,16,256]{3,2,1,0:T(8,128)(2,1)} %param.6) | data formatting | bytes 1048576 | tf_op args[0]
  6.6 5.2 %collective-permute-start = (bf16[32,2,16,256]{3,0,2,1:T(8,128)(2,1)S(1)}, bf16[32,2,16,256]{3,0,2,1:T(8,128)(2,1)S(1)}, u32[]{:S(2)}, u32[]{:S(2)}) collective-permute-start(bf16[32,2,16,256]{3,0,2,1:T(8,128)(2,1)S(1)} %copy.98), channel_id=1, source_target_pairs={{0,1},{1,2},{2,3},{3,4},{4,5},{5,6},{6,7},{7,8},{8,9},{9,10},{10,1... | collective-permute-start | bytes 1572872 | tf_op jit(solution)/shard_map/ppermute | solution.py:15
  11.8 1.3 %collective-permute-start.1 = (bf16[32,2,16,256]{3,0,2,1:T(8,128)(2,1)S(1)}, bf16[32,2,16,256]{3,0,2,1:T(8,128)(2,1)S(1)}, u32[]{:S(2)}, u32[]{:S(2)}) collective-permute-start(bf16[32,2,16,256]{3,0,2,1:T(8,128)(2,1)S(1)} %copy.98), channel_id=1, source_target_pairs={{1,0},{2,1},{3,2},{4,3},{5,4},{6,5},{7,6},{8,7},{9,8},{10,9},{11,1... | collective-permute-start | bytes 1572872 | tf_op jit(solution)/shard_map/ppermute | solution.py:16
  13.1 0.7 pad_clamp_fusion
  13.8 1.5 %gather_fusion = bf16[27,32,32]{2,1,0:T(8,128)(2,1)S(1)} fusion(bf16[27,32,32]{2,1,0:T(8,128)(2,1)} %param.8, s32[1024]{0:T(1024)S(1)} %pad_clamp_fusion), kind=kCustom, calls=%fused_computation | custom fusion | bytes 110700 | tf_op jit(solution)/shard_map/gather | solution.py:132
  16.2 0.6 fusion.46
  17.5 0.4 convolution_bitcast_fusion
  18.0 0.4 convolution_bitcast_fusion.3
  18.9 0.6 convolution_bitcast_fusion.2
  19.9 1.7 %select_maximum_fusion = bf16[32,6,18,258]{3,0,2,1:T(8,128)(2,1)S(1)} fusion(bf16[32,2,16,256]{3,0,2,1:T(8,128)(2,1)S(1)} %collective-permute-done.1, bf16[32,2,16,256]{3,0,2,1:T(8,128)(2,1)S(1)} %copy.98, bf16[32,2,16,256]{3,0,2,1:T(8,128)(2,1)S(1)} %collective-permute-done), kind=kLoop, calls=%fused_computation.28 | loop fusion | flops 16941312 | bytes 3356160 | tf_op jit(solution)/shard_map/concatenate | solution.py:17
  21.6 1.4 %fusion.174 = (bf16[32,6,18,256]{3,0,2,1:T(8,128)(2,1)S(1)}, bf16[32,6,18,256]{3,0,2,1:T(8,128)(2,1)S(1)}, bf16[32,6,18,256]{3,0,2,1:T(8,128)(2,1)S(1)}) fusion(bf16[32,6,18,258]{3,0,2,1:T(8,128)(2,1)S(1)} %select_maximum_fusion), kind=kLoop, calls=%fused_computation.258 | loop fusion | bytes 10616832 | tf_op jit(solution)/shard_map/slice | solution.py:29
  22.9 0.4 pad_maximum_fusion
  23.4 0.6 fusion.11
  23.9 0.6 fusion.13
  24.5 0.6 fusion.15
  25.0 0.6 fusion.17
  25.6 0.6 fusion.19
  26.1 0.6 fusion.5
  26.7 0.6 fusion.7
  27.2 0.6 fusion.9
  27.8 5.1 %fusion.173 = (bf16[96,2,16,256]{3,0,2,1:T(8,128)(2,1)}, bf16[96,2,16,256]{3,0,2,1:T(8,128)(2,1)}, bf16[96,2,16,256]{3,0,2,1:T(8,128)(2,1)}, bf16[96,2,16,256]{3...) fusion(bf16[96,6,18,256]{3,0,2,1:T(8,128)(2,1)S(1)} %pad_maximu, ...), kind=kLoop, calls=%fused_computation.257 | loop fusion | bytes 28311552 | tf_op jit(solution)/shard_map/slice | solution.py:167
  32.8 3.1 %select_convert_fusion = (bf16[32,4,16,256]{3,0,2,1:T(8,128)(2,1)S(1)}, f32[32,4,16,256]{3,0,2,1:T(8,128)}, f32[32,4,16,256]{3,0,2,1:T(8,128)}) fusion(f32[32,4,16,256]{3,0,2,1:T(8,128)S(1)} %bitcast.580, pred[4]{0:T(512)(128)(4,1)S(1)} %compare_and_fusion, bf16[96,6,18,256]{3,0,2,1:T(8,128)(2,1)S(1)} %pad_maximum_fusion, ...), kind=kOutput, calls=%fused_computation.35 | convolution fusion | flops 110100480 | bytes 27271680 | tf_op jit(solution)/shard_map/ok,kdhw->odhw/dot_general | solution.py:75
  36.0 2.3 %pad_slice_fusion.2 = (bf16[32,4,18,256]{3,0,2,1:T(8,128)(2,1)S(1)}, bf16[32,4,18,256]{3,0,2,1:T(8,128)(2,1)}, bf16[32,4,18,256]{3,0,2,1:T(8,128)(2,1)}) fusion(bf16[32,4,16,256]{3,0,2,1:T(8,128)(2,1)S(1)} %get-tuple-element.30), kind=kLoop, calls=%fused_computation.39 | loop fusion | bytes 4587520 | tf_op jit(solution)/shard_map/slice | solution.py:29
  38.3 0.5 fusion.97
  38.8 1.1 %copy-done.1 = f32[32,4,16,256]{3,0,2,1:T(8,128)S(1)} copy-done((f32[32,4,16,256]{3,0,2,1:T(8,128)S(1)}, f32[32,4,16,256]{3,0,2,1:T(8,128)}, u32[]{:S(2)}) %copy-start.1) | copy-done | bytes 2097176
  39.9 0.5 fusion.45
  40.4 0.7 fusion.47
  41.6 1.2 %copy-done.10 = bf16[96,2,16,256]{3,0,2,1:T(8,128)(2,1)S(1)} copy-done((bf16[96,2,16,256]{3,0,2,1:T(8,128)(2,1)S(1)}, bf16[96,2,16,256]{3,0,2,1:T(8,128)(2,1)}, u32[]{:S(2)}) %copy-start.10) | copy-done | bytes 1572888
  42.8 0.5 fusion.96
  43.3 0.5 fusion.95
  43.9 0.4 copy-done.8
  44.3 0.5 fusion.94
  44.8 0.5 fusion.93
  45.4 0.4 copy-done.6
  45.8 0.5 fusion.92
  46.4 0.5 fusion.91
  46.9 0.4 copy-done.4
  47.3 0.5 fusion.90
  47.9 0.5 fusion.89
  50.3 1.2 %copy.123 = f32[2,9,3,32,32]{4,3,2,1,0:T(8,128)} copy(f32[2,9,3,32,32]{3,4,2,1,0:T(8,128)S(1)} %pad_maximum_fusion.3) | data formatting | bytes 442368 | tf_op jit(solution)/shard_map/stack | solution.py:196
  51.5 2.2 %all_to_all.13 = f32[16,1,3456]{2,1,0:T(1,128)} reshape(f32[2,9,3,32,32]{4,3,2,1,0:T(8,128)} %copy.123) | data formatting | bytes 442368 | tf_op jit(solution)/shard_map/all_to_all | solution.py:38
  53.7 12.4 %all-to-all-start = ((f32[16,1,3456]{2,1,0:T(1,128)}), f32[16,1,3456]{2,1,0:T(1,128)S(1)}, u32[]{:S(2)}, u32[]{:S(2)}) async-start(f32[16,1,3456]{2,1,0:T(1,128)} %all_to_all.13), calls=%async_computation | async-start | bytes 442368 | tf_op jit(solution)/shard_map/all_to_all | solution.py:38
  66.1 1.8 %pad_maximum_fusion.1 = bf16[96,4,18,256]{3,0,2,1:T(8,128)(2,1)S(1)} fusion(bf16[32,4,18,256]{3,0,2,1:T(8,128)(2,1)} %get-tuple-element.67, bf16[32,4,18,256]{3,0,2,1:T(8,128)(2,1)} %get-tuple-element.66, bf16[32,4,18,256]{3,0,2,1:T(8,128)(2,1)S(1)} %get-tuple-element.65), kind=kLoop, calls=%fused_computation.9 | loop fusion | flops 10616832 | bytes 7077888 | tf_op jit(solution)/shard_map/concatenate | solution.py:30
  67.9 0.3 fusion.40
  68.2 0.4 fusion.48
  68.6 0.4 fusion.51
  69.0 0.4 fusion.54
  69.3 0.4 fusion.57
  69.7 0.4 fusion.60
  70.0 0.4 fusion.63
  70.4 0.4 fusion.66
  71.7 0.4 fusion.75
  72.1 3.4 %all-to-all-done = f32[16,1,3456]{2,1,0:T(1,128)S(1)} async-done(((f32[16,1,3456]{2,1,0:T(1,128)}), f32[16,1,3456]{2,1,0:T(1,128)S(1)}, u32[]{:S(2)}, u32[]{:S(2)}) %all-to-all-start) | async-done | bytes 221216 | tf_op jit(solution)/shard_map/all_to_all | solution.py:38
  75.6 0.8 broadcast_in_dim.35
  76.4 3.5 %all-to-all-start.1 = ((f32[16,1,3456]{2,1,0:T(1,128)}), f32[16,1,3456]{2,1,0:T(1,128)S(1)}, u32[]{:S(2)}, u32[]{:S(2)}) async-start(f32[16,1,3456]{2,1,0:T(1,128)} %broadcast_in_dim.35), calls=%async_computation.1 | async-start | bytes 442368 | tf_op jit(solution)/shard_map/all_to_all | solution.py:39
  80.1 1.1 %copy.126 = bf16[32,2,16,256]{3,2,1,0:T(8,128)(2,1)} copy(bf16[32,2,16,256]{3,0,2,1:T(8,128)(2,1)S(1)} %fusion.75) | data formatting | bytes 1048576
  81.5 0.7 copy.125
  82.2 7.1 %all-to-all-done.1 = f32[16,1,3456]{2,1,0:T(1,128)S(1)} async-done(((f32[16,1,3456]{2,1,0:T(1,128)}), f32[16,1,3456]{2,1,0:T(1,128)S(1)}, u32[]{:S(2)}, u32[]{:S(2)}) %all-to-all-start.1) | async-done | bytes 221216 | tf_op jit(solution)/shard_map/all_to_all | solution.py:39
  89.3 0.6 slice_reduce_fusion
  89.8 0.9 %squeeze.177 = f32[27,32,32]{2,1,0:T(8,128)} reshape(f32[8,3456]{1,0:T(8,128)S(1)} %get-tuple-element.17) | data formatting | bytes 221184 | tf_op jit(solution)/shard_map/squeeze | solution.py:198
  90.8 0.9 %squeeze.178 = f32[27,32,32]{2,1,0:T(8,128)} reshape(f32[8,3456]{1,0:T(8,128)S(1)} %get-tuple-element.16) | data formatting | bytes 221184 | tf_op jit(solution)/shard_map/squeeze | solution.py:198
  (81 shorter events, 6.0 us)
Async XLA Ops:
  0.6 15.2 %copy-start.14 = (bf16[27,32,32]{2,1,0:T(8,128)(2,1)S(1)}, bf16[27,32,32]{2,1,0:T(8,128)(2,1)}, u32[]{:S(2)}) copy-start(bf16[27,32,32]{2,1,0:T(8,128)(2,1)} %param.8) | copy-start | bytes 165892
  0.6 14.7 %copy-start.13 = (bf16[27,32,32]{2,1,0:T(8,128)(2,1)S(1)}, bf16[27,32,32]{2,1,0:T(8,128)(2,1)}, u32[]{:S(2)}) copy-start(bf16[27,32,32]{2,1,0:T(8,128)(2,1)} %param.7) | copy-start | bytes 165892
  1.6 14.6 %collective-permute-start.2 = (bf16[32,1,8,128]{3,0,2,1:T(8,128)(2,1)S(1)}, bf16[32,1,8,128]{3,0,2,1:T(8,128)(2,1)S(1)}, u32[]{:S(2)}, u32[]{:S(2)}) collective-permute-start(bf16[32,1,8,128]{3,0,2,1:T(8,128)(2,1)S(1)} %copy.105), channel_id=1, source_target_pairs={{0,1},{1,2},{2,3},{3,4},{4,5},{5,6},{6,7},{7,8},{8,9},{9,10},{10,1... | collective-permute-start | bytes 196616 | tf_op jit(solution)/shard_map/ppermute | solution.py:15
  4.0 12.2 %collective-permute-start.3 = (bf16[32,1,8,128]{3,0,2,1:T(8,128)(2,1)S(1)}, bf16[32,1,8,128]{3,0,2,1:T(8,128)(2,1)S(1)}, u32[]{:S(2)}, u32[]{:S(2)}) collective-permute-start(bf16[32,1,8,128]{3,0,2,1:T(8,128)(2,1)S(1)} %copy.105), channel_id=1, source_target_pairs={{1,0},{2,1},{3,2},{4,3},{5,4},{6,5},{7,6},{8,7},{9,8},{10,9},{11,1... | collective-permute-start | bytes 196616 | tf_op jit(solution)/shard_map/ppermute | solution.py:16
  6.6 13.3 %collective-permute-start = (bf16[32,2,16,256]{3,0,2,1:T(8,128)(2,1)S(1)}, bf16[32,2,16,256]{3,0,2,1:T(8,128)(2,1)S(1)}, u32[]{:S(2)}, u32[]{:S(2)}) collective-permute-start(bf16[32,2,16,256]{3,0,2,1:T(8,128)(2,1)S(1)} %copy.98), channel_id=1, source_target_pairs={{0,1},{1,2},{2,3},{3,4},{4,5},{5,6},{6,7},{7,8},{8,9},{9,10},{10,1... | collective-permute-start | bytes 1572872 | tf_op jit(solution)/shard_map/ppermute | solution.py:15
  11.8 8.1 %collective-permute-start.1 = (bf16[32,2,16,256]{3,0,2,1:T(8,128)(2,1)S(1)}, bf16[32,2,16,256]{3,0,2,1:T(8,128)(2,1)S(1)}, u32[]{:S(2)}, u32[]{:S(2)}) collective-permute-start(bf16[32,2,16,256]{3,0,2,1:T(8,128)(2,1)S(1)} %copy.98), channel_id=1, source_target_pairs={{1,0},{2,1},{3,2},{4,3},{5,4},{6,5},{7,6},{8,7},{9,8},{10,9},{11,1... | collective-permute-start | bytes 1572872 | tf_op jit(solution)/shard_map/ppermute | solution.py:16
  15.3 1.5 %copy-start.12 = (bf16[27,32,32]{2,1,0:T(8,128)(2,1)}, bf16[27,32,32]{2,1,0:T(8,128)(2,1)S(1)}, u32[]{:S(2)}) copy-start(bf16[27,32,32]{2,1,0:T(8,128)(2,1)S(1)} %gather_fusion) | copy-start | bytes 165892
  17.5 0.9 slice-start.1
  18.0 0.9 slice-start
  36.0 2.3 %copy-start.11 = (bf16[96,2,16,256]{3,0,2,1:T(8,128)(2,1)S(1)}, bf16[96,2,16,256]{3,0,2,1:T(8,128)(2,1)}, u32[]{:S(2)}) copy-start(bf16[96,2,16,256]{3,0,2,1:T(8,128)(2,1)} %get-tuple-element.26) | copy-start | bytes 4718596
  36.0 2.9 %copy-start.2 = (f32[32,4,16,256]{3,0,2,1:T(8,128)S(1)}, f32[32,4,16,256]{3,0,2,1:T(8,128)}, u32[]{:S(2)}) copy-start(f32[32,4,16,256]{3,0,2,1:T(8,128)} %get-tuple-element.70) | copy-start | bytes 6291460
  38.3 1.6 %copy-start.1 = (f32[32,4,16,256]{3,0,2,1:T(8,128)S(1)}, f32[32,4,16,256]{3,0,2,1:T(8,128)}, u32[]{:S(2)}) copy-start(f32[32,4,16,256]{3,0,2,1:T(8,128)} %get-tuple-element.31) | copy-start | bytes 6291460
  41.3 1.4 %copy-start.10 = (bf16[96,2,16,256]{3,0,2,1:T(8,128)(2,1)S(1)}, bf16[96,2,16,256]{3,0,2,1:T(8,128)(2,1)}, u32[]{:S(2)}) copy-start(bf16[96,2,16,256]{3,0,2,1:T(8,128)(2,1)} %get-tuple-element.25) | copy-start | bytes 4718596
  41.4 1.9 %copy-start.9 = (bf16[96,2,16,256]{3,0,2,1:T(8,128)(2,1)S(1)}, bf16[96,2,16,256]{3,0,2,1:T(8,128)(2,1)}, u32[]{:S(2)}) copy-start(bf16[96,2,16,256]{3,0,2,1:T(8,128)(2,1)} %get-tuple-element.24) | copy-start | bytes 4718596
  42.8 1.5 %copy-start.8 = (bf16[96,2,16,256]{3,0,2,1:T(8,128)(2,1)S(1)}, bf16[96,2,16,256]{3,0,2,1:T(8,128)(2,1)}, u32[]{:S(2)}) copy-start(bf16[96,2,16,256]{3,0,2,1:T(8,128)(2,1)} %get-tuple-element.23) | copy-start | bytes 4718596
  43.3 1.5 %copy-start.7 = (bf16[96,2,16,256]{3,0,2,1:T(8,128)(2,1)S(1)}, bf16[96,2,16,256]{3,0,2,1:T(8,128)(2,1)}, u32[]{:S(2)}) copy-start(bf16[96,2,16,256]{3,0,2,1:T(8,128)(2,1)} %get-tuple-element.22) | copy-start | bytes 4718596
  44.3 1.5 %copy-start.6 = (bf16[96,2,16,256]{3,0,2,1:T(8,128)(2,1)S(1)}, bf16[96,2,16,256]{3,0,2,1:T(8,128)(2,1)}, u32[]{:S(2)}) copy-start(bf16[96,2,16,256]{3,0,2,1:T(8,128)(2,1)} %get-tuple-element.21) | copy-start | bytes 4718596
  44.8 1.5 %copy-start.5 = (bf16[96,2,16,256]{3,0,2,1:T(8,128)(2,1)S(1)}, bf16[96,2,16,256]{3,0,2,1:T(8,128)(2,1)}, u32[]{:S(2)}) copy-start(bf16[96,2,16,256]{3,0,2,1:T(8,128)(2,1)} %get-tuple-element.20) | copy-start | bytes 4718596
  45.8 1.5 %copy-start.4 = (bf16[96,2,16,256]{3,0,2,1:T(8,128)(2,1)S(1)}, bf16[96,2,16,256]{3,0,2,1:T(8,128)(2,1)}, u32[]{:S(2)}) copy-start(bf16[96,2,16,256]{3,0,2,1:T(8,128)(2,1)} %get-tuple-element.19) | copy-start | bytes 4718596
  46.4 1.5 %copy-start.3 = (bf16[96,2,16,256]{3,0,2,1:T(8,128)(2,1)S(1)}, bf16[96,2,16,256]{3,0,2,1:T(8,128)(2,1)}, u32[]{:S(2)}) copy-start(bf16[96,2,16,256]{3,0,2,1:T(8,128)(2,1)} %get-tuple-element.18) | copy-start | bytes 4718596
  47.3 1.1 %copy-start = (bf16[32,1,8,128]{3,2,1,0:T(8,128)(2,1)S(1)}, bf16[32,1,8,128]{3,2,1,0:T(8,128)(2,1)}, u32[]{:S(2)}) copy-start(bf16[32,1,8,128]{3,2,1,0:T(8,128)(2,1)} %param.9) | copy-start | bytes 196612
  53.7 21.7 %all-to-all-start = ((f32[16,1,3456]{2,1,0:T(1,128)}), f32[16,1,3456]{2,1,0:T(1,128)S(1)}, u32[]{:S(2)}, u32[]{:S(2)}) async-start(f32[16,1,3456]{2,1,0:T(1,128)} %all_to_all.13), calls=%async_computation | async-start | bytes 442368 | tf_op jit(solution)/shard_map/all_to_all | solution.py:38
  76.4 12.9 %all-to-all-start.1 = ((f32[16,1,3456]{2,1,0:T(1,128)}), f32[16,1,3456]{2,1,0:T(1,128)S(1)}, u32[]{:S(2)}, u32[]{:S(2)}) async-start(f32[16,1,3456]{2,1,0:T(1,128)} %broadcast_in_dim.35), calls=%async_computation.1 | async-start | bytes 442368 | tf_op jit(solution)/shard_map/all_to_all | solution.py:39

commit v15 on v13

--- a/solution.py
+++ b/solution.py
@@ -32,16 +32,12 @@
 
 def summed_over(terms, axis):
     devices = lax.axis_size(axis)
-    width = terms.shape[-1]
-    rows = terms.size // width
-    lanes = -width % 128
-    room = -rows % (8 * devices)
-    flat = jnp.pad(terms.reshape(rows, width), ((0, room), (0, lanes)))
-    flat = flat.reshape(devices, -1, width + lanes)
+    flat = terms.reshape(-1)
+    room = -flat.shape[0] % (devices * 128)
+    flat = jnp.pad(flat, (0, room)).reshape(devices, -1, 128)
     mine = lax.all_to_all(flat, axis, 0, 0).sum(0, keepdims=True)
     whole = lax.all_to_all(jnp.broadcast_to(mine, flat.shape), axis, 0, 0)
-    whole = whole.reshape(-1, width + lanes)[:rows, :width]
-    return whole.reshape(terms.shape)
+    return whole.reshape(-1)[: terms.size].reshape(terms.shape)
 
 
 def forward_kernel(weights):

time: 85.8 us -> 84.1 us (0.980)
  waiting for transfers between devices: 13.9 us -> 11.8 us
    all_to_all x1, waiting for transfers between devices: 5.25 us -> 4.04 us  [summed_over(): mine = lax.all_to_all(flat, axis, 0, 0).sum(0, keepdims=True)]
    all_to_all x1, waiting for transfers between devices: 8.65 us -> 7.75 us  [summed_over(): whole = lax.all_to_all(jnp.broadcast_to(mine, flat.shape), axis, 0, 0)]
  transfers between devices with their start and end apart: 6 -> 6, of which waited for: 2 -> 2; matrix products, arithmetic and copies ran while one was open for 18% -> 19% of each run, Pallas kernels for 0% -> 0%
where the time goes in v15:
time: 84.1 us; the launch traced here: 83.6 us
  starting transfers between devices  26.1 us (31%)
  matrix products  22.6 us (27%)
  local copies, waits for them, and re-layouts  16.4 us (20%)
  waiting for transfers between devices  11.8 us (14%)
  other arithmetic  5.51 us (7%)
  between operations  1.21 us (1%)
    all_to_all x1, starting transfers between devices, summed_over(): mine = lax.all_to_all(flat, axis, 0, 0).sum(0, keepdims=True)  12.4 us
    all_to_all x1, waiting for transfers between devices, summed_over(): whole = lax.all_to_all(jnp.broadcast_to(mine, flat.shape), axis, 0, 0)  7.75 us
    dot_general x9, matrix products, layer(): jnp.einsum('ok,kdhw->odhw', front_one[along_depth, along_rows], window, p...  7.59 us
    ppermute x2, starting transfers between devices, extended_2(): before = lax.ppermute(last, axis, up)  7.58 us
    dot_general x9, matrix products, layer(): jnp.einsum('odhw,kdhw->ok', grad_pre, window, preferred_element_type=jnp....  5.75 us
    unnamed x26, local copies, waits for them, and re-layouts  5.44 us
    all_to_all x1, waiting for transfers between devices, summed_over(): mine = lax.all_to_all(flat, axis, 0, 0).sum(0, keepdims=True)  4.04 us
    slice x2, local copies, waits for them, and re-layouts, column_stack(): pieces.append(field[..., first:first + stride * (count - 1) + 1:stride])  3.82 us
  transfers between devices with their start and end apart: 6, of which 2 were waited for; matrix products, arithmetic and copies ran while one was open for 19% of the time, Pallas kernels for 0%

profile of v15, /device:TPU:0, one launch (start us, length us, event | category | flops | bytes accessed | tf_op | source)
XLA Modules:
  0.0 83.6 jit_solution(13757402972593727387)
XLA Ops:
  0.7 0.9 %copy.68 = bf16[32,1,8,128]{3,0,2,1:T(8,128)(2,1)S(1)} copy(bf16[32,1,8,128]{3,2,1,0:T(8,128)(2,1)} %param.9) | data formatting | bytes 131072 | tf_op args[3]
  1.6 2.4 %collective-permute-start.2 = (bf16[32,1,8,128]{3,0,2,1:T(8,128)(2,1)S(1)}, bf16[32,1,8,128]{3,0,2,1:T(8,128)(2,1)S(1)}, u32[]{:S(2)}, u32[]{:S(2)}) collective-permute-start(bf16[32,1,8,128]{3,0,2,1:T(8,128)(2,1)S(1)} %copy.68), channel_id=1, source_target_pairs={{0,1},{1,2},{2,3},{3,4},{4,5},{5,6},{6,7},{7,8},{8,9},{9,10},{10,1... | collective-permute-start | bytes 196616 | tf_op jit(solution)/shard_map/ppermute | solution.py:15
  4.0 1.3 %collective-permute-start.3 = (bf16[32,1,8,128]{3,0,2,1:T(8,128)(2,1)S(1)}, bf16[32,1,8,128]{3,0,2,1:T(8,128)(2,1)S(1)}, u32[]{:S(2)}, u32[]{:S(2)}) collective-permute-start(bf16[32,1,8,128]{3,0,2,1:T(8,128)(2,1)S(1)} %copy.68), channel_id=1, source_target_pairs={{1,0},{2,1},{3,2},{4,3},{5,4},{6,5},{7,6},{8,7},{9,8},{10,9},{11,1... | collective-permute-start | bytes 196616 | tf_op jit(solution)/shard_map/ppermute | solution.py:16
  5.3 1.3 %copy.61 = bf16[32,2,16,256]{3,0,2,1:T(8,128)(2,1)S(1)} copy(bf16[32,2,16,256]{3,2,1,0:T(8,128)(2,1)} %param.6) | data formatting | bytes 1048576 | tf_op args[0]
  6.6 5.2 %collective-permute-start = (bf16[32,2,16,256]{3,0,2,1:T(8,128)(2,1)S(1)}, bf16[32,2,16,256]{3,0,2,1:T(8,128)(2,1)S(1)}, u32[]{:S(2)}, u32[]{:S(2)}) collective-permute-start(bf16[32,2,16,256]{3,0,2,1:T(8,128)(2,1)S(1)} %copy.61), channel_id=1, source_target_pairs={{0,1},{1,2},{2,3},{3,4},{4,5},{5,6},{6,7},{7,8},{8,9},{9,10},{10,1... | collective-permute-start | bytes 1572872 | tf_op jit(solution)/shard_map/ppermute | solution.py:15
  11.8 1.3 %collective-permute-start.1 = (bf16[32,2,16,256]{3,0,2,1:T(8,128)(2,1)S(1)}, bf16[32,2,16,256]{3,0,2,1:T(8,128)(2,1)S(1)}, u32[]{:S(2)}, u32[]{:S(2)}) collective-permute-start(bf16[32,2,16,256]{3,0,2,1:T(8,128)(2,1)S(1)} %copy.61), channel_id=1, source_target_pairs={{1,0},{2,1},{3,2},{4,3},{5,4},{6,5},{7,6},{8,7},{9,8},{10,9},{11,1... | collective-permute-start | bytes 1572872 | tf_op jit(solution)/shard_map/ppermute | solution.py:16
  13.1 0.7 pad_clamp_fusion
  13.8 1.5 %gather_fusion = bf16[27,32,32]{2,1,0:T(8,128)(2,1)S(1)} fusion(bf16[27,32,32]{2,1,0:T(8,128)(2,1)} %param.8, s32[1024]{0:T(1024)S(1)} %pad_clamp_fusion), kind=kCustom, calls=%fused_computation | custom fusion | bytes 110700 | tf_op jit(solution)/shard_map/gather | solution.py:134
  16.2 0.6 fusion.64
  17.5 0.4 convolution_bitcast_fusion
  18.0 0.4 convolution_bitcast_fusion.3
  18.4 0.3 convolution_bitcast_fusion.1
  18.9 0.6 convolution_bitcast_fusion.2
  19.5 0.2 pad_maximum_fusion.2
  19.9 1.9 %select_maximum_fusion = bf16[32,6,18,258]{3,0,2,1:T(8,128)(2,1)S(1)} fusion(bf16[32,2,16,256]{3,0,2,1:T(8,128)(2,1)S(1)} %collective-permute-done.1, bf16[32,2,16,256]{3,0,2,1:T(8,128)(2,1)S(1)} %copy.61, bf16[32,2,16,256]{3,0,2,1:T(8,128)(2,1)S(1)} %collective-permute-done), kind=kLoop, calls=%fused_computation.28 | loop fusion | flops 16941312 | bytes 3356160 | tf_op jit(solution)/shard_map/concatenate | solution.py:17
  21.8 1.4 %fusion.254 = (bf16[32,6,18,256]{3,0,2,1:T(8,128)(2,1)S(1)}, bf16[32,6,18,256]{3,0,2,1:T(8,128)(2,1)S(1)}, bf16[32,6,18,256]{3,0,2,1:T(8,128)(2,1)S(1)}) fusion(bf16[32,6,18,258]{3,0,2,1:T(8,128)(2,1)S(1)} %select_maximum_fusion), kind=kLoop, calls=%fused_computation.290 | loop fusion | bytes 10616832 | tf_op jit(solution)/shard_map/slice | solution.py:29
  23.2 0.4 pad_maximum_fusion
  23.6 0.6 fusion.11
  24.1 0.6 fusion.13
  24.7 0.6 fusion.15
  25.3 0.6 fusion.17
  25.8 0.6 fusion.19
  26.4 0.6 fusion.5
  26.9 0.6 fusion.7
  27.5 0.6 fusion.9
  28.1 3.1 %select_convert_fusion = (bf16[32,4,16,256]{3,0,2,1:T(8,128)(2,1)S(1)}, f32[32,4,16,256]{3,0,2,1:T(8,128)}, f32[32,4,16,256]{3,0,2,1:T(8,128)}) fusion(f32[32,4,16,256]{3,0,2,1:T(8,128)S(1)} %bitcast.523, pred[4]{0:T(512)(128)(4,1)S(1)} %compare_and_fusion, bf16[96,6,18,256]{3,0,2,1:T(8,128)(2,1)S(1)} %pad_maximum_fusion, ...), kind=kOutput, calls=%fused_computation.35 | convolution fusion | flops 110100480 | bytes 27271680 | tf_op jit(solution)/shard_map/ok,kdhw->odhw/dot_general | solution.py:82
  31.2 0.6 fusion.110
  31.8 2.4 %pad_slice_fusion.2 = (bf16[32,4,18,256]{3,0,2,1:T(8,128)(2,1)S(1)}, bf16[32,4,18,256]{3,0,2,1:T(8,128)(2,1)}, bf16[32,4,18,256]{3,0,2,1:T(8,128)(2,1)}) fusion(bf16[32,4,16,256]{3,0,2,1:T(8,128)(2,1)S(1)} %get-tuple-element.19), kind=kLoop, calls=%fused_computation.39 | loop fusion | bytes 4587520 | tf_op jit(solution)/shard_map/slice | solution.py:29
  34.2 0.6 fusion.116
  34.8 0.6 fusion.122
  35.5 0.6 fusion.128
  36.1 0.6 fusion.134
  36.8 0.6 fusion.140
  37.4 0.6 fusion.146
  38.1 0.6 fusion.152
  38.7 0.6 fusion.158
  39.4 0.3 copy-done
  39.7 0.6 copy-done.1
  40.3 0.5 fusion.63
  40.9 0.7 fusion.65
  41.5 0.2 copy.65
  42.7 0.2 fusion.101
  43.5 0.8 %reshape.209 = f32[16,27,128]{2,1,0:T(8,128)} reshape(f32[2,9,32,96]{3,2,1,0:T(8,128)S(1)} %pad_maximum_fusion.3) | data formatting | bytes 442368 | tf_op jit(solution)/shard_map/reshape | solution.py:37
  44.3 12.4 %all-to-all-start = ((f32[16,27,128]{2,1,0:T(8,128)}), f32[16,27,128]{2,1,0:T(8,128)S(1)}, u32[]{:S(2)}, u32[]{:S(2)}) async-start(f32[16,27,128]{2,1,0:T(8,128)} %reshape.209), calls=%async_computation | async-start | bytes 524288 | tf_op jit(solution)/shard_map/all_to_all | solution.py:38
  56.7 1.8 %pad_maximum_fusion.1 = bf16[96,4,18,256]{3,0,2,1:T(8,128)(2,1)S(1)} fusion(bf16[32,4,18,256]{3,0,2,1:T(8,128)(2,1)} %get-tuple-element.49, bf16[32,4,18,256]{3,0,2,1:T(8,128)(2,1)} %get-tuple-element.48, bf16[32,4,18,256]{3,0,2,1:T(8,128)(2,1)S(1)} %get-tuple-element.47), kind=kLoop, calls=%fused_computation.9 | loop fusion | flops 10616832 | bytes 7077888 | tf_op jit(solution)/shard_map/concatenate | solution.py:30
  58.5 0.3 fusion.58
  58.8 0.4 fusion.66
  59.2 0.4 fusion.69
  59.6 0.4 fusion.72
  59.9 0.4 fusion.75
  60.3 0.4 fusion.78
  60.6 0.4 fusion.81
  61.0 0.4 fusion.84
  62.3 0.4 fusion.93
  62.7 4.0 %all-to-all-done = f32[16,27,128]{2,1,0:T(8,128)S(1)} async-done(((f32[16,27,128]{2,1,0:T(8,128)}), f32[16,27,128]{2,1,0:T(8,128)S(1)}, u32[]{:S(2)}, u32[]{:S(2)}) %all-to-all-start) | async-done | bytes 221216 | tf_op jit(solution)/shard_map/all_to_all | solution.py:38
  66.8 0.7 broadcast_in_dim.35
  67.5 3.5 %all-to-all-start.1 = ((f32[16,27,128]{2,1,0:T(8,128)}), f32[16,27,128]{2,1,0:T(8,128)S(1)}, u32[]{:S(2)}, u32[]{:S(2)}) async-start(f32[16,27,128]{2,1,0:T(8,128)} %broadcast_in_dim.35), calls=%async_computation.1 | async-start | bytes 524288 | tf_op jit(solution)/shard_map/all_to_all | solution.py:39
  71.2 1.1 %copy.89 = bf16[32,2,16,256]{3,2,1,0:T(8,128)(2,1)} copy(bf16[32,2,16,256]{3,0,2,1:T(8,128)(2,1)S(1)} %fusion.93) | data formatting | bytes 1048576
  72.6 0.7 copy.88
  73.2 7.8 %all-to-all-done.1 = f32[16,27,128]{2,1,0:T(8,128)S(1)} async-done(((f32[16,27,128]{2,1,0:T(8,128)}), f32[16,27,128]{2,1,0:T(8,128)S(1)}, u32[]{:S(2)}, u32[]{:S(2)}) %all-to-all-start.1) | async-done | bytes 221216 | tf_op jit(solution)/shard_map/all_to_all | solution.py:39
  81.0 0.6 reshape_reshape_reshape.3
  81.6 0.3 fusion.255
  81.9 0.8 copy.86
  82.8 0.8 copy.87
  (61 shorter events, 4.6 us)
Async XLA Ops:
  0.6 15.2 %copy-start.4 = (bf16[27,32,32]{2,1,0:T(8,128)(2,1)S(1)}, bf16[27,32,32]{2,1,0:T(8,128)(2,1)}, u32[]{:S(2)}) copy-start(bf16[27,32,32]{2,1,0:T(8,128)(2,1)} %param.8) | copy-start | bytes 165892
  0.6 14.7 %copy-start.3 = (bf16[27,32,32]{2,1,0:T(8,128)(2,1)S(1)}, bf16[27,32,32]{2,1,0:T(8,128)(2,1)}, u32[]{:S(2)}) copy-start(bf16[27,32,32]{2,1,0:T(8,128)(2,1)} %param.7) | copy-start | bytes 165892
  1.6 14.6 %collective-permute-start.2 = (bf16[32,1,8,128]{3,0,2,1:T(8,128)(2,1)S(1)}, bf16[32,1,8,128]{3,0,2,1:T(8,128)(2,1)S(1)}, u32[]{:S(2)}, u32[]{:S(2)}) collective-permute-start(bf16[32,1,8,128]{3,0,2,1:T(8,128)(2,1)S(1)} %copy.68), channel_id=1, source_target_pairs={{0,1},{1,2},{2,3},{3,4},{4,5},{5,6},{6,7},{7,8},{8,9},{9,10},{10,1... | collective-permute-start | bytes 196616 | tf_op jit(solution)/shard_map/ppermute | solution.py:15
  4.0 12.2 %collective-permute-start.3 = (bf16[32,1,8,128]{3,0,2,1:T(8,128)(2,1)S(1)}, bf16[32,1,8,128]{3,0,2,1:T(8,128)(2,1)S(1)}, u32[]{:S(2)}, u32[]{:S(2)}) collective-permute-start(bf16[32,1,8,128]{3,0,2,1:T(8,128)(2,1)S(1)} %copy.68), channel_id=1, source_target_pairs={{1,0},{2,1},{3,2},{4,3},{5,4},{6,5},{7,6},{8,7},{9,8},{10,9},{11,1... | collective-permute-start | bytes 196616 | tf_op jit(solution)/shard_map/ppermute | solution.py:16
  6.6 13.3 %collective-permute-start = (bf16[32,2,16,256]{3,0,2,1:T(8,128)(2,1)S(1)}, bf16[32,2,16,256]{3,0,2,1:T(8,128)(2,1)S(1)}, u32[]{:S(2)}, u32[]{:S(2)}) collective-permute-start(bf16[32,2,16,256]{3,0,2,1:T(8,128)(2,1)S(1)} %copy.61), channel_id=1, source_target_pairs={{0,1},{1,2},{2,3},{3,4},{4,5},{5,6},{6,7},{7,8},{8,9},{9,10},{10,1... | collective-permute-start | bytes 1572872 | tf_op jit(solution)/shard_map/ppermute | solution.py:15
  11.8 8.1 %collective-permute-start.1 = (bf16[32,2,16,256]{3,0,2,1:T(8,128)(2,1)S(1)}, bf16[32,2,16,256]{3,0,2,1:T(8,128)(2,1)S(1)}, u32[]{:S(2)}, u32[]{:S(2)}) collective-permute-start(bf16[32,2,16,256]{3,0,2,1:T(8,128)(2,1)S(1)} %copy.61), channel_id=1, source_target_pairs={{1,0},{2,1},{3,2},{4,3},{5,4},{6,5},{7,6},{8,7},{9,8},{10,9},{11,1... | collective-permute-start | bytes 1572872 | tf_op jit(solution)/shard_map/ppermute | solution.py:16
  15.3 1.5 %copy-start.2 = (bf16[27,32,32]{2,1,0:T(8,128)(2,1)}, bf16[27,32,32]{2,1,0:T(8,128)(2,1)S(1)}, u32[]{:S(2)}) copy-start(bf16[27,32,32]{2,1,0:T(8,128)(2,1)S(1)} %gather_fusion) | copy-start | bytes 165892
  17.5 0.9 %slice-start.1 = ((bf16[27,32,32]{2,1,0:T(8,128)(2,1)}), bf16[3,32,32]{2,1,0:T(8,128)(2,1)S(1)}, s32[]{:S(2)}) async-start(bf16[27,32,32]{2,1,0:T(8,128)(2,1)} %copy-done.2), calls=%async_computation.3 | async-start | bytes 49152 | tf_op jit(solution)/shard_map/slice | solution.py:153
  18.0 0.9 %slice-start = ((bf16[27,32,32]{2,1,0:T(8,128)(2,1)}), bf16[12,32,32]{2,1,0:T(8,128)(2,1)S(1)}, s32[]{:S(2)}) async-start(bf16[27,32,32]{2,1,0:T(8,128)(2,1)} %copy-done.2), calls=%async_computation.2 | async-start | bytes 196608 | tf_op jit(solution)/shard_map/slice | solution.py:153
  38.1 1.6 %copy-start = (f32[32,4,16,256]{3,0,2,1:T(8,128)S(1)}, f32[32,4,16,256]{3,0,2,1:T(8,128)}, u32[]{:S(2)}) copy-start(f32[32,4,16,256]{3,0,2,1:T(8,128)} %get-tuple-element.20) | copy-start | bytes 6291460
  38.1 2.3 %copy-start.1 = (f32[32,4,16,256]{3,0,2,1:T(8,128)S(1)}, f32[32,4,16,256]{3,0,2,1:T(8,128)}, u32[]{:S(2)}) copy-start(f32[32,4,16,256]{3,0,2,1:T(8,128)} %get-tuple-element.52) | copy-start | bytes 6291460
  40.8 0.9 %copy-start.5 = (bf16[32,1,8,128]{3,2,1,0:T(8,128)(2,1)S(1)}, bf16[32,1,8,128]{3,2,1,0:T(8,128)(2,1)}, u32[]{:S(2)}) copy-start(bf16[32,1,8,128]{3,2,1,0:T(8,128)(2,1)} %param.9) | copy-start | bytes 196612
  44.3 22.4 %all-to-all-start = ((f32[16,27,128]{2,1,0:T(8,128)}), f32[16,27,128]{2,1,0:T(8,128)S(1)}, u32[]{:S(2)}, u32[]{:S(2)}) async-start(f32[16,27,128]{2,1,0:T(8,128)} %reshape.209), calls=%async_computation | async-start | bytes 524288 | tf_op jit(solution)/shard_map/all_to_all | solution.py:38
  67.5 13.5 %all-to-all-start.1 = ((f32[16,27,128]{2,1,0:T(8,128)}), f32[16,27,128]{2,1,0:T(8,128)S(1)}, u32[]{:S(2)}, u32[]{:S(2)}) async-start(f32[16,27,128]{2,1,0:T(8,128)} %broadcast_in_dim.35), calls=%async_computation.1 | async-start | bytes 524288 | tf_op jit(solution)/shard_map/all_to_all | solution.py:39

commit v16 on v12

--- a/solution.py
+++ b/solution.py
@@ -163,15 +163,14 @@
     grad_rim = grad_hidden * (sigma * (1.0 + preact * (1.0 - sigma)))
     grad_rim = jnp.where(inside, grad_rim, 0.0).astype(jnp.bfloat16)
     grad_pre = grad_rim[:, 1 : planes + 1]
-    volume_minor = volume_cols[:, 1 : planes + 3].transpose(1, 2, 3, 0)
     terms_one = []
     for along_depth in range(3):
         for along_rows in range(3):
-            window = volume_minor[
-                along_depth : along_depth + planes, along_rows : along_rows + height
+            window = volume_cols[
+                :, along_depth + 1 : along_depth + 1 + planes, along_rows : along_rows + height, :
             ]
             terms_one.append(
-                jnp.einsum("odhw,dhwk->ok", grad_pre, window, preferred_element_type=jnp.float32)
+                jnp.einsum("odhw,kdhw->ok", grad_pre, window, preferred_element_type=jnp.float32)
             )
     rimmed = pad_sides(grad_rim)
     rimmed_cols = column_stack(rimmed, 1, columns, lambda along_cols: 2 - along_cols)

time: 86.6 us -> 83.5 us (0.964)
  matrix products: 25.4 us -> 22.5 us
  local copies, waits for them, and re-layouts: 18.2 us -> 16.7 us
  starting transfers between devices: 24.8 us -> 26.1 us
    dot_general x9, matrix products: 10.4 us -> 7.54 us  [layer(): jnp.einsum('ok,kdhw->odhw', front_one[along_depth, along_rows], window, p...]
    reshape x1, local copies, waits for them, and re-layouts: 1.47 us -> 0.14 us  [layer(): jnp.stack(classes).reshape(2, 2, channels, class_planes, half_rows, columns)]
    all_to_all x1, starting transfers between devices: 11.1 us -> 12.4 us  [summed_over(): mine = lax.all_to_all(flat, axis, 0, 0, tiled=True).sum(0, keepdims=True)]
  transfers between devices with their start and end apart: 6 -> 6, of which waited for: 2 -> 2; matrix products, arithmetic and copies ran while one was open for 20% -> 19% of each run, Pallas kernels for 0% -> 0%
where the time goes in v16:
time: 83.5 us; the launch traced here: 83 us
  starting transfers between devices  26.1 us (31%)
  matrix products  22.5 us (27%)
  local copies, waits for them, and re-layouts  16.7 us (20%)
  waiting for transfers between devices  10.5 us (13%)
  other arithmetic  5.96 us (7%)
  between operations  1.21 us (1%)
    all_to_all x1, starting transfers between devices, summed_over(): mine = lax.all_to_all(flat, axis, 0, 0, tiled=True).sum(0, keepdims=True)  12.4 us
    ppermute x2, starting transfers between devices, extended_2(): before = lax.ppermute(last, axis, up)  7.58 us
    dot_general x9, matrix products, layer(): jnp.einsum('ok,kdhw->odhw', front_one[along_depth, along_rows], window, p...  7.54 us
    all_to_all x1, waiting for transfers between devices, summed_over(): lax.all_to_all(jnp.broadcast_to(mine, flat.shape), axis, 0, 0, tiled=True)  7.1 us
    dot_general x9, matrix products, layer(): jnp.einsum('odhw,kdhw->ok', grad_pre, window, preferred_element_type=jnp....  5.75 us
    unnamed x26, local copies, waits for them, and re-layouts  5.44 us
    slice x2, local copies, waits for them, and re-layouts, column_stack(): pieces.append(field[..., first:first + stride * (count - 1) + 1:stride])  3.83 us
    all_to_all x1, starting transfers between devices, summed_over(): lax.all_to_all(jnp.broadcast_to(mine, flat.shape), axis, 0, 0, tiled=True)  3.53 us
  transfers between devices with their start and end apart: 6, of which 2 were waited for; matrix products, arithmetic and copies ran while one was open for 19% of the time, Pallas kernels for 0%

profile of v16, /device:TPU:0, one launch (start us, length us, event | category | flops | bytes accessed | tf_op | source)
XLA Modules:
  0.0 83.0 jit_solution(5328839461036063229)
XLA Ops:
  0.7 0.9 %copy.97 = bf16[32,1,8,128]{3,0,2,1:T(8,128)(2,1)S(1)} copy(bf16[32,1,8,128]{3,2,1,0:T(8,128)(2,1)} %param.9) | data formatting | bytes 131072 | tf_op args[3]
  1.6 2.4 %collective-permute-start.2 = (bf16[32,1,8,128]{3,0,2,1:T(8,128)(2,1)S(1)}, bf16[32,1,8,128]{3,0,2,1:T(8,128)(2,1)S(1)}, u32[]{:S(2)}, u32[]{:S(2)}) collective-permute-start(bf16[32,1,8,128]{3,0,2,1:T(8,128)(2,1)S(1)} %copy.97), channel_id=1, source_target_pairs={{0,1},{1,2},{2,3},{3,4},{4,5},{5,6},{6,7},{7,8},{8,9},{9,10},{10,1... | collective-permute-start | bytes 196616 | tf_op jit(solution)/shard_map/ppermute | solution.py:15
  4.0 1.3 %collective-permute-start.3 = (bf16[32,1,8,128]{3,0,2,1:T(8,128)(2,1)S(1)}, bf16[32,1,8,128]{3,0,2,1:T(8,128)(2,1)S(1)}, u32[]{:S(2)}, u32[]{:S(2)}) collective-permute-start(bf16[32,1,8,128]{3,0,2,1:T(8,128)(2,1)S(1)} %copy.97), channel_id=1, source_target_pairs={{1,0},{2,1},{3,2},{4,3},{5,4},{6,5},{7,6},{8,7},{9,8},{10,9},{11,1... | collective-permute-start | bytes 196616 | tf_op jit(solution)/shard_map/ppermute | solution.py:16
  5.3 1.3 %copy.90 = bf16[32,2,16,256]{3,0,2,1:T(8,128)(2,1)S(1)} copy(bf16[32,2,16,256]{3,2,1,0:T(8,128)(2,1)} %param.6) | data formatting | bytes 1048576 | tf_op args[0]
  6.6 5.2 %collective-permute-start = (bf16[32,2,16,256]{3,0,2,1:T(8,128)(2,1)S(1)}, bf16[32,2,16,256]{3,0,2,1:T(8,128)(2,1)S(1)}, u32[]{:S(2)}, u32[]{:S(2)}) collective-permute-start(bf16[32,2,16,256]{3,0,2,1:T(8,128)(2,1)S(1)} %copy.90), channel_id=1, source_target_pairs={{0,1},{1,2},{2,3},{3,4},{4,5},{5,6},{6,7},{7,8},{8,9},{9,10},{10,1... | collective-permute-start | bytes 1572872 | tf_op jit(solution)/shard_map/ppermute | solution.py:15
  11.8 1.3 %collective-permute-start.1 = (bf16[32,2,16,256]{3,0,2,1:T(8,128)(2,1)S(1)}, bf16[32,2,16,256]{3,0,2,1:T(8,128)(2,1)S(1)}, u32[]{:S(2)}, u32[]{:S(2)}) collective-permute-start(bf16[32,2,16,256]{3,0,2,1:T(8,128)(2,1)S(1)} %copy.90), channel_id=1, source_target_pairs={{1,0},{2,1},{3,2},{4,3},{5,4},{6,5},{7,6},{8,7},{9,8},{10,9},{11,1... | collective-permute-start | bytes 1572872 | tf_op jit(solution)/shard_map/ppermute | solution.py:16
  13.1 0.7 pad_clamp_fusion
  13.8 1.5 %gather_fusion = bf16[27,32,32]{2,1,0:T(8,128)(2,1)S(1)} fusion(bf16[27,32,32]{2,1,0:T(8,128)(2,1)} %param.8, s32[1024]{0:T(1024)S(1)} %pad_clamp_fusion), kind=kCustom, calls=%fused_computation | custom fusion | bytes 110700 | tf_op jit(solution)/shard_map/gather | solution.py:134
  16.2 0.6 fusion.64
  17.5 0.4 convolution_bitcast_fusion
  18.0 0.4 convolution_bitcast_fusion.3
  18.4 0.3 convolution_bitcast_fusion.1
  18.9 0.6 convolution_bitcast_fusion.2
  19.5 0.2 pad_maximum_fusion.2
  19.9 1.7 %select_maximum_fusion = bf16[32,6,18,258]{3,0,2,1:T(8,128)(2,1)S(1)} fusion(bf16[32,2,16,256]{3,0,2,1:T(8,128)(2,1)S(1)} %collective-permute-done.1, bf16[32,2,16,256]{3,0,2,1:T(8,128)(2,1)S(1)} %copy.90, bf16[32,2,16,256]{3,0,2,1:T(8,128)(2,1)S(1)} %collective-permute-done), kind=kLoop, calls=%fused_computation.28 | loop fusion | flops 16941312 | bytes 3356160 | tf_op jit(solution)/shard_map/concatenate | solution.py:17
  21.6 1.4 %fusion.254 = (bf16[32,6,18,256]{3,0,2,1:T(8,128)(2,1)S(1)}, bf16[32,6,18,256]{3,0,2,1:T(8,128)(2,1)S(1)}, bf16[32,6,18,256]{3,0,2,1:T(8,128)(2,1)S(1)}) fusion(bf16[32,6,18,258]{3,0,2,1:T(8,128)(2,1)S(1)} %select_maximum_fusion), kind=kLoop, calls=%fused_computation.290 | loop fusion | bytes 10616832 | tf_op jit(solution)/shard_map/slice | solution.py:29
  23.0 0.4 pad_maximum_fusion
  23.4 0.6 fusion.11
  24.0 0.6 fusion.13
  24.5 0.6 fusion.15
  25.1 0.6 fusion.17
  25.6 0.6 fusion.19
  26.2 0.6 fusion.5
  26.7 0.6 fusion.7
  27.3 0.6 fusion.9
  27.9 3.1 %select_convert_fusion = (bf16[32,4,16,256]{3,0,2,1:T(8,128)(2,1)S(1)}, f32[32,4,16,256]{3,0,2,1:T(8,128)}, f32[32,4,16,256]{3,0,2,1:T(8,128)}) fusion(f32[32,4,16,256]{3,0,2,1:T(8,128)S(1)} %bitcast.523, pred[4]{0:T(512)(128)(4,1)S(1)} %compare_and_fusion, bf16[96,6,18,256]{3,0,2,1:T(8,128)(2,1)S(1)} %pad_maximum_fusion, ...), kind=kOutput, calls=%fused_computation.35 | convolution fusion | flops 110100480 | bytes 27271680 | tf_op jit(solution)/shard_map/ok,kdhw->odhw/dot_general | solution.py:82
  31.0 0.6 fusion.110
  31.6 2.4 %pad_slice_fusion.2 = (bf16[32,4,18,256]{3,0,2,1:T(8,128)(2,1)S(1)}, bf16[32,4,18,256]{3,0,2,1:T(8,128)(2,1)}, bf16[32,4,18,256]{3,0,2,1:T(8,128)(2,1)}) fusion(bf16[32,4,16,256]{3,0,2,1:T(8,128)(2,1)S(1)} %get-tuple-element.23), kind=kLoop, calls=%fused_computation.39 | loop fusion | bytes 4587520 | tf_op jit(solution)/shard_map/slice | solution.py:29
  34.0 0.6 fusion.116
  34.6 0.6 fusion.122
  35.3 0.6 fusion.128
  35.9 0.6 fusion.134
  36.6 0.6 fusion.140
  37.2 0.6 fusion.146
  37.9 0.6 fusion.152
  38.5 0.6 fusion.158
  39.2 0.3 copy-done
  39.5 0.6 copy-done.1
  40.1 0.5 fusion.63
  40.7 0.7 fusion.65
  41.3 0.2 copy.94
  43.2 1.0 %all_to_all.13 = f32[16,1,3456]{2,1,0:T(1,128)} reshape(f32[2,9,32,96]{3,2,1,0:T(8,128)S(1)} %pad_maximum_fusion.3) | data formatting | bytes 442368 | tf_op jit(solution)/shard_map/all_to_all | solution.py:38
  44.2 12.4 %all-to-all-start = ((f32[16,1,3456]{2,1,0:T(1,128)}), f32[16,1,3456]{2,1,0:T(1,128)S(1)}, u32[]{:S(2)}, u32[]{:S(2)}) async-start(f32[16,1,3456]{2,1,0:T(1,128)} %all_to_all.13), calls=%async_computation | async-start | bytes 442368 | tf_op jit(solution)/shard_map/all_to_all | solution.py:38
  56.6 1.8 %pad_maximum_fusion.1 = bf16[96,4,18,256]{3,0,2,1:T(8,128)(2,1)S(1)} fusion(bf16[32,4,18,256]{3,0,2,1:T(8,128)(2,1)} %get-tuple-element.53, bf16[32,4,18,256]{3,0,2,1:T(8,128)(2,1)} %get-tuple-element.52, bf16[32,4,18,256]{3,0,2,1:T(8,128)(2,1)S(1)} %get-tuple-element.51), kind=kLoop, calls=%fused_computation.9 | loop fusion | flops 10616832 | bytes 7077888 | tf_op jit(solution)/shard_map/concatenate | solution.py:30
  58.4 0.3 fusion.58
  58.8 0.4 fusion.66
  59.1 0.4 fusion.69
  59.5 0.4 fusion.72
  59.8 0.4 fusion.75
  60.2 0.4 fusion.78
  60.6 0.4 fusion.81
  60.9 0.4 fusion.84
  62.2 0.4 fusion.93
  62.6 3.4 %all-to-all-done = f32[16,1,3456]{2,1,0:T(1,128)S(1)} async-done(((f32[16,1,3456]{2,1,0:T(1,128)}), f32[16,1,3456]{2,1,0:T(1,128)S(1)}, u32[]{:S(2)}, u32[]{:S(2)}) %all-to-all-start) | async-done | bytes 221216 | tf_op jit(solution)/shard_map/all_to_all | solution.py:38
  66.1 0.8 broadcast_in_dim.35
  66.9 3.5 %all-to-all-start.1 = ((f32[16,1,3456]{2,1,0:T(1,128)}), f32[16,1,3456]{2,1,0:T(1,128)S(1)}, u32[]{:S(2)}, u32[]{:S(2)}) async-start(f32[16,1,3456]{2,1,0:T(1,128)} %broadcast_in_dim.35), calls=%async_computation.1 | async-start | bytes 442368 | tf_op jit(solution)/shard_map/all_to_all | solution.py:39
  70.6 1.1 %copy.119 = bf16[32,2,16,256]{3,2,1,0:T(8,128)(2,1)} copy(bf16[32,2,16,256]{3,0,2,1:T(8,128)(2,1)S(1)} %fusion.93) | data formatting | bytes 1048576
  72.0 0.7 copy.118
  72.7 7.1 %all-to-all-done.1 = f32[16,1,3456]{2,1,0:T(1,128)S(1)} async-done(((f32[16,1,3456]{2,1,0:T(1,128)}), f32[16,1,3456]{2,1,0:T(1,128)S(1)}, u32[]{:S(2)}, u32[]{:S(2)}) %all-to-all-start.1) | async-done | bytes 221216 | tf_op jit(solution)/shard_map/all_to_all | solution.py:39
  79.8 0.5 reduce.1
  80.3 0.7 reshape_reshape_reshape.3
  81.0 0.3 fusion.255
  81.3 0.8 copy.116
  82.1 0.8 copy.117
  (62 shorter events, 4.9 us)
Async XLA Ops:
  0.6 15.2 %copy-start.4 = (bf16[27,32,32]{2,1,0:T(8,128)(2,1)S(1)}, bf16[27,32,32]{2,1,0:T(8,128)(2,1)}, u32[]{:S(2)}) copy-start(bf16[27,32,32]{2,1,0:T(8,128)(2,1)} %param.8) | copy-start | bytes 165892
  0.6 14.7 %copy-start.3 = (bf16[27,32,32]{2,1,0:T(8,128)(2,1)S(1)}, bf16[27,32,32]{2,1,0:T(8,128)(2,1)}, u32[]{:S(2)}) copy-start(bf16[27,32,32]{2,1,0:T(8,128)(2,1)} %param.7) | copy-start | bytes 165892
  1.6 14.6 %collective-permute-start.2 = (bf16[32,1,8,128]{3,0,2,1:T(8,128)(2,1)S(1)}, bf16[32,1,8,128]{3,0,2,1:T(8,128)(2,1)S(1)}, u32[]{:S(2)}, u32[]{:S(2)}) collective-permute-start(bf16[32,1,8,128]{3,0,2,1:T(8,128)(2,1)S(1)} %copy.97), channel_id=1, source_target_pairs={{0,1},{1,2},{2,3},{3,4},{4,5},{5,6},{6,7},{7,8},{8,9},{9,10},{10,1... | collective-permute-start | bytes 196616 | tf_op jit(solution)/shard_map/ppermute | solution.py:15
  4.0 12.2 %collective-permute-start.3 = (bf16[32,1,8,128]{3,0,2,1:T(8,128)(2,1)S(1)}, bf16[32,1,8,128]{3,0,2,1:T(8,128)(2,1)S(1)}, u32[]{:S(2)}, u32[]{:S(2)}) collective-permute-start(bf16[32,1,8,128]{3,0,2,1:T(8,128)(2,1)S(1)} %copy.97), channel_id=1, source_target_pairs={{1,0},{2,1},{3,2},{4,3},{5,4},{6,5},{7,6},{8,7},{9,8},{10,9},{11,1... | collective-permute-start | bytes 196616 | tf_op jit(solution)/shard_map/ppermute | solution.py:16
  6.6 13.3 %collective-permute-start = (bf16[32,2,16,256]{3,0,2,1:T(8,128)(2,1)S(1)}, bf16[32,2,16,256]{3,0,2,1:T(8,128)(2,1)S(1)}, u32[]{:S(2)}, u32[]{:S(2)}) collective-permute-start(bf16[32,2,16,256]{3,0,2,1:T(8,128)(2,1)S(1)} %copy.90), channel_id=1, source_target_pairs={{0,1},{1,2},{2,3},{3,4},{4,5},{5,6},{6,7},{7,8},{8,9},{9,10},{10,1... | collective-permute-start | bytes 1572872 | tf_op jit(solution)/shard_map/ppermute | solution.py:15
  11.8 8.1 %collective-permute-start.1 = (bf16[32,2,16,256]{3,0,2,1:T(8,128)(2,1)S(1)}, bf16[32,2,16,256]{3,0,2,1:T(8,128)(2,1)S(1)}, u32[]{:S(2)}, u32[]{:S(2)}) collective-permute-start(bf16[32,2,16,256]{3,0,2,1:T(8,128)(2,1)S(1)} %copy.90), channel_id=1, source_target_pairs={{1,0},{2,1},{3,2},{4,3},{5,4},{6,5},{7,6},{8,7},{9,8},{10,9},{11,1... | collective-permute-start | bytes 1572872 | tf_op jit(solution)/shard_map/ppermute | solution.py:16
  15.3 1.5 %copy-start.2 = (bf16[27,32,32]{2,1,0:T(8,128)(2,1)}, bf16[27,32,32]{2,1,0:T(8,128)(2,1)S(1)}, u32[]{:S(2)}) copy-start(bf16[27,32,32]{2,1,0:T(8,128)(2,1)S(1)} %gather_fusion) | copy-start | bytes 165892
  17.5 0.9 %slice-start.1 = ((bf16[27,32,32]{2,1,0:T(8,128)(2,1)}), bf16[3,32,32]{2,1,0:T(8,128)(2,1)S(1)}, s32[]{:S(2)}) async-start(bf16[27,32,32]{2,1,0:T(8,128)(2,1)} %copy-done.2), calls=%async_computation.3 | async-start | bytes 49152 | tf_op jit(solution)/shard_map/slice | solution.py:153
  18.0 0.9 %slice-start = ((bf16[27,32,32]{2,1,0:T(8,128)(2,1)}), bf16[12,32,32]{2,1,0:T(8,128)(2,1)S(1)}, s32[]{:S(2)}) async-start(bf16[27,32,32]{2,1,0:T(8,128)(2,1)} %copy-done.2), calls=%async_computation.2 | async-start | bytes 196608 | tf_op jit(solution)/shard_map/slice | solution.py:153
  37.9 1.6 %copy-start = (f32[32,4,16,256]{3,0,2,1:T(8,128)S(1)}, f32[32,4,16,256]{3,0,2,1:T(8,128)}, u32[]{:S(2)}) copy-start(f32[32,4,16,256]{3,0,2,1:T(8,128)} %get-tuple-element.24) | copy-start | bytes 6291460
  37.9 2.3 %copy-start.1 = (f32[32,4,16,256]{3,0,2,1:T(8,128)S(1)}, f32[32,4,16,256]{3,0,2,1:T(8,128)}, u32[]{:S(2)}) copy-start(f32[32,4,16,256]{3,0,2,1:T(8,128)} %get-tuple-element.56) | copy-start | bytes 6291460
  40.6 0.9 %copy-start.5 = (bf16[32,1,8,128]{3,2,1,0:T(8,128)(2,1)S(1)}, bf16[32,1,8,128]{3,2,1,0:T(8,128)(2,1)}, u32[]{:S(2)}) copy-start(bf16[32,1,8,128]{3,2,1,0:T(8,128)(2,1)} %param.9) | copy-start | bytes 196612
  44.2 21.7 %all-to-all-start = ((f32[16,1,3456]{2,1,0:T(1,128)}), f32[16,1,3456]{2,1,0:T(1,128)S(1)}, u32[]{:S(2)}, u32[]{:S(2)}) async-start(f32[16,1,3456]{2,1,0:T(1,128)} %all_to_all.13), calls=%async_computation | async-start | bytes 442368 | tf_op jit(solution)/shard_map/all_to_all | solution.py:38
  66.9 12.9 %all-to-all-start.1 = ((f32[16,1,3456]{2,1,0:T(1,128)}), f32[16,1,3456]{2,1,0:T(1,128)S(1)}, u32[]{:S(2)}, u32[]{:S(2)}) async-start(f32[16,1,3456]{2,1,0:T(1,128)} %broadcast_in_dim.35), calls=%async_computation.1 | async-start | bytes 442368 | tf_op jit(solution)/shard_map/all_to_all | solution.py:39

commit v17 on v16

--- a/solution.py
+++ b/solution.py
@@ -1,5 +1,4 @@
 import jax
-import numpy as np
 import jax.numpy as jnp
 from jax import lax
 from jax.sharding import PartitionSpec as P
@@ -131,7 +130,7 @@
                 for tap_row, _ in row_taps[row_parity]:
                     for tap_col in range(3):
                         order.append(9 * tap_depth + 3 * tap_row + tap_col)
-    ordered_two = weight_two[np.array(order)]
+    ordered_two = jnp.concatenate([weight_two[tap : tap + 1] for tap in order], 0)
     taken = 0
     classes = []
     for depth_slot in range(2):
@@ -190,7 +189,8 @@
                 preferred_element_type=jnp.float32,
             )
     grad_volume = grad_volume.astype(jnp.bfloat16)
-    summed = summed_over(jnp.stack([jnp.stack(terms_one), jnp.stack(terms_two)]), "slab")
+    stacked_terms = jnp.stack(terms_one + terms_two).reshape((2, 9) + terms_one[0].shape)
+    summed = summed_over(stacked_terms, "slab")
     grad_one, grad_two = fold_terms(summed)
     return (output.astype(jnp.bfloat16), grad_volume, grad_one, grad_two)
 

time: 83.5 us -> 83.6 us (level)
  local copies, waits for them, and re-layouts: 16.7 us -> 17.7 us
    gather x1 -> x0, local copies, waits for them, and re-layouts: 1.52 us -> none  [layer(): ordered_two = weight_two[np.array(order)]]
    slice x5 -> x2, local copies, waits for them, and re-layouts: 0.19 us -> 1.69 us  [layer(): ordered_two = jnp.concatenate([weight_two[tap:tap + 1] for tap in order], 0)]
    reshape x4, local copies, waits for them, and re-layouts: 0.64 us -> 1.57 us  [forward_kernel(): weights.reshape(3, 3, 3, size, size).transpose(0, 1, 3, 2, 4)]
    unnamed x26 -> x24, local copies, waits for them, and re-layouts: 5.44 us -> 5.43 us
  transfers between devices with their start and end apart: 6 -> 6, of which waited for: 2 -> 2; matrix products, arithmetic and copies ran while one was open for 19% -> 20% of each run, Pallas kernels for 0% -> 0%
where the time goes in v17:
time: 83.6 us; the launch traced here: 82.9 us
  starting transfers between devices  25.8 us (31%)
  matrix products  22.5 us (27%)
  local copies, waits for them, and re-layouts  17.7 us (21%)
  waiting for transfers between devices  10.5 us (13%)
  other arithmetic  5.3 us (6%)
  between operations  1.16 us (1%)
    all_to_all x1, starting transfers between devices, summed_over(): mine = lax.all_to_all(flat, axis, 0, 0, tiled=True).sum(0, keepdims=True)  12.1 us
    ppermute x2, starting transfers between devices, extended_2(): before = lax.ppermute(last, axis, up)  7.58 us
    dot_general x9, matrix products, layer(): jnp.einsum('ok,kdhw->odhw', front_one[along_depth, along_rows], window, p...  7.56 us
    all_to_all x1, waiting for transfers between devices, summed_over(): lax.all_to_all(jnp.broadcast_to(mine, flat.shape), axis, 0, 0, tiled=True)  7.1 us
    dot_general x9, matrix products, layer(): jnp.einsum('odhw,kdhw->ok', grad_pre, window, preferred_element_type=jnp....  5.75 us
    unnamed x24, local copies, waits for them, and re-layouts  5.43 us
    slice x2, local copies, waits for them, and re-layouts, column_stack(): pieces.append(field[..., first:first + stride * (count - 1) + 1:stride])  3.83 us
    all_to_all x1, starting transfers between devices, summed_over(): lax.all_to_all(jnp.broadcast_to(mine, flat.shape), axis, 0, 0, tiled=True)  3.53 us
  transfers between devices with their start and end apart: 6, of which 2 were waited for; matrix products, arithmetic and copies ran while one was open for 20% of the time, Pallas kernels for 0%

profile of v17, /device:TPU:0, one launch (start us, length us, event | category | flops | bytes accessed | tf_op | source)
XLA Modules:
  0.0 82.9 jit_solution(2384241088491259181)
XLA Ops:
  0.7 0.9 %copy.95 = bf16[32,1,8,128]{3,0,2,1:T(8,128)(2,1)S(1)} copy(bf16[32,1,8,128]{3,2,1,0:T(8,128)(2,1)} %param.7) | data formatting | bytes 131072 | tf_op args[3]
  1.6 2.4 %collective-permute-start.2 = (bf16[32,1,8,128]{3,0,2,1:T(8,128)(2,1)S(1)}, bf16[32,1,8,128]{3,0,2,1:T(8,128)(2,1)S(1)}, u32[]{:S(2)}, u32[]{:S(2)}) collective-permute-start(bf16[32,1,8,128]{3,0,2,1:T(8,128)(2,1)S(1)} %copy.95), channel_id=1, source_target_pairs={{0,1},{1,2},{2,3},{3,4},{4,5},{5,6},{6,7},{7,8},{8,9},{9,10},{10,1... | collective-permute-start | bytes 196616 | tf_op jit(solution)/shard_map/ppermute | solution.py:14
  4.0 1.3 %collective-permute-start.3 = (bf16[32,1,8,128]{3,0,2,1:T(8,128)(2,1)S(1)}, bf16[32,1,8,128]{3,0,2,1:T(8,128)(2,1)S(1)}, u32[]{:S(2)}, u32[]{:S(2)}) collective-permute-start(bf16[32,1,8,128]{3,0,2,1:T(8,128)(2,1)S(1)} %copy.95), channel_id=1, source_target_pairs={{1,0},{2,1},{3,2},{4,3},{5,4},{6,5},{7,6},{8,7},{9,8},{10,9},{11,1... | collective-permute-start | bytes 196616 | tf_op jit(solution)/shard_map/ppermute | solution.py:15
  5.3 1.3 %copy.88 = bf16[32,2,16,256]{3,0,2,1:T(8,128)(2,1)S(1)} copy(bf16[32,2,16,256]{3,2,1,0:T(8,128)(2,1)} %param.4) | data formatting | bytes 1048576 | tf_op args[0]
  6.6 5.2 %collective-permute-start = (bf16[32,2,16,256]{3,0,2,1:T(8,128)(2,1)S(1)}, bf16[32,2,16,256]{3,0,2,1:T(8,128)(2,1)S(1)}, u32[]{:S(2)}, u32[]{:S(2)}) collective-permute-start(bf16[32,2,16,256]{3,0,2,1:T(8,128)(2,1)S(1)} %copy.88), channel_id=1, source_target_pairs={{0,1},{1,2},{2,3},{3,4},{4,5},{5,6},{6,7},{7,8},{8,9},{9,10},{10,1... | collective-permute-start | bytes 1572872 | tf_op jit(solution)/shard_map/ppermute | solution.py:14
  11.8 1.3 %collective-permute-start.1 = (bf16[32,2,16,256]{3,0,2,1:T(8,128)(2,1)S(1)}, bf16[32,2,16,256]{3,0,2,1:T(8,128)(2,1)S(1)}, u32[]{:S(2)}, u32[]{:S(2)}) collective-permute-start(bf16[32,2,16,256]{3,0,2,1:T(8,128)(2,1)S(1)} %copy.88), channel_id=1, source_target_pairs={{1,0},{2,1},{3,2},{4,3},{5,4},{6,5},{7,6},{8,7},{9,8},{10,9},{11,1... | collective-permute-start | bytes 1572872 | tf_op jit(solution)/shard_map/ppermute | solution.py:15
  13.1 0.9 %fusion.256 = (bf16[3,32,32]{2,1,0:T(8,128)(2,1)S(1)}, bf16[3,32,32]{2,1,0:T(8,128)(2,1)S(1)}, bf16[3,32,32]{2,1,0:T(8,128)(2,1)S(1)}, bf16[3,32,32]{2,1,0:T(8,1...) fusion(bf16[27,32,32]{2,1,0:T(8,128)(2,1)} %param.6), kind=kLoop, calls=%fused_computation.292 | loop fusion | bytes 98304 | tf_op jit(solution)/shard_map/slice | solution.py:133
  14.0 0.8 slice.412
  14.8 1.1 %copy.186 = bf16[3,3,3,32,32]{4,2,3,1,0:T(4,128)(2,1)S(1)} copy(bf16[3,3,3,32,32]{4,3,2,1,0:T(8,128)(2,1)} %bitcast.544) | data formatting | bytes 110592 | tf_op jit(solution)/shard_map/reshape | solution.py:45
  16.7 0.6 fusion.64
  18.0 0.4 convolution_bitcast_fusion.1
  18.4 0.4 convolution_bitcast_fusion.3
  18.8 0.3 convolution_bitcast_fusion
  19.1 0.6 convolution_bitcast_fusion.2
  20.2 1.7 %select_maximum_fusion = bf16[32,6,18,258]{3,0,2,1:T(8,128)(2,1)S(1)} fusion(bf16[32,2,16,256]{3,0,2,1:T(8,128)(2,1)S(1)} %collective-permute-done.1, bf16[32,2,16,256]{3,0,2,1:T(8,128)(2,1)S(1)} %copy.88, bf16[32,2,16,256]{3,0,2,1:T(8,128)(2,1)S(1)} %collective-permute-done), kind=kLoop, calls=%fused_computation.27 | loop fusion | flops 16941312 | bytes 3356160 | tf_op jit(solution)/shard_map/concatenate | solution.py:16
  21.8 1.4 %fusion.254 = (bf16[32,6,18,256]{3,0,2,1:T(8,128)(2,1)S(1)}, bf16[32,6,18,256]{3,0,2,1:T(8,128)(2,1)S(1)}, bf16[32,6,18,256]{3,0,2,1:T(8,128)(2,1)S(1)}) fusion(bf16[32,6,18,258]{3,0,2,1:T(8,128)(2,1)S(1)} %select_maximum_fusion), kind=kLoop, calls=%fused_computation.290 | loop fusion | bytes 10616832 | tf_op jit(solution)/shard_map/slice | solution.py:28
  23.2 0.4 pad_maximum_fusion
  23.7 0.6 fusion.11
  24.2 0.6 fusion.13
  24.8 0.6 fusion.15
  25.3 0.6 fusion.17
  25.9 0.6 fusion.19
  26.4 0.6 fusion.5
  27.0 0.6 fusion.7
  27.6 0.6 fusion.9
  28.1 3.1 %select_convert_fusion = (bf16[32,4,16,256]{3,0,2,1:T(8,128)(2,1)S(1)}, f32[32,4,16,256]{3,0,2,1:T(8,128)}, f32[32,4,16,256]{3,0,2,1:T(8,128)}) fusion(f32[32,4,16,256]{3,0,2,1:T(8,128)S(1)} %bitcast.521, pred[4]{0:T(512)(128)(4,1)S(1)} %compare_and_fusion, bf16[96,6,18,256]{3,0,2,1:T(8,128)(2,1)S(1)} %pad_maximum_fusion, ...), kind=kOutput, calls=%fused_computation.34 | convolution fusion | flops 110100480 | bytes 27271680 | tf_op jit(solution)/shard_map/ok,kdhw->odhw/dot_general | solution.py:81
  31.2 0.6 fusion.110
  31.9 2.4 %pad_slice_fusion.2 = (bf16[32,4,18,256]{3,0,2,1:T(8,128)(2,1)S(1)}, bf16[32,4,18,256]{3,0,2,1:T(8,128)(2,1)}, bf16[32,4,18,256]{3,0,2,1:T(8,128)(2,1)}) fusion(bf16[32,4,16,256]{3,0,2,1:T(8,128)(2,1)S(1)} %get-tuple-element.23), kind=kLoop, calls=%fused_computation.38 | loop fusion | bytes 4587520 | tf_op jit(solution)/shard_map/slice | solution.py:28
  34.3 0.6 fusion.116
  34.9 0.6 fusion.122
  35.6 0.6 fusion.128
  36.2 0.6 fusion.134
  36.9 0.6 fusion.140
  37.5 0.6 fusion.146
  38.2 0.6 fusion.152
  38.8 0.6 fusion.158
  39.5 0.3 copy-done
  39.8 0.6 copy-done.1
  40.4 0.5 fusion.63
  40.9 0.7 fusion.65
  41.6 0.2 copy.92
  43.5 1.0 %all_to_all.13 = f32[16,1,3456]{2,1,0:T(1,128)} reshape(f32[18,32,96]{2,1,0:T(8,128)S(1)} %fusion.98) | data formatting | bytes 442368 | tf_op jit(solution)/shard_map/all_to_all | solution.py:37
  44.5 12.1 %all-to-all-start = ((f32[16,1,3456]{2,1,0:T(1,128)}), f32[16,1,3456]{2,1,0:T(1,128)S(1)}, u32[]{:S(2)}, u32[]{:S(2)}) async-start(f32[16,1,3456]{2,1,0:T(1,128)} %all_to_all.13), calls=%async_computation | async-start | bytes 442368 | tf_op jit(solution)/shard_map/all_to_all | solution.py:37
  56.6 1.8 %pad_maximum_fusion.1 = bf16[96,4,18,256]{3,0,2,1:T(8,128)(2,1)S(1)} fusion(bf16[32,4,18,256]{3,0,2,1:T(8,128)(2,1)} %get-tuple-element.53, bf16[32,4,18,256]{3,0,2,1:T(8,128)(2,1)} %get-tuple-element.52, bf16[32,4,18,256]{3,0,2,1:T(8,128)(2,1)S(1)} %get-tuple-element.51), kind=kLoop, calls=%fused_computation.8 | loop fusion | flops 10616832 | bytes 7077888 | tf_op jit(solution)/shard_map/concatenate | solution.py:29
  58.4 0.3 fusion.58
  58.7 0.4 fusion.66
  59.1 0.4 fusion.69
  59.5 0.4 fusion.72
  59.8 0.4 fusion.75
  60.2 0.4 fusion.78
  60.6 0.4 fusion.81
  60.9 0.4 fusion.84
  62.2 0.4 fusion.93
  62.6 3.4 %all-to-all-done = f32[16,1,3456]{2,1,0:T(1,128)S(1)} async-done(((f32[16,1,3456]{2,1,0:T(1,128)}), f32[16,1,3456]{2,1,0:T(1,128)S(1)}, u32[]{:S(2)}, u32[]{:S(2)}) %all-to-all-start) | async-done | bytes 221216 | tf_op jit(solution)/shard_map/all_to_all | solution.py:37
  66.1 0.8 broadcast_in_dim.31
  66.9 3.5 %all-to-all-start.1 = ((f32[16,1,3456]{2,1,0:T(1,128)}), f32[16,1,3456]{2,1,0:T(1,128)S(1)}, u32[]{:S(2)}, u32[]{:S(2)}) async-start(f32[16,1,3456]{2,1,0:T(1,128)} %broadcast_in_dim.31), calls=%async_computation.1 | async-start | bytes 442368 | tf_op jit(solution)/shard_map/all_to_all | solution.py:38
  70.6 1.1 %copy.117 = bf16[32,2,16,256]{3,2,1,0:T(8,128)(2,1)} copy(bf16[32,2,16,256]{3,0,2,1:T(8,128)(2,1)S(1)} %fusion.93) | data formatting | bytes 1048576
  72.0 0.7 copy.116
  72.7 7.1 %all-to-all-done.1 = f32[16,1,3456]{2,1,0:T(1,128)S(1)} async-done(((f32[16,1,3456]{2,1,0:T(1,128)}), f32[16,1,3456]{2,1,0:T(1,128)S(1)}, u32[]{:S(2)}, u32[]{:S(2)}) %all-to-all-start.1) | async-done | bytes 221216 | tf_op jit(solution)/shard_map/all_to_all | solution.py:38
  79.8 0.5 reduce.1
  80.3 0.7 reshape_reshape_reshape.3
  81.0 0.3 fusion.255
  81.3 0.8 copy.114
  82.1 0.8 copy.115
  (56 shorter events, 4.8 us)
Async XLA Ops:
  0.6 15.6 %copy-start.2 = (bf16[27,32,32]{2,1,0:T(8,128)(2,1)S(1)}, bf16[27,32,32]{2,1,0:T(8,128)(2,1)}, u32[]{:S(2)}) copy-start(bf16[27,32,32]{2,1,0:T(8,128)(2,1)} %param.6) | copy-start | bytes 165892
  0.6 15.4 %copy-start.3 = (bf16[27,32,32]{2,1,0:T(8,128)(2,1)S(1)}, bf16[27,32,32]{2,1,0:T(8,128)(2,1)}, u32[]{:S(2)}) copy-start(bf16[27,32,32]{2,1,0:T(8,128)(2,1)} %param.5) | copy-start | bytes 165892
  1.6 15.1 %collective-permute-start.2 = (bf16[32,1,8,128]{3,0,2,1:T(8,128)(2,1)S(1)}, bf16[32,1,8,128]{3,0,2,1:T(8,128)(2,1)S(1)}, u32[]{:S(2)}, u32[]{:S(2)}) collective-permute-start(bf16[32,1,8,128]{3,0,2,1:T(8,128)(2,1)S(1)} %copy.95), channel_id=1, source_target_pairs={{0,1},{1,2},{2,3},{3,4},{4,5},{5,6},{6,7},{7,8},{8,9},{9,10},{10,1... | collective-permute-start | bytes 196616 | tf_op jit(solution)/shard_map/ppermute | solution.py:14
  4.0 12.7 %collective-permute-start.3 = (bf16[32,1,8,128]{3,0,2,1:T(8,128)(2,1)S(1)}, bf16[32,1,8,128]{3,0,2,1:T(8,128)(2,1)S(1)}, u32[]{:S(2)}, u32[]{:S(2)}) collective-permute-start(bf16[32,1,8,128]{3,0,2,1:T(8,128)(2,1)S(1)} %copy.95), channel_id=1, source_target_pairs={{1,0},{2,1},{3,2},{4,3},{5,4},{6,5},{7,6},{8,7},{9,8},{10,9},{11,1... | collective-permute-start | bytes 196616 | tf_op jit(solution)/shard_map/ppermute | solution.py:15
  6.6 13.5 %collective-permute-start = (bf16[32,2,16,256]{3,0,2,1:T(8,128)(2,1)S(1)}, bf16[32,2,16,256]{3,0,2,1:T(8,128)(2,1)S(1)}, u32[]{:S(2)}, u32[]{:S(2)}) collective-permute-start(bf16[32,2,16,256]{3,0,2,1:T(8,128)(2,1)S(1)} %copy.88), channel_id=1, source_target_pairs={{0,1},{1,2},{2,3},{3,4},{4,5},{5,6},{6,7},{7,8},{8,9},{9,10},{10,1... | collective-permute-start | bytes 1572872 | tf_op jit(solution)/shard_map/ppermute | solution.py:14
  11.8 8.3 %collective-permute-start.1 = (bf16[32,2,16,256]{3,0,2,1:T(8,128)(2,1)S(1)}, bf16[32,2,16,256]{3,0,2,1:T(8,128)(2,1)S(1)}, u32[]{:S(2)}, u32[]{:S(2)}) collective-permute-start(bf16[32,2,16,256]{3,0,2,1:T(8,128)(2,1)S(1)} %copy.88), channel_id=1, source_target_pairs={{1,0},{2,1},{3,2},{4,3},{5,4},{6,5},{7,6},{8,7},{9,8},{10,9},{11,1... | collective-permute-start | bytes 1572872 | tf_op jit(solution)/shard_map/ppermute | solution.py:15
  38.2 1.6 %copy-start = (f32[32,4,16,256]{3,0,2,1:T(8,128)S(1)}, f32[32,4,16,256]{3,0,2,1:T(8,128)}, u32[]{:S(2)}) copy-start(f32[32,4,16,256]{3,0,2,1:T(8,128)} %get-tuple-element.24) | copy-start | bytes 6291460
  38.2 2.3 %copy-start.1 = (f32[32,4,16,256]{3,0,2,1:T(8,128)S(1)}, f32[32,4,16,256]{3,0,2,1:T(8,128)}, u32[]{:S(2)}) copy-start(f32[32,4,16,256]{3,0,2,1:T(8,128)} %get-tuple-element.62) | copy-start | bytes 6291460
  40.9 0.9 %copy-start.4 = (bf16[32,1,8,128]{3,2,1,0:T(8,128)(2,1)S(1)}, bf16[32,1,8,128]{3,2,1,0:T(8,128)(2,1)}, u32[]{:S(2)}) copy-start(bf16[32,1,8,128]{3,2,1,0:T(8,128)(2,1)} %param.7) | copy-start | bytes 196612
  44.5 21.5 %all-to-all-start = ((f32[16,1,3456]{2,1,0:T(1,128)}), f32[16,1,3456]{2,1,0:T(1,128)S(1)}, u32[]{:S(2)}, u32[]{:S(2)}) async-start(f32[16,1,3456]{2,1,0:T(1,128)} %all_to_all.13), calls=%async_computation | async-start | bytes 442368 | tf_op jit(solution)/shard_map/all_to_all | solution.py:37
  66.9 12.9 %all-to-all-start.1 = ((f32[16,1,3456]{2,1,0:T(1,128)}), f32[16,1,3456]{2,1,0:T(1,128)S(1)}, u32[]{:S(2)}, u32[]{:S(2)}) async-start(f32[16,1,3456]{2,1,0:T(1,128)} %broadcast_in_dim.31), calls=%async_computation.1 | async-start | bytes 442368 | tf_op jit(solution)/shard_map/all_to_all | solution.py:38
